TPU v7x, 32 devices: a whole 2x2x4 slice. The times are simulated.
32 devices in a mesh: wide: 16 (over z, y, core), narrow: 2 (over x).
Axes of the slice: x: 2, y: 2, z: 4, core: 2. Of those that a mesh axis runs over, the one named last changes fastest.
Arguments:
- inputs: bfloat16 [32, 680, 1024], P(('wide', 'narrow')), may hold values from -6 to 6
- condition: bfloat16 [32, 1024], P(('wide', 'narrow')), may hold values from -6 to 6
- scale_tokens: int32 [10], replicated, may hold values from 1 to 256, 680 in all
- w_ada: bfloat16 [1024, 6144], P(('wide', 'narrow')), may hold values from -0.1875 to 0.1875
- bias_ada: bfloat16 [6144], P(('wide', 'narrow')), may hold values from -3 to 3
- w_qkv: bfloat16 [1024, 3072], P(('wide', 'narrow')), may hold values from -0.1875 to 0.1875
- bias_query: bfloat16 [1024], P(('wide', 'narrow')), may hold values from -3 to 3
- bias_value: bfloat16 [1024], P(('wide', 'narrow')), may hold values from -3 to 3
- gain_query: bfloat16 [1024], P(('wide', 'narrow')), may hold values from 1 to 2
- gain_key: bfloat16 [1024], P(('wide', 'narrow')), may hold values from 1 to 2
- w_proj: bfloat16 [1024, 1024], P(('wide', 'narrow')), may hold values from -0.75 to 0.75
- bias_proj: bfloat16 [1024], P(('wide', 'narrow')), may hold values from -3 to 3
- w_up: bfloat16 [1024, 4096], P(('wide', 'narrow')), may hold values from -0.1875 to 0.1875
- bias_up: bfloat16 [4096], P(('wide', 'narrow')), may hold values from -3 to 3
- w_down: bfloat16 [4096, 1024], P(('wide', 'narrow')), may hold values from -0.1875 to 0.1875
- bias_down: bfloat16 [1024], P(('wide', 'narrow')), may hold values from -3 to 3
- cotangent: bfloat16 [32, 680, 1024], P(('wide', 'narrow')), may hold values from -6 to 6
Outputs:
- layer_output: bfloat16 [32, 680, 1024], P(('wide', 'narrow'))
- input_grad: float32 [32, 680, 1024], P(('wide', 'narrow'))
- condition_grad: float32 [32, 1024], P(('wide', 'narrow'))
- w_ada_grad: float32 [1024, 6144], P(('wide', 'narrow'))
- bias_ada_grad: float32 [6144], P(('wide', 'narrow'))
- w_qkv_grad: float32 [1024, 3072], P(('wide', 'narrow'))
- bias_query_grad: float32 [1024], P(('wide', 'narrow'))
- bias_value_grad: float32 [1024], P(('wide', 'narrow'))
- gain_query_grad: float32 [1024], P(('wide', 'narrow'))
- gain_key_grad: float32 [1024], P(('wide', 'narrow'))
- w_proj_grad: float32 [1024, 1024], P(('wide', 'narrow'))
- bias_proj_grad: float32 [1024], P(('wide', 'narrow'))
- w_up_grad: float32 [1024, 4096], P(('wide', 'narrow'))
- bias_up_grad: float32 [4096], P(('wide', 'narrow'))
- w_down_grad: float32 [4096, 1024], P(('wide', 'narrow'))
- bias_down_grad: float32 [1024], P(('wide', 'narrow'))
Inputs may be any that keep to these rules, and one draw needn't show every extreme that they name: `scale_tokens`: the 10 counts sum to 680; the largest is 256; they may come in any order.
All inputs are finite; a program needn't handle non-finite values.
Results may differ from a plain program's by a relative error of at most 0.02.
Values may be sent and summed in bfloat16 or wider, within the bound.
No kernel may reach another device: no remote copies, remote signals or barrier semaphores. Data moves between devices by JAX's collectives and lax.ppermute only.
A program may use at most 256 MiB of HBM per device.

v0:
```python
import jax
import jax.numpy as jnp
from jax import lax
from jax.sharding import PartitionSpec as P

HEADS = 16
HEAD_DIM = 64
SEQ_LEN = 680


EPSILON = 1e-06
MASKED = -1000000000.0


def layer_norm(values):
    centred = values - jnp.mean(values, axis=-1, keepdims=True)
    return centred * lax.rsqrt(jnp.mean(centred * centred, axis=-1, keepdims=True) + EPSILON)


def modulate(values, scaling, offset):
    return layer_norm(values) * (1.0 + scaling[:, None, :]) + offset[:, None, :]


def head_norm(values, channel_gain):
    shaped = values.reshape(values.shape[0], values.shape[1], HEADS, HEAD_DIM)
    scaled = shaped * lax.rsqrt(jnp.mean(shaped * shaped, axis=-1, keepdims=True) + EPSILON)
    return scaled * channel_gain.reshape(HEADS, HEAD_DIM)


def gelu_tanh(values):
    return jax.nn.gelu(values, approximate=True)


def block_mask(scale_tokens):
    block_ends = jnp.cumsum(scale_tokens)
    places = jnp.arange(SEQ_LEN, dtype=jnp.int32)
    limits = jnp.min(
        jnp.where(block_ends[None, :] > places[:, None], block_ends[None, :], SEQ_LEN), axis=1
    )
    return places[None, :] < limits[:, None]


def matmul_rows(first_operand, second_operand):
    return jnp.einsum(
        "fyg,gq->fyq", first_operand, second_operand, preferred_element_type=jnp.float32
    )


def matmul_back(first_operand, second_operand):
    return jnp.einsum(
        "rfw,uw->rfu", first_operand, second_operand, preferred_element_type=jnp.float32
    )


def weight_grad(first_operand, second_operand):
    return jnp.einsum(
        "crk,cre->ke", first_operand, second_operand, preferred_element_type=jnp.float32
    )


def split_owners(members, wide_count, narrow_count):
    return tuple(
        (
            member.reshape(
                (wide_count, narrow_count, member.shape[0] // (wide_count * narrow_count))
                + member.shape[1:]
            )
            for member in members
        )
    )


def join_owners(members):
    return tuple((member.reshape(member.shape[2:]) for member in members))


def masked_scores(query_sequence, key_sequence, allowed):
    scores = jnp.einsum(
        "nkz,vkz->knv", query_sequence, key_sequence, preferred_element_type=jnp.float32
    ) * HEAD_DIM ** (-0.5)
    return jnp.where(allowed[None], scores, MASKED)


def attend_forward(query_sequence, key_sequence, value_sequence, allowed):
    scores = masked_scores(query_sequence, key_sequence, allowed)
    row_max = jnp.max(scores, axis=-1, keepdims=True)
    exponent = jnp.exp(scores - row_max)
    row_total = jnp.sum(exponent, axis=-1, keepdims=True)
    probabilities_reduced = (exponent / row_total).astype(jnp.bfloat16)
    context = jnp.einsum(
        "wcv,vwn->cwn", probabilities_reduced, value_sequence, preferred_element_type=jnp.float32
    ).astype(jnp.bfloat16)
    return (context, row_max[..., 0] + jnp.log(row_total[..., 0]))


def attend_backward(
    query_sequence, key_sequence, value_sequence, logsum, context_gradient, allowed
):
    scores = masked_scores(query_sequence, key_sequence, allowed)
    attention_probabilities = jnp.exp(scores - logsum[..., None])
    prob_grad = jnp.einsum(
        "nkz,vkz->knv", context_gradient, value_sequence, preferred_element_type=jnp.float32
    )
    value_grad = jnp.einsum(
        "fgs,gfu->sfu",
        attention_probabilities.astype(jnp.bfloat16),
        context_gradient,
        preferred_element_type=jnp.float32,
    )
    score_gradient = (
        attention_probabilities
        * (prob_grad - jnp.sum(prob_grad * attention_probabilities, axis=-1, keepdims=True))
    ).astype(jnp.bfloat16)
    query_grad = jnp.einsum(
        "wcv,vwn->cwn", score_gradient, key_sequence, preferred_element_type=jnp.float32
    ) * HEAD_DIM ** (-0.5)
    key_grad = jnp.einsum(
        "fgs,gfu->sfu", score_gradient, query_sequence, preferred_element_type=jnp.float32
    ) * HEAD_DIM ** (-0.5)
    return (query_grad, key_grad, value_grad)


def shards(
    inputs,
    condition,
    scale_tokens,
    w_ada,
    bias_ada,
    w_qkv,
    bias_query,
    bias_value,
    gain_query,
    gain_key,
    w_proj,
    bias_proj,
    w_up,
    bias_up,
    w_down,
    bias_down,
    cotangent,
):
    gathered = (
        lax.all_gather(w_ada, ("wide", "narrow"), axis=0, tiled=True),
        lax.all_gather(w_qkv, ("wide", "narrow"), axis=0, tiled=True),
        lax.all_gather(w_proj, ("wide", "narrow"), axis=0, tiled=True),
        lax.all_gather(w_up, ("wide", "narrow"), axis=0, tiled=True),
        lax.all_gather(w_down, ("wide", "narrow"), axis=0, tiled=True),
        lax.all_gather(bias_ada, ("wide", "narrow"), axis=0, tiled=True),
        lax.all_gather(bias_query, ("wide", "narrow"), axis=0, tiled=True),
        lax.all_gather(bias_value, ("wide", "narrow"), axis=0, tiled=True),
        lax.all_gather(gain_query, ("wide", "narrow"), axis=0, tiled=True),
        lax.all_gather(gain_key, ("wide", "narrow"), axis=0, tiled=True),
        lax.all_gather(bias_proj, ("wide", "narrow"), axis=0, tiled=True),
        lax.all_gather(bias_up, ("wide", "narrow"), axis=0, tiled=True),
        lax.all_gather(bias_down, ("wide", "narrow"), axis=0, tiled=True),
    )
    ada_full, qkv_full, proj_full, up_full, down_full = gathered[:5]
    vectors = tuple((member.astype(jnp.float32) for member in gathered[5:]))
    ada_bias, query_bias, value_bias, query_gain, key_gain, proj_bias, up_bias, down_bias = vectors
    sequences, length, width = inputs.shape
    head_shape = (sequences, length, HEADS, HEAD_DIM)
    allowed = block_mask(scale_tokens)
    wide_count = lax.axis_size("wide")
    narrow_count = lax.axis_size("narrow")
    input_rows = inputs.astype(jnp.float32)
    cond_rows = condition.astype(jnp.float32)
    activated = jax.nn.silu(cond_rows).astype(jnp.bfloat16)
    adaptive = jnp.dot(activated, ada_full, preferred_element_type=jnp.float32) + ada_bias
    gamma_attn, gamma_mlp, scale_attn, scale_mlp, shift_attn, shift_mlp = jnp.split(
        adaptive, 6, axis=1
    )
    normed_attn = modulate(input_rows, scale_attn, shift_attn).astype(jnp.bfloat16)
    projected = matmul_rows(normed_attn, qkv_full)
    query_pre = projected[..., :width] + query_bias
    key_pre = projected[..., width : 2 * width]
    queries = head_norm(query_pre, query_gain).astype(jnp.bfloat16)
    key_rows = head_norm(key_pre, key_gain).astype(jnp.bfloat16)
    value_rows = (projected[..., 2 * width :] + value_bias).astype(jnp.bfloat16).reshape(head_shape)
    context, logsum = lax.map(
        lambda pieces: attend_forward(pieces[0], pieces[1], pieces[2], allowed),
        (queries, key_rows, value_rows),
    )
    context = context.reshape(sequences, length, width)
    attended = matmul_rows(context, proj_full) + proj_bias
    middle = input_rows + gamma_attn[:, None, :] * attended
    normed_mlp = modulate(middle, scale_mlp, shift_mlp).astype(jnp.bfloat16)
    hidden_pre = matmul_rows(normed_mlp, up_full) + up_bias
    hidden = gelu_tanh(hidden_pre).astype(jnp.bfloat16)
    branch = matmul_rows(hidden, down_full) + down_bias
    layer_output = (middle + gamma_mlp[:, None, :] * branch).astype(jnp.bfloat16)
    matrices = (
        lax.all_gather(w_ada, ("wide", "narrow"), axis=0, tiled=True),
        lax.all_gather(w_qkv, ("wide", "narrow"), axis=0, tiled=True),
        lax.all_gather(w_proj, ("wide", "narrow"), axis=0, tiled=True),
        lax.all_gather(w_up, ("wide", "narrow"), axis=0, tiled=True),
        lax.all_gather(w_down, ("wide", "narrow"), axis=0, tiled=True),
    )
    ada_back, qkv_back, proj_back, up_back, down_back = matrices
    upstream = cotangent.astype(jnp.float32)
    gamma_mlp_grad = jnp.sum(upstream * branch, axis=1)
    branch_grad = (upstream * gamma_mlp[:, None, :]).astype(jnp.bfloat16)
    down_grad = weight_grad(hidden, branch_grad)
    down_bias_grad = jnp.sum(branch_grad.astype(jnp.float32), axis=(0, 1))
    hidden_grad = matmul_back(branch_grad, down_back)
    gelu_pull = jax.vjp(gelu_tanh, hidden_pre)[1]
    pre_grad = gelu_pull(hidden_grad)[0].astype(jnp.bfloat16)
    up_grad = weight_grad(normed_mlp, pre_grad)
    up_bias_grad = jnp.sum(pre_grad.astype(jnp.float32), axis=(0, 1))
    normed_mlp_grad = matmul_back(pre_grad, up_back)
    mlp_pull = jax.vjp(modulate, middle, scale_mlp, shift_mlp)[1]
    middle_part, scale_mlp_grad, shift_mlp_grad = mlp_pull(normed_mlp_grad)
    middle_grad = upstream + middle_part
    gamma_attn_grad = jnp.sum(middle_grad * attended, axis=1)
    attended_grad = (middle_grad * gamma_attn[:, None, :]).astype(jnp.bfloat16)
    proj_grad = weight_grad(context, attended_grad)
    proj_bias_grad = jnp.sum(attended_grad.astype(jnp.float32), axis=(0, 1))
    context_gradient = (
        matmul_back(attended_grad, proj_back).astype(jnp.bfloat16).reshape(head_shape)
    )
    query_grad, key_grad, value_grad = lax.map(
        lambda pieces: attend_backward(
            pieces[0], pieces[1], pieces[2], pieces[3], pieces[4], allowed
        ),
        (queries, key_rows, value_rows, logsum, context_gradient),
    )
    query_pull = jax.vjp(head_norm, query_pre, query_gain)[1]
    query_pre_grad, query_gain_grad = query_pull(query_grad)
    key_pull = jax.vjp(head_norm, key_pre, key_gain)[1]
    key_pre_grad, key_gain_grad = key_pull(key_grad)
    value_grad = value_grad.reshape(sequences, length, width)
    query_bias_grad = jnp.sum(query_pre_grad, axis=(0, 1))
    value_bias_grad = jnp.sum(value_grad, axis=(0, 1))
    projected_grad = jnp.concatenate([query_pre_grad, key_pre_grad, value_grad], axis=2).astype(
        jnp.bfloat16
    )
    qkv_grad = weight_grad(normed_attn, projected_grad)
    normed_attn_grad = matmul_back(projected_grad, qkv_back)
    attn_pull = jax.vjp(modulate, input_rows, scale_attn, shift_attn)[1]
    input_part, scale_attn_grad, shift_attn_grad = attn_pull(normed_attn_grad)
    input_grad = middle_grad + input_part
    adaptive_grad = jnp.concatenate(
        [
            gamma_attn_grad,
            gamma_mlp_grad,
            scale_attn_grad,
            scale_mlp_grad,
            shift_attn_grad,
            shift_mlp_grad,
        ],
        axis=1,
    ).astype(jnp.bfloat16)
    ada_grad = jnp.einsum("sc,sn->cn", activated, adaptive_grad, preferred_element_type=jnp.float32)
    ada_bias_grad = jnp.sum(adaptive_grad.astype(jnp.float32), axis=0)
    activated_grad = jnp.einsum(
        "sn,cn->sc", adaptive_grad, ada_back, preferred_element_type=jnp.float32
    )
    silu_pull = jax.vjp(jax.nn.silu, cond_rows)[1]
    condition_grad = silu_pull(activated_grad)[0]
    all_parts = split_owners(
        (
            ada_grad,
            qkv_grad,
            proj_grad,
            up_grad,
            down_grad,
            ada_bias_grad,
            query_bias_grad,
            value_bias_grad,
            query_gain_grad,
            key_gain_grad,
            proj_bias_grad,
            up_bias_grad,
            down_bias_grad,
        ),
        wide_count,
        narrow_count,
    )
    group_sums = (
        lax.psum_scatter(
            all_parts[0].astype(jnp.bfloat16), "narrow", scatter_dimension=1, tiled=True
        ).astype(jnp.float32),
        lax.psum_scatter(
            all_parts[1].astype(jnp.bfloat16), "narrow", scatter_dimension=1, tiled=True
        ).astype(jnp.float32),
        lax.psum_scatter(
            all_parts[2].astype(jnp.bfloat16), "narrow", scatter_dimension=1, tiled=True
        ).astype(jnp.float32),
        lax.psum_scatter(
            all_parts[3].astype(jnp.bfloat16), "narrow", scatter_dimension=1, tiled=True
        ).astype(jnp.float32),
        lax.psum_scatter(
            all_parts[4].astype(jnp.bfloat16), "narrow", scatter_dimension=1, tiled=True
        ).astype(jnp.float32),
        lax.psum_scatter(
            all_parts[5].astype(jnp.bfloat16), "narrow", scatter_dimension=1, tiled=True
        ).astype(jnp.float32),
        lax.psum_scatter(
            all_parts[6].astype(jnp.bfloat16), "narrow", scatter_dimension=1, tiled=True
        ).astype(jnp.float32),
        lax.psum_scatter(
            all_parts[7].astype(jnp.bfloat16), "narrow", scatter_dimension=1, tiled=True
        ).astype(jnp.float32),
        lax.psum_scatter(
            all_parts[8].astype(jnp.bfloat16), "narrow", scatter_dimension=1, tiled=True
        ).astype(jnp.float32),
        lax.psum_scatter(
            all_parts[9].astype(jnp.bfloat16), "narrow", scatter_dimension=1, tiled=True
        ).astype(jnp.float32),
        lax.psum_scatter(
            all_parts[10].astype(jnp.bfloat16), "narrow", scatter_dimension=1, tiled=True
        ).astype(jnp.float32),
        lax.psum_scatter(
            all_parts[11].astype(jnp.bfloat16), "narrow", scatter_dimension=1, tiled=True
        ).astype(jnp.float32),
        lax.psum_scatter(
            all_parts[12].astype(jnp.bfloat16), "narrow", scatter_dimension=1, tiled=True
        ).astype(jnp.float32),
    )
    summed = join_owners(
        (
            lax.psum_scatter(
                group_sums[0].astype(jnp.bfloat16), "wide", scatter_dimension=0, tiled=True
            ).astype(jnp.float32),
            lax.psum_scatter(
                group_sums[1].astype(jnp.bfloat16), "wide", scatter_dimension=0, tiled=True
            ).astype(jnp.float32),
            lax.psum_scatter(
                group_sums[2].astype(jnp.bfloat16), "wide", scatter_dimension=0, tiled=True
            ).astype(jnp.float32),
            lax.psum_scatter(
                group_sums[3].astype(jnp.bfloat16), "wide", scatter_dimension=0, tiled=True
            ).astype(jnp.float32),
            lax.psum_scatter(
                group_sums[4].astype(jnp.bfloat16), "wide", scatter_dimension=0, tiled=True
            ).astype(jnp.float32),
            lax.psum_scatter(
                group_sums[5].astype(jnp.bfloat16), "wide", scatter_dimension=0, tiled=True
            ).astype(jnp.float32),
            lax.psum_scatter(
                group_sums[6].astype(jnp.bfloat16), "wide", scatter_dimension=0, tiled=True
            ).astype(jnp.float32),
            lax.psum_scatter(
                group_sums[7].astype(jnp.bfloat16), "wide", scatter_dimension=0, tiled=True
            ).astype(jnp.float32),
            lax.psum_scatter(
                group_sums[8].astype(jnp.bfloat16), "wide", scatter_dimension=0, tiled=True
            ).astype(jnp.float32),
            lax.psum_scatter(
                group_sums[9].astype(jnp.bfloat16), "wide", scatter_dimension=0, tiled=True
            ).astype(jnp.float32),
            lax.psum_scatter(
                group_sums[10].astype(jnp.bfloat16), "wide", scatter_dimension=0, tiled=True
            ).astype(jnp.float32),
            lax.psum_scatter(
                group_sums[11].astype(jnp.bfloat16), "wide", scatter_dimension=0, tiled=True
            ).astype(jnp.float32),
            lax.psum_scatter(
                group_sums[12].astype(jnp.bfloat16), "wide", scatter_dimension=0, tiled=True
            ).astype(jnp.float32),
        )
    )
    (
        ada_sum,
        qkv_sum,
        proj_sum,
        up_sum,
        down_sum,
        ada_bias_sum,
        query_bias_sum,
        value_bias_sum,
        query_gain_sum,
        key_gain_sum,
        proj_bias_sum,
        up_bias_sum,
        down_bias_sum,
    ) = summed
    return (
        layer_output,
        input_grad,
        condition_grad,
        ada_sum,
        ada_bias_sum,
        qkv_sum,
        query_bias_sum,
        value_bias_sum,
        query_gain_sum,
        key_gain_sum,
        proj_sum,
        proj_bias_sum,
        up_sum,
        up_bias_sum,
        down_sum,
        down_bias_sum,
    )


def solution(mesh):
    return jax.shard_map(
        shards,
        mesh=mesh,
        in_specs=(
            P(("wide", "narrow"), None, None),
            P(("wide", "narrow"), None),
            P(),
            P(("wide", "narrow"), None),
            P(("wide", "narrow")),
            P(("wide", "narrow"), None),
            P(("wide", "narrow")),
            P(("wide", "narrow")),
            P(("wide", "narrow")),
            P(("wide", "narrow")),
            P(("wide", "narrow"), None),
            P(("wide", "narrow")),
            P(("wide", "narrow"), None),
            P(("wide", "narrow")),
            P(("wide", "narrow"), None),
            P(("wide", "narrow")),
            P(("wide", "narrow"), None, None),
        ),
        out_specs=(
            P(("wide", "narrow"), None, None),
            P(("wide", "narrow"), None, None),
            P(("wide", "narrow"), None),
            P(("wide", "narrow"), None),
            P(("wide", "narrow")),
            P(("wide", "narrow"), None),
            P(("wide", "narrow")),
            P(("wide", "narrow")),
            P(("wide", "narrow")),
            P(("wide", "narrow")),
            P(("wide", "narrow"), None),
            P(("wide", "narrow")),
            P(("wide", "narrow"), None),
            P(("wide", "narrow")),
            P(("wide", "narrow"), None),
            P(("wide", "narrow")),
        ),
        check_vma=False,
    )
```

profile of v0, /device:TPU:0, one launch (start us, length us, event | category | flops | bytes accessed | tf_op | source)
XLA Modules:
  0.0 1936.8 jit_solution(8001107129554163438)
XLA Ops:
  16.5 43.7 %all-reduce.20 = (bf16[6144]{0:T(1024)(128)(2,1)S(1)}, bf16[1024]{0:T(1024)(128)(2,1)S(1)}, bf16[1024]{0:T(1024)(128)(2,1)S(1)}, bf16[1024]{0:T(1024)(128)(2,1)S...) all-reduce(bf16[6144]{0:T(1024)(128)(2,1)S(1)} %dynamic-update-slic, ...), channel_id=1, replica_groups=mesh['wide'=16,'narrow'=2] {'wide','narrow'}, use_global_device_ids=true, to_apply=%add | all-reduce | flops 12288 | bytes 49152
  60.4 67.6 %all-gather = bf16[32,1,128]{2,1,0:T(2,128)(2,1)S(1)} all-gather(bf16[1,1,128]{2,1,0:T(2,128)(2,1)} %bitcast.298), channel_id=1, replica_groups=mesh['wide'=16,'narrow'=2] {'wide','narrow'}, dimensions={0}, use_global_device_ids=true | all-gather | bytes 8448 | tf_op jit(solution)/shard_map/all_gather | solution.py:154
  141.9 38.1 %all-gather.9.cloned.1.call-done = bf16[1024,3072]{1,0:T(8,128)(2,1)} async-done(((bf16[32,3072]{1,0:T(8,128)(2,1)}), bf16[1024,3072]{1,0:T(8,128)(2,1)}) %all-gather.9.cloned.1.call-update) | async-done | bytes 6291472 | tf_op jit(solution)/shard_map/all_gather | solution.py:144
  210.2 15.7 fusion.106
  225.9 13.5 fusion
  239.4 15.8 fusion.49
  261.5 55.4 %all-gather.13.cloned.1.call-done = bf16[1024,4096]{1,0:T(8,128)(2,1)} async-done(((bf16[32,4096]{1,0:T(8,128)(2,1)}), bf16[1024,4096]{1,0:T(8,128)(2,1)}) %all-gather.13.cloned.1.call-update) | async-done | bytes 8388624 | tf_op jit(solution)/shard_map/all_gather | solution.py:146
  316.8 15.5 fusion.20
  332.4 63.0 %all-gather.15.cloned.1.call-done = bf16[4096,1024]{1,0:T(8,128)(2,1)} async-done(((bf16[128,1024]{1,0:T(8,128)(2,1)}), bf16[4096,1024]{1,0:T(8,128)(2,1)}) %all-gather.15.cloned.1.call-update) | async-done | bytes 8388624 | tf_op jit(solution)/shard_map/all_gather | solution.py:147
  395.4 19.3 fusion.108
  434.9 25.5 %multiply_reduce_fusion = (f32[16,680]{1,0:T(8,128)S(1)}, f32[16,680,680]{1,2,0:T(8,128)}) fusion(f32[16,680,680]{1,2,0:T(8,128)} %get-tuple-element.125, f32[16,680]{1,0:T(8,128)S(1)} %log_add_fusion, bf16[680,16,64]{0,2,1:T(8,128)(2,1)S(1)} %bitcast.263, bf16[680,16,64]{0,2,1:T(8,128)(2,1)S(1)} %bitcast.270), kind=kOutput, calls=%fused_computation.1 | convolution fusion | flops 969179520 | bytes 62059520 | tf_op jit(solution)/shard_map/while/body/eval_jaxpr/nkz,vkz->knv/dot_general | solution.py:101
  460.4 15.6 bitcast_convert_fusion
  476.0 29.0 %multiply_convert_fusion = bf16[16,680,680]{1,2,0:T(8,128)(2,1)} fusion(f32[16,680,680]{1,2,0:T(8,128)} %get-tuple-element.130, f32[16,680,680]{1,2,0:T(8,128)} %get-tuple-element.125, f32[16,680]{1,0:T(8,128)S(1)} %get-tuple-element.129, f32[16,680]{1,0:T(8,128)S(1)} %log_add_fusion), kind=kLoop, calls=%fused_computation | loop fusion | flops 29593600 | bytes 74071040 | tf_op jit(solution)/shard_map/while/body/eval_jaxpr/convert_element_type | solution.py:113
  505.1 10.0 fusion.35
  520.1 9.4 fusion.32
  535.8 10.2 fusion.40
  552.7 11.4 convolution_convert_fusion
  564.1 16.8 fusion.42
  582.7 9.4 convolution_convert_fusion.2
  595.2 13.5 dot_general.129
  608.8 14.1 convolution_convert_fusion.1
  638.0 818.7 %all-reduce.25.cloned.1.call-done = (bf16[16,2,32,6144]{3,2,1,0:T(8,128)(2,1)}, bf16[16,2,32,3072]{3,2,1,0:T(8,128)(2,1)}, bf16[16,2,32,1024]{3,2,1,0:T(8,128)(2...) async-done(((bf16[16,2,32,6144]{3,2,1,0:T(8,128)(2,1)}, bf16[16,2,32,3072]{3,2,1,0:T(8,128)(2,1)}, bf16[16,2,32,1024]{3,2,1,0:T(8,128)(2,1)}, ...) | async-done | bytes 37748752
  1497.2 11.9 reduce-scatter.37.cloned.1.call-done
  1509.8 11.5 reduce-scatter.45.cloned.1.call-done
  1522.0 11.3 reduce-scatter.53.cloned.1.call-done
  1534.0 12.0 reduce-scatter.49.cloned.1.call-done
  1546.7 11.9 reduce-scatter.31.cloned.1.call-done
  1559.3 61.8 %all-reduce.21 = (bf16[16,1,192]{2,1,0:T(2,128)(2,1)S(1)}, bf16[16,1,32]{2,1,0:T(2,128)(2,1)S(1)}, bf16[16,1,32]{2,1,0:T(2,128)(2,1)S(1)}, bf16[16,1,32]{2,1,0:T...) all-reduce(bf16[16,1,192]{2,1,0:T(2,128)(2,1)S(1)} %copy.139, ...), channel_id=5, replica_groups=mesh['wide'=16,'narrow'=2] {'wide'}, use_global_device_ids=true, to_apply=%region_26.27.clone | all-reduce | flops 8192 | bytes 32768
  1631.7 57.1 %reduce-scatter.33.cloned.1.call-done = bf16[1,1,32,3072]{3,2,1,0:T(8,128)(2,1)} async-done(((bf16[16,1,32,3072]{3,2,1,0:T(8,128)(2,1)}), bf16[1,1,32,3072]{3,2,1,0:T(8,128)(2,1)}) %reduce-scatter.33.cloned.1.call-update) | async-done | bytes 196624 | tf_op jit(solution)/shard_map/reduce_scatter | solution.py:324
  1690.5 73.9 %reduce-scatter.51.cloned.1.call-done = bf16[1,1,128,1024]{3,2,1,0:T(8,128)(2,1)} async-done(((bf16[16,1,128,1024]{3,2,1,0:T(8,128)(2,1)}), bf16[1,1,128,1024]{3,2,1,0:T(8,128)(2,1)}) %reduce-scatter.51.cloned.1.call-update) | async-done | bytes 262160 | tf_op jit(solution)/shard_map/reduce_scatter | solution.py:333
  1766.2 73.8 %reduce-scatter.47.cloned.1.call-done = bf16[1,1,32,4096]{3,2,1,0:T(8,128)(2,1)} async-done(((bf16[16,1,32,4096]{3,2,1,0:T(8,128)(2,1)}), bf16[1,1,32,4096]{3,2,1,0:T(8,128)(2,1)}) %reduce-scatter.47.cloned.1.call-update) | async-done | bytes 262160 | tf_op jit(solution)/shard_map/reduce_scatter | solution.py:330
  1841.7 86.3 %reduce-scatter.29.cloned.1.call-done = bf16[1,1,32,6144]{3,2,1,0:T(8,128)(2,1)} async-done(((bf16[16,1,32,6144]{3,2,1,0:T(8,128)(2,1)}), bf16[1,1,32,6144]{3,2,1,0:T(8,128)(2,1)}) %reduce-scatter.29.cloned.1.call-update) | async-done | bytes 393232 | tf_op jit(solution)/shard_map/reduce_scatter | solution.py:321
  (299 shorter events, 178.8 us)
Async XLA Ops:
  7.2 128.2 %copy-start.34 = (bf16[1,1024]{1,0:T(2,128)(2,1)S(1)}, bf16[1,1024]{1,0:T(2,128)(2,1)}, u32[]{:S(2)}) copy-start(bf16[1,1024]{1,0:T(2,128)(2,1)} %param.18) | copy-start | bytes 6148
  7.2 125.3 %copy-start.6 = (bf16[1,680,1024]{2,1,0:T(8,128)(2,1)S(1)}, bf16[1,680,1024]{2,1,0:T(8,128)(2,1)}, u32[]{:S(2)}) copy-start(bf16[1,680,1024]{2,1,0:T(8,128)(2,1)} %param.17) | copy-start | bytes 4177924
  7.2 128.2 %all-gather.7.cloned.1.call-start = ((), (), s32[]{:S(2)}) async-start(), calls=%async_computation.13 | async-start | bytes 12976128 | tf_op jit(solution)/shard_map/all_gather | solution.py:143
  7.9 172.1 %all-gather.9.cloned.1.call-start = ((), (), s32[]{:S(2)}) async-start(), calls=%async_computation.14 | async-start | bytes 6488064 | tf_op jit(solution)/shard_map/all_gather | solution.py:144
  8.7 246.5 %all-gather.11.cloned.1.call-start = ((), (), s32[]{:S(2)}) async-start(), calls=%async_computation.15 | async-start | bytes 2162688 | tf_op jit(solution)/shard_map/all_gather | solution.py:145
  9.4 307.4 %all-gather.13.cloned.1.call-start = ((), (), s32[]{:S(2)}) async-start(), calls=%async_computation.16 | async-start | bytes 8650752 | tf_op jit(solution)/shard_map/all_gather | solution.py:146
  10.0 385.4 %all-gather.15.cloned.1.call-start = ((), (), s32[]{:S(2)}) async-start(), calls=%async_computation.17 | async-start | bytes 8650752 | tf_op jit(solution)/shard_map/all_gather | solution.py:147
  10.6 1446.2 %all-reduce.25.cloned.1.call-start = ((), (), s32[]{:S(2)}) async-start(), calls=%async_computation.31 | async-start | bytes 75497472
  60.3 149.8 %copy-start.27 = (f32[16,64]{1,0:T(8,128)}, f32[16,64]{1,0:T(8,128)S(1)}, u32[]{:S(2)}) copy-start(f32[16,64]{1,0:T(8,128)S(1)} %reshape.744) | copy-start | bytes 12292
  60.4 149.8 %copy-start.29 = (f32[16,64]{1,0:T(8,128)}, f32[16,64]{1,0:T(8,128)S(1)}, u32[]{:S(2)}) copy-start(f32[16,64]{1,0:T(8,128)S(1)} %reshape.745) | copy-start | bytes 12292
  60.4 194.8 %copy-start.53 = (f32[1024]{0:T(1024)}, f32[1024]{0:T(1024)S(1)}, u32[]{:S(2)}) copy-start(f32[1024]{0:T(1024)S(1)} %convert_element_type.223) | copy-start | bytes 12292
  132.5 47.5 %copy-start.42 = (f32[680]{0:T(1024)}, f32[680]{0:T(1024)S(1)}, u32[]{:S(2)}) copy-start(f32[680]{0:T(1024)S(1)} %broadcast_multiply_fusion.3) | copy-start | bytes 8164
  133.1 47.0 %copy-start.38 = (f32[680]{0:T(1024)}, f32[680]{0:T(1024)S(1)}, u32[]{:S(2)}) copy-start(f32[680]{0:T(1024)S(1)} %fusion.74) | copy-start | bytes 8164
  141.9 45.7 %copy-start.45 = (f32[1,1024]{1,0:T(1,128)}, f32[1,1024]{1,0:T(1,128)S(1)}, u32[]{:S(2)}) copy-start(f32[1,1024]{1,0:T(1,128)S(1)} %get-tuple-element.122) | copy-start | bytes 12292
  141.9 45.7 %copy-start.51 = (f32[1,1024]{1,0:T(1,128)}, f32[1,1024]{1,0:T(1,128)S(1)}, u32[]{:S(2)}) copy-start(f32[1,1024]{1,0:T(1,128)S(1)} %get-tuple-element.121) | copy-start | bytes 12292
  261.0 165.5 %copy-start.3 = (f32[1,680,1024]{2,1,0:T(8,128)}, f32[1,680,1024]{2,1,0:T(8,128)S(1)}, u32[]{:S(2)}) copy-start(f32[1,680,1024]{2,1,0:T(8,128)S(1)} %get-tuple-element.104) | copy-start | bytes 8355844
  476.0 29.0 %copy-start.16 = (f32[680,16]{0,1:T(8,128)S(1)}, f32[680,16]{0,1:T(8,128)}, u32[]{:S(2)}) copy-start(f32[680,16]{0,1:T(8,128)} %copy-done.15) | copy-start | bytes 130564
  476.0 29.0 %copy-start.30 = (f32[16,64]{1,0:T(8,128)S(1)}, f32[16,64]{1,0:T(8,128)}, u32[]{:S(2)}) copy-start(f32[16,64]{1,0:T(8,128)} %copy-done.29) | copy-start | bytes 12292
  476.0 29.0 %copy-start.32 = (f32[16,64]{1,0:T(8,128)S(1)}, f32[16,64]{1,0:T(8,128)}, u32[]{:S(2)}) copy-start(f32[16,64]{1,0:T(8,128)} %broadcast_multiply_fusion.1) | copy-start | bytes 12292
  630.4 861.9 %reduce-scatter.35.cloned.1.call-start = ((), (), s32[]{:S(2)}) async-start(), calls=%async_computation.21 | async-start | bytes 12288 | tf_op jit(solution)/shard_map/reduce_scatter | solution.py:297
  632.3 860.7 %reduce-scatter.39.cloned.1.call-start = ((), (), s32[]{:S(2)}) async-start(), calls=%async_computation.23 | async-start | bytes 12288 | tf_op jit(solution)/shard_map/reduce_scatter | solution.py:303
  633.3 863.2 %reduce-scatter.41.cloned.1.call-start = ((), (), s32[]{:S(2)}) async-start(), calls=%async_computation.24 | async-start | bytes 12288 | tf_op jit(solution)/shard_map/reduce_scatter | solution.py:306
  634.0 875.1 %reduce-scatter.37.cloned.1.call-start = ((), (), s32[]{:S(2)}) async-start(), calls=%async_computation.22 | async-start | bytes 12288 | tf_op jit(solution)/shard_map/reduce_scatter | solution.py:300
  634.8 886.5 %reduce-scatter.45.cloned.1.call-start = ((), (), s32[]{:S(2)}) async-start(), calls=%async_computation.26 | async-start | bytes 12288 | tf_op jit(solution)/shard_map/reduce_scatter | solution.py:309
  635.6 897.7 %reduce-scatter.53.cloned.1.call-start = ((), (), s32[]{:S(2)}) async-start(), calls=%async_computation.30 | async-start | bytes 12288 | tf_op jit(solution)/shard_map/reduce_scatter | solution.py:315
  636.4 909.7 %reduce-scatter.49.cloned.1.call-start = ((), (), s32[]{:S(2)}) async-start(), calls=%async_computation.28 | async-start | bytes 12288 | tf_op jit(solution)/shard_map/reduce_scatter | solution.py:312
  637.1 921.5 %reduce-scatter.31.cloned.1.call-start = ((), (), s32[]{:S(2)}) async-start(), calls=%async_computation.19 | async-start | bytes 24576 | tf_op jit(solution)/shard_map/reduce_scatter | solution.py:294
  638.0 992.2 %reduce-scatter.43.cloned.1.call-start = ((), (), s32[]{:S(2)}) async-start(), calls=%async_computation.25 | async-start | bytes 1114112 | tf_op jit(solution)/shard_map/reduce_scatter | solution.py:327
  1459.7 229.1 %reduce-scatter.33.cloned.1.call-start = ((), (), s32[]{:S(2)}) async-start(), calls=%async_computation.20 | async-start | bytes 3342336 | tf_op jit(solution)/shard_map/reduce_scatter | solution.py:324
  1464.4 300.0 %reduce-scatter.51.cloned.1.call-start = ((), (), s32[]{:S(2)}) async-start(), calls=%async_computation.29 | async-start | bytes 4456448 | tf_op jit(solution)/shard_map/reduce_scatter | solution.py:333
  1469.9 370.0 %reduce-scatter.47.cloned.1.call-start = ((), (), s32[]{:S(2)}) async-start(), calls=%async_computation.27 | async-start | bytes 4456448 | tf_op jit(solution)/shard_map/reduce_scatter | solution.py:330
  1475.4 452.6 %reduce-scatter.29.cloned.1.call-start = ((), (), s32[]{:S(2)}) async-start(), calls=%async_computation.18 | async-start | bytes 6684672 | tf_op jit(solution)/shard_map/reduce_scatter | solution.py:321
  (48 other events, 400.4 us)
Sparse Core Ops, SparseCore 0:
  10.9 98.3 all-gather.6
  112.2 67.8 all-gather.8
  183.1 54.8 all-gather.10
  240.8 75.9 all-gather.12
  319.7 75.6 all-gather.14
  630.5 826.2 all-reduce.24
  1459.5 12.0 reduce-scatter.34
  1474.4 9.9 reduce-scatter.38
  1486.5 9.9 reduce-scatter.40
  1499.1 9.9 reduce-scatter.36
  1511.3 9.9 reduce-scatter.44
  1523.3 9.9 reduce-scatter.52
  1536.1 9.9 reduce-scatter.48
  1548.6 9.9 reduce-scatter.30
  1562.1 57.6 reduce-scatter.42
  1623.4 65.3 reduce-scatter.32
  1692.5 71.8 reduce-scatter.50
  1768.1 71.8 reduce-scatter.46
  1843.9 84.0 reduce-scatter.28
where the time goes:
time: 1940 us
  waiting for transfers between devices  1330 us (69%)
  matrix products  232 us (12%)
  blocking collectives  173 us (9%)
  other arithmetic  97.5 us (5%)
  local copies, waits for them, and re-layouts  86.8 us (4%)
    unnamed x20, waiting for transfers between devices  822 us
    unnamed x2, blocking collectives  106 us
    reduce_scatter x1, waiting for transfers between devices, shards(): lax.psum_scatter(group_sums[0].astype(jnp.bfloat16), 'wide', scatter_dime...  86.3 us
    reduce_scatter x1, waiting for transfers between devices, shards(): lax.psum_scatter(group_sums[4].astype(jnp.bfloat16), 'wide', scatter_dime...  73.9 us
    reduce_scatter x1, waiting for transfers between devices, shards(): lax.psum_scatter(group_sums[3].astype(jnp.bfloat16), 'wide', scatter_dime...  73.8 us
    all_gather x1, blocking collectives, shards(): lax.all_gather(bias_up, ('wide', 'narrow'), axis=0, tiled=True)  67.6 us
    all_gather x1, waiting for transfers between devices, shards(): lax.all_gather(w_down, ('wide', 'narrow'), axis=0, tiled=True)  63 us
    reduce_scatter x1, waiting for transfers between devices, shards(): lax.psum_scatter(group_sums[1].astype(jnp.bfloat16), 'wide', scatter_dime...  57.1 us
  transfers between devices with their start and end apart: 19, of which 14 were waited for; matrix products, arithmetic and copies ran while one was open for 9% of the time, Pallas kernels for 0%

commit v1 on v0

v1 whole, which is shorter than its diff:
```python
import jax
import jax.numpy as jnp
from jax import lax
from jax.sharding import PartitionSpec as P

HEADS = 16
HEAD_DIM = 64
SEQ_LEN = 680
AXES = ("wide", "narrow")

EPSILON = 1e-06
MASKED = -1000000000.0


def layer_norm(values):
    centred = values - jnp.mean(values, axis=-1, keepdims=True)
    return centred * lax.rsqrt(jnp.mean(centred * centred, axis=-1, keepdims=True) + EPSILON)


def modulate(values, scaling, offset):
    return layer_norm(values) * (1.0 + scaling[:, None, :]) + offset[:, None, :]


def head_norm(values, channel_gain):
    shaped = values.reshape(values.shape[0], values.shape[1], HEADS, HEAD_DIM)
    scaled = shaped * lax.rsqrt(jnp.mean(shaped * shaped, axis=-1, keepdims=True) + EPSILON)
    return scaled * channel_gain.reshape(HEADS, HEAD_DIM)


def gelu_tanh(values):
    return jax.nn.gelu(values, approximate=True)


def block_mask(scale_tokens):
    block_ends = jnp.cumsum(scale_tokens)
    places = jnp.arange(SEQ_LEN, dtype=jnp.int32)
    limits = jnp.min(
        jnp.where(block_ends[None, :] > places[:, None], block_ends[None, :], SEQ_LEN), axis=1
    )
    return places[None, :] < limits[:, None]


def matmul_rows(first_operand, second_operand):
    return jnp.einsum(
        "fyg,gq->fyq", first_operand, second_operand, preferred_element_type=jnp.float32
    )


def matmul_back(first_operand, second_operand):
    return jnp.einsum(
        "rfw,uw->rfu", first_operand, second_operand, preferred_element_type=jnp.float32
    )


def weight_grad(first_operand, second_operand):
    return jnp.einsum(
        "crk,cre->ke", first_operand, second_operand, preferred_element_type=jnp.float32
    )


def masked_scores(query_sequence, key_sequence, allowed):
    scores = jnp.einsum(
        "nkz,vkz->knv", query_sequence, key_sequence, preferred_element_type=jnp.float32
    ) * HEAD_DIM ** (-0.5)
    return jnp.where(allowed[None], scores, MASKED)


def attend_forward(query_sequence, key_sequence, value_sequence, allowed):
    scores = masked_scores(query_sequence, key_sequence, allowed)
    row_max = jnp.max(scores, axis=-1, keepdims=True)
    exponent = jnp.exp(scores - row_max)
    row_total = jnp.sum(exponent, axis=-1, keepdims=True)
    probabilities_reduced = (exponent / row_total).astype(jnp.bfloat16)
    context = jnp.einsum(
        "wcv,vwn->cwn", probabilities_reduced, value_sequence, preferred_element_type=jnp.float32
    ).astype(jnp.bfloat16)
    return (context, row_max[..., 0] + jnp.log(row_total[..., 0]))


def attend_backward(
    query_sequence, key_sequence, value_sequence, logsum, context_gradient, allowed
):
    scores = masked_scores(query_sequence, key_sequence, allowed)
    attention_probabilities = jnp.exp(scores - logsum[..., None])
    prob_grad = jnp.einsum(
        "nkz,vkz->knv", context_gradient, value_sequence, preferred_element_type=jnp.float32
    )
    value_grad = jnp.einsum(
        "fgs,gfu->sfu",
        attention_probabilities.astype(jnp.bfloat16),
        context_gradient,
        preferred_element_type=jnp.float32,
    )
    score_gradient = (
        attention_probabilities
        * (prob_grad - jnp.sum(prob_grad * attention_probabilities, axis=-1, keepdims=True))
    ).astype(jnp.bfloat16)
    query_grad = jnp.einsum(
        "wcv,vwn->cwn", score_gradient, key_sequence, preferred_element_type=jnp.float32
    ) * HEAD_DIM ** (-0.5)
    key_grad = jnp.einsum(
        "fgs,gfu->sfu", score_gradient, query_sequence, preferred_element_type=jnp.float32
    ) * HEAD_DIM ** (-0.5)
    return (query_grad, key_grad, value_grad)


def gather_vectors(vectors, count):
    packed = lax.all_gather(jnp.concatenate(vectors), AXES, axis=0, tiled=False)
    out, start = [], 0
    for member in vectors:
        size = member.shape[0]
        out.append(packed[:, start : start + size].reshape(count * size).astype(jnp.float32))
        start += size
    return out


def scatter_vectors(vectors, count):
    packed = jnp.concatenate([member.reshape(count, -1) for member in vectors], axis=1)
    summed = lax.psum_scatter(packed, AXES, scatter_dimension=0, tiled=True)[0]
    out, start = [], 0
    for member in vectors:
        size = member.shape[0] // count
        out.append(summed[start : start + size])
        start += size
    return out


def scatter_matrix(member):
    return lax.psum_scatter(
        member.astype(jnp.bfloat16), AXES, scatter_dimension=0, tiled=True
    ).astype(jnp.float32)


def shards(
    inputs,
    condition,
    scale_tokens,
    w_ada,
    bias_ada,
    w_qkv,
    bias_query,
    bias_value,
    gain_query,
    gain_key,
    w_proj,
    bias_proj,
    w_up,
    bias_up,
    w_down,
    bias_down,
    cotangent,
):
    count = lax.axis_size("wide") * lax.axis_size("narrow")
    me = lax.axis_index("wide") * lax.axis_size("narrow") + lax.axis_index("narrow")
    ada_bias, query_bias, value_bias, query_gain, key_gain, proj_bias, up_bias, down_bias = (
        gather_vectors(
            (bias_ada, bias_query, bias_value, gain_query, gain_key, bias_proj, bias_up, bias_down),
            count,
        )
    )
    qkv_full = lax.all_gather(w_qkv, AXES, axis=0, tiled=True)
    proj_full = lax.all_gather(w_proj, AXES, axis=0, tiled=True)
    up_full = lax.all_gather(w_up, AXES, axis=0, tiled=True)
    down_full = lax.all_gather(w_down, AXES, axis=0, tiled=True)
    sequences, length, width = inputs.shape
    head_shape = (sequences, length, HEADS, HEAD_DIM)
    allowed = block_mask(scale_tokens)
    input_rows = inputs.astype(jnp.float32)
    cond_rows = condition.astype(jnp.float32)
    activated = jax.nn.silu(cond_rows).astype(jnp.bfloat16)
    ada_rows = w_ada.shape[0]
    ada_cols = w_ada.shape[1]
    activated_all = lax.all_gather(activated, AXES, axis=0, tiled=True)
    activated_mine = lax.dynamic_slice_in_dim(activated_all, me * ada_rows, ada_rows, axis=1)
    ada_partial = jnp.dot(activated_mine, w_ada, preferred_element_type=jnp.float32)
    adaptive = lax.psum_scatter(ada_partial, AXES, scatter_dimension=0, tiled=True) + ada_bias
    gamma_attn, gamma_mlp, scale_attn, scale_mlp, shift_attn, shift_mlp = jnp.split(
        adaptive, 6, axis=1
    )
    normed_attn = modulate(input_rows, scale_attn, shift_attn).astype(jnp.bfloat16)
    projected = matmul_rows(normed_attn, qkv_full)
    query_pre = projected[..., :width] + query_bias
    key_pre = projected[..., width : 2 * width]
    queries = head_norm(query_pre, query_gain).astype(jnp.bfloat16)
    key_rows = head_norm(key_pre, key_gain).astype(jnp.bfloat16)
    value_rows = (projected[..., 2 * width :] + value_bias).astype(jnp.bfloat16).reshape(head_shape)
    context, logsum = jax.vmap(
        lambda q, k, v: attend_forward(q, k, v, allowed)
    )(queries, key_rows, value_rows)
    context = context.reshape(sequences, length, width)
    attended = matmul_rows(context, proj_full) + proj_bias
    middle = input_rows + gamma_attn[:, None, :] * attended
    normed_mlp = modulate(middle, scale_mlp, shift_mlp).astype(jnp.bfloat16)
    hidden_pre = matmul_rows(normed_mlp, up_full) + up_bias
    hidden = gelu_tanh(hidden_pre).astype(jnp.bfloat16)
    branch = matmul_rows(hidden, down_full) + down_bias
    layer_output = (middle + gamma_mlp[:, None, :] * branch).astype(jnp.bfloat16)
    upstream = cotangent.astype(jnp.float32)
    gamma_mlp_grad = jnp.sum(upstream * branch, axis=1)
    branch_grad = (upstream * gamma_mlp[:, None, :]).astype(jnp.bfloat16)
    down_sum = scatter_matrix(weight_grad(hidden, branch_grad))
    down_bias_grad = jnp.sum(branch_grad.astype(jnp.float32), axis=(0, 1))
    hidden_grad = matmul_back(branch_grad, down_full)
    gelu_pull = jax.vjp(gelu_tanh, hidden_pre)[1]
    pre_grad = gelu_pull(hidden_grad)[0].astype(jnp.bfloat16)
    up_sum = scatter_matrix(weight_grad(normed_mlp, pre_grad))
    up_bias_grad = jnp.sum(pre_grad.astype(jnp.float32), axis=(0, 1))
    normed_mlp_grad = matmul_back(pre_grad, up_full)
    mlp_pull = jax.vjp(modulate, middle, scale_mlp, shift_mlp)[1]
    middle_part, scale_mlp_grad, shift_mlp_grad = mlp_pull(normed_mlp_grad)
    middle_grad = upstream + middle_part
    gamma_attn_grad = jnp.sum(middle_grad * attended, axis=1)
    attended_grad = (middle_grad * gamma_attn[:, None, :]).astype(jnp.bfloat16)
    proj_sum = scatter_matrix(weight_grad(context, attended_grad))
    proj_bias_grad = jnp.sum(attended_grad.astype(jnp.float32), axis=(0, 1))
    context_gradient = (
        matmul_back(attended_grad, proj_full).astype(jnp.bfloat16).reshape(head_shape)
    )
    query_grad, key_grad, value_grad = jax.vmap(
        lambda q, k, v, l, c: attend_backward(q, k, v, l, c, allowed)
    )(queries, key_rows, value_rows, logsum, context_gradient)
    query_pull = jax.vjp(head_norm, query_pre, query_gain)[1]
    query_pre_grad, query_gain_grad = query_pull(query_grad)
    key_pull = jax.vjp(head_norm, key_pre, key_gain)[1]
    key_pre_grad, key_gain_grad = key_pull(key_grad)
    value_grad = value_grad.reshape(sequences, length, width)
    query_bias_grad = jnp.sum(query_pre_grad, axis=(0, 1))
    value_bias_grad = jnp.sum(value_grad, axis=(0, 1))
    projected_grad = jnp.concatenate([query_pre_grad, key_pre_grad, value_grad], axis=2).astype(
        jnp.bfloat16
    )
    qkv_sum = scatter_matrix(weight_grad(normed_attn, projected_grad))
    normed_attn_grad = matmul_back(projected_grad, qkv_full)
    attn_pull = jax.vjp(modulate, input_rows, scale_attn, shift_attn)[1]
    input_part, scale_attn_grad, shift_attn_grad = attn_pull(normed_attn_grad)
    input_grad = middle_grad + input_part
    adaptive_grad = jnp.concatenate(
        [
            gamma_attn_grad,
            gamma_mlp_grad,
            scale_attn_grad,
            scale_mlp_grad,
            shift_attn_grad,
            shift_mlp_grad,
        ],
        axis=1,
    ).astype(jnp.bfloat16)
    adaptive_grad_all = lax.all_gather(adaptive_grad, AXES, axis=0, tiled=True)
    ada_sum = jnp.einsum(
        "sc,sn->cn", activated_mine, adaptive_grad_all, preferred_element_type=jnp.float32
    )
    bias_share = ada_cols // count
    ada_bias_sum = jnp.sum(
        lax.dynamic_slice_in_dim(adaptive_grad_all, me * bias_share, bias_share, axis=1).astype(
            jnp.float32
        ),
        axis=0,
    )
    activated_grad_cols = jnp.einsum(
        "sn,cn->sc", adaptive_grad_all, w_ada, preferred_element_type=jnp.float32
    )
    activated_grad = lax.all_to_all(
        activated_grad_cols, AXES, split_axis=0, concat_axis=1, tiled=True
    )
    silu_pull = jax.vjp(jax.nn.silu, cond_rows)[1]
    condition_grad = silu_pull(activated_grad)[0]
    (
        query_bias_sum,
        value_bias_sum,
        query_gain_sum,
        key_gain_sum,
        proj_bias_sum,
        up_bias_sum,
        down_bias_sum,
    ) = scatter_vectors(
        (
            query_bias_grad,
            value_bias_grad,
            query_gain_grad,
            key_gain_grad,
            proj_bias_grad,
            up_bias_grad,
            down_bias_grad,
        ),
        count,
    )
    return (
        layer_output,
        input_grad,
        condition_grad,
        ada_sum,
        ada_bias_sum,
        qkv_sum,
        query_bias_sum,
        value_bias_sum,
        query_gain_sum,
        key_gain_sum,
        proj_sum,
        proj_bias_sum,
        up_sum,
        up_bias_sum,
        down_sum,
        down_bias_sum,
    )


def solution(mesh):
    row = P(AXES, None, None)
    mat = P(AXES, None)
    vec = P(AXES)
    return jax.shard_map(
        shards,
        mesh=mesh,
        in_specs=(row, mat, P(), mat, vec, mat, vec, vec, vec, vec, mat, vec, mat, vec, mat, vec, row),
        out_specs=(row, row, mat, mat, vec, mat, vec, vec, vec, vec, mat, vec, mat, vec, mat, vec),
        check_vma=False,
    )
```

time: 1940 us -> 1200 us (0.62)
  waiting for transfers between devices: 1330 us -> 593 us
  blocking collectives: 173 us -> 248 us
  local copies, waits for them, and re-layouts: 86.8 us -> 27.8 us
    unnamed x20 -> x10, waiting for transfers between devices: 822 us -> 55.9 us
    all_gather x1 -> x3, blocking collectives: 67.6 us -> 206 us  [the longest x1 72 us: shards(): adaptive_grad_all = lax.all_gather(adaptive_grad, AXES, axis=0, tiled=True)]
    unnamed x2 -> x1, blocking collectives: 106 us -> 42 us
    all_gather x5 -> x4, waiting for transfers between devices: 157 us -> 200 us  [the longest x1 69.7 us: shards(): qkv_full = lax.all_gather(w_qkv, AXES, axis=0, tiled=True)]
    unnamed x153 -> x189, local copies, waits for them, and re-layouts: 35.7 us -> 11.4 us
    reduce_scatter x13 -> x4, waiting for transfers between devices: 353 us -> 338 us  [scatter_matrix(): lax.psum_scatter(member.astype(jnp.bfloat16), AXES, scatter_dimension=0,...]
  transfers between devices with their start and end apart: 19 -> 10, of which waited for: 14 -> 6; matrix products, arithmetic and copies ran while one was open for 9% -> 22% of each run, Pallas kernels for 0% -> 0%
where the time goes in v1:
time: 1200 us; the launch traced here: 1190 us
  waiting for transfers between devices  593 us (49%)
  blocking collectives  248 us (21%)
  matrix products  222 us (18%)
  other arithmetic  83.2 us (7%)
  local copies, waits for them, and re-layouts  27.8 us (2%)
  between operations  15.4 us (1%)
    reduce_scatter x4, waiting for transfers between devices, scatter_matrix(): lax.psum_scatter(member.astype(jnp.bfloat16), AXES, scatter_dimension=0,...  338 us
    all_gather x1, blocking collectives, shards(): adaptive_grad_all = lax.all_gather(adaptive_grad, AXES, axis=0, tiled=True)  72 us
    all_gather x1, blocking collectives, shards(): activated_all = lax.all_gather(activated, AXES, axis=0, tiled=True)  70.4 us
    all_gather x1, waiting for transfers between devices, shards(): qkv_full = lax.all_gather(w_qkv, AXES, axis=0, tiled=True)  69.7 us
    all_gather x1, waiting for transfers between devices, shards(): down_full = lax.all_gather(w_down, AXES, axis=0, tiled=True)  66.3 us
    all_gather x1, blocking collectives, gather_vectors(): packed = lax.all_gather(jnp.concatenate(vectors), AXES, axis=0, tiled=False)  63.8 us
    all_gather x1, waiting for transfers between devices, shards(): up_full = lax.all_gather(w_up, AXES, axis=0, tiled=True)  63.7 us
    unnamed x10, waiting for transfers between devices  55.9 us
  transfers between devices with their start and end apart: 10, of which 6 were waited for; matrix products, arithmetic and copies ran while one was open for 22% of the time, Pallas kernels for 0%

profile of v1, /device:TPU:0, one launch (start us, length us, event | category | flops | bytes accessed | tf_op | source)
XLA Modules:
  0.0 1192.4 jit_solution(12533256275470036233)
XLA Ops:
  8.8 70.4 %all-gather.1 = bf16[32,1,1024]{2,1,0:T(2,128)(2,1)S(1)} all-gather(bf16[1,1,1024]{2,1,0:T(2,128)(2,1)S(1)} %get-tuple-element.33), channel_id=1, replica_groups=mesh['wide'=16,'narrow'=2] {'wide','narrow'}, dimensions={0}, use_global_device_ids=true | all-gather | bytes 67584 | tf_op jit(solution)/shard_map/all_gather | solution.py:173
  84.1 63.8 %all-gather.2 = bf16[32,1,512]{2,1,0:T(2,128)(2,1)S(1)} all-gather(bf16[1,1,512]{2,1,0:T(2,128)(2,1)S(1)} %reshape.821), channel_id=2, replica_groups=mesh['wide'=16,'narrow'=2] {'wide','narrow'}, dimensions={0}, use_global_device_ids=true | all-gather | bytes 33792 | tf_op jit(solution)/shard_map/all_gather | solution.py:108
  153.6 53.3 %all-reduce.4.cloned.1.call-done = f32[32,6144]{1,0:T(8,128)} async-done(((f32[32,6144]{1,0:T(8,128)}), f32[32,6144]{1,0:T(8,128)}) %all-reduce.4.cloned.1.call-update) | async-done | bytes 786448
  208.5 69.7 %all-gather.9.cloned.1.call-done = bf16[1024,3072]{1,0:T(8,128)(2,1)} async-done(((bf16[32,3072]{1,0:T(8,128)(2,1)}), bf16[1024,3072]{1,0:T(8,128)(2,1)}) %all-gather.9.cloned.1.call-update) | async-done | bytes 6291472 | tf_op jit(solution)/shard_map/all_gather | solution.py:161
  278.2 7.5 convolution_bitcast_fusion
  296.0 3.4 multiply_reduce_fusion.1
  300.1 13.9 %fusion.80 = (f32[16,680]{1,0:T(8,128)S(1)}, f32[16,680,680]{1,2,0:T(8,128)}) fusion(f32[680,16,64]{0,2,1:T(8,128)S(1)} %bitcast.200, f32[16,64]{1,0:T(8,128)S(1)} %reshape.814, f32[680,16]{0,1:T(8,128)S(1)} %get-tuple-element.76, f32[680,16,64]{0,2,1:T(8,128)S(1)} %bitcast.194, f32[16,64]{1,0:T(8,128)S(1)} %reshape.813, ...), kind=kOutput, calls=%fused_computation.175 | convolution fusion | flops 973357440 | bytes 35765312 | tf_op jit(solution)/shard_map/vmap(nkz,vkz->knv)/dot_general | solution.py:62
  314.1 13.5 %fusion = f32[16,680]{1,0:T(8,128)S(1)} fusion(f32[16,680,680]{1,2,0:T(8,128)} %get-tuple-element.61, f32[16,680]{1,0:T(8,128)S(1)} %get-tuple-element.60), kind=kLoop, calls=%fused_computation.6 | loop fusion | flops 14785920 | bytes 29680640 | tf_op jit(solution)/shard_map/vmap()/reduce_sum | solution.py:72
  327.6 15.5 %fusion.37 = bf16[16,64,680]{2,1,0:T(8,128)(2,1)} fusion(bf16[680,16,64]{0,2,1:T(8,128)(2,1)S(1)} %bitcast.204, f32[16,680,680]{1,2,0:T(8,128)} %get-tuple-element.61, f32[16,680]{1,0:T(8,128)S(1)} %fusion, f32[16,680]{1,0:T(8,128)S(1)} %get-tuple-element.60), kind=kOutput, calls=%fused_computation.91 | convolution fusion | flops 969886720 | bytes 32465920 | tf_op jit(solution)/shard_map/vmap(wcv,vwn->cwn)/dot_general | solution.py:74
  343.1 5.5 fusion.77
  351.2 63.7 %all-gather.13.cloned.1.call-done = bf16[1024,4096]{1,0:T(8,128)(2,1)} async-done(((bf16[32,4096]{1,0:T(8,128)(2,1)}), bf16[1024,4096]{1,0:T(8,128)(2,1)}) %all-gather.13.cloned.1.call-update) | async-done | bytes 8388624 | tf_op jit(solution)/shard_map/all_gather | solution.py:163
  414.9 12.2 %fusion.73 = f32[680,4096]{1,0:T(8,128)} fusion(bf16[1024,4096]{1,0:T(8,128)(2,1)} %all-gather.13.cloned.1.call-done, f32[1,680,1024]{2,1,0:T(8,128)} %copy-done.13, f32[1024]{0:T(1024)S(1)} %bitcast.229, f32[1024]{0:T(1024)S(1)} %bitcast.221, f32[680]{0:T(1024)S(1)} %fusion.65, f32[680]{0:T(1024)S(1)} %broadcast_multiply_fusion.2), kind=kOutput, calls=%fused_computation.169 | convolution fusion | flops 5707735040 | bytes 22328640 | tf_op jit(solution)/shard_map/fyg,gq->fyq/dot_general | solution.py:44
  427.1 66.3 %all-gather.15.cloned.1.call-done = bf16[4096,1024]{1,0:T(8,128)(2,1)} async-done(((bf16[128,1024]{1,0:T(8,128)(2,1)}), bf16[4096,1024]{1,0:T(8,128)(2,1)}) %all-gather.15.cloned.1.call-update) | async-done | bytes 8388624 | tf_op jit(solution)/shard_map/all_gather | solution.py:164
  493.4 17.3 %convert_reduce_fusion = (f32[4096]{0:T(1024)}, bf16[680,4096]{1,0:T(8,128)(2,1)S(1)}) fusion(f32[680,4096]{1,0:T(8,128)} %fusion.73, f32[4096]{0:T(1024)S(1)} %copy-done.62, bf16[4096,1024]{1,0:T(8,128)(2,1)} %all-gather.15.cloned.1.call-done, f32[1024]{0:T(1024)S(1)} %bitcast.226, bf16[1,680,1024]{2,1,0:T(8,128)(2,1)S(1)} %copy-done.24), kind=kOutput, calls=%fused_computation.20 | convolution fusion | flops 5770399744 | bytes 26529792 | tf_op jit(solution)/shard_map/rfw,uw->rfu/dot_general | solution.py:50
  510.8 11.4 fusion.32
  525.8 15.5 %convert_reduce_fusion.2 = (f32[1024]{0:T(1024)}, bf16[1024]{0:T(1024)(128)(2,1)}, bf16[1024]{0:T(1024)(128)(2,1)}, f32[1024]{0:T(1024)}, bf16[1,680,1024]{2,1,0:T(8,128)(2,1)S(1)}, /*index=5*/bf16[1,680,1024]{2,1,0:T(8,128)(2,1)}) fusion(f32[1024]{0:T(1024)S(1)} %bitcast.227, bf16[1,680,1024]{2,1,0:T(8,128)(2,1)S(1)} %copy-done.24, ...), kind=kOutput, calls=%fused_computation.82 | convolution fusion | flops 5746028544 | bytes 32111264 | tf_op jit(solution)/shard_map/fyg,gq->fyq/dot_general | solution.py:44
  545.6 4.8 convolution_convert_fusion.4
  552.1 26.4 %multiply_reduce_fusion = (f32[16,680]{1,0:T(8,128)}, f32[16,680,680]{1,2,0:T(8,128)}) fusion(f32[16,680,680]{1,2,0:T(8,128)} %get-tuple-element.61, f32[16,680]{1,0:T(8,128)} %log_add_fusion, bf16[680,16,64]{0,2,1:T(8,128)(2,1)S(1)} %bitcast.202, bf16[680,16,64]{0,2,1:T(8,128)(2,1)S(1)} %bitcast.205), kind=kOutput, calls=%fused_computation.1 | convolution fusion | flops 969179520 | bytes 62059520 | tf_op jit(solution)/shard_map/vmap(nkz,vkz->knv)/dot_general | solution.py:85
  578.5 28.9 %multiply_convert_fusion = bf16[16,680,680]{1,2,0:T(8,128)(2,1)} fusion(f32[16,680,680]{1,2,0:T(8,128)} %get-tuple-element.67, f32[16,680,680]{1,2,0:T(8,128)} %get-tuple-element.61, f32[16,680]{1,0:T(8,128)} %get-tuple-element.66, f32[16,680]{1,0:T(8,128)} %log_add_fusion), kind=kLoop, calls=%fused_computation | loop fusion | flops 29593600 | bytes 74071040 | tf_op jit(solution)/shard_map/vmap()/convert_element_type | solution.py:97
  607.5 11.7 fusion.23
  619.2 9.4 fusion.20
  631.2 3.4 fusion.21
  634.6 16.4 %bitcast_convert_fusion = (bf16[1,680,16,64]{1,3,2,0:T(8,128)(2,1)}, f32[16,64,680]{2,1,0:T(8,128)}) fusion(bf16[680,16,64]{0,2,1:T(8,128)(2,1)} %bitcast.203, f32[16,680,680]{1,2,0:T(8,128)} %get-tuple-element.61, f32[16,680]{1,0:T(8,128)} %log_add_fusion), kind=kOutput, calls=%fused_computation.49 | convolution fusion | flops 962488320 | bytes 35207680 | tf_op jit(solution)/shard_map/vmap(fgs,gfu->sfu)/dot_general | solution.py:88
  651.0 10.2 convolution_convert_fusion.2
  663.0 12.0 %convolution_convert_fusion.1 = bf16[1024,4096]{1,0:T(8,128)(2,1)} fusion(bf16[680,4096]{1,0:T(8,128)(2,1)} %copy-done.89, f32[1,680,1024]{2,1,0:T(8,128)S(1)} %copy-done.15, f32[1024]{0:T(1024)S(1)} %bitcast.230, f32[1024]{0:T(1024)S(1)} %bitcast.224, f32[680]{0:T(1024)S(1)} %copy-done.60, f32[680]{0:T(1024)S(1)} %copy-done.47), kind=kOutput, calls=%fused_computation.23 | convolution fusion | flops 5711929344 | bytes 16758080 | tf_op jit(solution)/shard_map/crk,cre->ke/dot_general | solution.py:56
  676.3 14.0 %convolution_convert_fusion = bf16[4096,1024]{1,0:T(8,128)(2,1)} fusion(bf16[1,680,1024]{2,1,0:T(8,128)(2,1)S(1)} %copy-done.25, f32[1024]{0:T(1024)S(1)} %bitcast.228, f32[680,4096]{1,0:T(8,128)} %fusion.73, f32[4096]{0:T(1024)S(1)} %copy-done.63), kind=kOutput, calls=%fused_computation.22 | convolution fusion | flops 5738389504 | bytes 20942848 | tf_op jit(solution)/shard_map/crk,cre->ke/dot_general | solution.py:56
  696.7 10.2 fusion.28
  710.7 72.0 %all-gather.3 = bf16[32,1,6144]{2,1,0:T(2,128)(2,1)S(1)} all-gather(bf16[1,1,6144]{2,1,0:T(2,128)(2,1)S(1)} %bitcast.220), channel_id=1, replica_groups=mesh['wide'=16,'narrow'=2] {'wide','narrow'}, dimensions={0}, use_global_device_ids=true | all-gather | bytes 405504 | tf_op jit(solution)/shard_map/all_gather | solution.py:248
  787.5 42.0 %all-reduce.1 = f32[32,320]{1,0:T(8,128)S(1)} all-reduce(f32[32,320]{1,0:T(8,128)S(1)} %concatenate.56), channel_id=5, replica_groups=mesh['wide'=16,'narrow'=2] {'wide','narrow'}, use_global_device_ids=true, to_apply=%region_33.34.clone | all-reduce | flops 10240 | bytes 81920
  832.5 4.3 add_add_fusion.4
  844.0 153.3 %reduce-scatter.9.cloned.1.call-done = bf16[32,4096]{1,0:T(8,128)(2,1)} async-done(((bf16[1024,4096]{1,0:T(8,128)(2,1)}), bf16[32,4096]{1,0:T(8,128)(2,1)}) %reduce-scatter.9.cloned.1.call-update) | async-done | bytes 262160 | tf_op jit(solution)/shard_map/reduce_scatter | solution.py:129
  999.1 184.5 %reduce-scatter.11.cloned.1.call-done = bf16[128,1024]{1,0:T(8,128)(2,1)} async-done(((bf16[4096,1024]{1,0:T(8,128)(2,1)}), bf16[128,1024]{1,0:T(8,128)(2,1)}) %reduce-scatter.11.cloned.1.call-update) | async-done | bytes 262160 | tf_op jit(solution)/shard_map/reduce_scatter | solution.py:129
  (282 shorter events, 70.9 us)
Async XLA Ops:
  7.2 76.7 %copy-start.85 = (bf16[32]{0:T(256)(128)(2,1)S(1)}, bf16[32]{0:T(256)(128)(2,1)}, u32[]{:S(2)}) copy-start(bf16[32]{0:T(256)(128)(2,1)} %param.32) | copy-start | bytes 196
  7.2 76.7 %copy-start.84 = (bf16[128]{0:T(256)(128)(2,1)S(1)}, bf16[128]{0:T(256)(128)(2,1)}, u32[]{:S(2)}) copy-start(bf16[128]{0:T(256)(128)(2,1)} %param.30) | copy-start | bytes 772
  7.2 76.7 %copy-start.83 = (bf16[32]{0:T(256)(128)(2,1)S(1)}, bf16[32]{0:T(256)(128)(2,1)}, u32[]{:S(2)}) copy-start(bf16[32]{0:T(256)(128)(2,1)} %param.28) | copy-start | bytes 196
  7.2 76.7 %copy-start.82 = (bf16[32]{0:T(256)(128)(2,1)S(1)}, bf16[32]{0:T(256)(128)(2,1)}, u32[]{:S(2)}) copy-start(bf16[32]{0:T(256)(128)(2,1)} %param.26) | copy-start | bytes 196
  7.2 76.7 %copy-start.81 = (bf16[32]{0:T(256)(128)(2,1)S(1)}, bf16[32]{0:T(256)(128)(2,1)}, u32[]{:S(2)}) copy-start(bf16[32]{0:T(256)(128)(2,1)} %param.25) | copy-start | bytes 196
  7.3 76.7 %copy-start.80 = (bf16[32]{0:T(256)(128)(2,1)S(1)}, bf16[32]{0:T(256)(128)(2,1)}, u32[]{:S(2)}) copy-start(bf16[32]{0:T(256)(128)(2,1)} %param.24) | copy-start | bytes 196
  7.3 142.5 %copy-start.5 = (bf16[1,680,1024]{2,1,0:T(8,128)(2,1)S(1)}, bf16[1,680,1024]{2,1,0:T(8,128)(2,1)}, u32[]{:S(2)}) copy-start(bf16[1,680,1024]{2,1,0:T(8,128)(2,1)} %param.17) | copy-start | bytes 4177924
  7.3 199.6 %all-reduce.4.cloned.1.call-start = ((), (), s32[]{:S(2)}) async-start(), calls=%async_computation.13 | async-start | bytes 1572864
  81.0 197.1 %all-gather.9.cloned.1.call-start = ((), (), s32[]{:S(2)}) async-start(), calls=%async_computation.5 | async-start | bytes 6488064 | tf_op jit(solution)/shard_map/all_gather | solution.py:161
  81.8 261.3 %all-gather.11.cloned.1.call-start = ((), (), s32[]{:S(2)}) async-start(), calls=%async_computation.6 | async-start | bytes 2162688 | tf_op jit(solution)/shard_map/all_gather | solution.py:162
  82.5 332.3 %all-gather.13.cloned.1.call-start = ((), (), s32[]{:S(2)}) async-start(), calls=%async_computation.7 | async-start | bytes 8650752 | tf_op jit(solution)/shard_map/all_gather | solution.py:163
  83.1 410.3 %all-gather.15.cloned.1.call-start = ((), (), s32[]{:S(2)}) async-start(), calls=%async_computation.8 | async-start | bytes 8650752 | tf_op jit(solution)/shard_map/all_gather | solution.py:164
  83.7 757.1 %reduce-scatter.7.cloned.1.call-start = ((), (), s32[]{:S(2)}) async-start(), calls=%async_computation.10 | async-start | bytes 2162688 | tf_op jit(solution)/shard_map/reduce_scatter | solution.py:129
  149.6 150.2 %copy-start.34 = (f32[16,64]{1,0:T(8,128)}, f32[16,64]{1,0:T(8,128)S(1)}, u32[]{:S(2)}) copy-start(f32[16,64]{1,0:T(8,128)S(1)} %reshape.814) | copy-start | bytes 12292
  149.7 150.2 %copy-start.32 = (f32[16,64]{1,0:T(8,128)}, f32[16,64]{1,0:T(8,128)S(1)}, u32[]{:S(2)}) copy-start(f32[16,64]{1,0:T(8,128)S(1)} %reshape.813) | copy-start | bytes 12292
  150.1 128.1 %copy-start.44 = (f32[680]{0:T(1024)}, f32[680]{0:T(1024)S(1)}, u32[]{:S(2)}) copy-start(f32[680]{0:T(1024)S(1)} %broadcast_multiply_fusion.3) | copy-start | bytes 8164
  150.6 127.6 %copy-start.48 = (f32[680]{0:T(1024)}, f32[680]{0:T(1024)S(1)}, u32[]{:S(2)}) copy-start(f32[680]{0:T(1024)S(1)} %fusion.27) | copy-start | bytes 8164
  150.6 127.6 %copy-start.38 = (f32[680]{0:T(1024)}, f32[680]{0:T(1024)S(1)}, u32[]{:S(2)}) copy-start(f32[680]{0:T(1024)S(1)} %fusion.64) | copy-start | bytes 8164
  348.6 173.6 %copy-start.46 = (f32[680]{0:T(1024)}, f32[680]{0:T(1024)S(1)}, u32[]{:S(2)}) copy-start(f32[680]{0:T(1024)S(1)} %broadcast_multiply_fusion.2) | copy-start | bytes 8164
  350.6 171.7 %copy-start.59 = (f32[680]{0:T(1024)}, f32[680]{0:T(1024)S(1)}, u32[]{:S(2)}) copy-start(f32[680]{0:T(1024)S(1)} %fusion.65) | copy-start | bytes 8164
  414.9 78.6 %copy-start.24 = (bf16[1,680,1024]{2,1,0:T(8,128)(2,1)S(1)}, bf16[1,680,1024]{2,1,0:T(8,128)(2,1)}, u32[]{:S(2)}) copy-start(bf16[1,680,1024]{2,1,0:T(8,128)(2,1)} %param.33) | copy-start | bytes 4177924
  414.9 78.6 %copy-start.62 = (f32[4096]{0:T(1024)S(1)}, f32[4096]{0:T(1024)}, u32[]{:S(2)}) copy-start(f32[4096]{0:T(1024)} %fusion.61) | copy-start | bytes 49156
  414.9 78.6 %copy-start.66 = (f32[1,1024]{1,0:T(1,128)S(1)}, f32[1,1024]{1,0:T(1,128)}, u32[]{:S(2)}) copy-start(f32[1,1024]{1,0:T(1,128)} %get-tuple-element.54) | copy-start | bytes 12292
  552.0 290.3 %reduce-scatter.5.cloned.1.call-start = ((), (), s32[]{:S(2)}) async-start(), calls=%async_computation.9 | async-start | bytes 6488064 | tf_op jit(solution)/shard_map/reduce_scatter | solution.py:129
  661.2 336.1 %reduce-scatter.9.cloned.1.call-start = ((), (), s32[]{:S(2)}) async-start(), calls=%async_computation.11 | async-start | bytes 8650752 | tf_op jit(solution)/shard_map/reduce_scatter | solution.py:129
  675.0 508.6 %reduce-scatter.11.cloned.1.call-start = ((), (), s32[]{:S(2)}) async-start(), calls=%async_computation.12 | async-start | bytes 8650752 | tf_op jit(solution)/shard_map/reduce_scatter | solution.py:129
  707.9 79.5 %copy-start.42 = (f32[32,32]{1,0:T(8,128)S(1)}, f32[32,32]{1,0:T(8,128)}, u32[]{:S(2)}) copy-start(f32[32,32]{1,0:T(8,128)} %reshape.809) | copy-start | bytes 12292
  707.9 79.5 %copy-start.43 = (f32[32,32]{1,0:T(8,128)S(1)}, f32[32,32]{1,0:T(8,128)}, u32[]{:S(2)}) copy-start(f32[32,32]{1,0:T(8,128)} %reshape.807) | copy-start | bytes 12292
  707.9 79.5 %copy-start.61 = (f32[4096]{0:T(1024)S(1)}, f32[4096]{0:T(1024)}, u32[]{:S(2)}) copy-start(f32[4096]{0:T(1024)} %get-tuple-element.73) | copy-start | bytes 49156
  707.9 122.1 %copy-start.41 = (bf16[32,1,32]{2,1,0:T(2,128)(2,1)S(1)}, bf16[32,1,32]{2,1,0:T(2,128)(2,1)}, u32[]{:S(2)}) copy-start(bf16[32,1,32]{2,1,0:T(2,128)(2,1)} %copy-done.40) | copy-start | bytes 6148
  708.0 124.5 %copy-start.58 = (f32[680]{0:T(1024)S(1)}, f32[680]{0:T(1024)}, u32[]{:S(2)}) copy-start(f32[680]{0:T(1024)} %copy-done.57) | copy-start | bytes 8164
  784.5 54.4 %all-to-all-start = ((f32[32,1,32]{2,1,0:T(1,128)}), f32[32,1,32]{2,1,0:T(1,128)S(1)}, u32[]{:S(2)}, u32[]{:S(2)}) async-start(f32[32,1,32]{2,1,0:T(1,128)} %bitcast.46), calls=%async_computation | async-start | bytes 32768 | tf_op jit(solution)/shard_map/all_to_all | solution.py:262
  (69 other events, 1144.0 us)
Sparse Core Ops, SparseCore 0:
  81.1 125.7 all-reduce.3
  209.8 68.2 all-gather.8
  281.1 54.8 all-gather.10
  338.9 75.9 all-gather.12
  417.7 75.6 all-gather.14
  552.2 137.8 reduce-scatter.6
  695.7 115.7 reduce-scatter.4
  813.8 183.4 reduce-scatter.8
  999.6 183.9 reduce-scatter.10

commit v2 on v1

--- a/solution.py
+++ b/solution.py
@@ -2,6 +2,7 @@
 import jax.numpy as jnp
 from jax import lax
 from jax.sharding import PartitionSpec as P
+
 
 HEADS = 16
 HEAD_DIM = 64
@@ -104,34 +105,54 @@
     return (query_grad, key_grad, value_grad)
 
 
-def gather_vectors(vectors, count):
-    packed = lax.all_gather(jnp.concatenate(vectors), AXES, axis=0, tiled=False)
+def nested_gather(member):
+    return lax.all_gather(
+        lax.all_gather(member, "narrow", axis=0, tiled=True), "wide", axis=0, tiled=True
+    )
+
+
+LANES = 1024
+
+
+def pack_rows(pieces, count):
+    flat = jnp.concatenate([piece.reshape(count, -1) for piece in pieces], axis=1)
+    pad = -flat.shape[1] % (LANES * 16)
+    if pad:
+        flat = jnp.concatenate([flat, jnp.zeros((count, pad), flat.dtype)], axis=1)
+    return flat.reshape(count * (flat.shape[1] // LANES), LANES)
+
+
+def unpack_rows(flat, members, count, leading):
+    flat = flat.reshape(leading, -1)
     out, start = [], 0
-    for member in vectors:
-        size = member.shape[0]
-        out.append(packed[:, start : start + size].reshape(count * size).astype(jnp.float32))
+    for member in members:
+        size = member.size // count
+        out.append(flat[:, start : start + size])
         start += size
     return out
 
 
-def scatter_vectors(vectors, count):
-    packed = jnp.concatenate([member.reshape(count, -1) for member in vectors], axis=1)
-    summed = lax.psum_scatter(packed, AXES, scatter_dimension=0, tiled=True)[0]
-    out, start = [], 0
-    for member in vectors:
-        size = member.shape[0] // count
-        out.append(summed[start : start + size])
-        start += size
-    return out
-
-
-def scatter_matrix(member):
-    return lax.psum_scatter(
-        member.astype(jnp.bfloat16), AXES, scatter_dimension=0, tiled=True
-    ).astype(jnp.float32)
-
-
-def shards(
+def gather_packed(members, count):
+    got = lax.all_gather(pack_rows([m[None] for m in members], 1), AXES, axis=0, tiled=True)
+    pieces = unpack_rows(got, [m[None] for m in members], 1, count)
+    return [
+        piece.reshape((count * member.shape[0],) + member.shape[1:])
+        for piece, member in zip(pieces, members)
+    ]
+
+
+def scatter_packed(members, count):
+    flat = pack_rows([member.astype(jnp.bfloat16) for member in members], count)
+    half = lax.psum_scatter(flat, "wide", scatter_dimension=0, tiled=True)
+    got = lax.psum_scatter(half, "narrow", scatter_dimension=0, tiled=True)
+    pieces = unpack_rows(got.astype(jnp.float32), members, count, 1)
+    return [
+        piece.reshape((member.shape[0] // count,) + member.shape[1:])
+        for piece, member in zip(pieces, members)
+    ]
+
+
+def layer(
     inputs,
     condition,
     scale_tokens,
@@ -152,28 +173,33 @@
 ):
     count = lax.axis_size("wide") * lax.axis_size("narrow")
     me = lax.axis_index("wide") * lax.axis_size("narrow") + lax.axis_index("narrow")
-    ada_bias, query_bias, value_bias, query_gain, key_gain, proj_bias, up_bias, down_bias = (
-        gather_vectors(
-            (bias_ada, bias_query, bias_value, gain_query, gain_key, bias_proj, bias_up, bias_down),
-            count,
-        )
-    )
-    qkv_full = lax.all_gather(w_qkv, AXES, axis=0, tiled=True)
-    proj_full = lax.all_gather(w_proj, AXES, axis=0, tiled=True)
-    up_full = lax.all_gather(w_up, AXES, axis=0, tiled=True)
-    down_full = lax.all_gather(w_down, AXES, axis=0, tiled=True)
     sequences, length, width = inputs.shape
     head_shape = (sequences, length, HEADS, HEAD_DIM)
+    cond_rows = condition.astype(jnp.float32)
+    activated = jax.nn.silu(cond_rows).astype(jnp.bfloat16)
+    vectors = (bias_ada, bias_query, bias_value, gain_query, gain_key, bias_proj, bias_up, bias_down)
+    small = nested_gather(
+        jnp.concatenate([activated.reshape(-1)] + list(vectors))[None, :]
+    )
+    activated_all = small[:, : activated.size].reshape(count * sequences, activated.shape[1])
+    unpacked, start = [], activated.size
+    for member in vectors:
+        size = member.shape[0]
+        unpacked.append(small[:, start : start + size].reshape(count * size).astype(jnp.float32))
+        start += size
+    ada_bias, query_bias, value_bias, query_gain, key_gain, proj_bias, up_bias, down_bias = unpacked
+    (qkv_full,) = gather_packed((w_qkv,), count)
+    proj_full, up_full, down_full = gather_packed((w_proj, w_up, w_down), count)
     allowed = block_mask(scale_tokens)
     input_rows = inputs.astype(jnp.float32)
-    cond_rows = condition.astype(jnp.float32)
-    activated = jax.nn.silu(cond_rows).astype(jnp.bfloat16)
     ada_rows = w_ada.shape[0]
     ada_cols = w_ada.shape[1]
-    activated_all = lax.all_gather(activated, AXES, axis=0, tiled=True)
     activated_mine = lax.dynamic_slice_in_dim(activated_all, me * ada_rows, ada_rows, axis=1)
     ada_partial = jnp.dot(activated_mine, w_ada, preferred_element_type=jnp.float32)
-    adaptive = lax.psum_scatter(ada_partial, AXES, scatter_dimension=0, tiled=True) + ada_bias
+    ada_parts = lax.all_to_all(
+        ada_partial.reshape(count, sequences, ada_cols), AXES, split_axis=0, concat_axis=0, tiled=True
+    )
+    adaptive = jnp.sum(ada_parts, axis=0) + ada_bias
     gamma_attn, gamma_mlp, scale_attn, scale_mlp, shift_attn, shift_mlp = jnp.split(
         adaptive, 6, axis=1
     )
@@ -198,12 +224,13 @@
     upstream = cotangent.astype(jnp.float32)
     gamma_mlp_grad = jnp.sum(upstream * branch, axis=1)
     branch_grad = (upstream * gamma_mlp[:, None, :]).astype(jnp.bfloat16)
-    down_sum = scatter_matrix(weight_grad(hidden, branch_grad))
+    down_grad = weight_grad(hidden, branch_grad)
     down_bias_grad = jnp.sum(branch_grad.astype(jnp.float32), axis=(0, 1))
     hidden_grad = matmul_back(branch_grad, down_full)
     gelu_pull = jax.vjp(gelu_tanh, hidden_pre)[1]
     pre_grad = gelu_pull(hidden_grad)[0].astype(jnp.bfloat16)
-    up_sum = scatter_matrix(weight_grad(normed_mlp, pre_grad))
+    up_grad = weight_grad(normed_mlp, pre_grad)
+    down_sum, up_sum = scatter_packed((down_grad, up_grad), count)
     up_bias_grad = jnp.sum(pre_grad.astype(jnp.float32), axis=(0, 1))
     normed_mlp_grad = matmul_back(pre_grad, up_full)
     mlp_pull = jax.vjp(modulate, middle, scale_mlp, shift_mlp)[1]
@@ -211,7 +238,7 @@
     middle_grad = upstream + middle_part
     gamma_attn_grad = jnp.sum(middle_grad * attended, axis=1)
     attended_grad = (middle_grad * gamma_attn[:, None, :]).astype(jnp.bfloat16)
-    proj_sum = scatter_matrix(weight_grad(context, attended_grad))
+    proj_grad = weight_grad(context, attended_grad)
     proj_bias_grad = jnp.sum(attended_grad.astype(jnp.float32), axis=(0, 1))
     context_gradient = (
         matmul_back(attended_grad, proj_full).astype(jnp.bfloat16).reshape(head_shape)
@@ -229,7 +256,31 @@
     projected_grad = jnp.concatenate([query_pre_grad, key_pre_grad, value_grad], axis=2).astype(
         jnp.bfloat16
     )
-    qkv_sum = scatter_matrix(weight_grad(normed_attn, projected_grad))
+    qkv_grad = weight_grad(normed_attn, projected_grad)
+    (
+        proj_sum,
+        qkv_sum,
+        query_bias_sum,
+        value_bias_sum,
+        query_gain_sum,
+        key_gain_sum,
+        proj_bias_sum,
+        up_bias_sum,
+        down_bias_sum,
+    ) = scatter_packed(
+        (
+            proj_grad,
+            qkv_grad,
+            query_bias_grad,
+            value_bias_grad,
+            query_gain_grad,
+            key_gain_grad,
+            proj_bias_grad,
+            up_bias_grad,
+            down_bias_grad,
+        ),
+        count,
+    )
     normed_attn_grad = matmul_back(projected_grad, qkv_full)
     attn_pull = jax.vjp(modulate, input_rows, scale_attn, shift_attn)[1]
     input_part, scale_attn_grad, shift_attn_grad = attn_pull(normed_attn_grad)
@@ -245,7 +296,7 @@
         ],
         axis=1,
     ).astype(jnp.bfloat16)
-    adaptive_grad_all = lax.all_gather(adaptive_grad, AXES, axis=0, tiled=True)
+    adaptive_grad_all = nested_gather(adaptive_grad)
     ada_sum = jnp.einsum(
         "sc,sn->cn", activated_mine, adaptive_grad_all, preferred_element_type=jnp.float32
     )
@@ -264,26 +315,6 @@
     )
     silu_pull = jax.vjp(jax.nn.silu, cond_rows)[1]
     condition_grad = silu_pull(activated_grad)[0]
-    (
-        query_bias_sum,
-        value_bias_sum,
-        query_gain_sum,
-        key_gain_sum,
-        proj_bias_sum,
-        up_bias_sum,
-        down_bias_sum,
-    ) = scatter_vectors(
-        (
-            query_bias_grad,
-            value_bias_grad,
-            query_gain_grad,
-            key_gain_grad,
-            proj_bias_grad,
-            up_bias_grad,
-            down_bias_grad,
-        ),
-        count,
-    )
     return (
         layer_output,
         input_grad,
@@ -309,7 +340,7 @@
     mat = P(AXES, None)
     vec = P(AXES)
     return jax.shard_map(
-        shards,
+        layer,
         mesh=mesh,
         in_specs=(row, mat, P(), mat, vec, mat, vec, vec, vec, vec, mat, vec, mat, vec, mat, vec, row),
         out_specs=(row, row, mat, mat, vec, mat, vec, vec, vec, vec, mat, vec, mat, vec, mat, vec),

time: 1200 us -> 903 us (0.75)
  waiting for transfers between devices: 593 us -> 299 us
  blocking collectives: 248 us -> 52.8 us
  local copies, waits for them, and re-layouts: 27.8 us -> 194 us
  other arithmetic: 83.2 us -> 105 us
    all_gather x4 -> x2, waiting for transfers between devices: 200 us -> 45.4 us  [gather_packed(): lax.all_gather(pack_rows([m[None] for m in members], 1), AXES, axis=0, ti...]
    all_gather x3 -> x4, blocking collectives: 206 us -> 52.8 us  [the longest x2 43 us: nested_gather(): lax.all_gather(lax.all_gather(member, 'narrow', axis=0, tiled=True), 'wid...]
    reduce_scatter x4, waiting for transfers between devices: 338 us -> 222 us  [the longest x2 222 us: scatter_packed(): half = lax.psum_scatter(flat, 'wide', scatter_dimension=0, tiled=True)]
    reshape x6 -> x20, local copies, waits for them, and re-layouts: 3.68 us -> 109 us  [the longest x6 29 us: pack_rows(): piece.reshape(count, -1)]
    unnamed x10 -> x6, waiting for transfers between devices: 55.9 us -> 0.1 us
    unnamed x1 -> x0, blocking collectives: 42 us -> none
    concatenate x0 -> x2, other arithmetic: none -> 34.7 us  [pack_rows(): jnp.concatenate([piece.reshape(count, -1) for piece in pieces], axis=1)]
    all_to_all x1 -> x2, waiting for transfers between devices: 0.01 us -> 31.3 us  [the longest x1 26.7 us: layer(): lax.all_to_all(ada_partial.reshape(count, sequences, ada_cols), AXES, spl...]
  transfers between devices with their start and end apart: 10 -> 8, of which waited for: 6 -> 5; matrix products, arithmetic and copies ran while one was open for 22% -> 21% of each run, Pallas kernels for 0% -> 0%
where the time goes in v2:
time: 903 us; the launch traced here: 893 us
  waiting for transfers between devices  299 us (33%)
  matrix products  221 us (24%)
  local copies, waits for them, and re-layouts  194 us (21%)
  other arithmetic  105 us (12%)
  blocking collectives  52.8 us (6%)
  between operations  15.6 us (2%)
    reduce_scatter x2, waiting for transfers between devices, scatter_packed(): half = lax.psum_scatter(flat, 'wide', scatter_dimension=0, tiled=True)  222 us
    all_gather x2, waiting for transfers between devices, gather_packed(): lax.all_gather(pack_rows([m[None] for m in members], 1), AXES, axis=0, ti...  45.4 us
    all_gather x2, blocking collectives, nested_gather(): lax.all_gather(lax.all_gather(member, 'narrow', axis=0, tiled=True), 'wid...  43 us
    dot_general x4, matrix products, matmul_rows(): jnp.einsum('fyg,gq->fyq', first_operand, second_operand, preferred_elemen...  42.9 us
    dot_general x4, matrix products, weight_grad(): jnp.einsum('crk,cre->ke', first_operand, second_operand, preferred_elemen...  41.7 us
    dot_general x4, matrix products, matmul_back(): jnp.einsum('rfw,uw->rfu', first_operand, second_operand, preferred_elemen...  38.1 us
    unnamed x188, local copies, waits for them, and re-layouts  35.6 us
    concatenate x2, other arithmetic, pack_rows(): jnp.concatenate([piece.reshape(count, -1) for piece in pieces], axis=1)  34.7 us
  transfers between devices with their start and end apart: 8, of which 5 were waited for; matrix products, arithmetic and copies ran while one was open for 21% of the time, Pallas kernels for 0%

profile of v2, /device:TPU:0, one launch (start us, length us, event | category | flops | bytes accessed | tf_op | source)
XLA Modules:
  0.0 893.2 jit_solution(7046384388813148858)
XLA Ops:
  13.0 16.5 %maximum_reduce_fusion = bf16[294912]{0:T(1024)(128)(2,1)S(1)} fusion(bf16[1,131072]{1,0:T(2,128)(2,1)S(1)} %bitcast.228, bf16[1,131072]{1,0:T(2,128)(2,1)S(1)} %bitcast.227, bf16[1,32768]{1,0:T(2,128)(2,1)S(1)} %bitcast.235), kind=kLoop, calls=%fused_computation.99 | loop fusion | flops 1769472 | bytes 1179648 | tf_op jit(solution)/shard_map/concatenate | solution.py:118
  36.6 22.5 %all-gather.2 = bf16[16,2,1536]{2,1,0:T(2,128)(2,1)S(1)} all-gather(bf16[1,2,1536]{2,1,0:T(2,128)(2,1)S(1)} %bitcast.242), channel_id=1, replica_groups=mesh['wide'=16,'narrow'=2] {'wide'}, dimensions={0}, use_global_device_ids=true | all-gather | bytes 104448 | tf_op jit(solution)/shard_map/all_gather | solution.py:109
  69.7 26.7 %all-to-all-done = f32[32,1,6144]{2,1,0:T(1,128)S(1)} async-done(((f32[32,1,6144]{2,1,0:T(1,128)}), f32[32,1,6144]{2,1,0:T(1,128)S(1)}, u32[]{:S(2)}, u32[]{:S(2)}) %all-to-all-start) | async-done | bytes 786464 | tf_op jit(solution)/shard_map/all_to_all | solution.py:199
  97.5 10.7 %reshape_reshape.3 = bf16[1024,3072]{1,0:T(8,128)(2,1)} reshape(bf16[3072,1024]{1,0:T(8,128)(2,1)} %all-gather.8.cloned.1.call-done) | data formatting | bytes 12582912 | tf_op jit(solution)/shard_map/reshape;reshape | solution.py:139
  130.6 14.0 %fusion.81 = (f32[16,680]{1,0:T(8,128)S(1)}, f32[16,680,680]{1,2,0:T(8,128)}) fusion(f32[680,16,64]{0,2,1:T(8,128)S(1)} %bitcast.214, f32[16,64]{1,0:T(8,128)S(1)} %reshape.924, f32[680,16]{0,1:T(8,128)S(1)} %get-tuple-element.79, f32[680,16,64]{0,2,1:T(8,128)S(1)} %bitcast.208, f32[16,64]{1,0:T(8,128)S(1)} %reshape.923, ...), kind=kOutput, calls=%fused_computation.182 | convolution fusion | flops 973357440 | bytes 35765312 | tf_op jit(solution)/shard_map/vmap(nkz,vkz->knv)/dot_general | solution.py:63
  144.6 13.4 %fusion = f32[16,680]{1,0:T(8,128)S(1)} fusion(f32[16,680,680]{1,2,0:T(8,128)} %get-tuple-element.64, f32[16,680]{1,0:T(8,128)S(1)} %get-tuple-element.63), kind=kLoop, calls=%fused_computation.6 | loop fusion | flops 14785920 | bytes 29680640 | tf_op jit(solution)/shard_map/vmap()/reduce_sum | solution.py:73
  158.6 17.7 %fusion.37 = bf16[16,64,680]{2,1,0:T(8,128)(2,1)} fusion(bf16[680,16,64]{0,2,1:T(8,128)(2,1)S(1)} %bitcast.220, f32[16,680,680]{1,2,0:T(8,128)} %get-tuple-element.64, f32[16,680]{1,0:T(8,128)S(1)} %fusion, f32[16,680]{1,0:T(8,128)S(1)} %get-tuple-element.63), kind=kOutput, calls=%fused_computation.90 | convolution fusion | flops 969886720 | bytes 32465920 | tf_op jit(solution)/shard_map/vmap(wcv,vwn->cwn)/dot_general | solution.py:75
  176.3 45.4 %all-gather.10.cloned.1.call-done = bf16[9216,1024]{1,0:T(8,128)(2,1)} async-done(((bf16[288,1024]{1,0:T(8,128)(2,1)}), bf16[9216,1024]{1,0:T(8,128)(2,1)}) %all-gather.10.cloned.1.call-update) | async-done | bytes 18874384 | tf_op jit(solution)/shard_map/all_gather | solution.py:136
  221.7 26.8 %reshape.888 = bf16[32,294912]{1,0:T(8,128)(2,1)} reshape(bf16[9216,1024]{1,0:T(8,128)(2,1)} %all-gather.10.cloned.1.call-done) | data formatting | bytes 37748736 | tf_op jit(solution)/shard_map/reshape | solution.py:126
  248.5 11.4 %fusion.78 = (bf16[32,131072]{1,0:T(8,128)(2,1)}, bf16[32,131072]{1,0:T(8,128)(2,1)}) fusion(bf16[32,294912]{1,0:T(8,128)(2,1)} %reshape.888), kind=kLoop, calls=%fused_computation.179 | loop fusion | bytes 33554432 | tf_op jit(solution)/shard_map/slice | solution.py:130
  268.5 9.4 %reshape.891 = bf16[1024,4096]{1,0:T(8,128)(2,1)} reshape(bf16[32,131072]{1,0:T(8,128)(2,1)} %get-tuple-element.36) | data formatting | bytes 16777216 | tf_op jit(solution)/shard_map/reshape | solution.py:139
  278.0 8.9 reshape.892
  286.9 12.6 %fusion.72 = f32[680,4096]{1,0:T(8,128)} fusion(bf16[1024,4096]{1,0:T(8,128)(2,1)} %reshape.891, f32[1,680,1024]{2,1,0:T(8,128)S(1)} %get-tuple-element.33, f32[1024]{0:T(1024)S(1)} %bitcast.261, f32[1024]{0:T(1024)S(1)} %bitcast.243, f32[680]{0:T(1024)S(1)} %fusion.63, f32[680]{0:T(1024)S(1)} %broadcast_multiply_fusion.2), kind=kOutput, calls=%fused_computation.174 | convolution fusion | flops 5707735040 | bytes 22328640 | tf_op jit(solution)/shard_map/fyg,gq->fyq/dot_general | solution.py:45
  299.5 14.1 %convolution_convert_fusion = bf16[4096,1024]{1,0:T(8,128)(2,1)} fusion(bf16[1,680,1024]{2,1,0:T(8,128)(2,1)S(1)} %copy-done.27, f32[1024]{0:T(1024)S(1)} %bitcast.247, f32[680,4096]{1,0:T(8,128)} %fusion.72, f32[4096]{0:T(1024)S(1)} %copy-done.50), kind=kOutput, calls=%fused_computation.22 | convolution fusion | flops 5738389504 | bytes 20942848 | tf_op jit(solution)/shard_map/crk,cre->ke/dot_general | solution.py:57
  313.6 16.7 %fusion.82 = (bf16[4096]{0:T(1024)(128)(2,1)}, bf16[680,4096]{1,0:T(8,128)(2,1)}) fusion(f32[680,4096]{1,0:T(8,128)} %fusion.72, f32[4096]{0:T(1024)S(1)} %copy-done.50, bf16[4096,1024]{1,0:T(8,128)(2,1)S(1)} %bitcast.219, f32[1024]{0:T(1024)S(1)} %bitcast.248, bf16[1,680,1024]{2,1,0:T(8,128)(2,1)S(1)} %copy-done.27), kind=kOutput, calls=%fused_computation.183 | convolution fusion | flops 5767614464 | bytes 26521600 | tf_op jit(solution)/shard_map/rfw,uw->rfu/dot_general | solution.py:51
  330.3 12.0 %convolution_convert_fusion.1 = bf16[1024,4096]{1,0:T(8,128)(2,1)} fusion(bf16[680,4096]{1,0:T(8,128)(2,1)} %get-tuple-element.77, f32[1,680,1024]{2,1,0:T(8,128)S(1)} %get-tuple-element.33, f32[1024]{0:T(1024)S(1)} %bitcast.262, f32[1024]{0:T(1024)S(1)} %bitcast.244, f32[680]{0:T(1024)S(1)} %fusion.63, f32[680]{0:T(1024)S(1)} %broadcast_multiply_fusion.2), kind=kOutput, calls=%fused_computation.23 | convolution fusion | flops 5711929344 | bytes 16758080 | tf_op jit(solution)/shard_map/crk,cre->ke/dot_general | solution.py:57
  342.3 9.6 %fusion.32 = (bf16[1024]{0:T(1024)(128)(2,1)}, f32[680]{0:T(1024)S(1)}, f32[680,1024]{1,0:T(8,128)S(1)}) fusion(f32[1,680,1024]{2,1,0:T(8,128)S(1)} %get-tuple-element.33, f32[680]{0:T(1024)S(1)} %fusion.63, f32[680]{0:T(1024)S(1)} %broadcast_multiply_fusion.2, f32[1024]{0:T(1024)S(1)} %bitcast.245, bf16[680,4096]{1,0:T(8,128)(2,1)S(1)} %copy-done.79, ...), kind=kOutput, calls=%fused_computation.76 | convolution fusion | flops 5709126144 | bytes 19544032 | tf_op jit(solution)/shard_map/rfw,uw->rfu/dot_general | solution.py:51
  361.2 26.0 %multiply_reduce_fusion = (f32[16,680]{1,0:T(8,128)}, f32[16,680,680]{1,2,0:T(8,128)}) fusion(f32[16,680,680]{1,2,0:T(8,128)} %get-tuple-element.64, f32[16,680]{1,0:T(8,128)} %log_add_fusion, bf16[680,16,64]{0,2,1:T(8,128)(2,1)S(1)} %bitcast.216, bf16[680,16,64]{0,2,1:T(8,128)(2,1)S(1)} %bitcast.221), kind=kOutput, calls=%fused_computation.1 | convolution fusion | flops 969179520 | bytes 62059520 | tf_op jit(solution)/shard_map/vmap(nkz,vkz->knv)/dot_general | solution.py:86
  387.2 16.3 %bitcast_convert_fusion = (bf16[1,680,16,64]{1,3,2,0:T(8,128)(2,1)}, f32[16,64,680]{2,1,0:T(8,128)}) fusion(bf16[680,16,64]{0,2,1:T(8,128)(2,1)S(1)} %bitcast.217, f32[16,680,680]{1,2,0:T(8,128)} %get-tuple-element.64, f32[16,680]{1,0:T(8,128)} %log_add_fusion), kind=kOutput, calls=%fused_computation.50 | convolution fusion | flops 962488320 | bytes 35207680 | tf_op jit(solution)/shard_map/vmap(fgs,gfu->sfu)/dot_general | solution.py:89
  408.0 8.9 reshape.912
  425.7 28.8 %multiply_convert_fusion = bf16[16,680,680]{1,2,0:T(8,128)(2,1)} fusion(f32[16,680,680]{1,2,0:T(8,128)} %get-tuple-element.70, f32[16,680,680]{1,2,0:T(8,128)} %get-tuple-element.64, f32[16,680]{1,0:T(8,128)} %get-tuple-element.69, f32[16,680]{1,0:T(8,128)} %log_add_fusion), kind=kLoop, calls=%fused_computation | loop fusion | flops 29593600 | bytes 74071040 | tf_op jit(solution)/shard_map/vmap()/convert_element_type | solution.py:98
  454.6 11.8 %fusion.23 = (f32[680,16]{0,1:T(8,128)S(1)}, f32[16,64,680]{2,1,0:T(8,128)}) fusion(f32[1,680,16,64]{1,3,2,0:T(8,128)S(1)} %bitcast.209, f32[16,64]{1,0:T(8,128)} %broadcast_multiply_fusion.1, bf16[16,680,680]{1,2,0:T(8,128)(2,1)} %multiply_convert_fusion, f32[680,16,64]{0,2,1:T(8,128)} %bitcast.212, f32[16,64]{1,0:T(8,128)S(1)} %copy-done.38, ...), kind=kOutput, calls=%fused_computation.58 | convolution fusion | flops 951162240 | bytes 23247872 | tf_op jit(solution)/shard_map/vmap(wcv,vwn->cwn)/dot_general | solution.py:99
  466.5 9.4 %fusion.20 = (bf16[16,64]{1,0:T(8,128)(2,1)}, f32[680,16]{0,1:T(8,128)S(1)}, f32[16,64,680]{2,1,0:T(8,128)S(1)}) fusion(f32[1,680,16,64]{1,3,2,0:T(8,128)S(1)} %bitcast.215, f32[680,16]{0,1:T(8,128)S(1)} %copy-done.17, f32[16,64]{1,0:T(8,128)S(1)} %copy-done.39, bf16[16,680,680]{1,2,0:T(8,128)(2,1)} %multiply_convert_fusion, ...), kind=kOutput, calls=%fused_computation.46 | convolution fusion | flops 953946496 | bytes 23293440 | tf_op jit(solution)/shard_map/vmap(fgs,gfu->sfu)/dot_general | solution.py:102
  483.5 11.1 %convolution_convert_fusion.2 = bf16[1024,3072]{1,0:T(8,128)(2,1)} fusion(bf16[680,1024]{0,1:T(8,128)(2,1)S(1)} %bitcast.234, bf16[680,1024]{0,1:T(8,128)(2,1)S(1)} %bitcast.229, bf16[680,1024]{0,1:T(8,128)(2,1)S(1)} %bitcast.232, bf16[1,680,1024]{2,1,0:T(8,128)(2,1)S(1)} %copy-done.7, f32[1024]{0:T(1024)S(1)} %bitcast.260, f32[1024]{0:T(1024)S(1)} %bitcast.252, ...), kind=kOutput, calls=%fused_computation.25 | convolution fusion | flops 4298047488 | bytes 11875648 | tf_op jit(solution)/shard_map/crk,cre->ke/dot_general | solution.py:57
  535.2 9.7 %reshape.901 = bf16[4608,1024]{1,0:T(8,128)(2,1)} reshape(bf16[32,147456]{1,0:T(8,128)(2,1)} %dynamic-update-slice.9) | data formatting | bytes 18874368 | tf_op jit(solution)/shard_map/reshape | solution.py:122
  544.9 18.2 %pad_maximum_fusion = bf16[32,262144]{1,0:T(8,128)(2,1)} fusion(bf16[32,131072]{1,0:T(8,128)(2,1)} %reshape.912, bf16[32,131072]{1,0:T(8,128)(2,1)} %reshape.911), kind=kLoop, calls=%fused_computation.8 | loop fusion | flops 33554432 | bytes 33554432 | tf_op jit(solution)/shard_map/concatenate | solution.py:118
  563.2 15.4 %reshape.913 = bf16[8192,1024]{1,0:T(8,128)(2,1)} reshape(bf16[32,262144]{1,0:T(8,128)(2,1)} %pad_maximum_fusion) | data formatting | bytes 33554432 | tf_op jit(solution)/shard_map/reshape | solution.py:122
  580.4 9.1 %fusion.28 = (f32[680]{0:T(1024)S(1)}, f32[680,1024]{1,0:T(8,128)S(1)}) fusion(bf16[1,680,1024]{2,1,0:T(8,128)(2,1)S(1)} %copy-done.8, f32[1024]{0:T(1024)S(1)} %bitcast.253, f32[680]{0:T(1024)S(1)} %copy-done.48, bf16[1024,3072]{1,0:T(8,128)(2,1)} %reshape_reshape.3, bf16[680,1024]{0,1:T(8,128)(2,1)} %bitcast.233, bf16[680,1024]{0,1:T(8,128)(2,1)S(1)} %bitcast.230, ...), kind=kOutput, calls=%fused_computation.69 | convolution fusion | flops 4294204672 | bytes 14656832 | tf_op jit(solution)/shard_map/rfw,uw->rfu/dot_general | solution.py:51
  592.4 62.1 %reduce-scatter.5.cloned.1.call-done = bf16[288,1024]{1,0:T(8,128)(2,1)} async-done(((bf16[4608,1024]{1,0:T(8,128)(2,1)}), bf16[288,1024]{1,0:T(8,128)(2,1)}) %reduce-scatter.5.cloned.1.call-update) | async-done | bytes 589840 | tf_op jit(solution)/shard_map/reduce_scatter | solution.py:146
  654.6 17.3 %fusion.30 = (bf16[1024]{0:T(1024)(128)(2,1)S(1)}, bf16[1024]{0:T(1024)(128)(2,1)S(1)}, f32[1,680,1024]{2,1,0:T(8,128)}, bf16[1,680,1024]{2,1,0:T(8,128)(2,1)}) fusion(bf16[1,680,1024]{2,1,0:T(8,128)(2,1)S(1)} %copy-done.28, f32[1024]{0:T(1024)S(1)} %reshape.927, f32[680,1024]{1,0:T(8,128)} %get-tuple-element.65, f32[1024]{0:T(1024)S(1)} %copy-done.65, ...), kind=kOutput, calls=%fused_computation.71 | convolution fusion | flops 5746726912 | bytes 37684512 | tf_op jit(solution)/shard_map/fyg,gq->fyq/dot_general | solution.py:45
  675.8 159.7 %reduce-scatter.9.cloned.1.call-done = bf16[512,1024]{1,0:T(8,128)(2,1)} async-done(((bf16[8192,1024]{1,0:T(8,128)(2,1)}), bf16[512,1024]{1,0:T(8,128)(2,1)}) %reduce-scatter.9.cloned.1.call-update) | async-done | bytes 1048592 | tf_op jit(solution)/shard_map/reduce_scatter | solution.py:146
  840.0 20.5 %all-gather.4 = bf16[16,2,6144]{2,1,0:T(2,128)(2,1)S(1)} all-gather(bf16[1,2,6144]{2,1,0:T(2,128)(2,1)S(1)} %bitcast.239), channel_id=1, replica_groups=mesh['wide'=16,'narrow'=2] {'wide'}, dimensions={0}, use_global_device_ids=true | all-gather | bytes 417792 | tf_op jit(solution)/shard_map/all_gather | solution.py:109
  (301 shorter events, 165.2 us)
Async XLA Ops:
  7.2 52.0 %copy-start = (bf16[32,6144]{1,0:T(8,128)(2,1)S(1)}, bf16[32,6144]{1,0:T(8,128)(2,1)}, u32[]{:S(2)}) copy-start(bf16[32,6144]{1,0:T(8,128)(2,1)} %param.20) | copy-start | bytes 1179652
  7.2 23.9 %copy-start.70 = (bf16[192]{0:T(256)(128)(2,1)S(1)}, bf16[192]{0:T(256)(128)(2,1)}, u32[]{:S(2)}) copy-start(bf16[192]{0:T(256)(128)(2,1)} %param.21) | copy-start | bytes 1156
  7.2 23.9 %copy-start.71 = (bf16[32]{0:T(256)(128)(2,1)S(1)}, bf16[32]{0:T(256)(128)(2,1)}, u32[]{:S(2)}) copy-start(bf16[32]{0:T(256)(128)(2,1)} %param.23) | copy-start | bytes 196
  7.2 23.9 %copy-start.72 = (bf16[32]{0:T(256)(128)(2,1)S(1)}, bf16[32]{0:T(256)(128)(2,1)}, u32[]{:S(2)}) copy-start(bf16[32]{0:T(256)(128)(2,1)} %param.24) | copy-start | bytes 196
  7.2 23.9 %copy-start.73 = (bf16[32]{0:T(256)(128)(2,1)S(1)}, bf16[32]{0:T(256)(128)(2,1)}, u32[]{:S(2)}) copy-start(bf16[32]{0:T(256)(128)(2,1)} %param.25) | copy-start | bytes 196
  7.3 23.9 %copy-start.74 = (bf16[32]{0:T(256)(128)(2,1)S(1)}, bf16[32]{0:T(256)(128)(2,1)}, u32[]{:S(2)}) copy-start(bf16[32]{0:T(256)(128)(2,1)} %param.26) | copy-start | bytes 196
  7.3 90.2 %all-gather.8.cloned.1.call-start = ((), (), s32[]{:S(2)}) async-start(), calls=%async_computation.6 | async-start | bytes 6488064 | tf_op jit(solution)/shard_map/all_gather | solution.py:136
  9.1 212.6 %all-gather.10.cloned.1.call-start = ((), (), s32[]{:S(2)}) async-start(), calls=%async_computation.7 | async-start | bytes 19464192 | tf_op jit(solution)/shard_map/all_gather | solution.py:136
  30.5 34.5 %copy-start.78 = (s32[10]{0:T(128)S(1)}, s32[10]{0:T(128)}, u32[]{:S(2)}) copy-start(s32[10]{0:T(128)} %param.19) | copy-start | bytes 124
  30.5 35.4 %copy-start.6 = (bf16[1,680,1024]{2,1,0:T(8,128)(2,1)S(1)}, bf16[1,680,1024]{2,1,0:T(8,128)(2,1)}, u32[]{:S(2)}) copy-start(bf16[1,680,1024]{2,1,0:T(8,128)(2,1)} %param.17) | copy-start | bytes 4177924
  61.2 35.2 %all-to-all-start = ((f32[32,1,6144]{2,1,0:T(1,128)}), f32[32,1,6144]{2,1,0:T(1,128)S(1)}, u32[]{:S(2)}, u32[]{:S(2)}) async-start(f32[32,1,6144]{2,1,0:T(1,128)} %copy.83), calls=%async_computation | async-start | bytes 1572864 | tf_op jit(solution)/shard_map/all_to_all | solution.py:199
  63.8 590.7 %reduce-scatter.5.cloned.1.call-start = ((), (), s32[]{:S(2)}) async-start(), calls=%async_computation.8 | async-start | bytes 10027008 | tf_op jit(solution)/shard_map/reduce_scatter | solution.py:146
  64.9 65.6 %copy-start.35 = (f32[16,64]{1,0:T(8,128)}, f32[16,64]{1,0:T(8,128)S(1)}, u32[]{:S(2)}) copy-start(f32[16,64]{1,0:T(8,128)S(1)} %reshape.923) | copy-start | bytes 12292
  65.0 65.6 %copy-start.37 = (f32[16,64]{1,0:T(8,128)}, f32[16,64]{1,0:T(8,128)S(1)}, u32[]{:S(2)}) copy-start(f32[16,64]{1,0:T(8,128)S(1)} %reshape.924) | copy-start | bytes 12292
  66.2 42.0 %copy-start.47 = (f32[680]{0:T(1024)}, f32[680]{0:T(1024)S(1)}, u32[]{:S(2)}) copy-start(f32[680]{0:T(1024)S(1)} %broadcast_multiply_fusion.3) | copy-start | bytes 8164
  66.7 41.5 %copy-start.45 = (f32[680]{0:T(1024)}, f32[680]{0:T(1024)S(1)}, u32[]{:S(2)}) copy-start(f32[680]{0:T(1024)S(1)} %fusion.27) | copy-start | bytes 8164
  66.7 41.5 %copy-start.43 = (f32[680]{0:T(1024)}, f32[680]{0:T(1024)S(1)}, u32[]{:S(2)}) copy-start(f32[680]{0:T(1024)S(1)} %fusion.62) | copy-start | bytes 8164
  268.1 83.8 %copy-start.9 = (f32[1,680,1024]{2,1,0:T(8,128)}, f32[1,680,1024]{2,1,0:T(8,128)S(1)}, u32[]{:S(2)}) copy-start(f32[1,680,1024]{2,1,0:T(8,128)S(1)} %get-tuple-element.33) | copy-start | bytes 8355844
  286.9 26.7 %slice-start.1 = ((s8[8388608]{0:T(1024)(128)(4,1)}), s8[4194304]{0:T(1024)(128)(4,1)S(1)}, s32[]{:S(2)}) async-start(s8[8388608]{0:T(1024)(128)(4,1)} %bitcast.218), calls=%async_computation.13 | async-start | bytes 8388608
  425.7 28.8 %copy-start.2 = (f32[1,680,1024]{1,2,0:T(8,128)S(1)}, f32[1,680,1024]{1,2,0:T(8,128)}, u32[]{:S(2)}) copy-start(f32[1,680,1024]{1,2,0:T(8,128)} %copy-done.1) | copy-start | bytes 8355844
  425.7 28.8 %copy-start.38 = (f32[16,64]{1,0:T(8,128)S(1)}, f32[16,64]{1,0:T(8,128)}, u32[]{:S(2)}) copy-start(f32[16,64]{1,0:T(8,128)} %copy-done.37) | copy-start | bytes 12292
  544.9 290.6 %reduce-scatter.9.cloned.1.call-start = ((), (), s32[]{:S(2)}) async-start(), calls=%async_computation.10 | async-start | bytes 17825792 | tf_op jit(solution)/shard_map/reduce_scatter | solution.py:146
  578.6 295.0 %reduce-scatter.7.cloned.1.call-start = ((), (), s32[]{:S(2)}) async-start(), calls=%async_computation.9 | async-start | bytes 884736 | tf_op jit(solution)/shard_map/reduce_scatter | solution.py:147
  589.5 65.1 %copy-start.28 = (bf16[1,680,1024]{2,1,0:T(8,128)(2,1)S(1)}, bf16[1,680,1024]{2,1,0:T(8,128)(2,1)}, u32[]{:S(2)}) copy-start(bf16[1,680,1024]{2,1,0:T(8,128)(2,1)} %param.33) | copy-start | bytes 4177924
  589.5 65.1 %copy-start.51 = (f32[4096]{0:T(1024)S(1)}, f32[4096]{0:T(1024)}, u32[]{:S(2)}) copy-start(f32[4096]{0:T(1024)} %fusion.56) | copy-start | bytes 49156
  589.5 65.1 %copy-start.56 = (f32[1,1024]{1,0:T(1,128)S(1)}, f32[1,1024]{1,0:T(1,128)}, u32[]{:S(2)}) copy-start(f32[1,1024]{1,0:T(1,128)} %get-tuple-element.57) | copy-start | bytes 12292
  589.5 65.1 %copy-start.62 = (f32[680]{0:T(1024)S(1)}, f32[680]{0:T(1024)}, u32[]{:S(2)}) copy-start(f32[680]{0:T(1024)} %copy-done.61) | copy-start | bytes 8164
  589.5 65.1 %copy-start.65 = (f32[1024]{0:T(1024)S(1)}, f32[1024]{0:T(1024)}, u32[]{:S(2)}) copy-start(f32[1024]{0:T(1024)} %reshape.925) | copy-start | bytes 12292
  654.5 224.7 %reduce-scatter.11.cloned.1.call-start = ((), (), s32[]{:S(2)}) async-start(), calls=%async_computation.11 | async-start | bytes 1572864 | tf_op jit(solution)/shard_map/reduce_scatter | solution.py:147
  675.5 197.4 %copy-start.53 = (bf16[1,1024]{1,0:T(2,128)(2,1)S(1)}, bf16[1,1024]{1,0:T(2,128)(2,1)}, u32[]{:S(2)}) copy-start(bf16[1,1024]{1,0:T(2,128)(2,1)} %param.18) | copy-start | bytes 6148
  675.5 197.4 %copy-start.54 = (f32[1,1024]{1,0:T(1,128)S(1)}, f32[1,1024]{1,0:T(1,128)}, u32[]{:S(2)}) copy-start(f32[1,1024]{1,0:T(1,128)} %get-tuple-element.35) | copy-start | bytes 12292
  861.6 10.1 %all-to-all-start.1 = ((f32[32,1,32]{2,1,0:T(1,128)}), f32[32,1,32]{2,1,0:T(1,128)S(1)}, u32[]{:S(2)}, u32[]{:S(2)}) async-start(f32[32,1,32]{2,1,0:T(1,128)} %bitcast.46), calls=%async_computation.1 | async-start | bytes 32768 | tf_op jit(solution)/shard_map/all_to_all | solution.py:313
  (59 other events, 488.0 us)
Sparse Core Ops, SparseCore 0:
  11.6 84.5 all-gather.7
  99.0 122.6 all-gather.9
  545.0 109.4 reduce-scatter.4
  658.5 176.9 reduce-scatter.8
  837.6 14.4 reduce-scatter.6
  854.1 20.5 reduce-scatter.10

commit v3 on v2

--- a/solution.py
+++ b/solution.py
@@ -112,44 +112,79 @@
 
 
 LANES = 1024
-
-
-def pack_rows(pieces, count):
-    flat = jnp.concatenate([piece.reshape(count, -1) for piece in pieces], axis=1)
-    pad = -flat.shape[1] % (LANES * 16)
+TILE_ROWS = 16
+
+
+def shard_rows(shard):
+    rows, cols = shard.shape
+    blocks = cols // LANES
+    if blocks == 1:
+        return shard
+    return shard.reshape(rows, blocks, LANES).transpose(1, 0, 2).reshape(blocks * rows, LANES)
+
+
+def rows_shard(piece, cols):
+    blocks = cols // LANES
+    if blocks == 1:
+        return piece
+    rows = piece.shape[0] // blocks
+    return piece.reshape(blocks, rows, LANES).transpose(1, 0, 2).reshape(rows, cols)
+
+
+def pad_rows(flat):
+    pad = -flat.shape[1] % TILE_ROWS
     if pad:
-        flat = jnp.concatenate([flat, jnp.zeros((count, pad), flat.dtype)], axis=1)
-    return flat.reshape(count * (flat.shape[1] // LANES), LANES)
-
-
-def unpack_rows(flat, members, count, leading):
-    flat = flat.reshape(leading, -1)
+        flat = jnp.concatenate([flat, jnp.zeros((flat.shape[0], pad, LANES), flat.dtype)], axis=1)
+    return flat
+
+
+def gather_packed(members, count):
+    flat = pad_rows(jnp.concatenate([shard_rows(m) for m in members], axis=0)[None])
+    got = lax.all_gather(flat[0], AXES, axis=0, tiled=True).reshape(count, flat.shape[1], LANES)
     out, start = [], 0
     for member in members:
-        size = member.size // count
-        out.append(flat[:, start : start + size])
-        start += size
+        rows, cols = member.shape
+        blocks = cols // LANES
+        piece = got[:, start : start + blocks * rows]
+        start += blocks * rows
+        full = piece.reshape(count, blocks, rows, LANES).transpose(0, 2, 1, 3)
+        out.append(full.reshape(count * rows, cols))
     return out
 
 
-def gather_packed(members, count):
-    got = lax.all_gather(pack_rows([m[None] for m in members], 1), AXES, axis=0, tiled=True)
-    pieces = unpack_rows(got, [m[None] for m in members], 1, count)
-    return [
-        piece.reshape((count * member.shape[0],) + member.shape[1:])
-        for piece, member in zip(pieces, members)
-    ]
-
-
-def scatter_packed(members, count):
-    flat = pack_rows([member.astype(jnp.bfloat16) for member in members], count)
+def scatter_packed(matrices, vectors, count):
+    pieces = []
+    for member in matrices:
+        rows, cols = member.shape
+        shard = member.astype(jnp.bfloat16).reshape(count, rows // count, cols)
+        blocks = cols // LANES
+        shard = shard.reshape(count, rows // count, blocks, LANES).transpose(0, 2, 1, 3)
+        pieces.append(shard.reshape(count, blocks * rows // count, LANES))
+    if vectors:
+        small = jnp.concatenate([v.reshape(count, -1) for v in vectors], axis=1)
+        pad = -small.shape[1] % LANES
+        small = jnp.concatenate([small, jnp.zeros((count, pad), small.dtype)], axis=1)
+        pieces.append(small.astype(jnp.bfloat16).reshape(count, -1, LANES))
+    flat = pad_rows(jnp.concatenate(pieces, axis=1))
+    flat = flat.reshape(count * flat.shape[1], LANES)
     half = lax.psum_scatter(flat, "wide", scatter_dimension=0, tiled=True)
     got = lax.psum_scatter(half, "narrow", scatter_dimension=0, tiled=True)
-    pieces = unpack_rows(got.astype(jnp.float32), members, count, 1)
-    return [
-        piece.reshape((member.shape[0] // count,) + member.shape[1:])
-        for piece, member in zip(pieces, members)
-    ]
+    got = got.astype(jnp.float32)
+    out, start = [], 0
+    for member in matrices:
+        rows, cols = member.shape
+        blocks = cols // LANES
+        size = blocks * rows // count
+        out.append(rows_shard(got[start : start + size], cols))
+        start += size
+    if vectors:
+        tail = got[start:].reshape(-1)
+        offset = 0
+        for v in vectors:
+            size = v.shape[0] // count
+            out.append(tail[offset : offset + size])
+            offset += size
+    return out
 
 
 def layer(
@@ -188,7 +223,7 @@
         unpacked.append(small[:, start : start + size].reshape(count * size).astype(jnp.float32))
         start += size
     ada_bias, query_bias, value_bias, query_gain, key_gain, proj_bias, up_bias, down_bias = unpacked
-    (qkv_full,) = gather_packed((w_qkv,), count)
+    qkv_full = lax.all_gather(w_qkv, AXES, axis=0, tiled=True)
     proj_full, up_full, down_full = gather_packed((w_proj, w_up, w_down), count)
     allowed = block_mask(scale_tokens)
     input_rows = inputs.astype(jnp.float32)
@@ -230,7 +265,6 @@
     gelu_pull = jax.vjp(gelu_tanh, hidden_pre)[1]
     pre_grad = gelu_pull(hidden_grad)[0].astype(jnp.bfloat16)
     up_grad = weight_grad(normed_mlp, pre_grad)
-    down_sum, up_sum = scatter_packed((down_grad, up_grad), count)
     up_bias_grad = jnp.sum(pre_grad.astype(jnp.float32), axis=(0, 1))
     normed_mlp_grad = matmul_back(pre_grad, up_full)
     mlp_pull = jax.vjp(modulate, middle, scale_mlp, shift_mlp)[1]
@@ -240,6 +274,7 @@
     attended_grad = (middle_grad * gamma_attn[:, None, :]).astype(jnp.bfloat16)
     proj_grad = weight_grad(context, attended_grad)
     proj_bias_grad = jnp.sum(attended_grad.astype(jnp.float32), axis=(0, 1))
+    down_sum, up_sum, proj_sum = scatter_packed((down_grad, up_grad, proj_grad), (), count)
     context_gradient = (
         matmul_back(attended_grad, proj_full).astype(jnp.bfloat16).reshape(head_shape)
     )
@@ -258,7 +293,6 @@
     )
     qkv_grad = weight_grad(normed_attn, projected_grad)
     (
-        proj_sum,
         qkv_sum,
         query_bias_sum,
         value_bias_sum,
@@ -268,9 +302,8 @@
         up_bias_sum,
         down_bias_sum,
     ) = scatter_packed(
+        (qkv_grad,),
         (
-            proj_grad,
-            qkv_grad,
             query_bias_grad,
             value_bias_grad,
             query_gain_grad,
@@ -281,6 +314,23 @@
         ),
         count,
     )
+    return tail(
+        projected_grad, qkv_full, input_rows, scale_attn, shift_attn, middle_grad,
+        gamma_attn_grad, gamma_mlp_grad, scale_mlp_grad, shift_mlp_grad, activated_mine,
+        w_ada, cond_rows, me, count, layer_output, qkv_sum, query_bias_sum, value_bias_sum,
+        query_gain_sum, key_gain_sum, proj_sum, proj_bias_sum, up_sum, up_bias_sum, down_sum,
+        down_bias_sum,
+    )
+
+
+def tail(
+    projected_grad, qkv_full, input_rows, scale_attn, shift_attn, middle_grad,
+    gamma_attn_grad, gamma_mlp_grad, scale_mlp_grad, shift_mlp_grad, activated_mine,
+    w_ada, cond_rows, me, count, layer_output, qkv_sum, query_bias_sum, value_bias_sum,
+    query_gain_sum, key_gain_sum, proj_sum, proj_bias_sum, up_sum, up_bias_sum, down_sum,
+    down_bias_sum,
+):
+    ada_cols = w_ada.shape[1]
     normed_attn_grad = matmul_back(projected_grad, qkv_full)
     attn_pull = jax.vjp(modulate, input_rows, scale_attn, shift_attn)[1]
     input_part, scale_attn_grad, shift_attn_grad = attn_pull(normed_attn_grad)

time: 903 us -> 823 us (0.911)
  local copies, waits for them, and re-layouts: 194 us -> 128 us
    reshape x19 -> x3, local copies, waits for them, and re-layouts: 107 us -> 2.57 us  [the longest x2 1.6 us: rows_shard(): piece.reshape(blocks, rows, LANES).transpose(1, 0, 2).reshape(rows, cols)]
    transpose x0 -> x3, local copies, waits for them, and re-layouts: none -> 28.5 us  [the longest x2 20.8 us: scatter_packed(): shard.reshape(count, rows // count, blocks, LANES).transpose(0, 2, 1, 3)]
    reduce_scatter x2, waiting for transfers between devices: 222 us -> 200 us  [scatter_packed(): half = lax.psum_scatter(flat, 'wide', scatter_dimension=0, tiled=True)]
    another operation x2, local copies, waits for them, and re-layouts: 12.5 us -> 33.4 us  [scatter_packed(): shard.reshape(count, rows // count, blocks, LANES).transpose(0, 2, 1, 3)]
    all_gather x2, waiting for transfers between devices: 45.4 us -> 66.1 us  [the longest x1 60.2 us: gather_packed(): lax.all_gather(flat[0], AXES, axis=0, tiled=True)]
    unnamed x188 -> x173, local copies, waits for them, and re-layouts: 35.6 us -> 19.7 us
    concatenate x2 -> x3, other arithmetic: 34.7 us -> 28.8 us  [the longest x1 18.5 us: scatter_packed(): flat = pad_rows(jnp.concatenate(pieces, axis=1))]
  transfers between devices with their start and end apart: 8 -> 8, of which waited for: 5 -> 6; matrix products, arithmetic and copies ran while one was open for 21% -> 24% of each run, Pallas kernels for 0% -> 0%
where the time goes in v3:
time: 823 us; the launch traced here: 818 us
  waiting for transfers between devices  298 us (36%)
  matrix products  214 us (26%)
  local copies, waits for them, and re-layouts  128 us (16%)
  other arithmetic  104 us (13%)
  blocking collectives  52.8 us (6%)
  between operations  15.3 us (2%)
    reduce_scatter x2, waiting for transfers between devices, scatter_packed(): half = lax.psum_scatter(flat, 'wide', scatter_dimension=0, tiled=True)  200 us
    all_gather x1, waiting for transfers between devices, gather_packed(): lax.all_gather(flat[0], AXES, axis=0, tiled=True)  60.2 us
    all_gather x2, blocking collectives, nested_gather(): lax.all_gather(lax.all_gather(member, 'narrow', axis=0, tiled=True), 'wid...  43 us
    dot_general x4, matrix products, weight_grad(): jnp.einsum('crk,cre->ke', first_operand, second_operand, preferred_elemen...  40.3 us
    dot_general x4, matrix products, matmul_back(): jnp.einsum('rfw,uw->rfu', first_operand, second_operand, preferred_elemen...  39.6 us
    dot_general x4, matrix products, matmul_rows(): jnp.einsum('fyg,gq->fyq', first_operand, second_operand, preferred_elemen...  39 us
    another operation x2, local copies, waits for them, and re-layouts, scatter_packed(): shard.reshape(count, rows // count, blocks, LANES).transpose(0, 2, 1, 3)  33.4 us
    convert_element_type x1, other arithmetic, attend_backward(): score_gradient = (attention_probabilities * (prob_grad - jnp.sum(prob_gra...  28.8 us
  transfers between devices with their start and end apart: 8, of which 6 were waited for; matrix products, arithmetic and copies ran while one was open for 24% of the time, Pallas kernels for 0%

profile of v3, /device:TPU:0, one launch (start us, length us, event | category | flops | bytes accessed | tf_op | source)
XLA Modules:
  0.0 817.5 jit_solution(6927452381931276416)
XLA Ops:
  23.0 22.5 %all-gather.2 = bf16[16,2,1536]{2,1,0:T(2,128)(2,1)S(1)} all-gather(bf16[1,2,1536]{2,1,0:T(2,128)(2,1)S(1)} %bitcast.263), channel_id=1, replica_groups=mesh['wide'=16,'narrow'=2] {'wide'}, dimensions={0}, use_global_device_ids=true | all-gather | bytes 104448 | tf_op jit(solution)/shard_map/all_gather | solution.py:109
  56.6 26.3 %all-to-all-done = f32[32,1,6144]{2,1,0:T(1,128)S(1)} async-done(((f32[32,1,6144]{2,1,0:T(1,128)}), f32[32,1,6144]{2,1,0:T(1,128)S(1)}, u32[]{:S(2)}, u32[]{:S(2)}) %all-to-all-start) | async-done | bytes 786464 | tf_op jit(solution)/shard_map/all_to_all | solution.py:234
  89.9 7.4 convolution_bitcast_fusion.1
  111.9 14.4 %fusion.83 = (f32[16,680]{1,0:T(8,128)S(1)}, f32[16,680,680]{1,2,0:T(8,128)}) fusion(f32[680,16,64]{0,2,1:T(8,128)S(1)} %bitcast.220, f32[16,64]{1,0:T(8,128)S(1)} %reshape.975, f32[680,16]{0,1:T(8,128)S(1)} %get-tuple-element.79, f32[680,16,64]{0,2,1:T(8,128)S(1)} %bitcast.214, f32[16,64]{1,0:T(8,128)S(1)} %reshape.974, ...), kind=kOutput, calls=%fused_computation.172 | convolution fusion | flops 973357440 | bytes 35765312 | tf_op jit(solution)/shard_map/vmap(nkz,vkz->knv)/dot_general | solution.py:63
  126.3 13.4 %fusion = f32[16,680]{1,0:T(8,128)S(1)} fusion(f32[16,680,680]{1,2,0:T(8,128)} %get-tuple-element.64, f32[16,680]{1,0:T(8,128)S(1)} %get-tuple-element.63), kind=kLoop, calls=%fused_computation.6 | loop fusion | flops 14785920 | bytes 29680640 | tf_op jit(solution)/shard_map/vmap()/reduce_sum | solution.py:73
  140.3 15.1 %fusion.37 = bf16[16,64,680]{2,1,0:T(8,128)(2,1)} fusion(bf16[680,16,64]{0,2,1:T(8,128)(2,1)S(1)} %bitcast.241, f32[16,680,680]{1,2,0:T(8,128)} %get-tuple-element.64, f32[16,680]{1,0:T(8,128)S(1)} %fusion, f32[16,680]{1,0:T(8,128)S(1)} %get-tuple-element.63), kind=kOutput, calls=%fused_computation.91 | convolution fusion | flops 969886720 | bytes 32465920 | tf_op jit(solution)/shard_map/vmap(wcv,vwn->cwn)/dot_general | solution.py:75
  155.4 60.2 %all-gather.10.cloned.1.call-done = bf16[9216,1024]{1,0:T(8,128)(2,1)} async-done(((bf16[288,1024]{1,0:T(8,128)(2,1)}), bf16[9216,1024]{1,0:T(8,128)(2,1)}) %all-gather.10.cloned.1.call-update) | async-done | bytes 18874384 | tf_op jit(solution)/shard_map/all_gather | solution.py:143
  217.3 10.2 %fusion.78 = (bf16[32,128,1024]{2,1,0:T(8,128)(2,1)S(1)}, bf16[32,128,1024]{2,1,0:T(8,128)(2,1)}) fusion(bf16[32,288,1024]{2,1,0:T(8,128)(2,1)} %bitcast.231), kind=kLoop, calls=%fused_computation.167 | loop fusion | bytes 33554432 | tf_op jit(solution)/shard_map/slice | solution.py:148
  227.5 7.8 copy.155
  235.3 12.2 %copy.181 = bf16[128,8,4,1024]{3,1,2,0:T(8,128)(2,1)} copy(bf16[128,8,4,1024]{3,2,1,0:T(4,128)(2,1)} %bitcast.224) | data formatting | bytes 16777216
  253.1 9.2 %fusion.72 = f32[680,4096]{1,0:T(8,128)} fusion(bf16[1024,4096]{1,0:T(8,128)(2,1)S(1)} %bitcast.234, f32[1,680,1024]{2,1,0:T(8,128)S(1)} %get-tuple-element.31, f32[1024]{0:T(1024)S(1)} %bitcast.280, f32[1024]{0:T(1024)S(1)} %bitcast.264, f32[680]{0:T(1024)S(1)} %fusion.63, f32[680]{0:T(1024)S(1)} %broadcast_multiply_fusion.2), kind=kOutput, calls=%fused_computation.162 | convolution fusion | flops 5707735040 | bytes 22328640 | tf_op jit(solution)/shard_map/fyg,gq->fyq/dot_general | solution.py:45
  262.3 18.4 %fusion.84 = (bf16[4096]{0:T(1024)(128)(2,1)S(1)}, bf16[680,4096]{1,0:T(8,128)(2,1)}) fusion(f32[680,4096]{1,0:T(8,128)} %fusion.72, f32[4096]{0:T(1024)S(1)} %copy-done.57, bf16[4096,1024]{1,0:T(8,128)(2,1)} %bitcast.238, f32[1024]{0:T(1024)S(1)} %bitcast.268, bf16[1,680,1024]{2,1,0:T(8,128)(2,1)S(1)} %copy-done.24), kind=kOutput, calls=%fused_computation.173 | convolution fusion | flops 5767614464 | bytes 26521600 | tf_op jit(solution)/shard_map/rfw,uw->rfu/dot_general | solution.py:51
  280.7 9.5 %fusion.32 = (bf16[1024]{0:T(1024)(128)(2,1)}, f32[680]{0:T(1024)S(1)}, f32[680,1024]{1,0:T(8,128)S(1)}) fusion(f32[1,680,1024]{2,1,0:T(8,128)S(1)} %get-tuple-element.31, f32[680]{0:T(1024)S(1)} %fusion.63, f32[680]{0:T(1024)S(1)} %broadcast_multiply_fusion.2, f32[1024]{0:T(1024)S(1)} %bitcast.265, bf16[680,4096]{1,0:T(8,128)(2,1)} %get-tuple-element.77, ...), kind=kOutput, calls=%fused_computation.77 | convolution fusion | flops 5709126144 | bytes 19544032 | tf_op jit(solution)/shard_map/rfw,uw->rfu/dot_general | solution.py:51
  299.2 15.8 %bitcast_convert_fusion = (bf16[1,680,16,64]{1,3,2,0:T(8,128)(2,1)}, f32[16,64,680]{2,1,0:T(8,128)}) fusion(bf16[680,16,64]{0,2,1:T(8,128)(2,1)S(1)} %bitcast.232, f32[16,680,680]{1,2,0:T(8,128)} %get-tuple-element.64, f32[16,680]{1,0:T(8,128)} %log_add_fusion), kind=kOutput, calls=%fused_computation.51 | convolution fusion | flops 962488320 | bytes 35207680 | tf_op jit(solution)/shard_map/vmap(fgs,gfu->sfu)/dot_general | solution.py:89
  315.0 26.1 %multiply_reduce_fusion = (f32[16,680]{1,0:T(8,128)}, f32[16,680,680]{1,2,0:T(8,128)}) fusion(f32[16,680,680]{1,2,0:T(8,128)} %get-tuple-element.64, f32[16,680]{1,0:T(8,128)} %log_add_fusion, bf16[680,16,64]{0,2,1:T(8,128)(2,1)S(1)} %bitcast.233, bf16[680,16,64]{0,2,1:T(8,128)(2,1)S(1)} %bitcast.242), kind=kOutput, calls=%fused_computation.1 | convolution fusion | flops 969179520 | bytes 62059520 | tf_op jit(solution)/shard_map/vmap(nkz,vkz->knv)/dot_general | solution.py:86
  345.9 28.8 %multiply_convert_fusion = bf16[16,680,680]{1,2,0:T(8,128)(2,1)} fusion(f32[16,680,680]{1,2,0:T(8,128)} %get-tuple-element.70, f32[16,680,680]{1,2,0:T(8,128)} %get-tuple-element.64, f32[16,680]{1,0:T(8,128)} %get-tuple-element.69, f32[16,680]{1,0:T(8,128)} %log_add_fusion), kind=kLoop, calls=%fused_computation | loop fusion | flops 29593600 | bytes 74071040 | tf_op jit(solution)/shard_map/vmap()/convert_element_type | solution.py:98
  374.8 10.1 %fusion.23 = (f32[680,16]{0,1:T(8,128)S(1)}, f32[16,64,680]{2,1,0:T(8,128)S(1)}) fusion(f32[1,680,16,64]{1,3,2,0:T(8,128)S(1)} %bitcast.215, f32[16,64]{1,0:T(8,128)} %broadcast_multiply_fusion.1, bf16[16,680,680]{1,2,0:T(8,128)(2,1)} %multiply_convert_fusion, f32[680,16,64]{0,2,1:T(8,128)} %bitcast.219, f32[16,64]{1,0:T(8,128)S(1)} %copy-done.36, ...), kind=kOutput, calls=%fused_computation.59 | convolution fusion | flops 951162240 | bytes 23247872 | tf_op jit(solution)/shard_map/vmap(wcv,vwn->cwn)/dot_general | solution.py:99
  384.9 10.5 %fusion.20 = (bf16[16,64]{1,0:T(8,128)(2,1)}, f32[680,16]{0,1:T(8,128)S(1)}, f32[16,64,680]{2,1,0:T(8,128)}) fusion(f32[1,680,16,64]{1,3,2,0:T(8,128)S(1)} %bitcast.221, f32[680,16]{0,1:T(8,128)S(1)} %copy-done.16, f32[16,64]{1,0:T(8,128)S(1)} %copy-done.37, bf16[16,680,680]{1,2,0:T(8,128)(2,1)} %multiply_convert_fusion, f32[680,16,64]{0,2,1:T(8,128)S(1)} %bitcast.216, ...), kind=kOutput, calls=%fused_computation.47 | convolution fusion | flops 953946496 | bytes 23293440 | tf_op jit(solution)/shard_map/vmap(fgs,gfu->sfu)/dot_general | solution.py:102
  406.8 10.8 %convolution_convert_fusion.2 = bf16[1024,3072]{1,0:T(8,128)(2,1)} fusion(bf16[680,1024]{0,1:T(8,128)(2,1)S(1)} %bitcast.253, bf16[680,1024]{0,1:T(8,128)(2,1)S(1)} %bitcast.248, bf16[680,1024]{0,1:T(8,128)(2,1)S(1)} %bitcast.251, bf16[1,680,1024]{2,1,0:T(8,128)(2,1)S(1)} %copy-done.7, f32[1024]{0:T(1024)S(1)} %bitcast.283, f32[1024]{0:T(1024)S(1)} %bitcast.273, ...), kind=kOutput, calls=%fused_computation.26 | convolution fusion | flops 4298047488 | bytes 11875648 | tf_op jit(solution)/shard_map/crk,cre->ke/dot_general | solution.py:57
  417.6 18.6 %reshape_reshape.6 = bf16[32,32,3,1024]{3,2,1,0:T(4,128)(2,1)} reshape(bf16[1024,3072]{1,0:T(8,128)(2,1)} %convolution_convert_fusion.2) | data formatting | bytes 12582912 | tf_op jit(solution)/shard_map/reshape;reshape | solution.py:161
  436.2 9.2 %copy.161 = bf16[32,3,32,1024]{3,2,1,0:T(8,128)(2,1)} copy(bf16[32,3,32,1024]{3,1,2,0:T(4,128)(2,1)} %bitcast.223) | data formatting | bytes 12582912 | tf_op jit(solution)/shard_map/transpose | solution.py:161
  448.1 8.4 %maximum_maximum_fusion = bf16[32,112,1024]{2,1,0:T(8,128)(2,1)} fusion(bf16[32,1,1024]{2,1,0:T(2,128)(2,1)S(1)} %concatenate.95, bf16[32,96,1024]{2,1,0:T(8,128)(2,1)} %bitcast.229, bf16[112]{0:T(256)(128)(2,1)} %pad.5.clone), kind=kLoop, calls=%fused_computation.24 | loop fusion | flops 22020096 | bytes 13697248 | tf_op jit(solution)/shard_map/concatenate | solution.py:137
  457.2 12.3 %convolution_convert_fusion.1 = bf16[1024,4096]{1,0:T(8,128)(2,1)} fusion(bf16[680,4096]{1,0:T(8,128)(2,1)} %get-tuple-element.77, f32[1,680,1024]{2,1,0:T(8,128)} %copy-done.8, f32[1024]{0:T(1024)S(1)} %bitcast.281, f32[1024]{0:T(1024)S(1)} %bitcast.267, f32[680]{0:T(1024)S(1)} %copy-done.56, f32[680]{0:T(1024)S(1)} %copy-done.47), kind=kOutput, calls=%fused_computation.23 | convolution fusion | flops 5711929344 | bytes 16758080 | tf_op jit(solution)/shard_map/crk,cre->ke/dot_general | solution.py:57
  469.5 14.8 %reshape_reshape.7 = bf16[32,32,4,1024]{3,2,1,0:T(4,128)(2,1)} reshape(bf16[1024,4096]{1,0:T(8,128)(2,1)} %convolution_convert_fusion.1) | data formatting | bytes 16777216 | tf_op jit(solution)/shard_map/reshape;reshape | solution.py:161
  484.3 11.5 %copy.170 = bf16[32,4,32,1024]{3,2,1,0:T(8,128)(2,1)} copy(bf16[32,4,32,1024]{3,1,2,0:T(4,128)(2,1)} %bitcast.225) | data formatting | bytes 16777216 | tf_op jit(solution)/shard_map/transpose | solution.py:161
  499.1 14.0 %convolution_convert_fusion = bf16[4096,1024]{1,0:T(8,128)(2,1)} fusion(bf16[1,680,1024]{2,1,0:T(8,128)(2,1)S(1)} %copy-done.25, f32[1024]{0:T(1024)S(1)} %bitcast.270, f32[680,4096]{1,0:T(8,128)} %fusion.72, f32[4096]{0:T(1024)S(1)} %copy-done.58), kind=kOutput, calls=%fused_computation.22 | convolution fusion | flops 5738389504 | bytes 20942848 | tf_op jit(solution)/shard_map/crk,cre->ke/dot_general | solution.py:57
  513.1 18.5 %pad_maximum_fusion = bf16[32,288,1024]{2,1,0:T(8,128)(2,1)} fusion(bf16[32,32,1024]{2,1,0:T(8,128)(2,1)} %bitcast.243, bf16[32,128,1024]{2,1,0:T(8,128)(2,1)} %bitcast.226, bf16[32,128,1024]{2,1,0:T(8,128)(2,1)} %bitcast.240), kind=kLoop, calls=%fused_computation.8 | loop fusion | flops 56623104 | bytes 37748736 | tf_op jit(solution)/shard_map/concatenate | solution.py:168
  532.4 14.1 %reduce-scatter.5.cloned.1.call-done = bf16[224,1024]{1,0:T(8,128)(2,1)} async-done(((bf16[3584,1024]{1,0:T(8,128)(2,1)}), bf16[224,1024]{1,0:T(8,128)(2,1)}) %reduce-scatter.5.cloned.1.call-update) | async-done | bytes 458768 | tf_op jit(solution)/shard_map/reduce_scatter | solution.py:170
  546.7 9.1 %fusion.28 = (f32[680]{0:T(1024)S(1)}, f32[680,1024]{1,0:T(8,128)S(1)}) fusion(bf16[1,680,1024]{2,1,0:T(8,128)(2,1)S(1)} %copy-done.7, f32[1024]{0:T(1024)S(1)} %bitcast.274, f32[680]{0:T(1024)S(1)} %copy-done.52, bf16[1024,3072]{1,0:T(8,128)(2,1)} %all-gather.8.cloned.1.call-done, bf16[680,1024]{0,1:T(8,128)(2,1)} %bitcast.252, ...), kind=kOutput, calls=%fused_computation.70 | convolution fusion | flops 4294204672 | bytes 14656832 | tf_op jit(solution)/shard_map/rfw,uw->rfu/dot_general | solution.py:51
  558.6 185.8 %reduce-scatter.9.cloned.1.call-done = bf16[576,1024]{1,0:T(8,128)(2,1)} async-done(((bf16[9216,1024]{1,0:T(8,128)(2,1)}), bf16[576,1024]{1,0:T(8,128)(2,1)}) %reduce-scatter.9.cloned.1.call-update) | async-done | bytes 1179664 | tf_op jit(solution)/shard_map/reduce_scatter | solution.py:170
  744.4 17.3 %fusion.30 = (bf16[1024]{0:T(1024)(128)(2,1)S(1)}, bf16[1024]{0:T(1024)(128)(2,1)S(1)}, f32[1,680,1024]{2,1,0:T(8,128)}, bf16[1,680,1024]{2,1,0:T(8,128)(2,1)}) fusion(bf16[1,680,1024]{2,1,0:T(8,128)(2,1)S(1)} %copy-done.26, f32[1024]{0:T(1024)S(1)} %reshape.978, f32[680,1024]{1,0:T(8,128)} %get-tuple-element.65, f32[1024]{0:T(1024)S(1)} %copy-done.70, ...), kind=kOutput, calls=%fused_computation.72 | convolution fusion | flops 5746726912 | bytes 37684512 | tf_op jit(solution)/shard_map/fyg,gq->fyq/dot_general | solution.py:45
  769.2 20.5 %all-gather.4 = bf16[16,2,6144]{2,1,0:T(2,128)(2,1)S(1)} all-gather(bf16[1,2,6144]{2,1,0:T(2,128)(2,1)S(1)} %bitcast.259), channel_id=1, replica_groups=mesh['wide'=16,'narrow'=2] {'wide'}, dimensions={0}, use_global_device_ids=true | all-gather | bytes 417792 | tf_op jit(solution)/shard_map/all_gather | solution.py:109
  (279 shorter events, 119.5 us)
Async XLA Ops:
  7.2 38.4 %copy-start = (bf16[32,6144]{1,0:T(8,128)(2,1)S(1)}, bf16[32,6144]{1,0:T(8,128)(2,1)}, u32[]{:S(2)}) copy-start(bf16[32,6144]{1,0:T(8,128)(2,1)} %param.20) | copy-start | bytes 1179652
  7.2 82.7 %all-gather.8.cloned.1.call-start = ((), (), s32[]{:S(2)}) async-start(), calls=%async_computation.6 | async-start | bytes 6488064 | tf_op jit(solution)/shard_map/all_gather | solution.py:226
  7.9 207.6 %all-gather.10.cloned.1.call-start = ((), (), s32[]{:S(2)}) async-start(), calls=%async_computation.7 | async-start | bytes 19464192 | tf_op jit(solution)/shard_map/all_gather | solution.py:143
  8.9 41.3 %copy-start.76 = (s32[10]{0:T(128)S(1)}, s32[10]{0:T(128)}, u32[]{:S(2)}) copy-start(s32[10]{0:T(128)} %param.19) | copy-start | bytes 124
  10.8 42.1 %copy-start.5 = (bf16[1,680,1024]{2,1,0:T(8,128)(2,1)S(1)}, bf16[1,680,1024]{2,1,0:T(8,128)(2,1)}, u32[]{:S(2)}) copy-start(bf16[1,680,1024]{2,1,0:T(8,128)(2,1)} %param.17) | copy-start | bytes 4177924
  47.6 35.3 %all-to-all-start = ((f32[32,1,6144]{2,1,0:T(1,128)}), f32[32,1,6144]{2,1,0:T(1,128)S(1)}, u32[]{:S(2)}, u32[]{:S(2)}) async-start(f32[32,1,6144]{2,1,0:T(1,128)} %copy.147), calls=%async_computation | async-start | bytes 1572864 | tf_op jit(solution)/shard_map/all_to_all | solution.py:234
  50.2 496.4 %reduce-scatter.5.cloned.1.call-start = ((), (), s32[]{:S(2)}) async-start(), calls=%async_computation.8 | async-start | bytes 7798784 | tf_op jit(solution)/shard_map/reduce_scatter | solution.py:170
  52.1 59.5 %copy-start.35 = (f32[16,64]{1,0:T(8,128)}, f32[16,64]{1,0:T(8,128)S(1)}, u32[]{:S(2)}) copy-start(f32[16,64]{1,0:T(8,128)S(1)} %reshape.975) | copy-start | bytes 12292
  52.2 59.4 %copy-start.33 = (f32[16,64]{1,0:T(8,128)}, f32[16,64]{1,0:T(8,128)S(1)}, u32[]{:S(2)}) copy-start(f32[16,64]{1,0:T(8,128)S(1)} %reshape.974) | copy-start | bytes 12292
  53.1 36.8 %copy-start.50 = (f32[680]{0:T(1024)}, f32[680]{0:T(1024)S(1)}, u32[]{:S(2)}) copy-start(f32[680]{0:T(1024)S(1)} %broadcast_multiply_fusion.3) | copy-start | bytes 8164
  53.6 36.3 %copy-start.48 = (f32[680]{0:T(1024)}, f32[680]{0:T(1024)S(1)}, u32[]{:S(2)}) copy-start(f32[680]{0:T(1024)S(1)} %fusion.27) | copy-start | bytes 8164
  53.6 36.2 %copy-start.43 = (f32[680]{0:T(1024)}, f32[680]{0:T(1024)S(1)}, u32[]{:S(2)}) copy-start(f32[680]{0:T(1024)S(1)} %fusion.62) | copy-start | bytes 8164
  111.2 15.1 %copy-start.31 = (f32[680,16]{0,1:T(8,128)}, f32[680,16]{0,1:T(8,128)S(1)}, u32[]{:S(2)}) copy-start(f32[680,16]{0,1:T(8,128)S(1)} %multiply_reduce_fusion.1) | copy-start | bytes 130564
  217.3 30.2 %copy-start.17 = (bf16[32,32,1024]{2,1,0:T(8,128)(2,1)}, bf16[32,32,1024]{2,1,0:T(8,128)(2,1)S(1)}, u32[]{:S(2)}) copy-start(bf16[32,32,1024]{2,1,0:T(8,128)(2,1)S(1)} %slice.117) | copy-start | bytes 6291460
  252.6 37.6 %copy-start.8 = (f32[1,680,1024]{2,1,0:T(8,128)}, f32[1,680,1024]{2,1,0:T(8,128)S(1)}, u32[]{:S(2)}) copy-start(f32[1,680,1024]{2,1,0:T(8,128)S(1)} %get-tuple-element.31) | copy-start | bytes 8355844
  252.6 37.7 %copy-start.46 = (f32[680]{0:T(1024)}, f32[680]{0:T(1024)S(1)}, u32[]{:S(2)}) copy-start(f32[680]{0:T(1024)S(1)} %broadcast_multiply_fusion.2) | copy-start | bytes 8164
  253.0 37.2 %copy-start.55 = (f32[680]{0:T(1024)}, f32[680]{0:T(1024)S(1)}, u32[]{:S(2)}) copy-start(f32[680]{0:T(1024)S(1)} %fusion.63) | copy-start | bytes 8164
  253.1 27.6 %slice-start = ((s8[8388608]{0:T(1024)(128)(4,1)}), s8[4194304]{0:T(1024)(128)(4,1)S(1)}, s32[]{:S(2)}) async-start(s8[8388608]{0:T(1024)(128)(4,1)} %bitcast.235), calls=%async_computation.12 | async-start | bytes 8388608
  262.3 18.4 %slice-start.1 = ((s8[8388608]{0:T(1024)(128)(4,1)}), s8[4194304]{0:T(1024)(128)(4,1)S(1)}, s32[]{:S(2)}) async-start(s8[8388608]{0:T(1024)(128)(4,1)} %bitcast.235), calls=%async_computation.13 | async-start | bytes 8388608
  345.9 28.8 %copy-start.2 = (f32[1,680,1024]{1,2,0:T(8,128)S(1)}, f32[1,680,1024]{1,2,0:T(8,128)}, u32[]{:S(2)}) copy-start(f32[1,680,1024]{1,2,0:T(8,128)} %copy-done.1) | copy-start | bytes 8355844
  345.9 28.8 %copy-start.36 = (f32[16,64]{1,0:T(8,128)S(1)}, f32[16,64]{1,0:T(8,128)}, u32[]{:S(2)}) copy-start(f32[16,64]{1,0:T(8,128)} %copy-done.35) | copy-start | bytes 12292
  456.5 287.8 %reduce-scatter.9.cloned.1.call-start = ((), (), s32[]{:S(2)}) async-start(), calls=%async_computation.10 | async-start | bytes 20054016 | tf_op jit(solution)/shard_map/reduce_scatter | solution.py:170
  531.6 15.0 %copy-start.52 = (f32[680]{0:T(1024)S(1)}, f32[680]{0:T(1024)}, u32[]{:S(2)}) copy-start(f32[680]{0:T(1024)} %copy-done.50) | copy-start | bytes 8164
  531.6 15.0 %copy-start.65 = (f32[1,1024]{1,0:T(1,128)S(1)}, f32[1,1024]{1,0:T(1,128)}, u32[]{:S(2)}) copy-start(f32[1,1024]{1,0:T(1,128)} %copy-done.63) | copy-start | bytes 12292
  531.7 270.7 %reduce-scatter.7.cloned.1.call-start = ((), (), s32[]{:S(2)}) async-start(), calls=%async_computation.9 | async-start | bytes 688128 | tf_op jit(solution)/shard_map/reduce_scatter | solution.py:171
  546.6 259.7 %reduce-scatter.11.cloned.1.call-start = ((), (), s32[]{:S(2)}) async-start(), calls=%async_computation.11 | async-start | bytes 1769472 | tf_op jit(solution)/shard_map/reduce_scatter | solution.py:171
  555.7 188.7 %copy-start.26 = (bf16[1,680,1024]{2,1,0:T(8,128)(2,1)S(1)}, bf16[1,680,1024]{2,1,0:T(8,128)(2,1)}, u32[]{:S(2)}) copy-start(bf16[1,680,1024]{2,1,0:T(8,128)(2,1)} %param.33) | copy-start | bytes 4177924
  555.7 188.7 %copy-start.68 = (f32[680]{0:T(1024)S(1)}, f32[680]{0:T(1024)}, u32[]{:S(2)}) copy-start(f32[680]{0:T(1024)} %copy-done.67) | copy-start | bytes 8164
  555.7 188.7 %copy-start.70 = (f32[1024]{0:T(1024)S(1)}, f32[1024]{0:T(1024)}, u32[]{:S(2)}) copy-start(f32[1024]{0:T(1024)} %reshape.976) | copy-start | bytes 12292
  764.4 37.3 %copy-start.59 = (bf16[1,1024]{1,0:T(2,128)(2,1)S(1)}, bf16[1,1024]{1,0:T(2,128)(2,1)}, u32[]{:S(2)}) copy-start(bf16[1,1024]{1,0:T(2,128)(2,1)} %param.18) | copy-start | bytes 6148
  764.4 37.3 %copy-start.60 = (f32[1,1024]{1,0:T(1,128)S(1)}, f32[1,1024]{1,0:T(1,128)}, u32[]{:S(2)}) copy-start(f32[1,1024]{1,0:T(1,128)} %get-tuple-element.33) | copy-start | bytes 12292
  790.7 9.7 %all-to-all-start.1 = ((f32[32,1,32]{2,1,0:T(1,128)}), f32[32,1,32]{2,1,0:T(1,128)S(1)}, u32[]{:S(2)}, u32[]{:S(2)}) async-start(f32[32,1,32]{2,1,0:T(1,128)} %bitcast.53), calls=%async_computation.1 | async-start | bytes 32768 | tf_op jit(solution)/shard_map/all_to_all | solution.py:363
  (56 other events, 368.6 us)
Sparse Core Ops, SparseCore 0:
  10.9 78.9 all-gather.7
  92.8 122.6 all-gather.9
  456.7 89.8 reduce-scatter.4
  550.5 193.8 reduce-scatter.8
  746.5 13.0 reduce-scatter.6
  761.6 21.8 reduce-scatter.10

commit v4 on v3

--- a/solution.py
+++ b/solution.py
@@ -150,6 +150,18 @@
         full = piece.reshape(count, blocks, rows, LANES).transpose(0, 2, 1, 3)
         out.append(full.reshape(count * rows, cols))
     return out
+
+
+def narrow_sum(half):
+    size = lax.axis_size("narrow")
+    if size != 2:
+        return lax.psum_scatter(half, "narrow", scatter_dimension=0, tiled=True).astype(jnp.float32)
+    rows = half.shape[0] // 2
+    here = lax.axis_index("narrow")
+    keep = lax.dynamic_slice_in_dim(half, here * rows, rows, axis=0)
+    send = lax.dynamic_slice_in_dim(half, (1 - here) * rows, rows, axis=0)
+    got = lax.ppermute(send, "narrow", [(0, 1), (1, 0)])
+    return keep.astype(jnp.float32) + got.astype(jnp.float32)
 
 
 def scatter_packed(matrices, vectors, count):
@@ -168,8 +180,7 @@
     flat = pad_rows(jnp.concatenate(pieces, axis=1))
     flat = flat.reshape(count * flat.shape[1], LANES)
     half = lax.psum_scatter(flat, "wide", scatter_dimension=0, tiled=True)
-    got = lax.psum_scatter(half, "narrow", scatter_dimension=0, tiled=True)
-    got = got.astype(jnp.float32)
+    got = narrow_sum(half)
     out, start = [], 0
     for member in matrices:
         rows, cols = member.shape

time: 823 us -> 776 us (0.943)
  waiting for transfers between devices: 298 us -> 246 us
    reduce_scatter x2, waiting for transfers between devices: 200 us -> 138 us  [scatter_packed(): half = lax.psum_scatter(flat, 'wide', scatter_dimension=0, tiled=True)]
    ppermute x0 -> x2, waiting for transfers between devices: none -> 10.5 us  [narrow_sum(): got = lax.ppermute(send, 'narrow', [(0, 1), (1, 0)])]
  transfers between devices with their start and end apart: 8 -> 8, of which waited for: 6 -> 6; matrix products, arithmetic and copies ran while one was open for 24% -> 27% of each run, Pallas kernels for 0% -> 0%
where the time goes in v4:
time: 776 us; the launch traced here: 770 us
  waiting for transfers between devices  246 us (32%)
  matrix products  216 us (28%)
  local copies, waits for them, and re-layouts  126 us (16%)
  other arithmetic  108 us (14%)
  blocking collectives  52.2 us (7%)
  between operations  15 us (2%)
    reduce_scatter x2, waiting for transfers between devices, scatter_packed(): half = lax.psum_scatter(flat, 'wide', scatter_dimension=0, tiled=True)  138 us
    all_gather x1, waiting for transfers between devices, gather_packed(): lax.all_gather(flat[0], AXES, axis=0, tiled=True)  60.1 us
    all_gather x2, blocking collectives, nested_gather(): lax.all_gather(lax.all_gather(member, 'narrow', axis=0, tiled=True), 'wid...  42.4 us
    dot_general x4, matrix products, matmul_back(): jnp.einsum('rfw,uw->rfu', first_operand, second_operand, preferred_elemen...  41.1 us
    dot_general x4, matrix products, weight_grad(): jnp.einsum('crk,cre->ke', first_operand, second_operand, preferred_elemen...  40.2 us
    dot_general x4, matrix products, matmul_rows(): jnp.einsum('fyg,gq->fyq', first_operand, second_operand, preferred_elemen...  39.3 us
    another operation x2, local copies, waits for them, and re-layouts, scatter_packed(): shard.reshape(count, rows // count, blocks, LANES).transpose(0, 2, 1, 3)  33.4 us
    convert_element_type x1, other arithmetic, attend_backward(): score_gradient = (attention_probabilities * (prob_grad - jnp.sum(prob_gra...  28.7 us
  transfers between devices with their start and end apart: 8, of which 6 were waited for; matrix products, arithmetic and copies ran while one was open for 27% of the time, Pallas kernels for 0%

profile of v4, /device:TPU:0, one launch (start us, length us, event | category | flops | bytes accessed | tf_op | source)
XLA Modules:
  0.0 770.3 jit_solution(18030070156074046396)
XLA Ops:
  23.0 22.5 %all-gather.2 = bf16[16,2,1536]{2,1,0:T(2,128)(2,1)S(1)} all-gather(bf16[1,2,1536]{2,1,0:T(2,128)(2,1)S(1)} %bitcast.263), channel_id=1, replica_groups=mesh['wide'=16,'narrow'=2] {'wide'}, dimensions={0}, use_global_device_ids=true | all-gather | bytes 104448 | tf_op jit(solution)/shard_map/all_gather | solution.py:109
  56.7 26.2 %all-to-all-done = f32[32,1,6144]{2,1,0:T(1,128)S(1)} async-done(((f32[32,1,6144]{2,1,0:T(1,128)}), f32[32,1,6144]{2,1,0:T(1,128)S(1)}, u32[]{:S(2)}, u32[]{:S(2)}) %all-to-all-start) | async-done | bytes 786464 | tf_op jit(solution)/shard_map/all_to_all | solution.py:245
  89.9 7.4 convolution_bitcast_fusion.1
  111.9 14.4 %fusion.83 = (f32[16,680]{1,0:T(8,128)S(1)}, f32[16,680,680]{1,2,0:T(8,128)}) fusion(f32[680,16,64]{0,2,1:T(8,128)S(1)} %bitcast.220, f32[16,64]{1,0:T(8,128)S(1)} %reshape.975, f32[680,16]{0,1:T(8,128)S(1)} %get-tuple-element.79, f32[680,16,64]{0,2,1:T(8,128)S(1)} %bitcast.214, f32[16,64]{1,0:T(8,128)S(1)} %reshape.974, ...), kind=kOutput, calls=%fused_computation.176 | convolution fusion | flops 973357440 | bytes 35765312 | tf_op jit(solution)/shard_map/vmap(nkz,vkz->knv)/dot_general | solution.py:63
  126.3 13.4 %fusion = f32[16,680]{1,0:T(8,128)S(1)} fusion(f32[16,680,680]{1,2,0:T(8,128)} %get-tuple-element.64, f32[16,680]{1,0:T(8,128)S(1)} %get-tuple-element.63), kind=kLoop, calls=%fused_computation.6 | loop fusion | flops 14785920 | bytes 29680640 | tf_op jit(solution)/shard_map/vmap()/reduce_sum | solution.py:73
  140.3 15.1 %fusion.37 = bf16[16,64,680]{2,1,0:T(8,128)(2,1)} fusion(bf16[680,16,64]{0,2,1:T(8,128)(2,1)S(1)} %bitcast.241, f32[16,680,680]{1,2,0:T(8,128)} %get-tuple-element.64, f32[16,680]{1,0:T(8,128)S(1)} %fusion, f32[16,680]{1,0:T(8,128)S(1)} %get-tuple-element.63), kind=kOutput, calls=%fused_computation.91 | convolution fusion | flops 969886720 | bytes 32465920 | tf_op jit(solution)/shard_map/vmap(wcv,vwn->cwn)/dot_general | solution.py:75
  155.4 60.1 %all-gather.10.cloned.1.call-done = bf16[9216,1024]{1,0:T(8,128)(2,1)} async-done(((bf16[288,1024]{1,0:T(8,128)(2,1)}), bf16[9216,1024]{1,0:T(8,128)(2,1)}) %all-gather.10.cloned.1.call-update) | async-done | bytes 18874384 | tf_op jit(solution)/shard_map/all_gather | solution.py:143
  217.4 10.2 %fusion.78 = (bf16[32,128,1024]{2,1,0:T(8,128)(2,1)S(1)}, bf16[32,128,1024]{2,1,0:T(8,128)(2,1)}) fusion(bf16[32,288,1024]{2,1,0:T(8,128)(2,1)} %bitcast.231), kind=kLoop, calls=%fused_computation.171 | loop fusion | bytes 33554432 | tf_op jit(solution)/shard_map/slice | solution.py:148
  227.6 7.8 %copy.155 = bf16[32,32,4,1024]{3,2,1,0:T(4,128)(2,1)} copy(bf16[32,32,4,1024]{3,1,2,0:T(8,128)(2,1)S(1)} %bitcast.227) | data formatting | bytes 16777216 | tf_op jit(solution)/shard_map/transpose | solution.py:150
  235.3 12.2 %copy.181 = bf16[128,8,4,1024]{3,1,2,0:T(8,128)(2,1)} copy(bf16[128,8,4,1024]{3,2,1,0:T(4,128)(2,1)} %bitcast.224) | data formatting | bytes 16777216
  253.1 9.2 %fusion.72 = f32[680,4096]{1,0:T(8,128)} fusion(bf16[1024,4096]{1,0:T(8,128)(2,1)S(1)} %bitcast.234, f32[1,680,1024]{2,1,0:T(8,128)S(1)} %get-tuple-element.31, f32[1024]{0:T(1024)S(1)} %bitcast.280, f32[1024]{0:T(1024)S(1)} %bitcast.264, f32[680]{0:T(1024)S(1)} %fusion.63, f32[680]{0:T(1024)S(1)} %broadcast_multiply_fusion.2), kind=kOutput, calls=%fused_computation.166 | convolution fusion | flops 5707735040 | bytes 22328640 | tf_op jit(solution)/shard_map/fyg,gq->fyq/dot_general | solution.py:45
  262.4 18.3 %fusion.84 = (bf16[4096]{0:T(1024)(128)(2,1)S(1)}, bf16[680,4096]{1,0:T(8,128)(2,1)}) fusion(f32[680,4096]{1,0:T(8,128)} %fusion.72, f32[4096]{0:T(1024)S(1)} %copy-done.57, bf16[4096,1024]{1,0:T(8,128)(2,1)} %bitcast.238, f32[1024]{0:T(1024)S(1)} %bitcast.268, bf16[1,680,1024]{2,1,0:T(8,128)(2,1)S(1)} %copy-done.23), kind=kOutput, calls=%fused_computation.177 | convolution fusion | flops 5767614464 | bytes 26521600 | tf_op jit(solution)/shard_map/rfw,uw->rfu/dot_general | solution.py:51
  280.7 9.5 %fusion.32 = (bf16[1024]{0:T(1024)(128)(2,1)}, f32[680]{0:T(1024)S(1)}, f32[680,1024]{1,0:T(8,128)S(1)}) fusion(f32[1,680,1024]{2,1,0:T(8,128)S(1)} %get-tuple-element.31, f32[680]{0:T(1024)S(1)} %fusion.63, f32[680]{0:T(1024)S(1)} %broadcast_multiply_fusion.2, f32[1024]{0:T(1024)S(1)} %bitcast.265, bf16[680,4096]{1,0:T(8,128)(2,1)} %get-tuple-element.77, ...), kind=kOutput, calls=%fused_computation.77 | convolution fusion | flops 5709126144 | bytes 19544032 | tf_op jit(solution)/shard_map/rfw,uw->rfu/dot_general | solution.py:51
  299.3 15.8 %bitcast_convert_fusion = (bf16[1,680,16,64]{1,3,2,0:T(8,128)(2,1)}, f32[16,64,680]{2,1,0:T(8,128)}) fusion(bf16[680,16,64]{0,2,1:T(8,128)(2,1)S(1)} %bitcast.232, f32[16,680,680]{1,2,0:T(8,128)} %get-tuple-element.64, f32[16,680]{1,0:T(8,128)} %log_add_fusion), kind=kOutput, calls=%fused_computation.51 | convolution fusion | flops 962488320 | bytes 35207680 | tf_op jit(solution)/shard_map/vmap(fgs,gfu->sfu)/dot_general | solution.py:89
  315.1 26.1 %multiply_reduce_fusion = (f32[16,680]{1,0:T(8,128)}, f32[16,680,680]{1,2,0:T(8,128)}) fusion(f32[16,680,680]{1,2,0:T(8,128)} %get-tuple-element.64, f32[16,680]{1,0:T(8,128)} %log_add_fusion, bf16[680,16,64]{0,2,1:T(8,128)(2,1)S(1)} %bitcast.233, bf16[680,16,64]{0,2,1:T(8,128)(2,1)S(1)} %bitcast.242), kind=kOutput, calls=%fused_computation.1 | convolution fusion | flops 969179520 | bytes 62059520 | tf_op jit(solution)/shard_map/vmap(nkz,vkz->knv)/dot_general | solution.py:86
  345.9 28.7 %multiply_convert_fusion = bf16[16,680,680]{1,2,0:T(8,128)(2,1)} fusion(f32[16,680,680]{1,2,0:T(8,128)} %get-tuple-element.70, f32[16,680,680]{1,2,0:T(8,128)} %get-tuple-element.64, f32[16,680]{1,0:T(8,128)} %get-tuple-element.69, f32[16,680]{1,0:T(8,128)} %log_add_fusion), kind=kLoop, calls=%fused_computation | loop fusion | flops 29593600 | bytes 74071040 | tf_op jit(solution)/shard_map/vmap()/convert_element_type | solution.py:98
  374.7 10.1 %fusion.23 = (f32[680,16]{0,1:T(8,128)S(1)}, f32[16,64,680]{2,1,0:T(8,128)S(1)}) fusion(f32[1,680,16,64]{1,3,2,0:T(8,128)S(1)} %bitcast.215, f32[16,64]{1,0:T(8,128)} %broadcast_multiply_fusion.1, bf16[16,680,680]{1,2,0:T(8,128)(2,1)} %multiply_convert_fusion, f32[680,16,64]{0,2,1:T(8,128)} %bitcast.219, f32[16,64]{1,0:T(8,128)S(1)} %copy-done.36, ...), kind=kOutput, calls=%fused_computation.59 | convolution fusion | flops 951162240 | bytes 23247872 | tf_op jit(solution)/shard_map/vmap(wcv,vwn->cwn)/dot_general | solution.py:99
  384.9 10.5 %fusion.20 = (bf16[16,64]{1,0:T(8,128)(2,1)}, f32[680,16]{0,1:T(8,128)S(1)}, f32[16,64,680]{2,1,0:T(8,128)}) fusion(f32[1,680,16,64]{1,3,2,0:T(8,128)S(1)} %bitcast.221, f32[680,16]{0,1:T(8,128)S(1)} %copy-done.15, f32[16,64]{1,0:T(8,128)S(1)} %copy-done.37, bf16[16,680,680]{1,2,0:T(8,128)(2,1)} %multiply_convert_fusion, f32[680,16,64]{0,2,1:T(8,128)S(1)} %bitcast.216, ...), kind=kOutput, calls=%fused_computation.47 | convolution fusion | flops 953946496 | bytes 23293440 | tf_op jit(solution)/shard_map/vmap(fgs,gfu->sfu)/dot_general | solution.py:102
  406.7 10.7 %convolution_convert_fusion.2 = bf16[1024,3072]{1,0:T(8,128)(2,1)} fusion(bf16[680,1024]{0,1:T(8,128)(2,1)S(1)} %bitcast.253, bf16[680,1024]{0,1:T(8,128)(2,1)S(1)} %bitcast.248, bf16[680,1024]{0,1:T(8,128)(2,1)S(1)} %bitcast.251, bf16[1,680,1024]{2,1,0:T(8,128)(2,1)S(1)} %copy-done.7, f32[1024]{0:T(1024)S(1)} %bitcast.283, f32[1024]{0:T(1024)S(1)} %bitcast.273, ...), kind=kOutput, calls=%fused_computation.26 | convolution fusion | flops 4298047488 | bytes 11875648 | tf_op jit(solution)/shard_map/crk,cre->ke/dot_general | solution.py:57
  417.5 18.6 %reshape_reshape.6 = bf16[32,32,3,1024]{3,2,1,0:T(4,128)(2,1)} reshape(bf16[1024,3072]{1,0:T(8,128)(2,1)} %convolution_convert_fusion.2) | data formatting | bytes 12582912 | tf_op jit(solution)/shard_map/reshape;reshape | solution.py:173
  436.1 9.2 %copy.161 = bf16[32,3,32,1024]{3,2,1,0:T(8,128)(2,1)} copy(bf16[32,3,32,1024]{3,1,2,0:T(4,128)(2,1)} %bitcast.223) | data formatting | bytes 12582912 | tf_op jit(solution)/shard_map/transpose | solution.py:173
  448.0 8.5 %maximum_maximum_fusion = bf16[32,112,1024]{2,1,0:T(8,128)(2,1)} fusion(bf16[32,1,1024]{2,1,0:T(2,128)(2,1)S(1)} %concatenate.95, bf16[32,96,1024]{2,1,0:T(8,128)(2,1)} %bitcast.229, bf16[112]{0:T(256)(128)(2,1)} %pad.5.clone), kind=kLoop, calls=%fused_computation.24 | loop fusion | flops 22020096 | bytes 13697248 | tf_op jit(solution)/shard_map/concatenate | solution.py:137
  457.1 12.3 %convolution_convert_fusion.1 = bf16[1024,4096]{1,0:T(8,128)(2,1)} fusion(bf16[680,4096]{1,0:T(8,128)(2,1)} %get-tuple-element.77, f32[1,680,1024]{2,1,0:T(8,128)} %copy-done.8, f32[1024]{0:T(1024)S(1)} %bitcast.281, f32[1024]{0:T(1024)S(1)} %bitcast.267, f32[680]{0:T(1024)S(1)} %copy-done.56, f32[680]{0:T(1024)S(1)} %copy-done.47), kind=kOutput, calls=%fused_computation.23 | convolution fusion | flops 5711929344 | bytes 16758080 | tf_op jit(solution)/shard_map/crk,cre->ke/dot_general | solution.py:57
  469.5 14.8 %reshape_reshape.7 = bf16[32,32,4,1024]{3,2,1,0:T(4,128)(2,1)} reshape(bf16[1024,4096]{1,0:T(8,128)(2,1)} %convolution_convert_fusion.1) | data formatting | bytes 16777216 | tf_op jit(solution)/shard_map/reshape;reshape | solution.py:173
  484.3 11.5 %copy.170 = bf16[32,4,32,1024]{3,2,1,0:T(8,128)(2,1)} copy(bf16[32,4,32,1024]{3,1,2,0:T(4,128)(2,1)} %bitcast.225) | data formatting | bytes 16777216 | tf_op jit(solution)/shard_map/transpose | solution.py:173
  499.0 14.0 %convolution_convert_fusion = bf16[4096,1024]{1,0:T(8,128)(2,1)} fusion(bf16[1,680,1024]{2,1,0:T(8,128)(2,1)S(1)} %copy-done.24, f32[1024]{0:T(1024)S(1)} %bitcast.270, f32[680,4096]{1,0:T(8,128)} %fusion.72, f32[4096]{0:T(1024)S(1)} %copy-done.58), kind=kOutput, calls=%fused_computation.22 | convolution fusion | flops 5738389504 | bytes 20942848 | tf_op jit(solution)/shard_map/crk,cre->ke/dot_general | solution.py:57
  513.0 18.6 %pad_maximum_fusion = bf16[32,288,1024]{2,1,0:T(8,128)(2,1)} fusion(bf16[32,32,1024]{2,1,0:T(8,128)(2,1)} %bitcast.243, bf16[32,128,1024]{2,1,0:T(8,128)(2,1)} %bitcast.226, bf16[32,128,1024]{2,1,0:T(8,128)(2,1)} %bitcast.240), kind=kLoop, calls=%fused_computation.8 | loop fusion | flops 56623104 | bytes 37748736 | tf_op jit(solution)/shard_map/concatenate | solution.py:180
  534.4 10.5 %fusion.28 = (f32[680]{0:T(1024)S(1)}, f32[680,1024]{1,0:T(8,128)}) fusion(bf16[1,680,1024]{2,1,0:T(8,128)(2,1)S(1)} %copy-done.7, f32[1024]{0:T(1024)S(1)} %bitcast.274, f32[680]{0:T(1024)S(1)} %copy-done.52, bf16[1024,3072]{1,0:T(8,128)(2,1)} %all-gather.8.cloned.1.call-done, bf16[680,1024]{0,1:T(8,128)(2,1)} %bitcast.252, ...), kind=kOutput, calls=%fused_computation.70 | convolution fusion | flops 4294204672 | bytes 14656832 | tf_op jit(solution)/shard_map/rfw,uw->rfu/dot_general | solution.py:51
  550.3 17.6 %fusion.30 = (bf16[1024]{0:T(1024)(128)(2,1)S(1)}, bf16[1024]{0:T(1024)(128)(2,1)S(1)}, f32[1,680,1024]{2,1,0:T(8,128)}, bf16[1,680,1024]{2,1,0:T(8,128)(2,1)}) fusion(bf16[1,680,1024]{2,1,0:T(8,128)(2,1)S(1)} %copy-done.25, f32[1024]{0:T(1024)S(1)} %reshape.978, f32[680,1024]{1,0:T(8,128)} %get-tuple-element.65, f32[1024]{0:T(1024)S(1)} %copy-done.70, ...), kind=kOutput, calls=%fused_computation.72 | convolution fusion | flops 5746726912 | bytes 37684512 | tf_op jit(solution)/shard_map/fyg,gq->fyq/dot_general | solution.py:45
  572.5 19.9 %all-gather.4 = bf16[16,2,6144]{2,1,0:T(2,128)(2,1)S(1)} all-gather(bf16[1,2,6144]{2,1,0:T(2,128)(2,1)S(1)} %bitcast.259), channel_id=1, replica_groups=mesh['wide'=16,'narrow'=2] {'wide'}, dimensions={0}, use_global_device_ids=true | all-gather | bytes 417792 | tf_op jit(solution)/shard_map/all_gather | solution.py:109
  606.9 137.8 %reduce-scatter.5.cloned.1.call-done = bf16[576,1024]{1,0:T(8,128)(2,1)} async-done(((bf16[9216,1024]{1,0:T(8,128)(2,1)}), bf16[576,1024]{1,0:T(8,128)(2,1)}) %reduce-scatter.5.cloned.1.call-update) | async-done | bytes 1179664 | tf_op jit(solution)/shard_map/reduce_scatter | solution.py:182
  750.4 10.5 %collective-permute-done.1 = bf16[288,1024]{1,0:T(8,128)(2,1)S(1)} collective-permute-done((bf16[288,1024]{1,0:T(8,128)(2,1)S(1)}, bf16[288,1024]{1,0:T(8,128)(2,1)S(1)}, u32[]{:S(2)}, u32[]{:S(2)}) %collective-permute-start.1) | collective-permute-done | bytes 589856 | tf_op jit(solution)/shard_map/ppermute | solution.py:163
  (280 shorter events, 123.2 us)
Async XLA Ops:
  7.2 38.4 %copy-start = (bf16[32,6144]{1,0:T(8,128)(2,1)S(1)}, bf16[32,6144]{1,0:T(8,128)(2,1)}, u32[]{:S(2)}) copy-start(bf16[32,6144]{1,0:T(8,128)(2,1)} %param.20) | copy-start | bytes 1179652
  7.2 82.7 %all-gather.8.cloned.1.call-start = ((), (), s32[]{:S(2)}) async-start(), calls=%async_computation.4 | async-start | bytes 6488064 | tf_op jit(solution)/shard_map/all_gather | solution.py:237
  7.9 207.7 %all-gather.10.cloned.1.call-start = ((), (), s32[]{:S(2)}) async-start(), calls=%async_computation.5 | async-start | bytes 19464192 | tf_op jit(solution)/shard_map/all_gather | solution.py:143
  8.9 41.3 %copy-start.76 = (s32[10]{0:T(128)S(1)}, s32[10]{0:T(128)}, u32[]{:S(2)}) copy-start(s32[10]{0:T(128)} %param.19) | copy-start | bytes 124
  10.8 42.1 %copy-start.5 = (bf16[1,680,1024]{2,1,0:T(8,128)(2,1)S(1)}, bf16[1,680,1024]{2,1,0:T(8,128)(2,1)}, u32[]{:S(2)}) copy-start(bf16[1,680,1024]{2,1,0:T(8,128)(2,1)} %param.17) | copy-start | bytes 4177924
  47.6 35.3 %all-to-all-start = ((f32[32,1,6144]{2,1,0:T(1,128)}), f32[32,1,6144]{2,1,0:T(1,128)S(1)}, u32[]{:S(2)}, u32[]{:S(2)}) async-start(f32[32,1,6144]{2,1,0:T(1,128)} %copy.147), calls=%async_computation | async-start | bytes 1572864 | tf_op jit(solution)/shard_map/all_to_all | solution.py:245
  50.2 554.5 %reduce-scatter.3.cloned.1.call-start = ((), (), s32[]{:S(2)}) async-start(), calls=%async_computation.6 | async-start | bytes 7798784 | tf_op jit(solution)/shard_map/reduce_scatter | solution.py:182
  52.1 59.5 %copy-start.35 = (f32[16,64]{1,0:T(8,128)}, f32[16,64]{1,0:T(8,128)S(1)}, u32[]{:S(2)}) copy-start(f32[16,64]{1,0:T(8,128)S(1)} %reshape.975) | copy-start | bytes 12292
  52.2 59.4 %copy-start.33 = (f32[16,64]{1,0:T(8,128)}, f32[16,64]{1,0:T(8,128)S(1)}, u32[]{:S(2)}) copy-start(f32[16,64]{1,0:T(8,128)S(1)} %reshape.974) | copy-start | bytes 12292
  53.2 36.8 %copy-start.50 = (f32[680]{0:T(1024)}, f32[680]{0:T(1024)S(1)}, u32[]{:S(2)}) copy-start(f32[680]{0:T(1024)S(1)} %broadcast_multiply_fusion.3) | copy-start | bytes 8164
  53.7 36.3 %copy-start.48 = (f32[680]{0:T(1024)}, f32[680]{0:T(1024)S(1)}, u32[]{:S(2)}) copy-start(f32[680]{0:T(1024)S(1)} %fusion.27) | copy-start | bytes 8164
  53.7 36.2 %copy-start.43 = (f32[680]{0:T(1024)}, f32[680]{0:T(1024)S(1)}, u32[]{:S(2)}) copy-start(f32[680]{0:T(1024)S(1)} %fusion.62) | copy-start | bytes 8164
  111.2 15.1 %copy-start.31 = (f32[680,16]{0,1:T(8,128)}, f32[680,16]{0,1:T(8,128)S(1)}, u32[]{:S(2)}) copy-start(f32[680,16]{0,1:T(8,128)S(1)} %multiply_reduce_fusion.1) | copy-start | bytes 130564
  111.5 14.8 %copy-start.29 = (f32[680,16]{0,1:T(8,128)}, f32[680,16]{0,1:T(8,128)S(1)}, u32[]{:S(2)}) copy-start(f32[680,16]{0,1:T(8,128)S(1)} %multiply_reduce_fusion.2) | copy-start | bytes 130564
  111.6 14.7 %copy-start.14 = (f32[680,16]{0,1:T(8,128)}, f32[680,16]{0,1:T(8,128)S(1)}, u32[]{:S(2)}) copy-start(f32[680,16]{0,1:T(8,128)S(1)} %get-tuple-element.79) | copy-start | bytes 130564
  111.6 14.7 %copy-start.19 = (f32[680,16]{0,1:T(8,128)}, f32[680,16]{0,1:T(8,128)S(1)}, u32[]{:S(2)}) copy-start(f32[680,16]{0,1:T(8,128)S(1)} %get-tuple-element.78) | copy-start | bytes 130564
  217.3 30.2 %copy-start.16 = (bf16[32,32,1024]{2,1,0:T(8,128)(2,1)}, bf16[32,32,1024]{2,1,0:T(8,128)(2,1)S(1)}, u32[]{:S(2)}) copy-start(bf16[32,32,1024]{2,1,0:T(8,128)(2,1)S(1)} %slice.117) | copy-start | bytes 6291460
  252.6 37.6 %copy-start.8 = (f32[1,680,1024]{2,1,0:T(8,128)}, f32[1,680,1024]{2,1,0:T(8,128)S(1)}, u32[]{:S(2)}) copy-start(f32[1,680,1024]{2,1,0:T(8,128)S(1)} %get-tuple-element.31) | copy-start | bytes 8355844
  252.6 37.6 %copy-start.46 = (f32[680]{0:T(1024)}, f32[680]{0:T(1024)S(1)}, u32[]{:S(2)}) copy-start(f32[680]{0:T(1024)S(1)} %broadcast_multiply_fusion.2) | copy-start | bytes 8164
  253.1 37.2 %copy-start.55 = (f32[680]{0:T(1024)}, f32[680]{0:T(1024)S(1)}, u32[]{:S(2)}) copy-start(f32[680]{0:T(1024)S(1)} %fusion.63) | copy-start | bytes 8164
  253.1 27.6 %slice-start = ((s8[8388608]{0:T(1024)(128)(4,1)}), s8[4194304]{0:T(1024)(128)(4,1)S(1)}, s32[]{:S(2)}) async-start(s8[8388608]{0:T(1024)(128)(4,1)} %bitcast.235), calls=%async_computation.8 | async-start | bytes 8388608
  262.4 18.3 %slice-start.1 = ((s8[8388608]{0:T(1024)(128)(4,1)}), s8[4194304]{0:T(1024)(128)(4,1)S(1)}, s32[]{:S(2)}) async-start(s8[8388608]{0:T(1024)(128)(4,1)} %bitcast.235), calls=%async_computation.9 | async-start | bytes 8388608
  345.9 28.8 %copy-start.2 = (f32[1,680,1024]{1,2,0:T(8,128)S(1)}, f32[1,680,1024]{1,2,0:T(8,128)}, u32[]{:S(2)}) copy-start(f32[1,680,1024]{1,2,0:T(8,128)} %copy-done.1) | copy-start | bytes 8355844
  345.9 28.8 %copy-start.36 = (f32[16,64]{1,0:T(8,128)S(1)}, f32[16,64]{1,0:T(8,128)}, u32[]{:S(2)}) copy-start(f32[16,64]{1,0:T(8,128)} %copy-done.35) | copy-start | bytes 12292
  456.5 288.2 %reduce-scatter.5.cloned.1.call-start = ((), (), s32[]{:S(2)}) async-start(), calls=%async_computation.7 | async-start | bytes 20054016 | tf_op jit(solution)/shard_map/reduce_scatter | solution.py:182
  550.3 17.6 %copy-start.75 = (bf16[1024]{0:T(1024)(128)(2,1)S(1)}, bf16[1024]{0:T(1024)(128)(2,1)}, u32[]{:S(2)}) copy-start(bf16[1024]{0:T(1024)(128)(2,1)} %get-tuple-element.20) | copy-start | bytes 6148
  567.9 38.4 %copy-start.59 = (bf16[1,1024]{1,0:T(2,128)(2,1)S(1)}, bf16[1,1024]{1,0:T(2,128)(2,1)}, u32[]{:S(2)}) copy-start(bf16[1,1024]{1,0:T(2,128)(2,1)} %param.18) | copy-start | bytes 6148
  567.9 38.4 %copy-start.60 = (f32[1,1024]{1,0:T(1,128)S(1)}, f32[1,1024]{1,0:T(1,128)}, u32[]{:S(2)}) copy-start(f32[1,1024]{1,0:T(1,128)} %get-tuple-element.33) | copy-start | bytes 12292
  593.4 10.1 %all-to-all-start.1 = ((f32[32,1,32]{2,1,0:T(1,128)}), f32[32,1,32]{2,1,0:T(1,128)S(1)}, u32[]{:S(2)}, u32[]{:S(2)}) async-start(f32[32,1,32]{2,1,0:T(1,128)} %bitcast.53), calls=%async_computation.1 | async-start | bytes 32768 | tf_op jit(solution)/shard_map/all_to_all | solution.py:374
  605.7 141.7 %collective-permute-start = (bf16[112,1024]{1,0:T(8,128)(2,1)S(1)}, bf16[112,1024]{1,0:T(8,128)(2,1)S(1)}, u32[]{:S(2)}, u32[]{:S(2)}) collective-permute-start(bf16[112,1024]{1,0:T(8,128)(2,1)S(1)} %constant_dynamic-slice_fusion.1), channel_id=1, source_target_pairs={{0,1},{1,0},{2,3},{3,2},{4,5},{5,4},{6,7},{7,6},{8,9},{9,8},{10,11... | collective-permute-start | bytes 688136 | tf_op jit(solution)/shard_map/ppermute | solution.py:163
  744.7 16.2 %copy-start.28 = (bf16[576,1024]{1,0:T(8,128)(2,1)S(1)}, bf16[576,1024]{1,0:T(8,128)(2,1)}, u32[]{:S(2)}) copy-start(bf16[576,1024]{1,0:T(8,128)(2,1)} %reduce-scatter.5.cloned.1.call-done) | copy-start | bytes 3538948
  745.9 15.0 %collective-permute-start.1 = (bf16[288,1024]{1,0:T(8,128)(2,1)S(1)}, bf16[288,1024]{1,0:T(8,128)(2,1)S(1)}, u32[]{:S(2)}, u32[]{:S(2)}) collective-permute-start(bf16[288,1024]{1,0:T(8,128)(2,1)S(1)} %constant_dynamic-slice_fusion), channel_id=1, source_target_pairs={{0,1},{1,0},{2,3},{3,2},{4,5},{5,4},{6,7},{7,6},{8,9},{9,8},{10,11... | collective-permute-start | bytes 1769480 | tf_op jit(solution)/shard_map/ppermute | solution.py:163
  (56 other events, 347.9 us)
Sparse Core Ops, SparseCore 0:
  10.9 78.9 all-gather.7
  92.8 122.6 all-gather.9
  456.6 89.8 reduce-scatter.2
  550.5 194.1 reduce-scatter.4

commit v5 on v4

--- a/solution.py
+++ b/solution.py
@@ -271,7 +271,26 @@
     gamma_mlp_grad = jnp.sum(upstream * branch, axis=1)
     branch_grad = (upstream * gamma_mlp[:, None, :]).astype(jnp.bfloat16)
     down_grad = weight_grad(hidden, branch_grad)
+    (down_sum,) = scatter_packed((down_grad,), (), count)
     down_bias_grad = jnp.sum(branch_grad.astype(jnp.float32), axis=(0, 1))
+    return mlp_back(
+        branch_grad, down_full, hidden_pre, normed_mlp, up_full, middle, scale_mlp, shift_mlp,
+        upstream, attended, gamma_attn, context, proj_full, head_shape, queries, key_rows,
+        value_rows, logsum, allowed, query_pre, query_gain, key_pre, key_gain, sequences,
+        length, width, normed_attn, qkv_full, input_rows, scale_attn, shift_attn,
+        gamma_mlp_grad, activated_mine, w_ada, cond_rows, me, count, layer_output,
+        down_sum, down_bias_grad,
+    )
+
+
+def mlp_back(
+    branch_grad, down_full, hidden_pre, normed_mlp, up_full, middle, scale_mlp, shift_mlp,
+    upstream, attended, gamma_attn, context, proj_full, head_shape, queries, key_rows,
+    value_rows, logsum, allowed, query_pre, query_gain, key_pre, key_gain, sequences,
+    length, width, normed_attn, qkv_full, input_rows, scale_attn, shift_attn,
+    gamma_mlp_grad, activated_mine, w_ada, cond_rows, me, count, layer_output,
+    down_sum, down_bias_grad,
+):
     hidden_grad = matmul_back(branch_grad, down_full)
     gelu_pull = jax.vjp(gelu_tanh, hidden_pre)[1]
     pre_grad = gelu_pull(hidden_grad)[0].astype(jnp.bfloat16)
@@ -285,7 +304,7 @@
     attended_grad = (middle_grad * gamma_attn[:, None, :]).astype(jnp.bfloat16)
     proj_grad = weight_grad(context, attended_grad)
     proj_bias_grad = jnp.sum(attended_grad.astype(jnp.float32), axis=(0, 1))
-    down_sum, up_sum, proj_sum = scatter_packed((down_grad, up_grad, proj_grad), (), count)
+    up_sum, proj_sum = scatter_packed((up_grad, proj_grad), (), count)
     context_gradient = (
         matmul_back(attended_grad, proj_full).astype(jnp.bfloat16).reshape(head_shape)
     )

time: 776 us -> 802 us (1.034)
  waiting for transfers between devices: 246 us -> 277 us
  other arithmetic: 108 us -> 99.2 us
    reduce_scatter x2 -> x3, waiting for transfers between devices: 138 us -> 178 us  [scatter_packed(): half = lax.psum_scatter(flat, 'wide', scatter_dimension=0, tiled=True)]
    transpose x2 -> x1, local copies, waits for them, and re-layouts: 20.8 us -> 9.22 us  [scatter_packed(): shard.reshape(count, rows // count, blocks, LANES).transpose(0, 2, 1, 3)]
    concatenate x1, other arithmetic: 18.6 us -> 7.86 us  [scatter_packed(): flat = pad_rows(jnp.concatenate(pieces, axis=1))]
    another operation x2 -> x3, local copies, waits for them, and re-layouts: 33.4 us -> 43.7 us  [scatter_packed(): shard.reshape(count, rows // count, blocks, LANES).transpose(0, 2, 1, 3)]
    unnamed x173 -> x174, local copies, waits for them, and re-layouts: 17.8 us -> 21.2 us
  transfers between devices with their start and end apart: 8 -> 10, of which waited for: 6 -> 7; matrix products, arithmetic and copies ran while one was open for 27% -> 24% of each run, Pallas kernels for 0% -> 0%
where the time goes in v5:
time: 802 us; the launch traced here: 796 us
  waiting for transfers between devices  277 us (35%)
  matrix products  215 us (27%)
  local copies, waits for them, and re-layouts  127 us (16%)
  other arithmetic  99.2 us (12%)
  blocking collectives  52.8 us (7%)
  between operations  15 us (2%)
  starting transfers between devices  10.1 us (1%)
    reduce_scatter x3, waiting for transfers between devices, scatter_packed(): half = lax.psum_scatter(flat, 'wide', scatter_dimension=0, tiled=True)  178 us
    all_gather x1, waiting for transfers between devices, gather_packed(): lax.all_gather(flat[0], AXES, axis=0, tiled=True)  59.8 us
    another operation x3, local copies, waits for them, and re-layouts, scatter_packed(): shard.reshape(count, rows // count, blocks, LANES).transpose(0, 2, 1, 3)  43.7 us
    all_gather x2, blocking collectives, nested_gather(): lax.all_gather(lax.all_gather(member, 'narrow', axis=0, tiled=True), 'wid...  43 us
    dot_general x4, matrix products, matmul_back(): jnp.einsum('rfw,uw->rfu', first_operand, second_operand, preferred_elemen...  41 us
    dot_general x4, matrix products, weight_grad(): jnp.einsum('crk,cre->ke', first_operand, second_operand, preferred_elemen...  40.1 us
    dot_general x4, matrix products, matmul_rows(): jnp.einsum('fyg,gq->fyq', first_operand, second_operand, preferred_elemen...  38.7 us
    convert_element_type x1, other arithmetic, attend_backward(): score_gradient = (attention_probabilities * (prob_grad - jnp.sum(prob_gra...  28.7 us
  transfers between devices with their start and end apart: 10, of which 7 were waited for; matrix products, arithmetic and copies ran while one was open for 24% of the time, Pallas kernels for 0%

profile of v5, /device:TPU:0, one launch (start us, length us, event | category | flops | bytes accessed | tf_op | source)
XLA Modules:
  0.0 796.2 jit_solution(4132663491011847646)
XLA Ops:
  23.0 22.5 %all-gather.2 = bf16[16,2,1536]{2,1,0:T(2,128)(2,1)S(1)} all-gather(bf16[1,2,1536]{2,1,0:T(2,128)(2,1)S(1)} %bitcast.261), channel_id=1, replica_groups=mesh['wide'=16,'narrow'=2] {'wide'}, dimensions={0}, use_global_device_ids=true | all-gather | bytes 104448 | tf_op jit(solution)/shard_map/all_gather | solution.py:109
  56.7 26.2 %all-to-all-done = f32[32,1,6144]{2,1,0:T(1,128)S(1)} async-done(((f32[32,1,6144]{2,1,0:T(1,128)}), f32[32,1,6144]{2,1,0:T(1,128)S(1)}, u32[]{:S(2)}, u32[]{:S(2)}) %all-to-all-start) | async-done | bytes 786464 | tf_op jit(solution)/shard_map/all_to_all | solution.py:245
  90.0 7.7 convolution_bitcast_fusion.1
  112.2 14.4 %fusion.82 = (f32[16,680]{1,0:T(8,128)S(1)}, f32[16,680,680]{1,2,0:T(8,128)}) fusion(f32[680,16,64]{0,2,1:T(8,128)S(1)} %bitcast.219, f32[16,64]{1,0:T(8,128)S(1)} %reshape.975, f32[680,16]{0,1:T(8,128)S(1)} %get-tuple-element.77, f32[680,16,64]{0,2,1:T(8,128)S(1)} %bitcast.213, f32[16,64]{1,0:T(8,128)S(1)} %reshape.974, ...), kind=kOutput, calls=%fused_computation.177 | convolution fusion | flops 973357440 | bytes 35765312 | tf_op jit(solution)/shard_map/vmap(nkz,vkz->knv)/dot_general | solution.py:63
  126.6 13.4 %fusion = f32[16,680]{1,0:T(8,128)S(1)} fusion(f32[16,680,680]{1,2,0:T(8,128)} %get-tuple-element.62, f32[16,680]{1,0:T(8,128)S(1)} %get-tuple-element.61), kind=kLoop, calls=%fused_computation.6 | loop fusion | flops 14785920 | bytes 29680640 | tf_op jit(solution)/shard_map/vmap()/reduce_sum | solution.py:73
  140.7 15.1 %fusion.37 = bf16[16,64,680]{2,1,0:T(8,128)(2,1)} fusion(bf16[680,16,64]{0,2,1:T(8,128)(2,1)S(1)} %bitcast.238, f32[16,680,680]{1,2,0:T(8,128)} %get-tuple-element.62, f32[16,680]{1,0:T(8,128)S(1)} %fusion, f32[16,680]{1,0:T(8,128)S(1)} %get-tuple-element.61), kind=kOutput, calls=%fused_computation.91 | convolution fusion | flops 969886720 | bytes 32465920 | tf_op jit(solution)/shard_map/vmap(wcv,vwn->cwn)/dot_general | solution.py:75
  155.7 59.8 %all-gather.10.cloned.1.call-done = bf16[9216,1024]{1,0:T(8,128)(2,1)} async-done(((bf16[288,1024]{1,0:T(8,128)(2,1)}), bf16[9216,1024]{1,0:T(8,128)(2,1)}) %all-gather.10.cloned.1.call-update) | async-done | bytes 18874384 | tf_op jit(solution)/shard_map/all_gather | solution.py:143
  217.4 10.2 %fusion.78 = (bf16[32,128,1024]{2,1,0:T(8,128)(2,1)S(1)}, bf16[32,128,1024]{2,1,0:T(8,128)(2,1)}) fusion(bf16[32,288,1024]{2,1,0:T(8,128)(2,1)} %bitcast.229), kind=kLoop, calls=%fused_computation.173 | loop fusion | bytes 33554432 | tf_op jit(solution)/shard_map/slice | solution.py:148
  227.6 7.7 copy.154
  235.3 12.2 %copy.179 = bf16[128,8,4,1024]{3,1,2,0:T(8,128)(2,1)} copy(bf16[128,8,4,1024]{3,2,1,0:T(4,128)(2,1)} %bitcast.224) | data formatting | bytes 16777216
  253.1 9.2 %fusion.72 = f32[680,4096]{1,0:T(8,128)} fusion(bf16[1024,4096]{1,0:T(8,128)(2,1)S(1)} %bitcast.232, f32[1,680,1024]{2,1,0:T(8,128)S(1)} %get-tuple-element.31, f32[1024]{0:T(1024)S(1)} %bitcast.278, f32[1024]{0:T(1024)S(1)} %bitcast.262, f32[680]{0:T(1024)S(1)} %fusion.63, f32[680]{0:T(1024)S(1)} %broadcast_multiply_fusion.2), kind=kOutput, calls=%fused_computation.168 | convolution fusion | flops 5707735040 | bytes 22328640 | tf_op jit(solution)/shard_map/fyg,gq->fyq/dot_general | solution.py:45
  262.4 18.1 %fusion.83 = (bf16[4096]{0:T(1024)(128)(2,1)S(1)}, bf16[680,4096]{1,0:T(8,128)(2,1)}) fusion(f32[680,4096]{1,0:T(8,128)} %fusion.72, f32[4096]{0:T(1024)S(1)} %copy-done.57, bf16[4096,1024]{1,0:T(8,128)(2,1)} %bitcast.236, f32[1024]{0:T(1024)S(1)} %bitcast.266, bf16[1,680,1024]{2,1,0:T(8,128)(2,1)S(1)} %copy-done.24), kind=kOutput, calls=%fused_computation.178 | convolution fusion | flops 5767614464 | bytes 26521600 | tf_op jit(solution)/shard_map/rfw,uw->rfu/dot_general | solution.py:51
  280.5 9.5 %fusion.32 = (bf16[1024]{0:T(1024)(128)(2,1)}, f32[680]{0:T(1024)S(1)}, f32[680,1024]{1,0:T(8,128)S(1)}) fusion(f32[1,680,1024]{2,1,0:T(8,128)S(1)} %get-tuple-element.31, f32[680]{0:T(1024)S(1)} %fusion.63, f32[680]{0:T(1024)S(1)} %broadcast_multiply_fusion.2, f32[1024]{0:T(1024)S(1)} %bitcast.263, bf16[680,4096]{1,0:T(8,128)(2,1)} %get-tuple-element.75, ...), kind=kOutput, calls=%fused_computation.77 | convolution fusion | flops 5709126144 | bytes 19544032 | tf_op jit(solution)/shard_map/rfw,uw->rfu/dot_general | solution.py:51
  299.0 16.1 %bitcast_convert_fusion = (bf16[1,680,16,64]{1,3,2,0:T(8,128)(2,1)}, f32[16,64,680]{2,1,0:T(8,128)}) fusion(bf16[680,16,64]{0,2,1:T(8,128)(2,1)S(1)} %bitcast.230, f32[16,680,680]{1,2,0:T(8,128)} %get-tuple-element.62, f32[16,680]{1,0:T(8,128)} %log_add_fusion), kind=kOutput, calls=%fused_computation.51 | convolution fusion | flops 962488320 | bytes 35207680 | tf_op jit(solution)/shard_map/vmap(fgs,gfu->sfu)/dot_general | solution.py:89
  315.1 26.1 %multiply_reduce_fusion = (f32[16,680]{1,0:T(8,128)}, f32[16,680,680]{1,2,0:T(8,128)}) fusion(f32[16,680,680]{1,2,0:T(8,128)} %get-tuple-element.62, f32[16,680]{1,0:T(8,128)} %log_add_fusion, bf16[680,16,64]{0,2,1:T(8,128)(2,1)S(1)} %bitcast.231, bf16[680,16,64]{0,2,1:T(8,128)(2,1)S(1)} %bitcast.239), kind=kOutput, calls=%fused_computation.1 | convolution fusion | flops 969179520 | bytes 62059520 | tf_op jit(solution)/shard_map/vmap(nkz,vkz->knv)/dot_general | solution.py:86
  345.9 28.7 %multiply_convert_fusion = bf16[16,680,680]{1,2,0:T(8,128)(2,1)} fusion(f32[16,680,680]{1,2,0:T(8,128)} %get-tuple-element.68, f32[16,680,680]{1,2,0:T(8,128)} %get-tuple-element.62, f32[16,680]{1,0:T(8,128)} %get-tuple-element.67, f32[16,680]{1,0:T(8,128)} %log_add_fusion), kind=kLoop, calls=%fused_computation | loop fusion | flops 29593600 | bytes 74071040 | tf_op jit(solution)/shard_map/vmap()/convert_element_type | solution.py:98
  374.7 10.1 %fusion.23 = (f32[680,16]{0,1:T(8,128)S(1)}, f32[16,64,680]{2,1,0:T(8,128)S(1)}) fusion(f32[1,680,16,64]{1,3,2,0:T(8,128)S(1)} %bitcast.214, f32[16,64]{1,0:T(8,128)} %broadcast_multiply_fusion.1, bf16[16,680,680]{1,2,0:T(8,128)(2,1)} %multiply_convert_fusion, f32[680,16,64]{0,2,1:T(8,128)} %bitcast.218, f32[16,64]{1,0:T(8,128)S(1)} %copy-done.36, ...), kind=kOutput, calls=%fused_computation.59 | convolution fusion | flops 951162240 | bytes 23247872 | tf_op jit(solution)/shard_map/vmap(wcv,vwn->cwn)/dot_general | solution.py:99
  384.9 10.5 %fusion.20 = (bf16[16,64]{1,0:T(8,128)(2,1)}, f32[680,16]{0,1:T(8,128)S(1)}, f32[16,64,680]{2,1,0:T(8,128)}) fusion(f32[1,680,16,64]{1,3,2,0:T(8,128)S(1)} %bitcast.220, f32[680,16]{0,1:T(8,128)S(1)} %copy-done.16, f32[16,64]{1,0:T(8,128)S(1)} %copy-done.37, bf16[16,680,680]{1,2,0:T(8,128)(2,1)} %multiply_convert_fusion, f32[680,16,64]{0,2,1:T(8,128)S(1)} %bitcast.215, ...), kind=kOutput, calls=%fused_computation.47 | convolution fusion | flops 953946496 | bytes 23293440 | tf_op jit(solution)/shard_map/vmap(fgs,gfu->sfu)/dot_general | solution.py:102
  406.7 10.7 %convolution_convert_fusion.2 = bf16[1024,3072]{1,0:T(8,128)(2,1)} fusion(bf16[680,1024]{0,1:T(8,128)(2,1)S(1)} %bitcast.251, bf16[680,1024]{0,1:T(8,128)(2,1)S(1)} %bitcast.246, bf16[680,1024]{0,1:T(8,128)(2,1)S(1)} %bitcast.249, bf16[1,680,1024]{2,1,0:T(8,128)(2,1)S(1)} %copy-done.8, f32[1024]{0:T(1024)S(1)} %bitcast.281, f32[1024]{0:T(1024)S(1)} %bitcast.271, ...), kind=kOutput, calls=%fused_computation.26 | convolution fusion | flops 4298047488 | bytes 11875648 | tf_op jit(solution)/shard_map/crk,cre->ke/dot_general | solution.py:57
  417.4 18.6 %reshape_reshape.6 = bf16[32,32,3,1024]{3,2,1,0:T(4,128)(2,1)} reshape(bf16[1024,3072]{1,0:T(8,128)(2,1)} %convolution_convert_fusion.2) | data formatting | bytes 12582912 | tf_op jit(solution)/shard_map/reshape;reshape | solution.py:173
  436.0 9.2 %copy.160 = bf16[32,3,32,1024]{3,2,1,0:T(8,128)(2,1)} copy(bf16[32,3,32,1024]{3,1,2,0:T(4,128)(2,1)} %bitcast.222) | data formatting | bytes 12582912 | tf_op jit(solution)/shard_map/transpose | solution.py:173
  447.5 8.4 %maximum_maximum_fusion = bf16[32,112,1024]{2,1,0:T(8,128)(2,1)} fusion(bf16[32,1,1024]{2,1,0:T(2,128)(2,1)S(1)} %concatenate.95, bf16[32,96,1024]{2,1,0:T(8,128)(2,1)} %bitcast.227, bf16[112]{0:T(256)(128)(2,1)} %pad.4.clone), kind=kLoop, calls=%fused_computation.24 | loop fusion | flops 22020096 | bytes 13697248 | tf_op jit(solution)/shard_map/concatenate | solution.py:137
  456.7 14.3 %convolution_convert_fusion = bf16[4096,1024]{1,0:T(8,128)(2,1)} fusion(bf16[1,680,1024]{2,1,0:T(8,128)(2,1)} %param.33, f32[1024]{0:T(1024)S(1)} %bitcast.268, f32[680,4096]{1,0:T(8,128)} %fusion.72, f32[4096]{0:T(1024)S(1)} %copy-done.58), kind=kOutput, calls=%fused_computation.22 | convolution fusion | flops 5738389504 | bytes 20942848 | tf_op jit(solution)/shard_map/crk,cre->ke/dot_general | solution.py:57
  471.6 13.3 %convolution_convert_fusion.1 = bf16[1024,4096]{1,0:T(8,128)(2,1)} fusion(bf16[680,4096]{1,0:T(8,128)(2,1)} %get-tuple-element.75, f32[1,680,1024]{2,1,0:T(8,128)} %copy-done.9, f32[1024]{0:T(1024)S(1)} %bitcast.279, f32[1024]{0:T(1024)S(1)} %bitcast.265, f32[680]{0:T(1024)S(1)} %copy-done.56, f32[680]{0:T(1024)S(1)} %copy-done.47), kind=kOutput, calls=%fused_computation.23 | convolution fusion | flops 5711929344 | bytes 16758080 | tf_op jit(solution)/shard_map/crk,cre->ke/dot_general | solution.py:57
  485.0 14.7 %reshape_reshape.7 = bf16[32,32,4,1024]{3,2,1,0:T(4,128)(2,1)} reshape(bf16[1024,4096]{1,0:T(8,128)(2,1)} %convolution_convert_fusion.1) | data formatting | bytes 16777216 | tf_op jit(solution)/shard_map/reshape;reshape | solution.py:173
  499.6 10.5 %copy.169 = bf16[32,32,4,1024]{3,1,2,0:T(8,128)(2,1)} copy(bf16[32,32,4,1024]{3,2,1,0:T(4,128)(2,1)} %reshape_reshape.7) | data formatting | bytes 16777216 | tf_op jit(solution)/shard_map/reshape;reshape | solution.py:173
  513.5 7.9 pad_maximum_fusion
  524.3 10.7 %fusion.28 = (f32[680]{0:T(1024)S(1)}, f32[680,1024]{1,0:T(8,128)}) fusion(bf16[1,680,1024]{2,1,0:T(8,128)(2,1)S(1)} %copy-done.8, f32[1024]{0:T(1024)S(1)} %bitcast.272, f32[680]{0:T(1024)S(1)} %copy-done.52, bf16[1024,3072]{1,0:T(8,128)(2,1)} %all-gather.8.cloned.1.call-done, bf16[680,1024]{0,1:T(8,128)(2,1)} %bitcast.250, ...), kind=kOutput, calls=%fused_computation.70 | convolution fusion | flops 4294204672 | bytes 14656832 | tf_op jit(solution)/shard_map/rfw,uw->rfu/dot_general | solution.py:51
  540.4 16.7 %fusion.30 = (bf16[1024]{0:T(1024)(128)(2,1)S(1)}, bf16[1024]{0:T(1024)(128)(2,1)S(1)}, f32[1,680,1024]{2,1,0:T(8,128)}, bf16[1,680,1024]{2,1,0:T(8,128)(2,1)}) fusion(bf16[1,680,1024]{2,1,0:T(8,128)(2,1)S(1)} %copy-done.25, f32[1024]{0:T(1024)S(1)} %reshape.978, f32[680,1024]{1,0:T(8,128)} %get-tuple-element.63, f32[1024]{0:T(1024)S(1)} %copy-done.70, ...), kind=kOutput, calls=%fused_computation.72 | convolution fusion | flops 5746726912 | bytes 37684512 | tf_op jit(solution)/shard_map/fyg,gq->fyq/dot_general | solution.py:45
  561.7 20.5 %all-gather.4 = bf16[16,2,6144]{2,1,0:T(2,128)(2,1)S(1)} all-gather(bf16[1,2,6144]{2,1,0:T(2,128)(2,1)S(1)} %bitcast.257), channel_id=1, replica_groups=mesh['wide'=16,'narrow'=2] {'wide'}, dimensions={0}, use_global_device_ids=true | all-gather | bytes 417792 | tf_op jit(solution)/shard_map/all_gather | solution.py:109
  596.2 57.7 %reduce-scatter.8.cloned.1.call-done = bf16[256,1024]{1,0:T(8,128)(2,1)} async-done(((bf16[4096,1024]{1,0:T(8,128)(2,1)}), bf16[256,1024]{1,0:T(8,128)(2,1)}) %reduce-scatter.8.cloned.1.call-update) | async-done | bytes 524304 | tf_op jit(solution)/shard_map/reduce_scatter | solution.py:182
  656.4 120.5 %reduce-scatter.6.cloned.1.call-done = bf16[320,1024]{1,0:T(8,128)(2,1)} async-done(((bf16[5120,1024]{1,0:T(8,128)(2,1)}), bf16[320,1024]{1,0:T(8,128)(2,1)}) %reduce-scatter.6.cloned.1.call-update) | async-done | bytes 655376 | tf_op jit(solution)/shard_map/reduce_scatter | solution.py:182
  (288 shorter events, 129.9 us)
Async XLA Ops:
  7.2 38.4 %copy-start = (bf16[32,6144]{1,0:T(8,128)(2,1)S(1)}, bf16[32,6144]{1,0:T(8,128)(2,1)}, u32[]{:S(2)}) copy-start(bf16[32,6144]{1,0:T(8,128)(2,1)} %param.20) | copy-start | bytes 1179652
  7.2 82.7 %all-gather.8.cloned.1.call-start = ((), (), s32[]{:S(2)}) async-start(), calls=%async_computation.5 | async-start | bytes 6488064 | tf_op jit(solution)/shard_map/all_gather | solution.py:237
  7.9 207.7 %all-gather.10.cloned.1.call-start = ((), (), s32[]{:S(2)}) async-start(), calls=%async_computation.6 | async-start | bytes 19464192 | tf_op jit(solution)/shard_map/all_gather | solution.py:143
  8.9 41.3 %copy-start.76 = (s32[10]{0:T(128)S(1)}, s32[10]{0:T(128)}, u32[]{:S(2)}) copy-start(s32[10]{0:T(128)} %param.19) | copy-start | bytes 124
  10.8 42.1 %copy-start.6 = (bf16[1,680,1024]{2,1,0:T(8,128)(2,1)S(1)}, bf16[1,680,1024]{2,1,0:T(8,128)(2,1)}, u32[]{:S(2)}) copy-start(bf16[1,680,1024]{2,1,0:T(8,128)(2,1)} %param.17) | copy-start | bytes 4177924
  47.6 35.3 %all-to-all-start = ((f32[32,1,6144]{2,1,0:T(1,128)}), f32[32,1,6144]{2,1,0:T(1,128)S(1)}, u32[]{:S(2)}, u32[]{:S(2)}) async-start(f32[32,1,6144]{2,1,0:T(1,128)} %copy.146), calls=%async_computation | async-start | bytes 1572864 | tf_op jit(solution)/shard_map/all_to_all | solution.py:245
  50.2 535.6 %reduce-scatter.4.cloned.1.call-start = ((), (), s32[]{:S(2)}) async-start(), calls=%async_computation.7 | async-start | bytes 7798784 | tf_op jit(solution)/shard_map/reduce_scatter | solution.py:182
  52.1 59.8 %copy-start.35 = (f32[16,64]{1,0:T(8,128)}, f32[16,64]{1,0:T(8,128)S(1)}, u32[]{:S(2)}) copy-start(f32[16,64]{1,0:T(8,128)S(1)} %reshape.975) | copy-start | bytes 12292
  52.2 59.7 %copy-start.33 = (f32[16,64]{1,0:T(8,128)}, f32[16,64]{1,0:T(8,128)S(1)}, u32[]{:S(2)}) copy-start(f32[16,64]{1,0:T(8,128)S(1)} %reshape.974) | copy-start | bytes 12292
  53.2 36.8 %copy-start.50 = (f32[680]{0:T(1024)}, f32[680]{0:T(1024)S(1)}, u32[]{:S(2)}) copy-start(f32[680]{0:T(1024)S(1)} %broadcast_multiply_fusion.3) | copy-start | bytes 8164
  53.7 36.3 %copy-start.48 = (f32[680]{0:T(1024)}, f32[680]{0:T(1024)S(1)}, u32[]{:S(2)}) copy-start(f32[680]{0:T(1024)S(1)} %fusion.27) | copy-start | bytes 8164
  53.7 36.2 %copy-start.43 = (f32[680]{0:T(1024)}, f32[680]{0:T(1024)S(1)}, u32[]{:S(2)}) copy-start(f32[680]{0:T(1024)S(1)} %fusion.62) | copy-start | bytes 8164
  111.5 15.1 %copy-start.31 = (f32[680,16]{0,1:T(8,128)}, f32[680,16]{0,1:T(8,128)S(1)}, u32[]{:S(2)}) copy-start(f32[680,16]{0,1:T(8,128)S(1)} %multiply_reduce_fusion.1) | copy-start | bytes 130564
  111.8 14.8 %copy-start.29 = (f32[680,16]{0,1:T(8,128)}, f32[680,16]{0,1:T(8,128)S(1)}, u32[]{:S(2)}) copy-start(f32[680,16]{0,1:T(8,128)S(1)} %multiply_reduce_fusion.2) | copy-start | bytes 130564
  111.9 14.7 %copy-start.15 = (f32[680,16]{0,1:T(8,128)}, f32[680,16]{0,1:T(8,128)S(1)}, u32[]{:S(2)}) copy-start(f32[680,16]{0,1:T(8,128)S(1)} %get-tuple-element.77) | copy-start | bytes 130564
  217.4 30.2 %copy-start.17 = (bf16[32,32,1024]{2,1,0:T(8,128)(2,1)}, bf16[32,32,1024]{2,1,0:T(8,128)(2,1)S(1)}, u32[]{:S(2)}) copy-start(bf16[32,32,1024]{2,1,0:T(8,128)(2,1)S(1)} %slice.113) | copy-start | bytes 6291460
  252.6 37.4 %copy-start.9 = (f32[1,680,1024]{2,1,0:T(8,128)}, f32[1,680,1024]{2,1,0:T(8,128)S(1)}, u32[]{:S(2)}) copy-start(f32[1,680,1024]{2,1,0:T(8,128)S(1)} %get-tuple-element.31) | copy-start | bytes 8355844
  252.6 37.4 %copy-start.46 = (f32[680]{0:T(1024)}, f32[680]{0:T(1024)S(1)}, u32[]{:S(2)}) copy-start(f32[680]{0:T(1024)S(1)} %broadcast_multiply_fusion.2) | copy-start | bytes 8164
  253.0 36.9 %copy-start.55 = (f32[680]{0:T(1024)}, f32[680]{0:T(1024)S(1)}, u32[]{:S(2)}) copy-start(f32[680]{0:T(1024)S(1)} %fusion.63) | copy-start | bytes 8164
  253.1 27.4 %slice-start = ((s8[8388608]{0:T(1024)(128)(4,1)}), s8[4194304]{0:T(1024)(128)(4,1)S(1)}, s32[]{:S(2)}) async-start(s8[8388608]{0:T(1024)(128)(4,1)} %bitcast.233), calls=%async_computation.10 | async-start | bytes 8388608
  262.4 18.1 %slice-start.1 = ((s8[8388608]{0:T(1024)(128)(4,1)}), s8[4194304]{0:T(1024)(128)(4,1)S(1)}, s32[]{:S(2)}) async-start(s8[8388608]{0:T(1024)(128)(4,1)} %bitcast.233), calls=%async_computation.11 | async-start | bytes 8388608
  345.9 28.8 %copy-start.2 = (f32[1,680,1024]{1,2,0:T(8,128)S(1)}, f32[1,680,1024]{1,2,0:T(8,128)}, u32[]{:S(2)}) copy-start(f32[1,680,1024]{1,2,0:T(8,128)} %copy-done.1) | copy-start | bytes 8355844
  345.9 28.8 %copy-start.36 = (f32[16,64]{1,0:T(8,128)S(1)}, f32[16,64]{1,0:T(8,128)}, u32[]{:S(2)}) copy-start(f32[16,64]{1,0:T(8,128)} %copy-done.35) | copy-start | bytes 12292
  456.0 197.9 %reduce-scatter.8.cloned.1.call-start = ((), (), s32[]{:S(2)}) async-start(), calls=%async_computation.9 | async-start | bytes 8912896 | tf_op jit(solution)/shard_map/reduce_scatter | solution.py:182
  471.0 306.0 %reduce-scatter.6.cloned.1.call-start = ((), (), s32[]{:S(2)}) async-start(), calls=%async_computation.8 | async-start | bytes 11141120 | tf_op jit(solution)/shard_map/reduce_scatter | solution.py:182
  540.4 16.7 %copy-start.75 = (bf16[1024]{0:T(1024)(128)(2,1)S(1)}, bf16[1024]{0:T(1024)(128)(2,1)}, u32[]{:S(2)}) copy-start(bf16[1024]{0:T(1024)(128)(2,1)} %get-tuple-element.20) | copy-start | bytes 6148
  557.1 37.5 %copy-start.59 = (bf16[1,1024]{1,0:T(2,128)(2,1)S(1)}, bf16[1,1024]{1,0:T(2,128)(2,1)}, u32[]{:S(2)}) copy-start(bf16[1,1024]{1,0:T(2,128)(2,1)} %param.18) | copy-start | bytes 6148
  557.1 37.5 %copy-start.60 = (f32[1,1024]{1,0:T(1,128)S(1)}, f32[1,1024]{1,0:T(1,128)}, u32[]{:S(2)}) copy-start(f32[1,1024]{1,0:T(1,128)} %get-tuple-element.33) | copy-start | bytes 12292
  583.2 10.1 %all-to-all-start.1 = ((f32[32,1,32]{2,1,0:T(1,128)}), f32[32,1,32]{2,1,0:T(1,128)S(1)}, u32[]{:S(2)}, u32[]{:S(2)}) async-start(f32[32,1,32]{2,1,0:T(1,128)} %bitcast.53), calls=%async_computation.1 | async-start | bytes 32768 | tf_op jit(solution)/shard_map/all_to_all | solution.py:393
  586.8 8.4 %collective-permute-start = (bf16[112,1024]{1,0:T(8,128)(2,1)S(1)}, bf16[112,1024]{1,0:T(8,128)(2,1)S(1)}, u32[]{:S(2)}, u32[]{:S(2)}) collective-permute-start(bf16[112,1024]{1,0:T(8,128)(2,1)S(1)} %constant_dynamic-slice_fusion.2), channel_id=1, source_target_pairs={{0,1},{1,0},{2,3},{3,2},{4,5},{5,4},{6,7},{7,6},{8,9},{9,8},{10,11... | collective-permute-start | bytes 688136 | tf_op jit(solution)/shard_map/ppermute | solution.py:163
  654.9 126.7 %collective-permute-start.2 = (bf16[128,1024]{1,0:T(8,128)(2,1)S(1)}, bf16[128,1024]{1,0:T(8,128)(2,1)S(1)}, u32[]{:S(2)}, u32[]{:S(2)}) collective-permute-start(bf16[128,1024]{1,0:T(8,128)(2,1)S(1)} %constant_dynamic-slice_fusion), channel_id=1, source_target_pairs={{0,1},{1,0},{2,3},{3,2},{4,5},{5,4},{6,7},{7,6},{8,9},{9,8},{10,11... | collective-permute-start | bytes 786440 | tf_op jit(solution)/shard_map/ppermute | solution.py:163
  778.0 9.2 %collective-permute-start.1 = (bf16[160,1024]{1,0:T(8,128)(2,1)S(1)}, bf16[160,1024]{1,0:T(8,128)(2,1)S(1)}, u32[]{:S(2)}, u32[]{:S(2)}) collective-permute-start(bf16[160,1024]{1,0:T(8,128)(2,1)S(1)} %constant_dynamic-slice_fusion.1), channel_id=1, source_target_pairs={{0,1},{1,0},{2,3},{3,2},{4,5},{5,4},{6,7},{7,6},{8,9},{9,8},{10,11... | collective-permute-start | bytes 983048 | tf_op jit(solution)/shard_map/ppermute | solution.py:163
  (58 other events, 366.6 us)
Sparse Core Ops, SparseCore 0:
  10.9 78.9 all-gather.7
  92.8 122.6 all-gather.9
  456.1 89.8 reduce-scatter.3
  549.9 103.9 reduce-scatter.7
  657.8 119.0 reduce-scatter.5

commit v6 on v5

--- a/solution.py
+++ b/solution.py
@@ -198,6 +198,25 @@
     return out
 
 
+def scatter_natural(member):
+    half = lax.psum_scatter(member.astype(jnp.bfloat16), "wide", scatter_dimension=0, tiled=True)
+    return narrow_sum(half)
+
+
+def sum_small(vectors, count):
+    small = jnp.concatenate([v.reshape(count, -1) for v in vectors], axis=1)
+    parts = lax.all_to_all(
+        small.reshape(count, 1, small.shape[1]), AXES, split_axis=0, concat_axis=0, tiled=True
+    )
+    total = jnp.sum(parts, axis=0)[0]
+    out, offset = [], 0
+    for v in vectors:
+        size = v.shape[0] // count
+        out.append(total[offset : offset + size])
+        offset += size
+    return out
+
+
 def layer(
     inputs,
     condition,
@@ -234,8 +253,10 @@
         unpacked.append(small[:, start : start + size].reshape(count * size).astype(jnp.float32))
         start += size
     ada_bias, query_bias, value_bias, query_gain, key_gain, proj_bias, up_bias, down_bias = unpacked
-    qkv_full = lax.all_gather(w_qkv, AXES, axis=0, tiled=True)
-    proj_full, up_full, down_full = gather_packed((w_proj, w_up, w_down), count)
+    first = lax.all_gather(jnp.concatenate([w_qkv, w_proj], axis=1), AXES, axis=0, tiled=True)
+    qkv_full = first[:, : w_qkv.shape[1]]
+    proj_full = first[:, w_qkv.shape[1] :]
+    up_full, down_full = gather_packed((w_up, w_down), count)
     allowed = block_mask(scale_tokens)
     input_rows = inputs.astype(jnp.float32)
     ada_rows = w_ada.shape[0]
@@ -322,8 +343,8 @@
         jnp.bfloat16
     )
     qkv_grad = weight_grad(normed_attn, projected_grad)
+    qkv_sum = scatter_natural(qkv_grad)
     (
-        qkv_sum,
         query_bias_sum,
         value_bias_sum,
         query_gain_sum,
@@ -331,8 +352,7 @@
         proj_bias_sum,
         up_bias_sum,
         down_bias_sum,
-    ) = scatter_packed(
-        (qkv_grad,),
+    ) = sum_small(
         (
             query_bias_grad,
             value_bias_grad,

time: 802 us -> 759 us (0.946)
  local copies, waits for them, and re-layouts: 127 us -> 95.2 us
  waiting for transfers between devices: 277 us -> 266 us
  other arithmetic: 99.2 us -> 89.7 us
    another operation x3 -> x2, local copies, waits for them, and re-layouts: 43.7 us -> 25.1 us  [scatter_packed(): shard.reshape(count, rows // count, blocks, LANES).transpose(0, 2, 1, 3)]
    all_gather x1, waiting for transfers between devices: 59.8 us -> 43.6 us  [gather_packed(): lax.all_gather(flat[0], AXES, axis=0, tiled=True)]
    transpose x1 -> x0, local copies, waits for them, and re-layouts: 9.22 us -> none  [scatter_packed(): shard.reshape(count, rows // count, blocks, LANES).transpose(0, 2, 1, 3)]
    unnamed x174 -> x182, local copies, waits for them, and re-layouts: 21.2 us -> 28.5 us
    reduce_scatter x3 -> x2, waiting for transfers between devices: 178 us -> 171 us  [scatter_packed(): half = lax.psum_scatter(flat, 'wide', scatter_dimension=0, tiled=True)]
  transfers between devices with their start and end apart: 10 -> 11, of which waited for: 7 -> 7; matrix products, arithmetic and copies ran while one was open for 24% -> 25% of each run, Pallas kernels for 0% -> 0%
where the time goes in v6:
time: 759 us; the launch traced here: 754 us
  waiting for transfers between devices  266 us (35%)
  matrix products  219 us (29%)
  local copies, waits for them, and re-layouts  95.2 us (13%)
  other arithmetic  89.7 us (12%)
  blocking collectives  54.1 us (7%)
  between operations  15 us (2%)
  starting transfers between devices  14.6 us (2%)
    reduce_scatter x2, waiting for transfers between devices, scatter_packed(): half = lax.psum_scatter(flat, 'wide', scatter_dimension=0, tiled=True)  171 us
    all_gather x2, blocking collectives, nested_gather(): lax.all_gather(lax.all_gather(member, 'narrow', axis=0, tiled=True), 'wid...  44.3 us
    all_gather x1, waiting for transfers between devices, gather_packed(): lax.all_gather(flat[0], AXES, axis=0, tiled=True)  43.6 us
    dot_general x4, matrix products, matmul_back(): jnp.einsum('rfw,uw->rfu', first_operand, second_operand, preferred_elemen...  41.7 us
    dot_general x4, matrix products, matmul_rows(): jnp.einsum('fyg,gq->fyq', first_operand, second_operand, preferred_elemen...  41.1 us
    dot_general x4, matrix products, weight_grad(): jnp.einsum('crk,cre->ke', first_operand, second_operand, preferred_elemen...  39 us
    convert_element_type x1, other arithmetic, attend_backward(): score_gradient = (attention_probabilities * (prob_grad - jnp.sum(prob_gra...  29.1 us
    unnamed x182, local copies, waits for them, and re-layouts  28.5 us
  transfers between devices with their start and end apart: 11, of which 7 were waited for; matrix products, arithmetic and copies ran while one was open for 25% of the time, Pallas kernels for 0%

profile of v6, /device:TPU:0, one launch (start us, length us, event | category | flops | bytes accessed | tf_op | source)
XLA Modules:
  0.0 753.8 jit_solution(16741047830524339147)
XLA Ops:
  24.0 22.7 %all-gather.2 = bf16[16,2,1536]{2,1,0:T(2,128)(2,1)S(1)} all-gather(bf16[1,2,1536]{2,1,0:T(2,128)(2,1)S(1)} %bitcast.254), channel_id=1, replica_groups=mesh['wide'=16,'narrow'=2] {'wide'}, dimensions={0}, use_global_device_ids=true | all-gather | bytes 104448 | tf_op jit(solution)/shard_map/all_gather | solution.py:109
  57.3 28.1 %all-to-all-done = f32[32,1,6144]{2,1,0:T(1,128)S(1)} async-done(((f32[32,1,6144]{2,1,0:T(1,128)}), f32[32,1,6144]{2,1,0:T(1,128)S(1)}, u32[]{:S(2)}, u32[]{:S(2)}) %all-to-all-start) | async-done | bytes 786464 | tf_op jit(solution)/shard_map/all_to_all | solution.py:266
  86.6 12.5 %all-gather.8.cloned.1.call-done = bf16[1024,4096]{1,0:T(8,128)(2,1)} async-done(((bf16[32,4096]{1,0:T(8,128)(2,1)}), bf16[1024,4096]{1,0:T(8,128)(2,1)}) %all-gather.8.cloned.1.call-update) | async-done | bytes 8388624 | tf_op jit(solution)/shard_map/all_gather | solution.py:256
  99.1 7.4 fusion.17
  121.1 14.4 %fusion.92 = (f32[16,680]{1,0:T(8,128)S(1)}, f32[16,680,680]{1,2,0:T(8,128)}) fusion(f32[680,16,64]{0,2,1:T(8,128)S(1)} %bitcast.217, f32[16,64]{1,0:T(8,128)S(1)} %reshape.872, f32[680,16]{0,1:T(8,128)S(1)} %get-tuple-element.78, f32[680,16,64]{0,2,1:T(8,128)S(1)} %bitcast.211, f32[16,64]{1,0:T(8,128)S(1)} %reshape.871, ...), kind=kOutput, calls=%fused_computation.190 | convolution fusion | flops 973357440 | bytes 35765312 | tf_op jit(solution)/shard_map/vmap(nkz,vkz->knv)/dot_general | solution.py:63
  135.5 13.4 %fusion = f32[16,680]{1,0:T(8,128)S(1)} fusion(f32[16,680,680]{1,2,0:T(8,128)} %get-tuple-element.63, f32[16,680]{1,0:T(8,128)S(1)} %get-tuple-element.62), kind=kLoop, calls=%fused_computation.6 | loop fusion | flops 14785920 | bytes 29680640 | tf_op jit(solution)/shard_map/vmap()/reduce_sum | solution.py:73
  149.0 15.3 %fusion.47 = bf16[16,64,680]{2,1,0:T(8,128)(2,1)} fusion(bf16[680,16,64]{0,2,1:T(8,128)(2,1)S(1)} %bitcast.232, f32[16,680,680]{1,2,0:T(8,128)} %get-tuple-element.63, f32[16,680]{1,0:T(8,128)S(1)} %fusion, f32[16,680]{1,0:T(8,128)S(1)} %get-tuple-element.62), kind=kOutput, calls=%fused_computation.100 | convolution fusion | flops 969886720 | bytes 32465920 | tf_op jit(solution)/shard_map/vmap(wcv,vwn->cwn)/dot_general | solution.py:75
  171.3 43.6 %all-gather.10.cloned.1.call-done = bf16[8192,1024]{1,0:T(8,128)(2,1)} async-done(((bf16[256,1024]{1,0:T(8,128)(2,1)}), bf16[8192,1024]{1,0:T(8,128)(2,1)}) %all-gather.10.cloned.1.call-update) | async-done | bytes 16777232 | tf_op jit(solution)/shard_map/all_gather | solution.py:143
  214.9 9.5 %fusion.89 = (bf16[32,128,1024]{2,1,0:T(8,128)(2,1)S(1)}, bf16[32,128,1024]{2,1,0:T(8,128)(2,1)}) fusion(bf16[32,256,1024]{2,1,0:T(8,128)(2,1)} %bitcast.223), kind=kLoop, calls=%fused_computation.187 | loop fusion | bytes 33554432 | tf_op jit(solution)/shard_map/slice | solution.py:148
  224.4 7.6 %copy.118 = bf16[32,32,4,1024]{3,2,1,0:T(4,128)(2,1)} copy(bf16[32,32,4,1024]{3,1,2,0:T(8,128)(2,1)S(1)} %bitcast.222) | data formatting | bytes 16777216 | tf_op jit(solution)/shard_map/transpose | solution.py:150
  232.0 12.1 %copy.133 = bf16[128,8,4,1024]{3,1,2,0:T(8,128)(2,1)} copy(bf16[128,8,4,1024]{3,2,1,0:T(4,128)(2,1)} %bitcast.221) | data formatting | bytes 16777216
  244.1 12.6 %fusion.84 = f32[680,4096]{1,0:T(8,128)} fusion(bf16[1024,4096]{1,0:T(8,128)(2,1)} %bitcast.226, f32[1,680,1024]{2,1,0:T(8,128)S(1)} %get-tuple-element.32, f32[1024]{0:T(1024)S(1)} %bitcast.260, f32[1024]{0:T(1024)S(1)} %bitcast.255, f32[680]{0:T(1024)S(1)} %fusion.75, f32[680]{0:T(1024)S(1)} %broadcast_multiply_fusion.2), kind=kOutput, calls=%fused_computation.183 | convolution fusion | flops 5707735040 | bytes 22328640 | tf_op jit(solution)/shard_map/fyg,gq->fyq/dot_general | solution.py:45
  256.7 18.8 %convert_reduce_fusion = (f32[4096]{0:T(1024)}, bf16[680,4096]{1,0:T(8,128)(2,1)}) fusion(f32[680,4096]{1,0:T(8,128)} %fusion.84, f32[4096]{0:T(1024)S(1)} %copy-done.60, bf16[4096,1024]{1,0:T(8,128)(2,1)} %bitcast.230, f32[1024]{0:T(1024)S(1)} %bitcast.262, bf16[1,680,1024]{2,1,0:T(8,128)(2,1)S(1)} %copy-done.26), kind=kOutput, calls=%fused_computation.20 | convolution fusion | flops 5770399744 | bytes 26529792 | tf_op jit(solution)/shard_map/rfw,uw->rfu/dot_general | solution.py:51
  275.5 9.4 %fusion.39 = (bf16[1024]{0:T(1024)(128)(2,1)}, f32[680]{0:T(1024)S(1)}, f32[680,1024]{1,0:T(8,128)S(1)}) fusion(f32[1,680,1024]{2,1,0:T(8,128)S(1)} %get-tuple-element.32, f32[680]{0:T(1024)S(1)} %fusion.75, f32[680]{0:T(1024)S(1)} %broadcast_multiply_fusion.2, f32[1024]{0:T(1024)S(1)} %bitcast.256, bf16[680,4096]{1,0:T(8,128)(2,1)} %get-tuple-element.76, ...), kind=kOutput, calls=%fused_computation.81 | convolution fusion | flops 5709126144 | bytes 19544032 | tf_op jit(solution)/shard_map/rfw,uw->rfu/dot_general | solution.py:51
  288.6 15.6 %convert_reduce_fusion.2 = (f32[1024]{0:T(1024)}, bf16[1024]{0:T(1024)(128)(2,1)}, bf16[1024]{0:T(1024)(128)(2,1)}, f32[1024]{0:T(1024)}, bf16[1,680,1024]{2,1,0:T(8,128)(2,1)S(1)}, /*index=5*/bf16[1,680,1024]{2,1,0:T(8,128)(2,1)}) fusion(f32[1024]{0:T(1024)S(1)} %bitcast.263, bf16[1,680,1024]{2,1,0:T(8,128)(2,1)S(1)} %copy-done.26, ...), kind=kOutput, calls=%fused_computation.88 | convolution fusion | flops 5746028544 | bytes 32111264 | tf_op jit(solution)/shard_map/fyg,gq->fyq/dot_general | solution.py:45
  309.3 15.8 %bitcast_convert_fusion = (bf16[1,680,16,64]{1,3,2,0:T(8,128)(2,1)}, f32[16,64,680]{2,1,0:T(8,128)}) fusion(bf16[680,16,64]{0,2,1:T(8,128)(2,1)S(1)} %bitcast.224, f32[16,680,680]{1,2,0:T(8,128)} %get-tuple-element.63, f32[16,680]{1,0:T(8,128)} %log_add_fusion), kind=kOutput, calls=%fused_computation.55 | convolution fusion | flops 962488320 | bytes 35207680 | tf_op jit(solution)/shard_map/vmap(fgs,gfu->sfu)/dot_general | solution.py:89
  325.1 26.1 %multiply_reduce_fusion = (f32[16,680]{1,0:T(8,128)}, f32[16,680,680]{1,2,0:T(8,128)}) fusion(f32[16,680,680]{1,2,0:T(8,128)} %get-tuple-element.63, f32[16,680]{1,0:T(8,128)} %log_add_fusion, bf16[680,16,64]{0,2,1:T(8,128)(2,1)S(1)} %bitcast.225, bf16[680,16,64]{0,2,1:T(8,128)(2,1)S(1)} %bitcast.233), kind=kOutput, calls=%fused_computation.1 | convolution fusion | flops 969179520 | bytes 62059520 | tf_op jit(solution)/shard_map/vmap(nkz,vkz->knv)/dot_general | solution.py:86
  351.2 29.1 %multiply_convert_fusion = bf16[16,680,680]{1,2,0:T(8,128)(2,1)} fusion(f32[16,680,680]{1,2,0:T(8,128)} %get-tuple-element.69, f32[16,680,680]{1,2,0:T(8,128)} %get-tuple-element.63, f32[16,680]{1,0:T(8,128)} %get-tuple-element.68, f32[16,680]{1,0:T(8,128)} %log_add_fusion), kind=kLoop, calls=%fused_computation | loop fusion | flops 29593600 | bytes 74071040 | tf_op jit(solution)/shard_map/vmap()/convert_element_type | solution.py:98
  380.4 11.7 %fusion.30 = (f32[680,16]{0,1:T(8,128)S(1)}, f32[16,64,680]{2,1,0:T(8,128)}) fusion(f32[1,680,16,64]{1,3,2,0:T(8,128)S(1)} %bitcast.212, f32[16,64]{1,0:T(8,128)S(1)} %copy-done.36, bf16[16,680,680]{1,2,0:T(8,128)(2,1)} %multiply_convert_fusion, f32[680,16,64]{0,2,1:T(8,128)} %bitcast.216, f32[16,64]{1,0:T(8,128)S(1)} %copy-done.35, f32[680,16]{0,1:T(8,128)} %copy-done.18), kind=kOutput, calls=%fused_computation.63 | convolution fusion | flops 951162240 | bytes 23247872 | tf_op jit(solution)/shard_map/vmap(wcv,vwn->cwn)/dot_general | solution.py:99
  392.2 9.4 %fusion.27 = (f32[16,64]{1,0:T(8,128)}, f32[680,16]{0,1:T(8,128)S(1)}, f32[16,64,680]{2,1,0:T(8,128)S(1)}) fusion(f32[1,680,16,64]{1,3,2,0:T(8,128)S(1)} %bitcast.218, f32[680,16]{0,1:T(8,128)S(1)} %copy-done.19, f32[16,64]{1,0:T(8,128)S(1)} %copy-done.37, bf16[16,680,680]{1,2,0:T(8,128)(2,1)} %multiply_convert_fusion, f32[680,16,64]{0,2,1:T(8,128)S(1)} %bitcast.213, ...), kind=kOutput, calls=%fused_computation.51 | convolution fusion | flops 953946496 | bytes 23295488 | tf_op jit(solution)/shard_map/vmap(fgs,gfu->sfu)/dot_general | solution.py:102
  407.9 10.7 %convolution_convert_fusion.2 = bf16[1024,3072]{1,0:T(8,128)(2,1)} fusion(bf16[680,1024]{0,1:T(8,128)(2,1)S(1)} %bitcast.242, bf16[680,1024]{0,1:T(8,128)(2,1)S(1)} %bitcast.240, bf16[680,1024]{0,1:T(8,128)(2,1)S(1)} %bitcast.237, bf16[1,680,1024]{2,1,0:T(8,128)(2,1)S(1)} %copy-done.8, f32[1024]{0:T(1024)S(1)} %bitcast.266, f32[1024]{0:T(1024)S(1)} %bitcast.249, ...), kind=kOutput, calls=%fused_computation.26 | convolution fusion | flops 4298047488 | bytes 11875648 | tf_op jit(solution)/shard_map/crk,cre->ke/dot_general | solution.py:57
  419.9 14.1 %convolution_convert_fusion = bf16[4096,1024]{1,0:T(8,128)(2,1)} fusion(bf16[1,680,1024]{2,1,0:T(8,128)(2,1)S(1)} %copy-done.27, f32[1024]{0:T(1024)S(1)} %bitcast.264, f32[680,4096]{1,0:T(8,128)} %fusion.84, f32[4096]{0:T(1024)S(1)} %copy-done.61), kind=kOutput, calls=%fused_computation.23 | convolution fusion | flops 5738389504 | bytes 20942848 | tf_op jit(solution)/shard_map/crk,cre->ke/dot_general | solution.py:57
  436.1 12.4 %convolution_convert_fusion.1 = bf16[1024,4096]{1,0:T(8,128)(2,1)} fusion(bf16[680,4096]{1,0:T(8,128)(2,1)} %get-tuple-element.76, f32[1,680,1024]{2,1,0:T(8,128)S(1)} %copy-done.15, f32[1024]{0:T(1024)S(1)} %bitcast.261, f32[1024]{0:T(1024)S(1)} %bitcast.258, f32[680]{0:T(1024)S(1)} %copy-done.58, f32[680]{0:T(1024)S(1)} %copy-done.44), kind=kOutput, calls=%fused_computation.24 | convolution fusion | flops 5711929344 | bytes 16758080 | tf_op jit(solution)/shard_map/crk,cre->ke/dot_general | solution.py:57
  448.5 14.6 %reshape_reshape.3 = bf16[32,32,4,1024]{3,2,1,0:T(4,128)(2,1)} reshape(bf16[1024,4096]{1,0:T(8,128)(2,1)} %convolution_convert_fusion.1) | data formatting | bytes 16777216 | tf_op jit(solution)/shard_map/reshape;reshape | solution.py:173
  463.1 10.5 %copy.124 = bf16[32,32,4,1024]{3,1,2,0:T(8,128)(2,1)} copy(bf16[32,32,4,1024]{3,2,1,0:T(4,128)(2,1)} %reshape_reshape.3) | data formatting | bytes 16777216 | tf_op jit(solution)/shard_map/reshape;reshape | solution.py:173
  477.0 7.8 %pad_maximum_fusion = bf16[32,160,1024]{2,1,0:T(8,128)(2,1)} fusion(bf16[32,32,1024]{2,1,0:T(8,128)(2,1)S(1)} %bitcast.234, bf16[32,128,1024]{2,1,0:T(8,128)(2,1)S(1)} %bitcast.220), kind=kLoop, calls=%fused_computation.22 | loop fusion | flops 20971520 | bytes 20971520 | tf_op jit(solution)/shard_map/concatenate | solution.py:180
  486.9 10.1 %fusion.35 = (f32[680]{0:T(1024)S(1)}, f32[680,1024]{1,0:T(8,128)S(1)}) fusion(bf16[1,680,1024]{2,1,0:T(8,128)(2,1)} %param.17, f32[1024]{0:T(1024)S(1)} %bitcast.250, f32[680]{0:T(1024)S(1)} %copy-done.42, bf16[1024,4096]{1,0:T(8,128)(2,1)} %all-gather.8.cloned.1.call-done, bf16[680,1024]{0,1:T(8,128)(2,1)} %bitcast.241, bf16[680,1024]{0,1:T(8,128)(2,1)} %bitcast.239, ...), kind=kOutput, calls=%fused_computation.74 | convolution fusion | flops 4294204672 | bytes 15197504 | tf_op jit(solution)/shard_map/rfw,uw->rfu/dot_general | solution.py:51
  504.5 21.6 %all-gather.4 = bf16[16,2,6144]{2,1,0:T(2,128)(2,1)} all-gather(bf16[1,2,6144]{2,1,0:T(2,128)(2,1)S(1)} %bitcast.247), channel_id=1, replica_groups=mesh['wide'=16,'narrow'=2] {'wide'}, dimensions={0}, use_global_device_ids=true | all-gather | bytes 417792 | tf_op jit(solution)/shard_map/all_gather | solution.py:109
  543.2 5.8 all-to-all-start.2
  550.9 6.6 all-to-all-done.2
  560.1 50.6 %reduce-scatter.8.cloned.1.call-done = bf16[256,1024]{1,0:T(8,128)(2,1)} async-done(((bf16[4096,1024]{1,0:T(8,128)(2,1)}), bf16[256,1024]{1,0:T(8,128)(2,1)}) %reduce-scatter.8.cloned.1.call-update) | async-done | bytes 524304 | tf_op jit(solution)/shard_map/reduce_scatter | solution.py:182
  613.1 120.6 %reduce-scatter.6.cloned.1.call-done = bf16[320,1024]{1,0:T(8,128)(2,1)} async-done(((bf16[5120,1024]{1,0:T(8,128)(2,1)}), bf16[320,1024]{1,0:T(8,128)(2,1)}) %reduce-scatter.6.cloned.1.call-update) | async-done | bytes 655376 | tf_op jit(solution)/shard_map/reduce_scatter | solution.py:182
  (292 shorter events, 118.2 us)
Async XLA Ops:
  7.2 39.6 %copy-start = (bf16[32,6144]{1,0:T(8,128)(2,1)S(1)}, bf16[32,6144]{1,0:T(8,128)(2,1)}, u32[]{:S(2)}) copy-start(bf16[32,6144]{1,0:T(8,128)(2,1)} %param.20) | copy-start | bytes 1179652
  7.2 91.9 %all-gather.8.cloned.1.call-start = ((), (), s32[]{:S(2)}) async-start(), calls=%async_computation.6 | async-start | bytes 8650752 | tf_op jit(solution)/shard_map/all_gather | solution.py:256
  9.0 205.9 %all-gather.10.cloned.1.call-start = ((), (), s32[]{:S(2)}) async-start(), calls=%async_computation.7 | async-start | bytes 17301504 | tf_op jit(solution)/shard_map/all_gather | solution.py:143
  10.0 41.4 %copy-start.78 = (s32[10]{0:T(128)S(1)}, s32[10]{0:T(128)}, u32[]{:S(2)}) copy-start(s32[10]{0:T(128)} %param.19) | copy-start | bytes 124
  11.8 41.7 %copy-start.6 = (bf16[1,680,1024]{2,1,0:T(8,128)(2,1)S(1)}, bf16[1,680,1024]{2,1,0:T(8,128)(2,1)}, u32[]{:S(2)}) copy-start(bf16[1,680,1024]{2,1,0:T(8,128)(2,1)} %param.17) | copy-start | bytes 4177924
  48.8 36.7 %all-to-all-start = ((f32[32,1,6144]{2,1,0:T(1,128)}), f32[32,1,6144]{2,1,0:T(1,128)S(1)}, u32[]{:S(2)}, u32[]{:S(2)}) async-start(f32[32,1,6144]{2,1,0:T(1,128)} %copy.110), calls=%async_computation | async-start | bytes 1572864 | tf_op jit(solution)/shard_map/all_to_all | solution.py:266
  51.4 507.4 %reduce-scatter.4.cloned.1.call-start = ((), (), s32[]{:S(2)}) async-start(), calls=%async_computation.8 | async-start | bytes 6684672 | tf_op jit(solution)/shard_map/reduce_scatter | solution.py:202
  53.4 67.5 %copy-start.34 = (f32[16,64]{1,0:T(8,128)}, f32[16,64]{1,0:T(8,128)S(1)}, u32[]{:S(2)}) copy-start(f32[16,64]{1,0:T(8,128)S(1)} %reshape.872) | copy-start | bytes 12292
  53.4 67.4 %copy-start.32 = (f32[16,64]{1,0:T(8,128)}, f32[16,64]{1,0:T(8,128)S(1)}, u32[]{:S(2)}) copy-start(f32[16,64]{1,0:T(8,128)S(1)} %reshape.871) | copy-start | bytes 12292
  53.8 45.3 %copy-start.41 = (f32[680]{0:T(1024)}, f32[680]{0:T(1024)S(1)}, u32[]{:S(2)}) copy-start(f32[680]{0:T(1024)S(1)} %broadcast_multiply_fusion.3) | copy-start | bytes 8164
  54.3 44.8 %copy-start.45 = (f32[680]{0:T(1024)}, f32[680]{0:T(1024)S(1)}, u32[]{:S(2)}) copy-start(f32[680]{0:T(1024)S(1)} %fusion.34) | copy-start | bytes 8164
  54.3 44.8 %copy-start.39 = (f32[680]{0:T(1024)}, f32[680]{0:T(1024)S(1)}, u32[]{:S(2)}) copy-start(f32[680]{0:T(1024)S(1)} %fusion.74) | copy-start | bytes 8164
  148.9 15.3 %copy-start.7 = (bf16[1,680,1024]{2,1,0:T(8,128)(2,1)S(1)}, bf16[1,680,1024]{2,1,0:T(8,128)(2,1)}, u32[]{:S(2)}) copy-start(bf16[1,680,1024]{2,1,0:T(8,128)(2,1)} %param.17) | copy-start | bytes 4177924
  169.8 116.7 %copy-start.14 = (f32[1,680,1024]{2,1,0:T(8,128)}, f32[1,680,1024]{2,1,0:T(8,128)S(1)}, u32[]{:S(2)}) copy-start(f32[1,680,1024]{2,1,0:T(8,128)S(1)} %get-tuple-element.32) | copy-start | bytes 8355844
  169.8 115.2 %copy-start.43 = (f32[680]{0:T(1024)}, f32[680]{0:T(1024)S(1)}, u32[]{:S(2)}) copy-start(f32[680]{0:T(1024)S(1)} %broadcast_multiply_fusion.2) | copy-start | bytes 8164
  170.2 114.8 %copy-start.57 = (f32[680]{0:T(1024)}, f32[680]{0:T(1024)S(1)}, u32[]{:S(2)}) copy-start(f32[680]{0:T(1024)S(1)} %fusion.75) | copy-start | bytes 8164
  244.1 31.4 %slice-start = ((s8[8388608]{0:T(1024)(128)(4,1)}), s8[4194304]{0:T(1024)(128)(4,1)S(1)}, s32[]{:S(2)}) async-start(s8[8388608]{0:T(1024)(128)(4,1)} %bitcast.227), calls=%async_computation.11 | async-start | bytes 8388608
  256.7 18.9 %slice-start.1 = ((s8[8388608]{0:T(1024)(128)(4,1)}), s8[4194304]{0:T(1024)(128)(4,1)S(1)}, s32[]{:S(2)}) async-start(s8[8388608]{0:T(1024)(128)(4,1)} %bitcast.227), calls=%async_computation.12 | async-start | bytes 8388608
  286.5 17.7 %copy-start.11 = (f32[1,680,1024]{2,1,0:T(8,128)}, f32[1,680,1024]{2,1,0:T(8,128)S(1)}, u32[]{:S(2)}) copy-start(f32[1,680,1024]{2,1,0:T(8,128)S(1)} %get-tuple-element.30) | copy-start | bytes 8355844
  286.5 17.7 %copy-start.55 = (f32[680]{0:T(1024)}, f32[680]{0:T(1024)S(1)}, u32[]{:S(2)}) copy-start(f32[680]{0:T(1024)S(1)} %negate_multiply_fusion.1) | copy-start | bytes 8164
  309.3 15.8 %copy-start.17 = (bf16[1,680,1024]{1,2,0:T(8,128)(2,1)S(1)}, bf16[1,680,1024]{1,2,0:T(8,128)(2,1)}, u32[]{:S(2)}) copy-start(bf16[1,680,1024]{1,2,0:T(8,128)(2,1)} %copy.111) | copy-start | bytes 4177924
  351.2 29.1 %copy-start.2 = (f32[1,680,1024]{1,2,0:T(8,128)S(1)}, f32[1,680,1024]{1,2,0:T(8,128)}, u32[]{:S(2)}) copy-start(f32[1,680,1024]{1,2,0:T(8,128)} %copy-done.1) | copy-start | bytes 8355844
  351.2 29.1 %copy-start.35 = (f32[16,64]{1,0:T(8,128)S(1)}, f32[16,64]{1,0:T(8,128)}, u32[]{:S(2)}) copy-start(f32[16,64]{1,0:T(8,128)} %copy-done.34) | copy-start | bytes 12292
  351.2 29.1 %copy-start.36 = (f32[16,64]{1,0:T(8,128)S(1)}, f32[16,64]{1,0:T(8,128)}, u32[]{:S(2)}) copy-start(f32[16,64]{1,0:T(8,128)} %broadcast_multiply_fusion.1) | copy-start | bytes 12292
  418.6 192.0 %reduce-scatter.8.cloned.1.call-start = ((), (), s32[]{:S(2)}) async-start(), calls=%async_computation.10 | async-start | bytes 8912896 | tf_op jit(solution)/shard_map/reduce_scatter | solution.py:182
  434.1 299.6 %reduce-scatter.6.cloned.1.call-start = ((), (), s32[]{:S(2)}) async-start(), calls=%async_computation.9 | async-start | bytes 11141120 | tf_op jit(solution)/shard_map/reduce_scatter | solution.py:182
  497.4 37.4 %copy-start.56 = (f32[680]{0:T(1024)S(1)}, f32[680]{0:T(1024)}, u32[]{:S(2)}) copy-start(f32[680]{0:T(1024)} %copy-done.55) | copy-start | bytes 8164
  529.9 13.3 %all-to-all-start.1 = ((f32[32,1,32]{2,1,0:T(1,128)}), f32[32,1,32]{2,1,0:T(1,128)S(1)}, u32[]{:S(2)}, u32[]{:S(2)}) async-start(f32[32,1,32]{2,1,0:T(1,128)} %bitcast.52), calls=%async_computation.1 | async-start | bytes 32768 | tf_op jit(solution)/shard_map/all_to_all | solution.py:413
  543.2 14.3 %all-to-all-start.2 = ((f32[32,1,320]{2,1,0:T(1,128)}), f32[32,1,320]{2,1,0:T(1,128)S(1)}, u32[]{:S(2)}, u32[]{:S(2)}) async-start(f32[32,1,320]{2,1,0:T(1,128)} %reshape.863), calls=%async_computation.3 | async-start | bytes 98304 | tf_op jit(solution)/shard_map/all_to_all | solution.py:208
  559.7 176.5 %collective-permute-start = (bf16[32,3072]{1,0:T(8,128)(2,1)S(1)}, bf16[32,3072]{1,0:T(8,128)(2,1)S(1)}, u32[]{:S(2)}, u32[]{:S(2)}) collective-permute-start(bf16[32,3072]{1,0:T(8,128)(2,1)S(1)} %constant_dynamic-slice_fusion.2), channel_id=1, source_target_pairs={{0,1},{1,0},{2,3},{3,2},{4,5},{5,4},{6,7},{7,6},{8,9},{9,8},{10,11... | collective-permute-start | bytes 589832 | tf_op jit(solution)/shard_map/ppermute | solution.py:163
  611.6 126.3 %collective-permute-start.2 = (bf16[128,1024]{1,0:T(8,128)(2,1)S(1)}, bf16[128,1024]{1,0:T(8,128)(2,1)S(1)}, u32[]{:S(2)}, u32[]{:S(2)}) collective-permute-start(bf16[128,1024]{1,0:T(8,128)(2,1)S(1)} %constant_dynamic-slice_fusion), channel_id=1, source_target_pairs={{0,1},{1,0},{2,3},{3,2},{4,5},{5,4},{6,7},{7,6},{8,9},{9,8},{10,11... | collective-permute-start | bytes 786440 | tf_op jit(solution)/shard_map/ppermute | solution.py:163
  734.7 9.2 %collective-permute-start.1 = (bf16[160,1024]{1,0:T(8,128)(2,1)S(1)}, bf16[160,1024]{1,0:T(8,128)(2,1)S(1)}, u32[]{:S(2)}, u32[]{:S(2)}) collective-permute-start(bf16[160,1024]{1,0:T(8,128)(2,1)S(1)} %constant_dynamic-slice_fusion.1), channel_id=1, source_target_pairs={{0,1},{1,0},{2,3},{3,2},{4,5},{5,4},{6,7},{7,6},{8,9},{9,8},{10,11... | collective-permute-start | bytes 983048 | tf_op jit(solution)/shard_map/ppermute | solution.py:163
  (64 other events, 427.4 us)
Sparse Core Ops, SparseCore 0:
  11.6 87.4 all-gather.7
  102.7 112.2 all-gather.9
  418.7 83.2 reduce-scatter.3
  505.9 104.6 reduce-scatter.7
  614.5 119.1 reduce-scatter.5

commit v7 on v6

--- a/solution.py
+++ b/solution.py
@@ -111,47 +111,6 @@
     )
 
 
-LANES = 1024
-TILE_ROWS = 16
-
-
-def shard_rows(shard):
-    rows, cols = shard.shape
-    blocks = cols // LANES
-    if blocks == 1:
-        return shard
-    return shard.reshape(rows, blocks, LANES).transpose(1, 0, 2).reshape(blocks * rows, LANES)
-
-
-def rows_shard(piece, cols):
-    blocks = cols // LANES
-    if blocks == 1:
-        return piece
-    rows = piece.shape[0] // blocks
-    return piece.reshape(blocks, rows, LANES).transpose(1, 0, 2).reshape(rows, cols)
-
-
-def pad_rows(flat):
-    pad = -flat.shape[1] % TILE_ROWS
-    if pad:
-        flat = jnp.concatenate([flat, jnp.zeros((flat.shape[0], pad, LANES), flat.dtype)], axis=1)
-    return flat
-
-
-def gather_packed(members, count):
-    flat = pad_rows(jnp.concatenate([shard_rows(m) for m in members], axis=0)[None])
-    got = lax.all_gather(flat[0], AXES, axis=0, tiled=True).reshape(count, flat.shape[1], LANES)
-    out, start = [], 0
-    for member in members:
-        rows, cols = member.shape
-        blocks = cols // LANES
-        piece = got[:, start : start + blocks * rows]
-        start += blocks * rows
-        full = piece.reshape(count, blocks, rows, LANES).transpose(0, 2, 1, 3)
-        out.append(full.reshape(count * rows, cols))
-    return out
-
-
 def narrow_sum(half):
     size = lax.axis_size("narrow")
     if size != 2:
@@ -162,40 +121,6 @@
     send = lax.dynamic_slice_in_dim(half, (1 - here) * rows, rows, axis=0)
     got = lax.ppermute(send, "narrow", [(0, 1), (1, 0)])
     return keep.astype(jnp.float32) + got.astype(jnp.float32)
-
-
-def scatter_packed(matrices, vectors, count):
-    pieces = []
-    for member in matrices:
-        rows, cols = member.shape
-        shard = member.astype(jnp.bfloat16).reshape(count, rows // count, cols)
-        blocks = cols // LANES
-        shard = shard.reshape(count, rows // count, blocks, LANES).transpose(0, 2, 1, 3)
-        pieces.append(shard.reshape(count, blocks * rows // count, LANES))
-    if vectors:
-        small = jnp.concatenate([v.reshape(count, -1) for v in vectors], axis=1)
-        pad = -small.shape[1] % LANES
-        small = jnp.concatenate([small, jnp.zeros((count, pad), small.dtype)], axis=1)
-        pieces.append(small.astype(jnp.bfloat16).reshape(count, -1, LANES))
-    flat = pad_rows(jnp.concatenate(pieces, axis=1))
-    flat = flat.reshape(count * flat.shape[1], LANES)
-    half = lax.psum_scatter(flat, "wide", scatter_dimension=0, tiled=True)
-    got = narrow_sum(half)
-    out, start = [], 0
-    for member in matrices:
-        rows, cols = member.shape
-        blocks = cols // LANES
-        size = blocks * rows // count
-        out.append(rows_shard(got[start : start + size], cols))
-        start += size
-    if vectors:
-        tail = got[start:].reshape(-1)
-        offset = 0
-        for v in vectors:
-            size = v.shape[0] // count
-            out.append(tail[offset : offset + size])
-            offset += size
-    return out
 
 
 def scatter_natural(member):
@@ -253,10 +178,14 @@
         unpacked.append(small[:, start : start + size].reshape(count * size).astype(jnp.float32))
         start += size
     ada_bias, query_bias, value_bias, query_gain, key_gain, proj_bias, up_bias, down_bias = unpacked
-    first = lax.all_gather(jnp.concatenate([w_qkv, w_proj], axis=1), AXES, axis=0, tiled=True)
-    qkv_full = first[:, : w_qkv.shape[1]]
-    proj_full = first[:, w_qkv.shape[1] :]
-    up_full, down_full = gather_packed((w_up, w_down), count)
+    first = lax.all_gather(
+        jnp.concatenate([w_qkv, w_proj, w_up], axis=1), AXES, axis=0, tiled=True
+    )
+    qkv_cols, proj_cols = w_qkv.shape[1], w_proj.shape[1]
+    qkv_full = first[:, :qkv_cols]
+    proj_full = first[:, qkv_cols : qkv_cols + proj_cols]
+    up_full = first[:, qkv_cols + proj_cols :]
+    down_full = lax.all_gather(w_down, AXES, axis=0, tiled=True)
     allowed = block_mask(scale_tokens)
     input_rows = inputs.astype(jnp.float32)
     ada_rows = w_ada.shape[0]
@@ -292,7 +221,7 @@
     gamma_mlp_grad = jnp.sum(upstream * branch, axis=1)
     branch_grad = (upstream * gamma_mlp[:, None, :]).astype(jnp.bfloat16)
     down_grad = weight_grad(hidden, branch_grad)
-    (down_sum,) = scatter_packed((down_grad,), (), count)
+    down_sum = scatter_natural(down_grad)
     down_bias_grad = jnp.sum(branch_grad.astype(jnp.float32), axis=(0, 1))
     return mlp_back(
         branch_grad, down_full, hidden_pre, normed_mlp, up_full, middle, scale_mlp, shift_mlp,
@@ -325,7 +254,9 @@
     attended_grad = (middle_grad * gamma_attn[:, None, :]).astype(jnp.bfloat16)
     proj_grad = weight_grad(context, attended_grad)
     proj_bias_grad = jnp.sum(attended_grad.astype(jnp.float32), axis=(0, 1))
-    up_sum, proj_sum = scatter_packed((up_grad, proj_grad), (), count)
+    both_sum = scatter_natural(jnp.concatenate([up_grad, proj_grad], axis=1))
+    up_sum = both_sum[:, : up_grad.shape[1]]
+    proj_sum = both_sum[:, up_grad.shape[1] :]
     context_gradient = (
         matmul_back(attended_grad, proj_full).astype(jnp.bfloat16).reshape(head_shape)
     )

time: 759 us -> 730 us (0.962)
  local copies, waits for them, and re-layouts: 95.2 us -> 34.5 us
  waiting for transfers between devices: 266 us -> 297 us
    reduce_scatter x1 -> x3, waiting for transfers between devices: 0.01 us -> 199 us  [scatter_natural(): lax.psum_scatter(member.astype(jnp.bfloat16), 'wide', scatter_dimension=0...]
    reduce_scatter x2 -> x0, waiting for transfers between devices: 171 us -> none  [scatter_packed(): half = lax.psum_scatter(flat, 'wide', scatter_dimension=0, tiled=True)]
    another operation x2 -> x0, local copies, waits for them, and re-layouts: 25.1 us -> none  [scatter_packed(): shard.reshape(count, rows // count, blocks, LANES).transpose(0, 2, 1, 3)]
    unnamed x182 -> x170, local copies, waits for them, and re-layouts: 28.5 us -> 10.4 us
    slice x3 -> x2, local copies, waits for them, and re-layouts: 10.2 us -> 1.49 us  [the longest x1 0.83 us: mlp_back(): up_sum = both_sum[:, :up_grad.shape[1]]]
  transfers between devices with their start and end apart: 11 -> 11, of which waited for: 7 -> 6; matrix products, arithmetic and copies ran while one was open for 25% -> 24% of each run, Pallas kernels for 0% -> 0%
where the time goes in v7:
time: 730 us; the launch traced here: 725 us
  waiting for transfers between devices  297 us (41%)
  matrix products  220 us (30%)
  other arithmetic  87 us (12%)
  blocking collectives  57.4 us (8%)
  local copies, waits for them, and re-layouts  34.5 us (5%)
  between operations  15 us (2%)
  starting transfers between devices  14.9 us (2%)
    reduce_scatter x3, waiting for transfers between devices, scatter_natural(): lax.psum_scatter(member.astype(jnp.bfloat16), 'wide', scatter_dimension=0...  199 us
    all_gather x1, waiting for transfers between devices, layer(): lax.all_gather(jnp.concatenate([w_qkv, w_proj, w_up], axis=1), AXES, axis...  56.7 us
    all_gather x2, blocking collectives, nested_gather(): lax.all_gather(lax.all_gather(member, 'narrow', axis=0, tiled=True), 'wid...  47.6 us
    dot_general x4, matrix products, matmul_back(): jnp.einsum('rfw,uw->rfu', first_operand, second_operand, preferred_elemen...  43.5 us
    dot_general x4, matrix products, matmul_rows(): jnp.einsum('fyg,gq->fyq', first_operand, second_operand, preferred_elemen...  39.6 us
    dot_general x4, matrix products, weight_grad(): jnp.einsum('crk,cre->ke', first_operand, second_operand, preferred_elemen...  39.2 us
    all_to_all x1, waiting for transfers between devices, layer(): lax.all_to_all(ada_partial.reshape(count, sequences, ada_cols), AXES, spl...  30.7 us
    convert_element_type x1, other arithmetic, attend_backward(): score_gradient = (attention_probabilities * (prob_grad - jnp.sum(prob_gra...  28.8 us
  transfers between devices with their start and end apart: 11, of which 6 were waited for; matrix products, arithmetic and copies ran while one was open for 24% of the time, Pallas kernels for 0%

profile of v7, /device:TPU:0, one launch (start us, length us, event | category | flops | bytes accessed | tf_op | source)
XLA Modules:
  0.0 725.1 jit_solution(1896698685945582652)
XLA Ops:
  11.2 5.4 concatenate.51
  16.7 5.3 all-gather.1
  22.0 22.8 %all-gather.2 = bf16[16,2,1536]{2,1,0:T(2,128)(2,1)S(1)} all-gather(bf16[1,2,1536]{2,1,0:T(2,128)(2,1)S(1)} %bitcast.211), channel_id=1, replica_groups=mesh['wide'=16,'narrow'=2] {'wide'}, dimensions={0}, use_global_device_ids=true | all-gather | bytes 104448 | tf_op jit(solution)/shard_map/all_gather | solution.py:109
  55.5 30.7 %all-to-all-done = f32[32,1,6144]{2,1,0:T(1,128)S(1)} async-done(((f32[32,1,6144]{2,1,0:T(1,128)}), f32[32,1,6144]{2,1,0:T(1,128)S(1)}, u32[]{:S(2)}, u32[]{:S(2)}) %all-to-all-start) | async-done | bytes 786464 | tf_op jit(solution)/shard_map/all_to_all | solution.py:195
  87.3 56.7 %all-gather.8.cloned.1.call-done = bf16[1024,8192]{1,0:T(8,128)(2,1)} async-done(((bf16[32,8192]{1,0:T(8,128)(2,1)}), bf16[1024,8192]{1,0:T(8,128)(2,1)}) %all-gather.8.cloned.1.call-update) | async-done | bytes 16777232 | tf_op jit(solution)/shard_map/all_gather | solution.py:181
  144.0 7.6 %fusion.21 = f32[1,680,3072]{2,1,0:T(8,128)S(1)} fusion(bf16[1024,8192]{1,0:T(8,128)(2,1)} %all-gather.8.cloned.1.call-done, bf16[1,680,1024]{2,1,0:T(8,128)(2,1)S(1)} %copy-done.5, f32[1024]{0:T(1024)S(1)} %bitcast.222, f32[1024]{0:T(1024)S(1)} %bitcast.205, f32[680]{0:T(1024)S(1)} %fusion.78, f32[680]{0:T(1024)S(1)} %broadcast_multiply_fusion.3), kind=kOutput, calls=%fused_computation.35 | convolution fusion | flops 4282368000 | bytes 16053568 | tf_op jit(solution)/shard_map/fyg,gq->fyq/dot_general | solution.py:45
  166.0 14.0 %fusion.94 = (f32[16,680]{1,0:T(8,128)S(1)}, f32[16,680,680]{1,2,0:T(8,128)}) fusion(f32[680,16,64]{0,2,1:T(8,128)S(1)} %bitcast.191, f32[16,64]{1,0:T(8,128)S(1)} %reshape.836, f32[680,16]{0,1:T(8,128)S(1)} %get-tuple-element.76, f32[680,16,64]{0,2,1:T(8,128)S(1)} %bitcast.185, f32[16,64]{1,0:T(8,128)S(1)} %reshape.835, ...), kind=kOutput, calls=%fused_computation.190 | convolution fusion | flops 973357440 | bytes 35765312 | tf_op jit(solution)/shard_map/vmap(nkz,vkz->knv)/dot_general | solution.py:63
  180.1 13.4 %fusion = f32[16,680]{1,0:T(8,128)S(1)} fusion(f32[16,680,680]{1,2,0:T(8,128)} %get-tuple-element.61, f32[16,680]{1,0:T(8,128)S(1)} %get-tuple-element.60), kind=kLoop, calls=%fused_computation.6 | loop fusion | flops 14785920 | bytes 29680640 | tf_op jit(solution)/shard_map/vmap()/reduce_sum | solution.py:73
  193.5 15.8 %fusion.51 = bf16[16,64,680]{2,1,0:T(8,128)(2,1)} fusion(bf16[680,16,64]{0,2,1:T(8,128)(2,1)S(1)} %bitcast.195, f32[16,680,680]{1,2,0:T(8,128)} %get-tuple-element.61, f32[16,680]{1,0:T(8,128)S(1)} %fusion, f32[16,680]{1,0:T(8,128)S(1)} %get-tuple-element.60), kind=kOutput, calls=%fused_computation.104 | convolution fusion | flops 969886720 | bytes 32465920 | tf_op jit(solution)/shard_map/vmap(wcv,vwn->cwn)/dot_general | solution.py:75
  209.4 5.6 fusion.91
  216.4 12.6 %fusion.15 = f32[680,4096]{1,0:T(8,128)} fusion(bf16[1024,8192]{1,0:T(8,128)(2,1)} %all-gather.8.cloned.1.call-done, f32[1,680,1024]{2,1,0:T(8,128)S(1)} %get-tuple-element.32, f32[1024]{0:T(1024)S(1)} %bitcast.217, f32[1024]{0:T(1024)S(1)} %bitcast.212, f32[680]{0:T(1024)S(1)} %fusion.79, f32[680]{0:T(1024)S(1)} %broadcast_multiply_fusion.2), kind=kOutput, calls=%fused_computation.27 | convolution fusion | flops 5707735040 | bytes 22328640 | tf_op jit(solution)/shard_map/fyg,gq->fyq/dot_general | solution.py:45
  229.0 19.0 %convert_reduce_fusion = (f32[4096]{0:T(1024)}, bf16[680,4096]{1,0:T(8,128)(2,1)}) fusion(f32[680,4096]{1,0:T(8,128)} %fusion.15, f32[4096]{0:T(1024)S(1)} %copy-done.59, bf16[4096,1024]{1,0:T(8,128)(2,1)} %all-gather.10.cloned.1.call-done, f32[1024]{0:T(1024)S(1)} %bitcast.219, bf16[1,680,1024]{2,1,0:T(8,128)(2,1)} %param.33), kind=kOutput, calls=%fused_computation.20 | convolution fusion | flops 5770399744 | bytes 26529792 | tf_op jit(solution)/shard_map/rfw,uw->rfu/dot_general | solution.py:51
  248.0 11.4 %fusion.43 = (bf16[1024]{0:T(1024)(128)(2,1)}, f32[680]{0:T(1024)S(1)}, f32[680,1024]{1,0:T(8,128)S(1)}) fusion(f32[1,680,1024]{2,1,0:T(8,128)S(1)} %get-tuple-element.32, f32[680]{0:T(1024)S(1)} %fusion.79, f32[680]{0:T(1024)S(1)} %broadcast_multiply_fusion.2, f32[1024]{0:T(1024)S(1)} %bitcast.213, bf16[680,4096]{1,0:T(8,128)(2,1)} %get-tuple-element.74, ...), kind=kOutput, calls=%fused_computation.85 | convolution fusion | flops 5709126144 | bytes 19544032 | tf_op jit(solution)/shard_map/rfw,uw->rfu/dot_general | solution.py:51
  261.8 13.8 %convert_reduce_fusion.2 = (f32[1024]{0:T(1024)}, bf16[1024]{0:T(1024)(128)(2,1)}, bf16[1024]{0:T(1024)(128)(2,1)}, f32[1024]{0:T(1024)}, bf16[1,680,1024]{2,1,0:T(8,128)(2,1)S(1)}, /*index=5*/bf16[1,680,1024]{2,1,0:T(8,128)(2,1)}) fusion(f32[1024]{0:T(1024)S(1)} %bitcast.220, bf16[1,680,1024]{2,1,0:T(8,128)(2,1)S(1)} %copy-done.25, ...), kind=kOutput, calls=%fused_computation.92 | convolution fusion | flops 5746028544 | bytes 32111264 | tf_op jit(solution)/shard_map/fyg,gq->fyq/dot_general | solution.py:45
  280.7 16.0 %bitcast_convert_fusion = (bf16[1,680,16,64]{1,3,2,0:T(8,128)(2,1)}, f32[16,64,680]{2,1,0:T(8,128)}) fusion(bf16[680,16,64]{0,2,1:T(8,128)(2,1)S(1)} %bitcast.193, f32[16,680,680]{1,2,0:T(8,128)} %get-tuple-element.61, f32[16,680]{1,0:T(8,128)} %log_add_fusion), kind=kOutput, calls=%fused_computation.59 | convolution fusion | flops 962488320 | bytes 35207680 | tf_op jit(solution)/shard_map/vmap(fgs,gfu->sfu)/dot_general | solution.py:89
  296.7 26.0 %multiply_reduce_fusion = (f32[16,680]{1,0:T(8,128)}, f32[16,680,680]{1,2,0:T(8,128)}) fusion(f32[16,680,680]{1,2,0:T(8,128)} %get-tuple-element.61, f32[16,680]{1,0:T(8,128)} %log_add_fusion, bf16[680,16,64]{0,2,1:T(8,128)(2,1)S(1)} %bitcast.194, bf16[680,16,64]{0,2,1:T(8,128)(2,1)S(1)} %bitcast.196), kind=kOutput, calls=%fused_computation.1 | convolution fusion | flops 969179520 | bytes 62059520 | tf_op jit(solution)/shard_map/vmap(nkz,vkz->knv)/dot_general | solution.py:86
  322.7 28.8 %multiply_convert_fusion = bf16[16,680,680]{1,2,0:T(8,128)(2,1)} fusion(f32[16,680,680]{1,2,0:T(8,128)} %get-tuple-element.67, f32[16,680,680]{1,2,0:T(8,128)} %get-tuple-element.61, f32[16,680]{1,0:T(8,128)} %get-tuple-element.66, f32[16,680]{1,0:T(8,128)} %log_add_fusion), kind=kLoop, calls=%fused_computation | loop fusion | flops 29593600 | bytes 74071040 | tf_op jit(solution)/shard_map/vmap()/convert_element_type | solution.py:98
  351.6 11.7 %fusion.34 = (f32[680,16]{0,1:T(8,128)S(1)}, f32[16,64,680]{2,1,0:T(8,128)}) fusion(f32[1,680,16,64]{1,3,2,0:T(8,128)S(1)} %bitcast.186, f32[16,64]{1,0:T(8,128)S(1)} %copy-done.35, bf16[16,680,680]{1,2,0:T(8,128)(2,1)} %multiply_convert_fusion, f32[680,16,64]{0,2,1:T(8,128)} %bitcast.190, f32[16,64]{1,0:T(8,128)S(1)} %copy-done.34, f32[680,16]{0,1:T(8,128)} %copy-done.17), kind=kOutput, calls=%fused_computation.67 | convolution fusion | flops 951162240 | bytes 23247872 | tf_op jit(solution)/shard_map/vmap(wcv,vwn->cwn)/dot_general | solution.py:99
  363.4 9.4 %fusion.31 = (f32[16,64]{1,0:T(8,128)}, f32[680,16]{0,1:T(8,128)S(1)}, f32[16,64,680]{2,1,0:T(8,128)S(1)}) fusion(f32[1,680,16,64]{1,3,2,0:T(8,128)S(1)} %bitcast.192, f32[680,16]{0,1:T(8,128)S(1)} %copy-done.18, f32[16,64]{1,0:T(8,128)S(1)} %copy-done.36, bf16[16,680,680]{1,2,0:T(8,128)(2,1)} %multiply_convert_fusion, f32[680,16,64]{0,2,1:T(8,128)S(1)} %bitcast.187, ...), kind=kOutput, calls=%fused_computation.55 | convolution fusion | flops 953946496 | bytes 23295488 | tf_op jit(solution)/shard_map/vmap(fgs,gfu->sfu)/dot_general | solution.py:102
  379.1 11.1 %convolution_convert_fusion.2 = bf16[1024,3072]{1,0:T(8,128)(2,1)} fusion(bf16[680,1024]{0,1:T(8,128)(2,1)S(1)} %bitcast.202, bf16[680,1024]{0,1:T(8,128)(2,1)S(1)} %bitcast.200, bf16[680,1024]{0,1:T(8,128)(2,1)S(1)} %bitcast.197, bf16[1,680,1024]{2,1,0:T(8,128)(2,1)S(1)} %copy-done.7, f32[1024]{0:T(1024)S(1)} %bitcast.223, f32[1024]{0:T(1024)S(1)} %bitcast.206, ...), kind=kOutput, calls=%fused_computation.30 | convolution fusion | flops 4298047488 | bytes 11875648 | tf_op jit(solution)/shard_map/crk,cre->ke/dot_general | solution.py:57
  391.6 13.7 %convolution_convert_fusion = bf16[4096,1024]{1,0:T(8,128)(2,1)} fusion(bf16[1,680,1024]{2,1,0:T(8,128)(2,1)S(1)} %copy-done.26, f32[1024]{0:T(1024)S(1)} %bitcast.221, f32[680,4096]{1,0:T(8,128)} %fusion.15, f32[4096]{0:T(1024)S(1)} %copy-done.60), kind=kOutput, calls=%fused_computation.23 | convolution fusion | flops 5738389504 | bytes 20942848 | tf_op jit(solution)/shard_map/crk,cre->ke/dot_general | solution.py:57
  409.4 10.3 %convolution_convert_fusion.1 = bf16[1024,4096]{1,0:T(8,128)(2,1)S(1)} fusion(bf16[680,4096]{1,0:T(8,128)(2,1)} %get-tuple-element.74, f32[1,680,1024]{2,1,0:T(8,128)S(1)} %copy-done.14, f32[1024]{0:T(1024)S(1)} %bitcast.218, f32[1024]{0:T(1024)S(1)} %bitcast.215, f32[680]{0:T(1024)S(1)} %copy-done.57, f32[680]{0:T(1024)S(1)} %copy-done.43), kind=kOutput, calls=%fused_computation.24 | convolution fusion | flops 5711929344 | bytes 16758080 | tf_op jit(solution)/shard_map/crk,cre->ke/dot_general | solution.py:57
  419.8 7.9 %pad_maximum_fusion = bf16[1024,5120]{1,0:T(8,128)(2,1)} fusion(bf16[1024,1024]{1,0:T(8,128)(2,1)S(1)} %convolution_convert_fusion.3, bf16[1024,4096]{1,0:T(8,128)(2,1)S(1)} %convolution_convert_fusion.1), kind=kLoop, calls=%fused_computation.22 | loop fusion | flops 20971520 | bytes 20971520 | tf_op jit(solution)/shard_map/concatenate | solution.py:257
  429.8 9.9 %fusion.39 = (f32[680]{0:T(1024)S(1)}, f32[680,1024]{1,0:T(8,128)S(1)}) fusion(bf16[1,680,1024]{2,1,0:T(8,128)(2,1)} %param.17, f32[1024]{0:T(1024)S(1)} %bitcast.207, f32[680]{0:T(1024)S(1)} %copy-done.41, bf16[1024,8192]{1,0:T(8,128)(2,1)} %all-gather.8.cloned.1.call-done, bf16[680,1024]{0,1:T(8,128)(2,1)} %bitcast.201, bf16[680,1024]{0,1:T(8,128)(2,1)} %bitcast.199, ...), kind=kOutput, calls=%fused_computation.78 | convolution fusion | flops 4294204672 | bytes 15197504 | tf_op jit(solution)/shard_map/rfw,uw->rfu/dot_general | solution.py:51
  442.6 4.5 all-gather.3
  447.1 24.8 %all-gather.4 = bf16[16,2,6144]{2,1,0:T(2,128)(2,1)} all-gather(bf16[1,2,6144]{2,1,0:T(2,128)(2,1)S(1)} %bitcast.204), channel_id=1, replica_groups=mesh['wide'=16,'narrow'=2] {'wide'}, dimensions={0}, use_global_device_ids=true | all-gather | bytes 417792 | tf_op jit(solution)/shard_map/all_gather | solution.py:109
  480.5 4.4 add_add_fusion.4
  488.2 5.8 all-to-all-start.2
  496.0 5.6 all-to-all-done.2
  504.3 78.2 %reduce-scatter.8.cloned.1.call-done = bf16[256,1024]{1,0:T(8,128)(2,1)} async-done(((bf16[4096,1024]{1,0:T(8,128)(2,1)}), bf16[256,1024]{1,0:T(8,128)(2,1)}) %reduce-scatter.8.cloned.1.call-update) | async-done | bytes 524304 | tf_op jit(solution)/shard_map/reduce_scatter | solution.py:127
  585.1 120.6 %reduce-scatter.6.cloned.1.call-done = bf16[64,5120]{1,0:T(8,128)(2,1)} async-done(((bf16[1024,5120]{1,0:T(8,128)(2,1)}), bf16[64,5120]{1,0:T(8,128)(2,1)}) %reduce-scatter.6.cloned.1.call-update) | async-done | bytes 655376 | tf_op jit(solution)/shard_map/reduce_scatter | solution.py:127
  711.7 4.1 collective-permute-done.1
  (272 shorter events, 83.0 us)
Async XLA Ops:
  7.2 37.7 %copy-start = (bf16[32,6144]{1,0:T(8,128)(2,1)S(1)}, bf16[32,6144]{1,0:T(8,128)(2,1)}, u32[]{:S(2)}) copy-start(bf16[32,6144]{1,0:T(8,128)(2,1)} %param.20) | copy-start | bytes 1179652
  7.2 42.4 %copy-start.78 = (s32[10]{0:T(128)S(1)}, s32[10]{0:T(128)}, u32[]{:S(2)}) copy-start(s32[10]{0:T(128)} %param.19) | copy-start | bytes 124
  7.2 136.8 %all-gather.8.cloned.1.call-start = ((), (), s32[]{:S(2)}) async-start(), calls=%async_computation.6 | async-start | bytes 17301504 | tf_op jit(solution)/shard_map/all_gather | solution.py:181
  9.2 42.5 %copy-start.5 = (bf16[1,680,1024]{2,1,0:T(8,128)(2,1)S(1)}, bf16[1,680,1024]{2,1,0:T(8,128)(2,1)}, u32[]{:S(2)}) copy-start(bf16[1,680,1024]{2,1,0:T(8,128)(2,1)} %param.17) | copy-start | bytes 4177924
  9.2 219.8 %all-gather.10.cloned.1.call-start = ((), (), s32[]{:S(2)}) async-start(), calls=%async_computation.7 | async-start | bytes 8650752 | tf_op jit(solution)/shard_map/all_gather | solution.py:188
  46.9 39.3 %all-to-all-start = ((f32[32,1,6144]{2,1,0:T(1,128)}), f32[32,1,6144]{2,1,0:T(1,128)S(1)}, u32[]{:S(2)}, u32[]{:S(2)}) async-start(f32[32,1,6144]{2,1,0:T(1,128)} %copy.87), calls=%async_computation | async-start | bytes 1572864 | tf_op jit(solution)/shard_map/all_to_all | solution.py:195
  49.5 453.3 %reduce-scatter.4.cloned.1.call-start = ((), (), s32[]{:S(2)}) async-start(), calls=%async_computation.8 | async-start | bytes 6684672 | tf_op jit(solution)/shard_map/reduce_scatter | solution.py:127
  51.5 114.3 %copy-start.33 = (f32[16,64]{1,0:T(8,128)}, f32[16,64]{1,0:T(8,128)S(1)}, u32[]{:S(2)}) copy-start(f32[16,64]{1,0:T(8,128)S(1)} %reshape.836) | copy-start | bytes 12292
  51.6 114.2 %copy-start.31 = (f32[16,64]{1,0:T(8,128)}, f32[16,64]{1,0:T(8,128)S(1)}, u32[]{:S(2)}) copy-start(f32[16,64]{1,0:T(8,128)S(1)} %reshape.835) | copy-start | bytes 12292
  51.9 92.0 %copy-start.40 = (f32[680]{0:T(1024)}, f32[680]{0:T(1024)S(1)}, u32[]{:S(2)}) copy-start(f32[680]{0:T(1024)S(1)} %broadcast_multiply_fusion.3) | copy-start | bytes 8164
  52.5 91.5 %copy-start.44 = (f32[680]{0:T(1024)}, f32[680]{0:T(1024)S(1)}, u32[]{:S(2)}) copy-start(f32[680]{0:T(1024)S(1)} %fusion.38) | copy-start | bytes 8164
  52.5 91.5 %copy-start.38 = (f32[680]{0:T(1024)}, f32[680]{0:T(1024)S(1)}, u32[]{:S(2)}) copy-start(f32[680]{0:T(1024)S(1)} %fusion.78) | copy-start | bytes 8164
  87.3 56.7 %copy-start.46 = (f32[1,1024]{1,0:T(1,128)}, f32[1,1024]{1,0:T(1,128)S(1)}, u32[]{:S(2)}) copy-start(f32[1,1024]{1,0:T(1,128)S(1)} %get-tuple-element.52) | copy-start | bytes 12292
  87.3 56.7 %copy-start.69 = (f32[1,1024]{1,0:T(1,128)}, f32[1,1024]{1,0:T(1,128)S(1)}, u32[]{:S(2)}) copy-start(f32[1,1024]{1,0:T(1,128)S(1)} %get-tuple-element.51) | copy-start | bytes 12292
  193.5 15.8 %copy-start.6 = (bf16[1,680,1024]{2,1,0:T(8,128)(2,1)S(1)}, bf16[1,680,1024]{2,1,0:T(8,128)(2,1)}, u32[]{:S(2)}) copy-start(bf16[1,680,1024]{2,1,0:T(8,128)(2,1)} %param.17) | copy-start | bytes 4177924
  193.5 15.8 %copy-start.72 = (f32[1024]{0:T(1024)S(1)}, f32[1024]{0:T(1024)}, u32[]{:S(2)}) copy-start(f32[1024]{0:T(1024)} %reshape.837) | copy-start | bytes 12292
  193.5 15.8 %copy-start.73 = (f32[1,1024]{1,0:T(1,128)S(1)}, f32[1,1024]{1,0:T(1,128)}, u32[]{:S(2)}) copy-start(f32[1,1024]{1,0:T(1,128)} %get-tuple-element.53) | copy-start | bytes 12292
  214.9 46.1 %copy-start.13 = (f32[1,680,1024]{2,1,0:T(8,128)}, f32[1,680,1024]{2,1,0:T(8,128)S(1)}, u32[]{:S(2)}) copy-start(f32[1,680,1024]{2,1,0:T(8,128)S(1)} %get-tuple-element.32) | copy-start | bytes 8355844
  214.9 44.5 %copy-start.42 = (f32[680]{0:T(1024)}, f32[680]{0:T(1024)S(1)}, u32[]{:S(2)}) copy-start(f32[680]{0:T(1024)S(1)} %broadcast_multiply_fusion.2) | copy-start | bytes 8164
  215.4 44.1 %copy-start.56 = (f32[680]{0:T(1024)}, f32[680]{0:T(1024)S(1)}, u32[]{:S(2)}) copy-start(f32[680]{0:T(1024)S(1)} %fusion.79) | copy-start | bytes 8164
  280.7 16.0 %copy-start.16 = (bf16[1,680,1024]{1,2,0:T(8,128)(2,1)S(1)}, bf16[1,680,1024]{1,2,0:T(8,128)(2,1)}, u32[]{:S(2)}) copy-start(bf16[1,680,1024]{1,2,0:T(8,128)(2,1)} %copy.88) | copy-start | bytes 4177924
  322.7 28.8 %copy-start.2 = (f32[1,680,1024]{1,2,0:T(8,128)S(1)}, f32[1,680,1024]{1,2,0:T(8,128)}, u32[]{:S(2)}) copy-start(f32[1,680,1024]{1,2,0:T(8,128)} %copy-done.1) | copy-start | bytes 8355844
  322.7 28.8 %copy-start.34 = (f32[16,64]{1,0:T(8,128)S(1)}, f32[16,64]{1,0:T(8,128)}, u32[]{:S(2)}) copy-start(f32[16,64]{1,0:T(8,128)} %copy-done.33) | copy-start | bytes 12292
  322.7 28.8 %copy-start.35 = (f32[16,64]{1,0:T(8,128)S(1)}, f32[16,64]{1,0:T(8,128)}, u32[]{:S(2)}) copy-start(f32[16,64]{1,0:T(8,128)} %broadcast_multiply_fusion.1) | copy-start | bytes 12292
  390.2 192.3 %reduce-scatter.8.cloned.1.call-start = ((), (), s32[]{:S(2)}) async-start(), calls=%async_computation.10 | async-start | bytes 8912896 | tf_op jit(solution)/shard_map/reduce_scatter | solution.py:127
  405.3 300.3 %reduce-scatter.6.cloned.1.call-start = ((), (), s32[]{:S(2)}) async-start(), calls=%async_computation.9 | async-start | bytes 11141120 | tf_op jit(solution)/shard_map/reduce_scatter | solution.py:127
  439.9 40.6 %copy-start.55 = (f32[680]{0:T(1024)S(1)}, f32[680]{0:T(1024)}, u32[]{:S(2)}) copy-start(f32[680]{0:T(1024)} %copy-done.54) | copy-start | bytes 8164
  475.7 12.6 %all-to-all-start.1 = ((f32[32,1,32]{2,1,0:T(1,128)}), f32[32,1,32]{2,1,0:T(1,128)S(1)}, u32[]{:S(2)}, u32[]{:S(2)}) async-start(f32[32,1,32]{2,1,0:T(1,128)} %bitcast.46), calls=%async_computation.1 | async-start | bytes 32768 | tf_op jit(solution)/shard_map/all_to_all | solution.py:344
  488.2 13.3 %all-to-all-start.2 = ((f32[32,1,320]{2,1,0:T(1,128)}), f32[32,1,320]{2,1,0:T(1,128)S(1)}, u32[]{:S(2)}, u32[]{:S(2)}) async-start(f32[32,1,320]{2,1,0:T(1,128)} %reshape.831), calls=%async_computation.3 | async-start | bytes 98304 | tf_op jit(solution)/shard_map/all_to_all | solution.py:133
  503.8 204.4 %collective-permute-start = (bf16[32,3072]{1,0:T(8,128)(2,1)S(1)}, bf16[32,3072]{1,0:T(8,128)(2,1)S(1)}, u32[]{:S(2)}, u32[]{:S(2)}) collective-permute-start(bf16[32,3072]{1,0:T(8,128)(2,1)S(1)} %constant_dynamic-slice_fusion.2), channel_id=1, source_target_pairs={{0,1},{1,0},{2,3},{3,2},{4,5},{5,4},{6,7},{7,6},{8,9},{9,8},{10,11... | collective-permute-start | bytes 589832 | tf_op jit(solution)/shard_map/ppermute | solution.py:122
  583.5 126.4 %collective-permute-start.2 = (bf16[128,1024]{1,0:T(8,128)(2,1)S(1)}, bf16[128,1024]{1,0:T(8,128)(2,1)S(1)}, u32[]{:S(2)}, u32[]{:S(2)}) collective-permute-start(bf16[128,1024]{1,0:T(8,128)(2,1)S(1)} %constant_dynamic-slice_fusion), channel_id=1, source_target_pairs={{0,1},{1,0},{2,3},{3,2},{4,5},{5,4},{6,7},{7,6},{8,9},{9,8},{10,11... | collective-permute-start | bytes 786440 | tf_op jit(solution)/shard_map/ppermute | solution.py:122
  706.6 9.2 %collective-permute-start.1 = (bf16[32,5120]{1,0:T(8,128)(2,1)S(1)}, bf16[32,5120]{1,0:T(8,128)(2,1)S(1)}, u32[]{:S(2)}, u32[]{:S(2)}) collective-permute-start(bf16[32,5120]{1,0:T(8,128)(2,1)S(1)} %constant_dynamic-slice_fusion.1), channel_id=1, source_target_pairs={{0,1},{1,0},{2,3},{3,2},{4,5},{5,4},{6,7},{7,6},{8,9},{9,8},{10,11... | collective-permute-start | bytes 983048 | tf_op jit(solution)/shard_map/ppermute | solution.py:122
  (59 other events, 373.7 us)
Sparse Core Ops, SparseCore 0:
  11.6 132.3 all-gather.7
  147.0 75.2 all-gather.9
  390.4 85.4 reduce-scatter.3
  479.8 102.7 reduce-scatter.7
  586.4 119.1 reduce-scatter.5

commit v8 on v7

--- a/solution.py
+++ b/solution.py
@@ -121,6 +121,30 @@
     send = lax.dynamic_slice_in_dim(half, (1 - here) * rows, rows, axis=0)
     got = lax.ppermute(send, "narrow", [(0, 1), (1, 0)])
     return keep.astype(jnp.float32) + got.astype(jnp.float32)
+
+
+def tree_sum(member):
+    wide, narrow = lax.axis_size("wide"), lax.axis_size("narrow")
+    if (wide, narrow) != (16, 2):
+        return scatter_natural(member)
+    w = lax.axis_index("wide")
+    x = lax.axis_index("narrow")
+    rows = member.shape[0] // 32
+    part = member.astype(jnp.bfloat16).reshape((4, 2, 2, 2, rows) + member.shape[1:])
+
+    def swap(total, axis, mine, axis_name, flip):
+        keep = lax.dynamic_index_in_dim(total, mine, axis, keepdims=False)
+        send = lax.dynamic_index_in_dim(total, 1 - mine, axis, keepdims=False)
+        size = lax.axis_size(axis_name)
+        pairs = [(i, i ^ flip) for i in range(size)]
+        got = lax.ppermute(send.astype(jnp.bfloat16), axis_name, pairs)
+        return keep.astype(jnp.float32) + got.astype(jnp.float32)
+
+    total = swap(part, 2, w % 2, "wide", 1)
+    total = swap(total, 2, x, "narrow", 1)
+    total = swap(total, 1, (w // 2) % 2, "wide", 2)
+    total = swap(total.reshape((2, 2, rows) + member.shape[1:]), 0, w // 8, "wide", 8)
+    return swap(total, 0, (w // 4) % 2, "wide", 4)
 
 
 def scatter_natural(member):
@@ -221,7 +245,7 @@
     gamma_mlp_grad = jnp.sum(upstream * branch, axis=1)
     branch_grad = (upstream * gamma_mlp[:, None, :]).astype(jnp.bfloat16)
     down_grad = weight_grad(hidden, branch_grad)
-    down_sum = scatter_natural(down_grad)
+    down_sum = tree_sum(down_grad)
     down_bias_grad = jnp.sum(branch_grad.astype(jnp.float32), axis=(0, 1))
     return mlp_back(
         branch_grad, down_full, hidden_pre, normed_mlp, up_full, middle, scale_mlp, shift_mlp,

time: 730 us -> 673 us (0.922)
  waiting for transfers between devices: 297 us -> 149 us
  blocking collectives: 57.4 us -> 121 us
  local copies, waits for them, and re-layouts: 34.5 us -> 51.5 us
  other arithmetic: 87 us -> 101 us
    reduce_scatter x3 -> x2, waiting for transfers between devices: 199 us -> 0.01 us  [scatter_natural(): lax.psum_scatter(member.astype(jnp.bfloat16), 'wide', scatter_dimension=0...]
    all_to_all x1, waiting for transfers between devices: 0.01 us -> 34.6 us  [tail(): lax.all_to_all(activated_grad_cols, AXES, split_axis=0, concat_axis=1, ti...]
    all_gather x2, blocking collectives: 9.79 us -> 41.9 us  [nested_gather(): lax.all_gather(member, 'narrow', axis=0, tiled=True)]
    all_gather x2, blocking collectives: 47.6 us -> 79.3 us  [nested_gather(): lax.all_gather(lax.all_gather(member, 'narrow', axis=0, tiled=True), 'wid...]
    add x0 -> x5, other arithmetic: none -> 14.3 us  [swap(): return keep.astype(jnp.float32) + got.astype(jnp.float32)]
    ppermute x0 -> x5, waiting for transfers between devices: none -> 13.5 us  [swap(): got = lax.ppermute(send.astype(jnp.bfloat16), axis_name, pairs)]
    unnamed x170 -> x174, local copies, waits for them, and re-layouts: 10.4 us -> 17.3 us
  transfers between devices with their start and end apart: 11 -> 14, of which waited for: 6 -> 8; matrix products, arithmetic and copies ran while one was open for 24% -> 29% of each run, Pallas kernels for 0% -> 0%
where the time goes in v8:
time: 673 us; the launch traced here: 668 us
  matrix products  215 us (32%)
  waiting for transfers between devices  149 us (22%)
  blocking collectives  121 us (18%)
  other arithmetic  101 us (15%)
  local copies, waits for them, and re-layouts  51.5 us (8%)
  starting transfers between devices  15.5 us (2%)
  between operations  15.1 us (2%)
    all_gather x2, blocking collectives, nested_gather(): lax.all_gather(lax.all_gather(member, 'narrow', axis=0, tiled=True), 'wid...  79.3 us
    all_gather x1, waiting for transfers between devices, layer(): lax.all_gather(jnp.concatenate([w_qkv, w_proj, w_up], axis=1), AXES, axis...  56.7 us
    dot_general x4, matrix products, matmul_back(): jnp.einsum('rfw,uw->rfu', first_operand, second_operand, preferred_elemen...  42 us
    all_gather x2, blocking collectives, nested_gather(): lax.all_gather(member, 'narrow', axis=0, tiled=True)  41.9 us
    dot_general x4, matrix products, matmul_rows(): jnp.einsum('fyg,gq->fyq', first_operand, second_operand, preferred_elemen...  39.7 us
    dot_general x4, matrix products, weight_grad(): jnp.einsum('crk,cre->ke', first_operand, second_operand, preferred_elemen...  37 us
    all_to_all x1, waiting for transfers between devices, tail(): lax.all_to_all(activated_grad_cols, AXES, split_axis=0, concat_axis=1, ti...  34.6 us
    all_to_all x1, waiting for transfers between devices, layer(): lax.all_to_all(ada_partial.reshape(count, sequences, ada_cols), AXES, spl...  30.7 us
  transfers between devices with their start and end apart: 14, of which 8 were waited for; matrix products, arithmetic and copies ran while one was open for 29% of the time, Pallas kernels for 0%

profile of v8, /device:TPU:0, one launch (start us, length us, event | category | flops | bytes accessed | tf_op | source)
XLA Modules:
  0.0 668.2 jit_solution(3196330681017919160)
XLA Ops:
  11.2 5.4 concatenate.51
  16.7 5.3 all-gather.1
  22.0 22.8 %all-gather.2 = bf16[16,2,1536]{2,1,0:T(2,128)(2,1)S(1)} all-gather(bf16[1,2,1536]{2,1,0:T(2,128)(2,1)S(1)} %bitcast.238), channel_id=1, replica_groups=mesh['wide'=16,'narrow'=2] {'wide'}, dimensions={0}, use_global_device_ids=true | all-gather | bytes 104448 | tf_op jit(solution)/shard_map/all_gather | solution.py:109
  55.5 30.7 %all-to-all-done = f32[32,1,6144]{2,1,0:T(1,128)S(1)} async-done(((f32[32,1,6144]{2,1,0:T(1,128)}), f32[32,1,6144]{2,1,0:T(1,128)S(1)}, u32[]{:S(2)}, u32[]{:S(2)}) %all-to-all-start) | async-done | bytes 786464 | tf_op jit(solution)/shard_map/all_to_all | solution.py:219
  87.3 56.7 %all-gather.8.cloned.1.call-done = bf16[1024,8192]{1,0:T(8,128)(2,1)} async-done(((bf16[32,8192]{1,0:T(8,128)(2,1)}), bf16[1024,8192]{1,0:T(8,128)(2,1)}) %all-gather.8.cloned.1.call-update) | async-done | bytes 16777232 | tf_op jit(solution)/shard_map/all_gather | solution.py:205
  144.0 7.8 %fusion.21 = f32[1,680,3072]{2,1,0:T(8,128)S(1)} fusion(bf16[1024,8192]{1,0:T(8,128)(2,1)} %all-gather.8.cloned.1.call-done, bf16[1,680,1024]{2,1,0:T(8,128)(2,1)S(1)} %copy-done.6, f32[1024]{0:T(1024)S(1)} %bitcast.249, f32[1024]{0:T(1024)S(1)} %bitcast.232, f32[680]{0:T(1024)S(1)} %fusion.84, f32[680]{0:T(1024)S(1)} %broadcast_multiply_fusion.3), kind=kOutput, calls=%fused_computation.36 | convolution fusion | flops 4282368000 | bytes 16053568 | tf_op jit(solution)/shard_map/fyg,gq->fyq/dot_general | solution.py:45
  166.2 14.0 %fusion.98 = (f32[16,680]{1,0:T(8,128)S(1)}, f32[16,680,680]{1,2,0:T(8,128)}) fusion(f32[680,16,64]{0,2,1:T(8,128)S(1)} %bitcast.214, f32[16,64]{1,0:T(8,128)S(1)} %reshape.850, f32[680,16]{0,1:T(8,128)S(1)} %get-tuple-element.76, f32[680,16,64]{0,2,1:T(8,128)S(1)} %bitcast.208, f32[16,64]{1,0:T(8,128)S(1)} %reshape.849, ...), kind=kOutput, calls=%fused_computation.202 | convolution fusion | flops 973357440 | bytes 35765312 | tf_op jit(solution)/shard_map/vmap(nkz,vkz->knv)/dot_general | solution.py:63
  180.3 13.4 %fusion = f32[16,680]{1,0:T(8,128)S(1)} fusion(f32[16,680,680]{1,2,0:T(8,128)} %get-tuple-element.61, f32[16,680]{1,0:T(8,128)S(1)} %get-tuple-element.60), kind=kLoop, calls=%fused_computation.6 | loop fusion | flops 14785920 | bytes 29680640 | tf_op jit(solution)/shard_map/vmap()/reduce_sum | solution.py:73
  193.7 15.4 %fusion.52 = bf16[16,64,680]{2,1,0:T(8,128)(2,1)} fusion(bf16[680,16,64]{0,2,1:T(8,128)(2,1)S(1)} %bitcast.222, f32[16,680,680]{1,2,0:T(8,128)} %get-tuple-element.61, f32[16,680]{1,0:T(8,128)S(1)} %fusion, f32[16,680]{1,0:T(8,128)S(1)} %get-tuple-element.60), kind=kOutput, calls=%fused_computation.111 | convolution fusion | flops 969886720 | bytes 32465920 | tf_op jit(solution)/shard_map/vmap(wcv,vwn->cwn)/dot_general | solution.py:75
  209.2 5.5 fusion.95
  216.1 12.6 %fusion.15 = f32[680,4096]{1,0:T(8,128)} fusion(bf16[1024,8192]{1,0:T(8,128)(2,1)} %all-gather.8.cloned.1.call-done, f32[1,680,1024]{2,1,0:T(8,128)S(1)} %get-tuple-element.32, f32[1024]{0:T(1024)S(1)} %bitcast.247, f32[1024]{0:T(1024)S(1)} %bitcast.239, f32[680]{0:T(1024)S(1)} %fusion.85, f32[680]{0:T(1024)S(1)} %broadcast_multiply_fusion.2), kind=kOutput, calls=%fused_computation.28 | convolution fusion | flops 5707735040 | bytes 22328640 | tf_op jit(solution)/shard_map/fyg,gq->fyq/dot_general | solution.py:45
  228.7 19.0 %convert_reduce_fusion = (f32[4096]{0:T(1024)}, bf16[680,4096]{1,0:T(8,128)(2,1)}) fusion(f32[680,4096]{1,0:T(8,128)} %fusion.15, f32[4096]{0:T(1024)S(1)} %copy-done.65, bf16[4096,1024]{1,0:T(8,128)(2,1)} %all-gather.10.cloned.1.call-done, f32[1024]{0:T(1024)S(1)} %bitcast.244, bf16[1,680,1024]{2,1,0:T(8,128)(2,1)} %param.33), kind=kOutput, calls=%fused_computation.20 | convolution fusion | flops 5770399744 | bytes 26529792 | tf_op jit(solution)/shard_map/rfw,uw->rfu/dot_general | solution.py:51
  247.8 11.5 %fusion.43 = (bf16[1024]{0:T(1024)(128)(2,1)}, f32[680]{0:T(1024)S(1)}, f32[680,1024]{1,0:T(8,128)S(1)}) fusion(f32[1,680,1024]{2,1,0:T(8,128)S(1)} %get-tuple-element.32, f32[680]{0:T(1024)S(1)} %fusion.85, f32[680]{0:T(1024)S(1)} %broadcast_multiply_fusion.2, f32[1024]{0:T(1024)S(1)} %bitcast.240, bf16[680,4096]{1,0:T(8,128)(2,1)} %get-tuple-element.74, ...), kind=kOutput, calls=%fused_computation.89 | convolution fusion | flops 5709126144 | bytes 19544032 | tf_op jit(solution)/shard_map/rfw,uw->rfu/dot_general | solution.py:51
  261.6 13.9 %convert_reduce_fusion.2 = (f32[1024]{0:T(1024)}, bf16[1024]{0:T(1024)(128)(2,1)}, bf16[1024]{0:T(1024)(128)(2,1)}, f32[1024]{0:T(1024)}, bf16[1,680,1024]{2,1,0:T(8,128)(2,1)S(1)}, /*index=5*/bf16[1,680,1024]{2,1,0:T(8,128)(2,1)}) fusion(f32[1024]{0:T(1024)S(1)} %bitcast.245, bf16[1,680,1024]{2,1,0:T(8,128)(2,1)S(1)} %copy-done.35, ...), kind=kOutput, calls=%fused_computation.96 | convolution fusion | flops 5746028544 | bytes 32111264 | tf_op jit(solution)/shard_map/fyg,gq->fyq/dot_general | solution.py:45
  280.5 16.1 %bitcast_convert_fusion = (bf16[1,680,16,64]{1,3,2,0:T(8,128)(2,1)}, f32[16,64,680]{2,1,0:T(8,128)}) fusion(bf16[680,16,64]{0,2,1:T(8,128)(2,1)S(1)} %bitcast.216, f32[16,680,680]{1,2,0:T(8,128)} %get-tuple-element.61, f32[16,680]{1,0:T(8,128)} %log_add_fusion), kind=kOutput, calls=%fused_computation.63 | convolution fusion | flops 962488320 | bytes 35207680 | tf_op jit(solution)/shard_map/vmap(fgs,gfu->sfu)/dot_general | solution.py:89
  296.6 26.1 %multiply_reduce_fusion = (f32[16,680]{1,0:T(8,128)}, f32[16,680,680]{1,2,0:T(8,128)}) fusion(f32[16,680,680]{1,2,0:T(8,128)} %get-tuple-element.61, f32[16,680]{1,0:T(8,128)} %log_add_fusion, bf16[680,16,64]{0,2,1:T(8,128)(2,1)S(1)} %bitcast.217, bf16[680,16,64]{0,2,1:T(8,128)(2,1)S(1)} %bitcast.223), kind=kOutput, calls=%fused_computation.1 | convolution fusion | flops 969179520 | bytes 62059520 | tf_op jit(solution)/shard_map/vmap(nkz,vkz->knv)/dot_general | solution.py:86
  322.7 28.8 %multiply_convert_fusion = bf16[16,680,680]{1,2,0:T(8,128)(2,1)} fusion(f32[16,680,680]{1,2,0:T(8,128)} %get-tuple-element.67, f32[16,680,680]{1,2,0:T(8,128)} %get-tuple-element.61, f32[16,680]{1,0:T(8,128)} %get-tuple-element.66, f32[16,680]{1,0:T(8,128)} %log_add_fusion), kind=kLoop, calls=%fused_computation | loop fusion | flops 29593600 | bytes 74071040 | tf_op jit(solution)/shard_map/vmap()/convert_element_type | solution.py:98
  351.5 11.7 %fusion.34 = (f32[680,16]{0,1:T(8,128)S(1)}, f32[16,64,680]{2,1,0:T(8,128)}) fusion(f32[1,680,16,64]{1,3,2,0:T(8,128)S(1)} %bitcast.209, f32[16,64]{1,0:T(8,128)S(1)} %copy-done.45, bf16[16,680,680]{1,2,0:T(8,128)(2,1)} %multiply_convert_fusion, f32[680,16,64]{0,2,1:T(8,128)} %bitcast.213, f32[16,64]{1,0:T(8,128)S(1)} %copy-done.44, f32[680,16]{0,1:T(8,128)} %copy-done.23), kind=kOutput, calls=%fused_computation.71 | convolution fusion | flops 951162240 | bytes 23247872 | tf_op jit(solution)/shard_map/vmap(wcv,vwn->cwn)/dot_general | solution.py:99
  363.3 9.4 %fusion.31 = (f32[16,64]{1,0:T(8,128)}, f32[680,16]{0,1:T(8,128)S(1)}, f32[16,64,680]{2,1,0:T(8,128)S(1)}) fusion(f32[1,680,16,64]{1,3,2,0:T(8,128)S(1)} %bitcast.215, f32[680,16]{0,1:T(8,128)S(1)} %copy-done.24, f32[16,64]{1,0:T(8,128)S(1)} %copy-done.46, bf16[16,680,680]{1,2,0:T(8,128)(2,1)} %multiply_convert_fusion, f32[680,16,64]{0,2,1:T(8,128)S(1)} %bitcast.210, ...), kind=kOutput, calls=%fused_computation.59 | convolution fusion | flops 953946496 | bytes 23295488 | tf_op jit(solution)/shard_map/vmap(fgs,gfu->sfu)/dot_general | solution.py:102
  379.1 11.0 %convolution_convert_fusion.2 = bf16[1024,3072]{1,0:T(8,128)(2,1)} fusion(bf16[680,1024]{0,1:T(8,128)(2,1)S(1)} %bitcast.228, bf16[680,1024]{0,1:T(8,128)(2,1)S(1)} %bitcast.226, bf16[680,1024]{0,1:T(8,128)(2,1)S(1)} %bitcast.224, bf16[1,680,1024]{2,1,0:T(8,128)(2,1)S(1)} %copy-done.8, f32[1024]{0:T(1024)S(1)} %bitcast.250, f32[1024]{0:T(1024)S(1)} %bitcast.233, ...), kind=kOutput, calls=%fused_computation.31 | convolution fusion | flops 4298047488 | bytes 11875648 | tf_op jit(solution)/shard_map/crk,cre->ke/dot_general | solution.py:57
  394.0 10.2 %convolution_convert_fusion.1 = bf16[1024,4096]{1,0:T(8,128)(2,1)S(1)} fusion(bf16[680,4096]{1,0:T(8,128)(2,1)} %get-tuple-element.74, f32[1,680,1024]{2,1,0:T(8,128)S(1)} %copy-done.18, f32[1024]{0:T(1024)S(1)} %bitcast.248, f32[1024]{0:T(1024)S(1)} %bitcast.242, f32[680]{0:T(1024)S(1)} %copy-done.64, f32[680]{0:T(1024)S(1)} %copy-done.53), kind=kOutput, calls=%fused_computation.25 | convolution fusion | flops 5711929344 | bytes 16758080 | tf_op jit(solution)/shard_map/crk,cre->ke/dot_general | solution.py:57
  404.2 7.8 %pad_maximum_fusion = bf16[1024,5120]{1,0:T(8,128)(2,1)} fusion(bf16[1024,1024]{1,0:T(8,128)(2,1)S(1)} %convolution_convert_fusion.3, bf16[1024,4096]{1,0:T(8,128)(2,1)S(1)} %convolution_convert_fusion.1), kind=kLoop, calls=%fused_computation.22 | loop fusion | flops 20971520 | bytes 20971520 | tf_op jit(solution)/shard_map/concatenate | solution.py:281
  413.4 12.0 %convolution_convert_fusion = bf16[4096,1024]{1,0:T(8,128)(2,1)S(1)} fusion(bf16[1,680,1024]{2,1,0:T(8,128)(2,1)S(1)} %copy-done.36, f32[1024]{0:T(1024)S(1)} %bitcast.246, f32[680,4096]{1,0:T(8,128)} %fusion.15, f32[4096]{0:T(1024)S(1)} %copy-done.66), kind=kOutput, calls=%fused_computation.24 | convolution fusion | flops 5738389504 | bytes 20942848 | tf_op jit(solution)/shard_map/crk,cre->ke/dot_general | solution.py:57
  431.4 6.9 %collective-permute-done.2 = bf16[4,2,2,128,1024]{4,3,2,1,0:T(8,128)(2,1)} collective-permute-done((bf16[4,2,2,128,1024]{4,3,2,1,0:T(8,128)(2,1)}, bf16[4,2,2,128,1024]{4,3,2,1,0:T(8,128)(2,1)}, u32[]{:S(2)}, u32[]{:S(2)}) %collective-permute-start.2) | collective-permute-done | bytes 4194336 | tf_op jit(solution)/shard_map/ppermute | solution.py:140
  438.4 5.9 convert_add_fusion
  450.0 8.3 %fusion.39 = (f32[680]{0:T(1024)S(1)}, f32[680,1024]{1,0:T(8,128)S(1)}) fusion(bf16[1,680,1024]{2,1,0:T(8,128)(2,1)S(1)} %copy-done.9, f32[1024]{0:T(1024)S(1)} %bitcast.234, f32[680]{0:T(1024)S(1)} %copy-done.51, bf16[1024,8192]{1,0:T(8,128)(2,1)} %all-gather.8.cloned.1.call-done, bf16[680,1024]{0,1:T(8,128)(2,1)S(1)} %bitcast.229, ...), kind=kOutput, calls=%fused_computation.82 | convolution fusion | flops 4294204672 | bytes 14656832 | tf_op jit(solution)/shard_map/rfw,uw->rfu/dot_general | solution.py:51
  461.3 36.6 %all-gather.3 = bf16[2,1,6144]{2,1,0:T(2,128)(2,1)S(1)} all-gather(bf16[1,1,6144]{2,1,0:T(2,128)(2,1)S(1)} %bitcast.237), channel_id=1, replica_groups=mesh['wide'=16,'narrow'=2] {'narrow'}, dimensions={0}, use_global_device_ids=true | all-gather | bytes 36864 | tf_op jit(solution)/shard_map/all_gather | solution.py:110
  506.8 56.5 %all-gather.4 = bf16[16,2,6144]{2,1,0:T(2,128)(2,1)} all-gather(bf16[1,2,6144]{2,1,0:T(2,128)(2,1)S(1)} %bitcast.231), channel_id=1, replica_groups=mesh['wide'=16,'narrow'=2] {'wide'}, dimensions={0}, use_global_device_ids=true | all-gather | bytes 417792 | tf_op jit(solution)/shard_map/all_gather | solution.py:109
  567.5 4.7 add_add_fusion.4
  588.7 34.6 %all-to-all-done.1 = f32[32,1,32]{2,1,0:T(1,128)S(1)} async-done(((f32[32,1,32]{2,1,0:T(1,128)}), f32[32,1,32]{2,1,0:T(1,128)S(1)}, u32[]{:S(2)}, u32[]{:S(2)}) %all-to-all-start.1) | async-done | bytes 4128 | tf_op jit(solution)/shard_map/all_to_all | solution.py:368
  629.8 4.9 all-to-all-done.2
  637.8 6.6 collective-permute-done.6
  (289 shorter events, 121.1 us)
Async XLA Ops:
  7.2 37.7 %copy-start = (bf16[32,6144]{1,0:T(8,128)(2,1)S(1)}, bf16[32,6144]{1,0:T(8,128)(2,1)}, u32[]{:S(2)}) copy-start(bf16[32,6144]{1,0:T(8,128)(2,1)} %param.20) | copy-start | bytes 1179652
  7.2 42.4 %copy-start.80 = (s32[10]{0:T(128)S(1)}, s32[10]{0:T(128)}, u32[]{:S(2)}) copy-start(s32[10]{0:T(128)} %param.19) | copy-start | bytes 124
  7.2 136.8 %all-gather.8.cloned.1.call-start = ((), (), s32[]{:S(2)}) async-start(), calls=%async_computation.5 | async-start | bytes 17301504 | tf_op jit(solution)/shard_map/all_gather | solution.py:205
  9.2 42.5 %copy-start.6 = (bf16[1,680,1024]{2,1,0:T(8,128)(2,1)S(1)}, bf16[1,680,1024]{2,1,0:T(8,128)(2,1)}, u32[]{:S(2)}) copy-start(bf16[1,680,1024]{2,1,0:T(8,128)(2,1)} %param.17) | copy-start | bytes 4177924
  9.2 219.5 %all-gather.10.cloned.1.call-start = ((), (), s32[]{:S(2)}) async-start(), calls=%async_computation.6 | async-start | bytes 8650752 | tf_op jit(solution)/shard_map/all_gather | solution.py:212
  46.9 39.3 %all-to-all-start = ((f32[32,1,6144]{2,1,0:T(1,128)}), f32[32,1,6144]{2,1,0:T(1,128)S(1)}, u32[]{:S(2)}, u32[]{:S(2)}) async-start(f32[32,1,6144]{2,1,0:T(1,128)} %copy.87), calls=%async_computation | async-start | bytes 1572864 | tf_op jit(solution)/shard_map/all_to_all | solution.py:219
  49.5 595.7 %reduce-scatter.3.cloned.1.call-start = ((), (), s32[]{:S(2)}) async-start(), calls=%async_computation.7 | async-start | bytes 6684672 | tf_op jit(solution)/shard_map/reduce_scatter | solution.py:151
  51.5 114.5 %copy-start.43 = (f32[16,64]{1,0:T(8,128)}, f32[16,64]{1,0:T(8,128)S(1)}, u32[]{:S(2)}) copy-start(f32[16,64]{1,0:T(8,128)S(1)} %reshape.850) | copy-start | bytes 12292
  51.6 114.4 %copy-start.41 = (f32[16,64]{1,0:T(8,128)}, f32[16,64]{1,0:T(8,128)S(1)}, u32[]{:S(2)}) copy-start(f32[16,64]{1,0:T(8,128)S(1)} %reshape.849) | copy-start | bytes 12292
  51.9 92.0 %copy-start.50 = (f32[680]{0:T(1024)}, f32[680]{0:T(1024)S(1)}, u32[]{:S(2)}) copy-start(f32[680]{0:T(1024)S(1)} %broadcast_multiply_fusion.3) | copy-start | bytes 8164
  52.5 91.5 %copy-start.54 = (f32[680]{0:T(1024)}, f32[680]{0:T(1024)S(1)}, u32[]{:S(2)}) copy-start(f32[680]{0:T(1024)S(1)} %fusion.38) | copy-start | bytes 8164
  52.5 91.5 %copy-start.48 = (f32[680]{0:T(1024)}, f32[680]{0:T(1024)S(1)}, u32[]{:S(2)}) copy-start(f32[680]{0:T(1024)S(1)} %fusion.84) | copy-start | bytes 8164
  87.3 56.7 %copy-start.56 = (f32[1,1024]{1,0:T(1,128)}, f32[1,1024]{1,0:T(1,128)S(1)}, u32[]{:S(2)}) copy-start(f32[1,1024]{1,0:T(1,128)S(1)} %get-tuple-element.52) | copy-start | bytes 12292
  87.3 56.7 %copy-start.71 = (f32[1,1024]{1,0:T(1,128)}, f32[1,1024]{1,0:T(1,128)S(1)}, u32[]{:S(2)}) copy-start(f32[1,1024]{1,0:T(1,128)S(1)} %get-tuple-element.51) | copy-start | bytes 12292
  214.7 46.1 %copy-start.17 = (f32[1,680,1024]{2,1,0:T(8,128)}, f32[1,680,1024]{2,1,0:T(8,128)S(1)}, u32[]{:S(2)}) copy-start(f32[1,680,1024]{2,1,0:T(8,128)S(1)} %get-tuple-element.32) | copy-start | bytes 8355844
  214.7 44.5 %copy-start.52 = (f32[680]{0:T(1024)}, f32[680]{0:T(1024)S(1)}, u32[]{:S(2)}) copy-start(f32[680]{0:T(1024)S(1)} %broadcast_multiply_fusion.2) | copy-start | bytes 8164
  215.1 44.1 %copy-start.63 = (f32[680]{0:T(1024)}, f32[680]{0:T(1024)S(1)}, u32[]{:S(2)}) copy-start(f32[680]{0:T(1024)S(1)} %fusion.85) | copy-start | bytes 8164
  280.5 16.1 %copy-start.22 = (bf16[1,680,1024]{1,2,0:T(8,128)(2,1)S(1)}, bf16[1,680,1024]{1,2,0:T(8,128)(2,1)}, u32[]{:S(2)}) copy-start(bf16[1,680,1024]{1,2,0:T(8,128)(2,1)} %copy.88) | copy-start | bytes 4177924
  322.7 28.8 %copy-start.2 = (f32[1,680,1024]{1,2,0:T(8,128)S(1)}, f32[1,680,1024]{1,2,0:T(8,128)}, u32[]{:S(2)}) copy-start(f32[1,680,1024]{1,2,0:T(8,128)} %copy-done.1) | copy-start | bytes 8355844
  322.7 28.8 %copy-start.44 = (f32[16,64]{1,0:T(8,128)S(1)}, f32[16,64]{1,0:T(8,128)}, u32[]{:S(2)}) copy-start(f32[16,64]{1,0:T(8,128)} %copy-done.43) | copy-start | bytes 12292
  322.7 28.8 %copy-start.45 = (f32[16,64]{1,0:T(8,128)S(1)}, f32[16,64]{1,0:T(8,128)}, u32[]{:S(2)}) copy-start(f32[16,64]{1,0:T(8,128)} %broadcast_multiply_fusion.1) | copy-start | bytes 12292
  390.1 256.7 %reduce-scatter.5.cloned.1.call-start = ((), (), s32[]{:S(2)}) async-start(), calls=%async_computation.8 | async-start | bytes 11141120 | tf_op jit(solution)/shard_map/reduce_scatter | solution.py:151
  430.6 7.8 %collective-permute-start.2 = (bf16[4,2,2,128,1024]{4,3,2,1,0:T(8,128)(2,1)}, bf16[4,2,2,128,1024]{4,3,2,1,0:T(8,128)(2,1)}, u32[]{:S(2)}, u32[]{:S(2)}) collective-permute-start(bf16[4,2,2,128,1024]{4,3,2,1,0:T(8,128)(2,1)} %dynamic-slice_bitcast_fusion), channel_id=1, source_target_pairs={{0,2},{2,0},{4,6},{6,4},{8,10},{10,8},{12,14},{14,12},{16,18},{18,... | collective-permute-start | bytes 12582920 | tf_op jit(solution)/shard_map/ppermute | solution.py:140
  449.1 48.8 %collective-permute-start.3 = (bf16[4,2,128,1024]{3,2,1,0:T(8,128)(2,1)}, bf16[4,2,128,1024]{3,2,1,0:T(8,128)(2,1)}, u32[]{:S(2)}, u32[]{:S(2)}) collective-permute-start(bf16[4,2,128,1024]{3,2,1,0:T(8,128)(2,1)} %fusion.47), channel_id=1, source_target_pairs={{0,1},{1,0},{2,3},{3,2},{4,5},{5,4},{6,7},{7,6},{8,9},{9,8},{10,11... | collective-permute-start | bytes 6291464 | tf_op jit(solution)/shard_map/ppermute | solution.py:140
  504.1 63.3 %copy-start.62 = (f32[680]{0:T(1024)S(1)}, f32[680]{0:T(1024)}, u32[]{:S(2)}) copy-start(f32[680]{0:T(1024)} %copy-done.61) | copy-start | bytes 8164
  505.3 66.9 %collective-permute-start.4 = (bf16[4,128,1024]{2,1,0:T(8,128)(2,1)}, bf16[4,128,1024]{2,1,0:T(8,128)(2,1)}, u32[]{:S(2)}, u32[]{:S(2)}) collective-permute-start(bf16[4,128,1024]{2,1,0:T(8,128)(2,1)} %fusion.67), channel_id=1, source_target_pairs={{0,4},{2,6},{4,0},{6,2},{8,12},{10,14},{12,8},{14,10},{16,20},{18,... | collective-permute-start | bytes 3145736 | tf_op jit(solution)/shard_map/ppermute | solution.py:140
  576.3 58.5 %collective-permute-start.5 = (bf16[2,128,1024]{2,1,0:T(8,128)(2,1)}, bf16[2,128,1024]{2,1,0:T(8,128)(2,1)}, u32[]{:S(2)}, u32[]{:S(2)}) collective-permute-start(bf16[2,128,1024]{2,1,0:T(8,128)(2,1)} %fusion.70), channel_id=1, source_target_pairs={{0,16},{2,18},{4,20},{6,22},{8,24},{10,26},{12,28},{14,30},{16,0},... | collective-permute-start | bytes 1572872 | tf_op jit(solution)/shard_map/ppermute | solution.py:140
  577.6 45.7 %all-to-all-start.1 = ((f32[32,1,32]{2,1,0:T(1,128)}), f32[32,1,32]{2,1,0:T(1,128)S(1)}, u32[]{:S(2)}, u32[]{:S(2)}) async-start(f32[32,1,32]{2,1,0:T(1,128)} %bitcast.46), calls=%async_computation.1 | async-start | bytes 32768 | tf_op jit(solution)/shard_map/all_to_all | solution.py:368
  623.2 11.4 %all-to-all-start.2 = ((f32[32,1,320]{2,1,0:T(1,128)}), f32[32,1,320]{2,1,0:T(1,128)S(1)}, u32[]{:S(2)}, u32[]{:S(2)}) async-start(f32[32,1,320]{2,1,0:T(1,128)} %reshape.843), calls=%async_computation.3 | async-start | bytes 98304 | tf_op jit(solution)/shard_map/all_to_all | solution.py:157
  636.3 8.0 %collective-permute-start.6 = (bf16[128,1024]{1,0:T(8,128)(2,1)S(1)}, bf16[128,1024]{1,0:T(8,128)(2,1)S(1)}, u32[]{:S(2)}, u32[]{:S(2)}) collective-permute-start(bf16[128,1024]{1,0:T(8,128)(2,1)S(1)} %fusion.73), channel_id=1, source_target_pairs={{0,8},{2,10},{4,12},{6,14},{8,0},{10,2},{12,4},{14,6},{16,24},{18,... | collective-permute-start | bytes 786440 | tf_op jit(solution)/shard_map/ppermute | solution.py:140
  646.1 7.8 %collective-permute-start = (bf16[32,3072]{1,0:T(8,128)(2,1)S(1)}, bf16[32,3072]{1,0:T(8,128)(2,1)S(1)}, u32[]{:S(2)}, u32[]{:S(2)}) collective-permute-start(bf16[32,3072]{1,0:T(8,128)(2,1)S(1)} %constant_dynamic-slice_fusion.1), channel_id=1, source_target_pairs={{0,1},{1,0},{2,3},{3,2},{4,5},{5,4},{6,7},{7,6},{8,9},{9,8},{10,11... | collective-permute-start | bytes 589832 | tf_op jit(solution)/shard_map/ppermute | solution.py:122
  647.8 11.1 %collective-permute-start.1 = (bf16[32,5120]{1,0:T(8,128)(2,1)S(1)}, bf16[32,5120]{1,0:T(8,128)(2,1)S(1)}, u32[]{:S(2)}, u32[]{:S(2)}) collective-permute-start(bf16[32,5120]{1,0:T(8,128)(2,1)S(1)} %constant_dynamic-slice_fusion), channel_id=1, source_target_pairs={{0,1},{1,0},{2,3},{3,2},{4,5},{5,4},{6,7},{7,6},{8,9},{9,8},{10,11... | collective-permute-start | bytes 983048 | tf_op jit(solution)/shard_map/ppermute | solution.py:122
  (64 other events, 448.3 us)
Sparse Core Ops, SparseCore 0:
  11.6 132.3 all-gather.7
  147.0 75.2 all-gather.9
  390.2 84.7 reduce-scatter.2
  478.9 143.8 reduce-scatter.4

commit v9 on v7

--- a/solution.py
+++ b/solution.py
@@ -1,13 +1,14 @@
 import jax
 import jax.numpy as jnp
 from jax import lax
-from jax.sharding import PartitionSpec as P
+from jax.sharding import Mesh, PartitionSpec as P
 
 
 HEADS = 16
 HEAD_DIM = 64
 SEQ_LEN = 680
-AXES = ("wide", "narrow")
+WIDE = ("outer", "core")
+AXES = ("outer", "core", "narrow")
 
 EPSILON = 1e-06
 MASKED = -1000000000.0
@@ -107,7 +108,7 @@
 
 def nested_gather(member):
     return lax.all_gather(
-        lax.all_gather(member, "narrow", axis=0, tiled=True), "wide", axis=0, tiled=True
+        lax.all_gather(member, "narrow", axis=0, tiled=True), WIDE, axis=0, tiled=True
     )
 
 
@@ -124,7 +125,16 @@
 
 
 def scatter_natural(member):
-    half = lax.psum_scatter(member.astype(jnp.bfloat16), "wide", scatter_dimension=0, tiled=True)
+    outer, narrow = lax.axis_size("outer"), lax.axis_size("narrow")
+    rows = member.shape[0] // (outer * 2 * narrow)
+    blocks = member.reshape((outer, 2, narrow * rows) + member.shape[1:])
+    here = lax.axis_index("core")
+    keep = lax.dynamic_index_in_dim(blocks, here, 1, keepdims=False)
+    send = lax.dynamic_index_in_dim(blocks, 1 - here, 1, keepdims=False)
+    got = lax.ppermute(send.astype(jnp.bfloat16), "core", [(0, 1), (1, 0)])
+    chip = (keep.astype(jnp.float32) + got.astype(jnp.float32)).astype(jnp.bfloat16)
+    chip = chip.reshape((outer * narrow * rows,) + member.shape[1:])
+    half = lax.psum_scatter(chip, "outer", scatter_dimension=0, tiled=True)
     return narrow_sum(half)
 
 
@@ -161,8 +171,10 @@
     bias_down,
     cotangent,
 ):
-    count = lax.axis_size("wide") * lax.axis_size("narrow")
-    me = lax.axis_index("wide") * lax.axis_size("narrow") + lax.axis_index("narrow")
+    count = lax.axis_size("outer") * 2 * lax.axis_size("narrow")
+    me = (lax.axis_index("outer") * 2 + lax.axis_index("core")) * lax.axis_size(
+        "narrow"
+    ) + lax.axis_index("narrow")
     sequences, length, width = inputs.shape
     head_shape = (sequences, length, HEADS, HEAD_DIM)
     cond_rows = condition.astype(jnp.float32)
@@ -367,6 +379,8 @@
 
 
 def solution(mesh):
+    wide, narrow = mesh.shape["wide"], mesh.shape["narrow"]
+    mesh = Mesh(mesh.devices.reshape(wide // 2, 2, narrow), AXES)
     row = P(AXES, None, None)
     mat = P(AXES, None)
     vec = P(AXES)

time: 730 us -> 743 us (1.018)
  waiting for transfers between devices: 297 us -> 226 us
  local copies, waits for them, and re-layouts: 34.5 us -> 76.8 us
  other arithmetic: 87 us -> 124 us
    reduce_scatter x3, waiting for transfers between devices: 199 us -> 121 us  [scatter_natural(): half = lax.psum_scatter(chip, 'outer', scatter_dimension=0, tiled=True)]
    convert_element_type x0 -> x3, other arithmetic: none -> 24.4 us  [scatter_natural(): (keep.astype(jnp.float32) + got.astype(jnp.float32)).astype(jnp.bfloat16)]
    dot_general x0 -> x2, local copies, waits for them, and re-layouts: none -> 16.1 us  [weight_grad(): jnp.einsum('crk,cre->ke', first_operand, second_operand, preferred_elemen...]
    convert_element_type x0 -> x3, local copies, waits for them, and re-layouts: none -> 9.54 us  [scatter_natural(): got = lax.ppermute(send.astype(jnp.bfloat16), 'core', [(0, 1), (1, 0)])]
    ppermute x0 -> x3, waiting for transfers between devices: none -> 8.42 us  [scatter_natural(): got = lax.ppermute(send.astype(jnp.bfloat16), 'core', [(0, 1), (1, 0)])]
    concatenate x1, other arithmetic: 7.93 us -> 16.3 us  [mlp_back(): both_sum = scatter_natural(jnp.concatenate([up_grad, proj_grad], axis=1))]
    concatenate x0 -> x3, local copies, waits for them, and re-layouts: none -> 7.63 us  [mlp_back(): jnp.concatenate([query_pre_grad, key_pre_grad, value_grad], axis=2)]
  transfers between devices with their start and end apart: 11 -> 14, of which waited for: 6 -> 7; matrix products, arithmetic and copies ran while one was open for 24% -> 29% of each run, Pallas kernels for 0% -> 0%
where the time goes in v9:
time: 743 us; the launch traced here: 737 us
  waiting for transfers between devices  226 us (30%)
  matrix products  221 us (30%)
  other arithmetic  124 us (17%)
  local copies, waits for them, and re-layouts  76.8 us (10%)
  blocking collectives  57.7 us (8%)
  starting transfers between devices  16.6 us (2%)
  between operations  14.9 us (2%)
    reduce_scatter x3, waiting for transfers between devices, scatter_natural(): half = lax.psum_scatter(chip, 'outer', scatter_dimension=0, tiled=True)  121 us
    all_gather x1, waiting for transfers between devices, layer(): lax.all_gather(jnp.concatenate([w_qkv, w_proj, w_up], axis=1), AXES, axis...  56.7 us
    all_gather x2, blocking collectives, nested_gather(): lax.all_gather(lax.all_gather(member, 'narrow', axis=0, tiled=True), WIDE...  47.9 us
    dot_general x4, matrix products, matmul_rows(): jnp.einsum('fyg,gq->fyq', first_operand, second_operand, preferred_elemen...  43.5 us
    dot_general x4, matrix products, matmul_back(): jnp.einsum('rfw,uw->rfu', first_operand, second_operand, preferred_elemen...  41.4 us
    dot_general x4, matrix products, weight_grad(): jnp.einsum('crk,cre->ke', first_operand, second_operand, preferred_elemen...  38.6 us
    all_to_all x1, waiting for transfers between devices, layer(): lax.all_to_all(ada_partial.reshape(count, sequences, ada_cols), AXES, spl...  30.7 us
    convert_element_type x1, other arithmetic, attend_backward(): score_gradient = (attention_probabilities * (prob_grad - jnp.sum(prob_gra...  28.8 us
  transfers between devices with their start and end apart: 14, of which 7 were waited for; matrix products, arithmetic and copies ran while one was open for 29% of the time, Pallas kernels for 0%

profile of v9, /device:TPU:0, one launch (start us, length us, event | category | flops | bytes accessed | tf_op | source)
XLA Modules:
  0.0 737.4 jit_solution(12963625456618138808)
XLA Ops:
  22.0 22.8 %all-gather.2 = bf16[16,2,1536]{2,1,0:T(2,128)(2,1)S(1)} all-gather(bf16[1,2,1536]{2,1,0:T(2,128)(2,1)S(1)} %bitcast.260), channel_id=1, replica_groups=mesh['outer'=8,'core'=2,'narrow'=2] {'outer','core'}, dimensions={0}, use_global_device_ids=true | all-gather | bytes 104448 | tf_op jit(solution)/shard_map/all_gather | solution.py:110
  55.5 30.7 %all-to-all-done = f32[32,1,6144]{2,1,0:T(1,128)S(1)} async-done(((f32[32,1,6144]{2,1,0:T(1,128)}), f32[32,1,6144]{2,1,0:T(1,128)S(1)}, u32[]{:S(2)}, u32[]{:S(2)}) %all-to-all-start) | async-done | bytes 786464 | tf_op jit(solution)/shard_map/all_to_all | solution.py:207
  87.3 56.7 %all-gather.8.cloned.1.call-done = bf16[1024,8192]{1,0:T(8,128)(2,1)} async-done(((bf16[32,8192]{1,0:T(8,128)(2,1)}), bf16[1024,8192]{1,0:T(8,128)(2,1)}) %all-gather.8.cloned.1.call-update) | async-done | bytes 16777232 | tf_op jit(solution)/shard_map/all_gather | solution.py:193
  144.0 7.8 %fusion.35 = f32[1,680,3072]{2,1,0:T(8,128)S(1)} fusion(bf16[1024,8192]{1,0:T(8,128)(2,1)} %all-gather.8.cloned.1.call-done, bf16[1,680,1024]{2,1,0:T(8,128)(2,1)S(1)} %copy-done.7, f32[1024]{0:T(1024)S(1)} %bitcast.261, f32[1024]{0:T(1024)S(1)} %bitcast.255, f32[680]{0:T(1024)S(1)} %fusion.98, f32[680]{0:T(1024)S(1)} %broadcast_multiply_fusion.3), kind=kOutput, calls=%fused_computation.53 | convolution fusion | flops 4282368000 | bytes 16053568 | tf_op jit(solution)/shard_map/fyg,gq->fyq/dot_general | solution.py:46
  166.3 14.0 %fusion.118 = (f32[16,680]{1,0:T(8,128)S(1)}, f32[16,680,680]{1,2,0:T(8,128)}) fusion(f32[680,16,64]{0,2,1:T(8,128)S(1)} %bitcast.232, f32[16,64]{1,0:T(8,128)S(1)} %copy-done.40, f32[680,16]{0,1:T(8,128)S(1)} %get-tuple-element.80, f32[680,16,64]{0,2,1:T(8,128)S(1)} %bitcast.226, f32[16,64]{1,0:T(8,128)S(1)} %reshape.858, ...), kind=kOutput, calls=%fused_computation.218 | convolution fusion | flops 973357440 | bytes 35765312 | tf_op jit(solution)/shard_map/vmap(nkz,vkz->knv)/dot_general | solution.py:64
  180.4 13.4 %fusion = f32[16,680]{1,0:T(8,128)S(1)} fusion(f32[16,680,680]{1,2,0:T(8,128)} %get-tuple-element.63, f32[16,680]{1,0:T(8,128)S(1)} %get-tuple-element.62), kind=kLoop, calls=%fused_computation.6 | loop fusion | flops 14785920 | bytes 29680640 | tf_op jit(solution)/shard_map/vmap()/reduce_sum | solution.py:74
  193.8 15.4 %fusion.70 = bf16[16,64,680]{2,1,0:T(8,128)(2,1)} fusion(bf16[680,16,64]{0,2,1:T(8,128)(2,1)S(1)} %bitcast.243, f32[16,680,680]{1,2,0:T(8,128)} %get-tuple-element.63, f32[16,680]{1,0:T(8,128)S(1)} %fusion, f32[16,680]{1,0:T(8,128)S(1)} %get-tuple-element.62), kind=kOutput, calls=%fused_computation.126 | convolution fusion | flops 969886720 | bytes 32465920 | tf_op jit(solution)/shard_map/vmap(wcv,vwn->cwn)/dot_general | solution.py:76
  209.3 5.5 fusion.115
  216.3 14.7 %fusion.20 = (bf16[4096,680]{0,1:T(8,128)(2,1)}, f32[680,4096]{1,0:T(8,128)}) fusion(f32[4096]{0:T(1024)S(1)} %copy-done.57, bf16[1024,8192]{1,0:T(8,128)(2,1)} %all-gather.8.cloned.1.call-done, f32[1,680,1024]{2,1,0:T(8,128)S(1)} %get-tuple-element.32, f32[1024]{0:T(1024)S(1)} %bitcast.251, f32[1024]{0:T(1024)S(1)} %bitcast.247, f32[680]{0:T(1024)S(1)} %fusion.99, ...), kind=kOutput, calls=%fused_computation.29 | convolution fusion | flops 5735587840 | bytes 27915584 | tf_op jit(solution)/shard_map/fyg,gq->fyq/dot_general | solution.py:46
  231.0 17.6 %convert_reduce_fusion = (f32[4096]{0:T(1024)}, bf16[680,4096]{1,0:T(8,128)(2,1)S(1)}) fusion(f32[680,4096]{1,0:T(8,128)} %get-tuple-element.78, f32[4096]{0:T(1024)S(1)} %copy-done.57, bf16[4096,1024]{1,0:T(8,128)(2,1)} %all-gather.10.cloned.1.call-done, f32[1024]{0:T(1024)S(1)} %bitcast.264, bf16[1,680,1024]{2,1,0:T(8,128)(2,1)} %param.33), kind=kOutput, calls=%fused_computation.30 | convolution fusion | flops 5770399744 | bytes 26529792 | tf_op jit(solution)/shard_map/rfw,uw->rfu/dot_general | solution.py:52
  248.6 11.4 %fusion.62 = (bf16[1024]{0:T(1024)(128)(2,1)}, f32[680]{0:T(1024)S(1)}, f32[680,1024]{1,0:T(8,128)S(1)}) fusion(f32[1,680,1024]{2,1,0:T(8,128)S(1)} %get-tuple-element.32, f32[680]{0:T(1024)S(1)} %fusion.99, f32[680]{0:T(1024)S(1)} %broadcast_multiply_fusion.2, f32[1024]{0:T(1024)S(1)} %bitcast.248, bf16[680,4096]{1,0:T(8,128)(2,1)S(1)} %get-tuple-element.76, ...), kind=kOutput, calls=%fused_computation.108 | convolution fusion | flops 5709126144 | bytes 19544032 | tf_op jit(solution)/shard_map/rfw,uw->rfu/dot_general | solution.py:52
  264.3 15.5 %convert_reduce_fusion.2 = (f32[1024]{0:T(1024)}, bf16[1024]{0:T(1024)(128)(2,1)}, bf16[1024]{0:T(1024)(128)(2,1)}, f32[1024]{0:T(1024)}, bf16[1,680,1024]{2,1,0:T(8,128)(2,1)S(1)}, /*index=5*/bf16[1,680,1024]{2,1,0:T(8,128)(2,1)}) fusion(f32[1024]{0:T(1024)S(1)} %bitcast.265, bf16[1,680,1024]{2,1,0:T(8,128)(2,1)S(1)} %copy-done.24, ...), kind=kOutput, calls=%fused_computation.115 | convolution fusion | flops 5746028544 | bytes 32111264 | tf_op jit(solution)/shard_map/fyg,gq->fyq/dot_general | solution.py:46
  284.9 16.1 %bitcast_convert_fusion = (bf16[1,680,16,64]{1,3,2,0:T(8,128)(2,1)}, f32[16,64,680]{2,1,0:T(8,128)}) fusion(bf16[680,16,64]{0,2,1:T(8,128)(2,1)S(1)} %bitcast.238, f32[16,680,680]{1,2,0:T(8,128)} %get-tuple-element.63, f32[16,680]{1,0:T(8,128)} %log_add_fusion), kind=kOutput, calls=%fused_computation.82 | convolution fusion | flops 962488320 | bytes 35207680 | tf_op jit(solution)/shard_map/vmap(fgs,gfu->sfu)/dot_general | solution.py:90
  301.0 26.1 %multiply_reduce_fusion = (f32[16,680]{1,0:T(8,128)}, f32[16,680,680]{1,2,0:T(8,128)}) fusion(f32[16,680,680]{1,2,0:T(8,128)} %get-tuple-element.63, f32[16,680]{1,0:T(8,128)} %log_add_fusion, bf16[680,16,64]{0,2,1:T(8,128)(2,1)S(1)} %bitcast.239, bf16[680,16,64]{0,2,1:T(8,128)(2,1)S(1)} %bitcast.244), kind=kOutput, calls=%fused_computation.1 | convolution fusion | flops 969179520 | bytes 62059520 | tf_op jit(solution)/shard_map/vmap(nkz,vkz->knv)/dot_general | solution.py:87
  329.6 28.8 %multiply_convert_fusion = bf16[16,680,680]{1,2,0:T(8,128)(2,1)} fusion(f32[16,680,680]{1,2,0:T(8,128)} %get-tuple-element.69, f32[16,680,680]{1,2,0:T(8,128)} %get-tuple-element.63, f32[16,680]{1,0:T(8,128)} %get-tuple-element.68, f32[16,680]{1,0:T(8,128)} %log_add_fusion), kind=kLoop, calls=%fused_computation | loop fusion | flops 29593600 | bytes 74071040 | tf_op jit(solution)/shard_map/vmap()/convert_element_type | solution.py:99
  358.5 12.4 %fusion.53 = (f32[680,16]{0,1:T(8,128)}, f32[16,64,680]{2,1,0:T(8,128)}) fusion(f32[1,680,16,64]{1,3,2,0:T(8,128)S(1)} %bitcast.227, f32[16,64]{1,0:T(8,128)S(1)} %copy-done.42, bf16[16,680,680]{1,2,0:T(8,128)(2,1)} %multiply_convert_fusion, f32[680,16,64]{0,2,1:T(8,128)} %bitcast.231, f32[16,64]{1,0:T(8,128)S(1)} %copy-done.41, f32[680,16]{0,1:T(8,128)} %copy-done.19), kind=kOutput, calls=%fused_computation.90 | convolution fusion | flops 951162240 | bytes 23247872 | tf_op jit(solution)/shard_map/vmap(wcv,vwn->cwn)/dot_general | solution.py:100
  370.9 9.4 %fusion.50 = (f32[16,64]{1,0:T(8,128)}, f32[680,16]{0,1:T(8,128)S(1)}, f32[16,64,680]{2,1,0:T(8,128)S(1)}) fusion(f32[1,680,16,64]{1,3,2,0:T(8,128)S(1)} %bitcast.233, f32[680,16]{0,1:T(8,128)S(1)} %copy-done.20, f32[16,64]{1,0:T(8,128)S(1)} %copy-done.43, bf16[16,680,680]{1,2,0:T(8,128)(2,1)} %multiply_convert_fusion, f32[680,16,64]{0,2,1:T(8,128)S(1)} %bitcast.228, ...), kind=kOutput, calls=%fused_computation.78 | convolution fusion | flops 953946496 | bytes 23295488 | tf_op jit(solution)/shard_map/vmap(fgs,gfu->sfu)/dot_general | solution.py:103
  392.9 9.1 %fusion.58 = (f32[680]{0:T(1024)S(1)}, f32[680,1024]{1,0:T(8,128)S(1)}) fusion(bf16[1,680,1024]{2,1,0:T(8,128)(2,1)} %param.17, f32[1024]{0:T(1024)S(1)} %bitcast.256, f32[680]{0:T(1024)S(1)} %copy-done.48, bf16[1024,8192]{1,0:T(8,128)(2,1)} %all-gather.8.cloned.1.call-done, bf16[680,1024]{1,0:T(8,128)(2,1)} %copy.120, bf16[680,1024]{1,0:T(8,128)(2,1)} %copy.119, ...), kind=kOutput, calls=%fused_computation.101 | convolution fusion | flops 4294204672 | bytes 14656832 | tf_op jit(solution)/shard_map/rfw,uw->rfu/dot_general | solution.py:52
  410.0 7.6 %fusion.40 = f32[8,2,64,3072]{3,2,1,0:T(8,128)S(1)} fusion(bf16[8,2,64,680]{3,2,1,0:T(8,128)(2,1)} %bitcast.246, bf16[680,1024]{1,0:T(8,128)(2,1)} %copy.120, bf16[680,1024]{1,0:T(8,128)(2,1)} %copy.119, bf16[680,1024]{1,0:T(8,128)(2,1)} %copy.118), kind=kOutput, calls=%fused_computation.59 | convolution fusion | flops 4290723840 | bytes 18153472 | tf_op jit(solution)/shard_map/crk,cre->ke/dot_general | solution.py:58
  424.8 13.5 %dot_general.110 = bf16[8,2,256,680]{2,1,0,3:T(2,128)(2,1)} reshape(bf16[4096,680]{0,1:T(8,128)(2,1)} %get-tuple-element.77) | data formatting | bytes 11141120 | tf_op jit(solution)/shard_map/crk,cre->ke/dot_general | solution.py:58
  438.3 6.5 fusion.27
  445.5 9.9 %fusion.28 = f32[8,2,256,1024]{3,2,1,0:T(8,128)S(1)} fusion(bf16[8,2,256,680]{2,1,0,3:T(2,128)(2,1)} %dot_general.110, bf16[1,680,1024]{2,1,0:T(8,128)(2,1)} %param.33, f32[1024]{0:T(1024)S(1)} %bitcast.266), kind=kOutput, calls=%fused_computation.46 | convolution fusion | flops 5706342400 | bytes 23744512 | tf_op jit(solution)/shard_map/crk,cre->ke/dot_general | solution.py:58
  458.1 6.8 fusion.76
  464.9 14.3 %fusion.111 = f32[1024,4096]{1,0:T(8,128)} fusion(bf16[680,4096]{1,0:T(8,128)(2,1)} %copy-done.18, f32[1,680,1024]{2,1,0:T(8,128)S(1)} %copy-done.6, f32[1024]{0:T(1024)S(1)} %bitcast.252, f32[1024]{0:T(1024)S(1)} %bitcast.250, f32[680]{0:T(1024)S(1)} %copy-done.34, f32[680]{0:T(1024)S(1)} %copy-done.27), kind=kOutput, calls=%fused_computation.213 | convolution fusion | flops 5707735040 | bytes 25146688 | tf_op jit(solution)/shard_map/crk,cre->ke/dot_general | solution.py:58
  479.2 8.4 %fusion.22 = bf16[8,256,1024]{2,1,0:T(8,128)(2,1)} fusion(bf16[8,256,1024]{2,1,0:T(8,128)(2,1)} %collective-permute-done.4, f32[8,2,256,1024]{3,2,1,0:T(8,128)} %copy-done.14, s32[]{:T(128)S(6)} %select_n.47), kind=kLoop, calls=%fused_computation.36 | loop fusion | flops 6291456 | bytes 16777220 | tf_op jit(solution)/shard_map/convert_element_type | solution.py:135
  487.7 16.3 %pad_maximum_fusion = f32[1024,5120]{1,0:T(8,128)} fusion(f32[1024,1024]{1,0:T(8,128)} %fusion.76, f32[1024,4096]{1,0:T(8,128)} %fusion.111), kind=kLoop, calls=%fused_computation.8 | loop fusion | flops 5242880 | bytes 41943040 | tf_op jit(solution)/shard_map/concatenate | solution.py:269
  510.0 8.4 %collective-permute-done.2 = bf16[8,64,5120]{2,1,0:T(8,128)(2,1)} collective-permute-done((bf16[8,64,5120]{2,1,0:T(8,128)(2,1)S(1)}, bf16[8,64,5120]{2,1,0:T(8,128)(2,1)}, u32[]{:S(2)}, u32[]{:S(2)}) %collective-permute-start.2) | collective-permute-done | bytes 5242912 | tf_op jit(solution)/shard_map/ppermute | solution.py:134
  518.4 9.5 %fusion.21 = bf16[8,64,5120]{2,1,0:T(8,128)(2,1)} fusion(bf16[8,64,5120]{2,1,0:T(8,128)(2,1)} %collective-permute-done.2, f32[8,2,64,5120]{3,2,1,0:T(8,128)} %bitcast.235, s32[]{:T(128)S(6)} %select_n.47), kind=kLoop, calls=%fused_computation.33 | loop fusion | flops 7864320 | bytes 20971524 | tf_op jit(solution)/shard_map/convert_element_type | solution.py:135
  536.6 25.1 %all-gather.4 = bf16[16,2,6144]{2,1,0:T(2,128)(2,1)} all-gather(bf16[1,2,6144]{2,1,0:T(2,128)(2,1)S(1)} %bitcast.254), channel_id=1, replica_groups=mesh['outer'=8,'core'=2,'narrow'=2] {'outer','core'}, dimensions={0}, use_global_device_ids=true | all-gather | bytes 417792 | tf_op jit(solution)/shard_map/all_gather | solution.py:110
  578.5 5.8 all-to-all-start.2
  594.6 17.2 %reduce-scatter.8.cloned.1.call-done = bf16[256,1024]{1,0:T(8,128)(2,1)} async-done(((bf16[2048,1024]{1,0:T(8,128)(2,1)}), bf16[256,1024]{1,0:T(8,128)(2,1)}) %reduce-scatter.8.cloned.1.call-update) | async-done | bytes 524304 | tf_op jit(solution)/shard_map/reduce_scatter | solution.py:137
  614.3 103.6 %reduce-scatter.6.cloned.1.call-done = bf16[64,5120]{1,0:T(8,128)(2,1)} async-done(((bf16[512,5120]{1,0:T(8,128)(2,1)}), bf16[64,5120]{1,0:T(8,128)(2,1)}) %reduce-scatter.6.cloned.1.call-update) | async-done | bytes 655376 | tf_op jit(solution)/shard_map/reduce_scatter | solution.py:137
  (265 shorter events, 142.0 us)
Async XLA Ops:
  7.2 37.7 %copy-start = (bf16[32,6144]{1,0:T(8,128)(2,1)S(1)}, bf16[32,6144]{1,0:T(8,128)(2,1)}, u32[]{:S(2)}) copy-start(bf16[32,6144]{1,0:T(8,128)(2,1)} %param.20) | copy-start | bytes 1179652
  7.2 42.4 %copy-start.64 = (s32[10]{0:T(128)S(1)}, s32[10]{0:T(128)}, u32[]{:S(2)}) copy-start(s32[10]{0:T(128)} %param.19) | copy-start | bytes 124
  7.2 136.8 %all-gather.8.cloned.1.call-start = ((), (), s32[]{:S(2)}) async-start(), calls=%async_computation.6 | async-start | bytes 17301504 | tf_op jit(solution)/shard_map/all_gather | solution.py:193
  9.2 42.5 %copy-start.7 = (bf16[1,680,1024]{2,1,0:T(8,128)(2,1)S(1)}, bf16[1,680,1024]{2,1,0:T(8,128)(2,1)}, u32[]{:S(2)}) copy-start(bf16[1,680,1024]{2,1,0:T(8,128)(2,1)} %param.17) | copy-start | bytes 4177924
  9.2 221.8 %all-gather.10.cloned.1.call-start = ((), (), s32[]{:S(2)}) async-start(), calls=%async_computation.7 | async-start | bytes 8650752 | tf_op jit(solution)/shard_map/all_gather | solution.py:200
  46.9 39.3 %all-to-all-start = ((f32[32,1,6144]{2,1,0:T(1,128)}), f32[32,1,6144]{2,1,0:T(1,128)S(1)}, u32[]{:S(2)}, u32[]{:S(2)}) async-start(f32[32,1,6144]{2,1,0:T(1,128)} %copy.107), calls=%async_computation | async-start | bytes 1572864 | tf_op jit(solution)/shard_map/all_to_all | solution.py:207
  49.5 543.6 %reduce-scatter.4.cloned.1.call-start = ((), (), s32[]{:S(2)}) async-start(), calls=%async_computation.8 | async-start | bytes 3538944 | tf_op jit(solution)/shard_map/reduce_scatter | solution.py:137
  51.5 92.5 %copy-start.39 = (f32[16,64]{1,0:T(8,128)}, f32[16,64]{1,0:T(8,128)S(1)}, u32[]{:S(2)}) copy-start(f32[16,64]{1,0:T(8,128)S(1)} %reshape.859) | copy-start | bytes 12292
  51.6 114.5 %copy-start.37 = (f32[16,64]{1,0:T(8,128)}, f32[16,64]{1,0:T(8,128)S(1)}, u32[]{:S(2)}) copy-start(f32[16,64]{1,0:T(8,128)S(1)} %reshape.858) | copy-start | bytes 12292
  51.9 92.1 %copy-start.47 = (f32[680]{0:T(1024)}, f32[680]{0:T(1024)S(1)}, u32[]{:S(2)}) copy-start(f32[680]{0:T(1024)S(1)} %broadcast_multiply_fusion.3) | copy-start | bytes 8164
  52.5 91.6 %copy-start.51 = (f32[680]{0:T(1024)}, f32[680]{0:T(1024)S(1)}, u32[]{:S(2)}) copy-start(f32[680]{0:T(1024)S(1)} %fusion.57) | copy-start | bytes 8164
  52.5 91.5 %copy-start.45 = (f32[680]{0:T(1024)}, f32[680]{0:T(1024)S(1)}, u32[]{:S(2)}) copy-start(f32[680]{0:T(1024)S(1)} %fusion.98) | copy-start | bytes 8164
  87.3 56.7 %copy-start.49 = (f32[1,1024]{1,0:T(1,128)}, f32[1,1024]{1,0:T(1,128)S(1)}, u32[]{:S(2)}) copy-start(f32[1,1024]{1,0:T(1,128)S(1)} %get-tuple-element.54) | copy-start | bytes 12292
  87.3 56.7 %copy-start.53 = (f32[1,1024]{1,0:T(1,128)}, f32[1,1024]{1,0:T(1,128)S(1)}, u32[]{:S(2)}) copy-start(f32[1,1024]{1,0:T(1,128)S(1)} %get-tuple-element.53) | copy-start | bytes 12292
  87.3 129.0 %copy-start.35 = (f32[1,1024]{1,0:T(1,128)}, f32[1,1024]{1,0:T(1,128)S(1)}, u32[]{:S(2)}) copy-start(f32[1,1024]{1,0:T(1,128)S(1)} %get-tuple-element.51) | copy-start | bytes 12292
  87.3 172.7 %copy-start.31 = (f32[1,1024]{1,0:T(1,128)}, f32[1,1024]{1,0:T(1,128)S(1)}, u32[]{:S(2)}) copy-start(f32[1,1024]{1,0:T(1,128)S(1)} %get-tuple-element.52) | copy-start | bytes 12292
  214.8 46.8 %copy-start.5 = (f32[1,680,1024]{2,1,0:T(8,128)}, f32[1,680,1024]{2,1,0:T(8,128)S(1)}, u32[]{:S(2)}) copy-start(f32[1,680,1024]{2,1,0:T(8,128)S(1)} %get-tuple-element.32) | copy-start | bytes 8355844
  214.8 45.3 %copy-start.26 = (f32[680]{0:T(1024)}, f32[680]{0:T(1024)S(1)}, u32[]{:S(2)}) copy-start(f32[680]{0:T(1024)S(1)} %broadcast_multiply_fusion.2) | copy-start | bytes 8164
  215.2 44.8 %copy-start.33 = (f32[680]{0:T(1024)}, f32[680]{0:T(1024)S(1)}, u32[]{:S(2)}) copy-start(f32[680]{0:T(1024)S(1)} %fusion.99) | copy-start | bytes 8164
  329.6 28.8 %copy-start.41 = (f32[16,64]{1,0:T(8,128)S(1)}, f32[16,64]{1,0:T(8,128)}, u32[]{:S(2)}) copy-start(f32[16,64]{1,0:T(8,128)} %copy-done.39) | copy-start | bytes 12292
  329.6 28.8 %copy-start.42 = (f32[16,64]{1,0:T(8,128)S(1)}, f32[16,64]{1,0:T(8,128)}, u32[]{:S(2)}) copy-start(f32[16,64]{1,0:T(8,128)} %broadcast_multiply_fusion.1) | copy-start | bytes 12292
  424.3 14.0 %collective-permute-start = (bf16[8,64,3072]{2,1,0:T(8,128)(2,1)}, bf16[8,64,3072]{2,1,0:T(8,128)(2,1)}, u32[]{:S(2)}, u32[]{:S(2)}) collective-permute-start(bf16[8,64,3072]{2,1,0:T(8,128)(2,1)} %fusion.49), channel_id=1, source_target_pairs={{0,2},{2,0},{1,3},{3,1},{4,6},{6,4},{5,7},{7,5},{8,10},{10,8},{9,1... | collective-permute-start | bytes 9437192 | tf_op jit(solution)/shard_map/ppermute | solution.py:134
  444.8 167.0 %reduce-scatter.8.cloned.1.call-start = ((), (), s32[]{:S(2)}) async-start(), calls=%async_computation.10 | async-start | bytes 4718592 | tf_op jit(solution)/shard_map/reduce_scatter | solution.py:137
  458.0 21.2 %collective-permute-start.4 = (bf16[8,256,1024]{2,1,0:T(8,128)(2,1)}, bf16[8,256,1024]{2,1,0:T(8,128)(2,1)}, u32[]{:S(2)}, u32[]{:S(2)}) collective-permute-start(bf16[8,256,1024]{2,1,0:T(8,128)(2,1)} %fusion.39), channel_id=1, source_target_pairs={{0,2},{2,0},{1,3},{3,1},{4,6},{6,4},{5,7},{7,5},{8,10},{10,8},{9,1... | collective-permute-start | bytes 12582920 | tf_op jit(solution)/shard_map/ppermute | solution.py:134
  487.7 230.3 %reduce-scatter.6.cloned.1.call-start = ((), (), s32[]{:S(2)}) async-start(), calls=%async_computation.9 | async-start | bytes 5898240 | tf_op jit(solution)/shard_map/reduce_scatter | solution.py:137
  508.7 9.7 %collective-permute-start.2 = (bf16[8,64,5120]{2,1,0:T(8,128)(2,1)S(1)}, bf16[8,64,5120]{2,1,0:T(8,128)(2,1)}, u32[]{:S(2)}, u32[]{:S(2)}) collective-permute-start(bf16[8,64,5120]{2,1,0:T(8,128)(2,1)S(1)} %fusion.38), channel_id=1, source_target_pairs={{0,2},{2,0},{1,3},{3,1},{4,6},{6,4},{5,7},{7,5},{8,10},{10,8},{9,1... | collective-permute-start | bytes 15728648 | tf_op jit(solution)/shard_map/ppermute | solution.py:134
  530.4 39.9 %copy-start.10 = (f32[16,64,680]{2,1,0:T(8,128)S(1)}, f32[16,64,680]{2,1,0:T(8,128)}, u32[]{:S(2)}) copy-start(f32[16,64,680]{2,1,0:T(8,128)} %get-tuple-element.67) | copy-start | bytes 8355844
  565.5 13.1 %all-to-all-start.1 = ((f32[32,1,32]{2,1,0:T(1,128)}), f32[32,1,32]{2,1,0:T(1,128)S(1)}, u32[]{:S(2)}, u32[]{:S(2)}) async-start(f32[32,1,32]{2,1,0:T(1,128)} %bitcast.46), calls=%async_computation.1 | async-start | bytes 32768 | tf_op jit(solution)/shard_map/all_to_all | solution.py:356
  578.5 13.3 %all-to-all-start.2 = ((f32[32,1,320]{2,1,0:T(1,128)}), f32[32,1,320]{2,1,0:T(1,128)S(1)}, u32[]{:S(2)}, u32[]{:S(2)}) async-start(f32[32,1,320]{2,1,0:T(1,128)} %reshape.851), calls=%async_computation.3 | async-start | bytes 98304 | tf_op jit(solution)/shard_map/all_to_all | solution.py:143
  594.0 126.4 %collective-permute-start.1 = (bf16[32,3072]{1,0:T(8,128)(2,1)S(1)}, bf16[32,3072]{1,0:T(8,128)(2,1)S(1)}, u32[]{:S(2)}, u32[]{:S(2)}) collective-permute-start(bf16[32,3072]{1,0:T(8,128)(2,1)S(1)} %constant_dynamic-slice_fusion.2), channel_id=1, source_target_pairs={{0,1},{1,0},{2,3},{3,2},{4,5},{5,4},{6,7},{7,6},{8,9},{9,8},{10,11... | collective-permute-start | bytes 589832 | tf_op jit(solution)/shard_map/ppermute | solution.py:123
  612.8 109.4 %collective-permute-start.5 = (bf16[128,1024]{1,0:T(8,128)(2,1)S(1)}, bf16[128,1024]{1,0:T(8,128)(2,1)S(1)}, u32[]{:S(2)}, u32[]{:S(2)}) collective-permute-start(bf16[128,1024]{1,0:T(8,128)(2,1)S(1)} %constant_dynamic-slice_fusion), channel_id=1, source_target_pairs={{0,1},{1,0},{2,3},{3,2},{4,5},{5,4},{6,7},{7,6},{8,9},{9,8},{10,11... | collective-permute-start | bytes 786440 | tf_op jit(solution)/shard_map/ppermute | solution.py:123
  718.9 9.2 %collective-permute-start.3 = (bf16[32,5120]{1,0:T(8,128)(2,1)S(1)}, bf16[32,5120]{1,0:T(8,128)(2,1)S(1)}, u32[]{:S(2)}, u32[]{:S(2)}) collective-permute-start(bf16[32,5120]{1,0:T(8,128)(2,1)S(1)} %constant_dynamic-slice_fusion.1), channel_id=1, source_target_pairs={{0,1},{1,0},{2,3},{3,2},{4,5},{5,4},{6,7},{7,6},{8,9},{9,8},{10,11... | collective-permute-start | bytes 983048 | tf_op jit(solution)/shard_map/ppermute | solution.py:123
  (50 other events, 454.2 us)
Sparse Core Ops, SparseCore 0:
  11.6 132.3 all-gather.7
  147.0 75.2 all-gather.9
  444.9 73.7 reduce-scatter.3
  522.2 89.5 reduce-scatter.7
  615.3 102.6 reduce-scatter.5

commit v10 on v7

--- a/solution.py
+++ b/solution.py
@@ -1,6 +1,7 @@
 import jax
 import jax.numpy as jnp
 from jax import lax
+from jax.experimental import pallas as pl
 from jax.sharding import PartitionSpec as P
 
 
@@ -32,13 +33,59 @@
     return jax.nn.gelu(values, approximate=True)
 
 
-def block_mask(scale_tokens):
+def block_limits(scale_tokens):
     block_ends = jnp.cumsum(scale_tokens)
     places = jnp.arange(SEQ_LEN, dtype=jnp.int32)
-    limits = jnp.min(
+    return jnp.min(
         jnp.where(block_ends[None, :] > places[:, None], block_ends[None, :], SEQ_LEN), axis=1
     )
-    return places[None, :] < limits[:, None]
+
+
+def block_mask(scale_tokens):
+    places = jnp.arange(SEQ_LEN, dtype=jnp.int32)
+    return places[None, :] < block_limits(scale_tokens)[:, None]
+
+
+def attn_kernel(limit_ref, q_ref, k_ref, v_ref, ctx_ref, lse_ref):
+    length = q_ref.shape[0]
+    dim = q_ref.shape[1] // 2
+    cols = lax.broadcasted_iota(jnp.int32, (length, length), 1)
+    allowed = cols < limit_ref[...]
+    outs = []
+    for i in range(2):
+        q = q_ref[:, i * dim : (i + 1) * dim]
+        k = k_ref[:, i * dim : (i + 1) * dim]
+        v = v_ref[:, i * dim : (i + 1) * dim]
+        s = lax.dot_general(q, k, (((1,), (1,)), ((), ())), preferred_element_type=jnp.float32)
+        s = jnp.where(allowed, s * dim ** (-0.5), MASKED)
+        m = jnp.max(s, axis=1, keepdims=True)
+        e = jnp.exp(s - m)
+        l = jnp.sum(e, axis=1, keepdims=True)
+        p = (e / l).astype(jnp.bfloat16)
+        outs.append(jnp.dot(p, v, preferred_element_type=jnp.float32).astype(jnp.bfloat16))
+        lse_ref[i] = m + jnp.log(l)
+    ctx_ref[...] = jnp.concatenate(outs, axis=1)
+
+
+def attention_forward(queries, keys, values, limits, heads):
+    length, width = queries.shape
+    pair = 2 * (width // heads)
+    spec = pl.BlockSpec((length, pair), lambda h: (0, h))
+    return pl.pallas_call(
+        attn_kernel,
+        grid=(heads // 2,),
+        in_specs=[pl.BlockSpec((length, 1), lambda h: (0, 0)), spec, spec, spec],
+        out_specs=[spec, pl.BlockSpec((2, length, 1), lambda h: (h, 0, 0))],
+        out_shape=[
+            jax.ShapeDtypeStruct((length, width), jnp.bfloat16),
+            jax.ShapeDtypeStruct((heads, length, 1), jnp.float32),
+        ],
+        cost_estimate=pl.CostEstimate(
+            flops=4 * length * length * width,
+            transcendentals=heads * length * length,
+            bytes_accessed=4 * length * width * 2 + heads * length * 4,
+        ),
+    )(limits, queries, keys, values)
 
 
 def matmul_rows(first_operand, second_operand):
@@ -64,18 +111,6 @@
         "nkz,vkz->knv", query_sequence, key_sequence, preferred_element_type=jnp.float32
     ) * HEAD_DIM ** (-0.5)
     return jnp.where(allowed[None], scores, MASKED)
-
-
-def attend_forward(query_sequence, key_sequence, value_sequence, allowed):
-    scores = masked_scores(query_sequence, key_sequence, allowed)
-    row_max = jnp.max(scores, axis=-1, keepdims=True)
-    exponent = jnp.exp(scores - row_max)
-    row_total = jnp.sum(exponent, axis=-1, keepdims=True)
-    probabilities_reduced = (exponent / row_total).astype(jnp.bfloat16)
-    context = jnp.einsum(
-        "wcv,vwn->cwn", probabilities_reduced, value_sequence, preferred_element_type=jnp.float32
-    ).astype(jnp.bfloat16)
-    return (context, row_max[..., 0] + jnp.log(row_total[..., 0]))
 
 
 def attend_backward(
@@ -206,10 +241,16 @@
     queries = head_norm(query_pre, query_gain).astype(jnp.bfloat16)
     key_rows = head_norm(key_pre, key_gain).astype(jnp.bfloat16)
     value_rows = (projected[..., 2 * width :] + value_bias).astype(jnp.bfloat16).reshape(head_shape)
-    context, logsum = jax.vmap(
-        lambda q, k, v: attend_forward(q, k, v, allowed)
-    )(queries, key_rows, value_rows)
+    limits = block_limits(scale_tokens).astype(jnp.int32)[:, None]
+    context, logsum = attention_forward(
+        queries.reshape(length, width),
+        key_rows.reshape(length, width),
+        value_rows.reshape(length, width),
+        limits,
+        HEADS,
+    )
     context = context.reshape(sequences, length, width)
+    logsum = logsum.reshape(sequences, HEADS, length)
     attended = matmul_rows(context, proj_full) + proj_bias
     middle = input_rows + gamma_attn[:, None, :] * attended
     normed_mlp = modulate(middle, scale_mlp, shift_mlp).astype(jnp.bfloat16)

time: 730 us -> 769 us (1.053)
  Pallas kernels: 0 us -> 31 us
  local copies, waits for them, and re-layouts: 34.5 us -> 53.8 us
    pallas_call x0 -> x1, Pallas kernels: none -> 31 us  [attention_forward(): pl.pallas_call(attn_kernel, grid=(heads // 2,), in_specs=[pl.BlockSpec((l...]
    dot_general x1 -> x0, matrix products: 15.8 us -> none  [attend_forward(): jnp.einsum('wcv,vwn->cwn', probabilities_reduced, value_sequence, preferr...]
    reduce_sum x1 -> x0, other arithmetic: 13.4 us -> none  [attend_forward(): row_total = jnp.sum(exponent, axis=-1, keepdims=True)]
    mul x0 -> x4, local copies, waits for them, and re-layouts: none -> 10.9 us  [head_norm(): shaped * lax.rsqrt(jnp.mean(shaped * shaped, axis=-1, keepdims=True) + EP...]
    convert_element_type x0 -> x2, other arithmetic: none -> 10.6 us  [the longest x1 6.69 us: layer(): key_rows = head_norm(key_pre, key_gain).astype(jnp.bfloat16)]
  transfers between devices with their start and end apart: 11 -> 11, of which waited for: 6 -> 6; matrix products, arithmetic and copies ran while one was open for 24% -> 19% of each run, Pallas kernels for 0% -> 4%
where the time goes in v10:
time: 769 us; the launch traced here: 765 us
  waiting for transfers between devices  294 us (38%)
  matrix products  216 us (28%)
  other arithmetic  83.9 us (11%)
  blocking collectives  56.1 us (7%)
  local copies, waits for them, and re-layouts  53.8 us (7%)
  Pallas kernels  31 us (4%)
  between operations  14.9 us (2%)
  starting transfers between devices  14.8 us (2%)
    reduce_scatter x3, waiting for transfers between devices, scatter_natural(): lax.psum_scatter(member.astype(jnp.bfloat16), 'wide', scatter_dimension=0...  199 us
    all_gather x1, waiting for transfers between devices, layer(): lax.all_gather(jnp.concatenate([w_qkv, w_proj, w_up], axis=1), AXES, axis...  56.7 us
    all_gather x2, blocking collectives, nested_gather(): lax.all_gather(lax.all_gather(member, 'narrow', axis=0, tiled=True), 'wid...  46.3 us
    dot_general x4, matrix products, matmul_back(): jnp.einsum('rfw,uw->rfu', first_operand, second_operand, preferred_elemen...  45.2 us
    dot_general x4, matrix products, matmul_rows(): jnp.einsum('fyg,gq->fyq', first_operand, second_operand, preferred_elemen...  41.7 us
    dot_general x4, matrix products, weight_grad(): jnp.einsum('crk,cre->ke', first_operand, second_operand, preferred_elemen...  38.9 us
    dot_general x1, matrix products, attend_backward(): jnp.einsum('nkz,vkz->knv', context_gradient, value_sequence, preferred_el...  31.7 us
    pallas_call x1, Pallas kernels, attention_forward(): pl.pallas_call(attn_kernel, grid=(heads // 2,), in_specs=[pl.BlockSpec((l...  31 us
  transfers between devices with their start and end apart: 11, of which 6 were waited for; matrix products, arithmetic and copies ran while one was open for 19% of the time, Pallas kernels for 4%

profile of v10, /device:TPU:0, one launch (start us, length us, event | category | flops | bytes accessed | tf_op | source)
XLA Modules:
  0.0 764.7 jit_solution(11656865210359578535)
XLA Ops:
  11.2 5.4 concatenate.51
  16.7 5.3 all-gather.1
  22.0 22.8 %all-gather.2 = bf16[16,2,1536]{2,1,0:T(2,128)(2,1)S(1)} all-gather(bf16[1,2,1536]{2,1,0:T(2,128)(2,1)S(1)} %bitcast.220), channel_id=1, replica_groups=mesh['wide'=16,'narrow'=2] {'wide'}, dimensions={0}, use_global_device_ids=true | all-gather | bytes 104448 | tf_op jit(solution)/shard_map/all_gather | solution.py:144
  57.6 28.5 %all-to-all-done = f32[32,1,6144]{2,1,0:T(1,128)S(1)} async-done(((f32[32,1,6144]{2,1,0:T(1,128)}), f32[32,1,6144]{2,1,0:T(1,128)S(1)}, u32[]{:S(2)}, u32[]{:S(2)}) %all-to-all-start) | async-done | bytes 786464 | tf_op jit(solution)/shard_map/all_to_all | solution.py:230
  87.3 56.7 %all-gather.8.cloned.1.call-done = bf16[1024,8192]{1,0:T(8,128)(2,1)} async-done(((bf16[32,8192]{1,0:T(8,128)(2,1)}), bf16[1024,8192]{1,0:T(8,128)(2,1)}) %all-gather.8.cloned.1.call-update) | async-done | bytes 16777232 | tf_op jit(solution)/shard_map/all_gather | solution.py:216
  144.0 7.8 %fusion.19 = f32[1,680,3072]{2,1,0:T(8,128)S(1)} fusion(bf16[1024,8192]{1,0:T(8,128)(2,1)} %all-gather.8.cloned.1.call-done, bf16[1,680,1024]{2,1,0:T(8,128)(2,1)S(1)} %copy-done.2, f32[1024]{0:T(1024)S(1)} %bitcast.231, f32[1024]{0:T(1024)S(1)} %bitcast.214, f32[680]{0:T(1024)S(1)} %fusion.80, f32[680]{0:T(1024)S(1)} %broadcast_multiply_fusion.3), kind=kOutput, calls=%fused_computation.30 | convolution fusion | flops 4282368000 | bytes 16053568 | tf_op jit(solution)/shard_map/fyg,gq->fyq/dot_general | solution.py:92
  178.6 6.7 fusion.46
  185.3 31.0 %shard_map.288 = (bf16[680,1024]{1,0:T(8,128)(2,1)}, f32[16,680,1]{2,1,0:T(8,128)}) custom-call(s32[680,1]{1,0:T(8,128)} %broadcast_in_dim.49.limit_ref, bf16[680,1024]{1,0:T(8,128)(2,1)} %get-tuple-element.78.q_ref, bf16[680,1024]{1,0:T(8,128)(2,1)} %get-tuple-element.77.k_ref, bf16[680,1024]{1,0:T(8,128)(2,1)} %bitcast.207), custom_call_target="tpu_custom_call" | custom-call | flops 1893990400 | bytes 5614080 | tf_op jit(solution)/shard_map/pallas_call | solution.py:74
  216.3 5.8 fusion.95
  224.0 12.6 %fusion.13 = f32[680,4096]{1,0:T(8,128)} fusion(bf16[1024,8192]{1,0:T(8,128)(2,1)} %all-gather.8.cloned.1.call-done, f32[1,680,1024]{2,1,0:T(8,128)S(1)} %get-tuple-element.36, f32[1024]{0:T(1024)S(1)} %bitcast.226, f32[1024]{0:T(1024)S(1)} %bitcast.221, f32[680]{0:T(1024)S(1)} %fusion.81, f32[680]{0:T(1024)S(1)} %broadcast_multiply_fusion.2), kind=kOutput, calls=%fused_computation.22 | convolution fusion | flops 5707735040 | bytes 22328640 | tf_op jit(solution)/shard_map/fyg,gq->fyq/dot_general | solution.py:92
  236.6 19.3 %convert_reduce_fusion = (f32[4096]{0:T(1024)}, bf16[680,4096]{1,0:T(8,128)(2,1)S(1)}) fusion(f32[680,4096]{1,0:T(8,128)} %fusion.13, f32[4096]{0:T(1024)} %fusion.74, bf16[4096,1024]{1,0:T(8,128)(2,1)} %all-gather.10.cloned.1.call-done, f32[1024]{0:T(1024)} %bitcast.228, bf16[1,680,1024]{2,1,0:T(8,128)(2,1)} %param.33), kind=kOutput, calls=%fused_computation.15 | convolution fusion | flops 5770399744 | bytes 26529792 | tf_op jit(solution)/shard_map/rfw,uw->rfu/dot_general | solution.py:98
  255.9 11.7 %fusion.41 = (bf16[1024]{0:T(1024)(128)(2,1)}, f32[680]{0:T(1024)S(1)}, f32[680,1024]{1,0:T(8,128)S(1)}) fusion(f32[1,680,1024]{2,1,0:T(8,128)S(1)} %copy-done.10, f32[680]{0:T(1024)S(1)} %copy-done.50, f32[680]{0:T(1024)S(1)} %copy-done.33, f32[1024]{0:T(1024)S(1)} %bitcast.222, bf16[680,4096]{1,0:T(8,128)(2,1)S(1)} %get-tuple-element.76, ...), kind=kOutput, calls=%fused_computation.80 | convolution fusion | flops 5709126144 | bytes 19544032 | tf_op jit(solution)/shard_map/rfw,uw->rfu/dot_general | solution.py:98
  271.9 15.5 %convert_reduce_fusion.2 = (f32[1024]{0:T(1024)}, bf16[1024]{0:T(1024)(128)(2,1)}, bf16[1024]{0:T(1024)(128)(2,1)}, f32[1024]{0:T(1024)}, bf16[1,680,1024]{2,1,0:T(8,128)(2,1)S(1)}, /*index=5*/bf16[1,680,1024]{2,1,0:T(8,128)(2,1)}) fusion(f32[1024]{0:T(1024)S(1)} %bitcast.229, bf16[1,680,1024]{2,1,0:T(8,128)(2,1)S(1)} %copy-done.19, ...), kind=kOutput, calls=%fused_computation.93 | convolution fusion | flops 5746028544 | bytes 32111264 | tf_op jit(solution)/shard_map/fyg,gq->fyq/dot_general | solution.py:92
  295.4 4.9 reduce.31
  300.2 14.6 %fusion.70 = f32[16,680,680]{1,2,0:T(8,128)} fusion(f32[680,16,64]{0,2,1:T(8,128)} %bitcast.199, f32[16,64]{1,0:T(8,128)S(1)} %reshape.826, f32[680,16]{0,1:T(8,128)} %copy-done.12, f32[680,16,64]{0,2,1:T(8,128)S(1)} %bitcast.194, f32[16,64]{1,0:T(8,128)S(1)} %reshape.827, f32[680,16]{0,1:T(8,128)} %copy-done.15), kind=kOutput, calls=%fused_computation.120 | convolution fusion | flops 951173120 | bytes 35259392 | tf_op jit(solution)/shard_map/vmap(nkz,vkz->knv)/dot_general | solution.py:110
  314.9 18.0 %bitcast_convert_fusion = (bf16[1,680,16,64]{1,3,2,0:T(8,128)(2,1)}, f32[16,64,680]{2,1,0:T(8,128)}) fusion(bf16[680,16,64]{0,2,1:T(8,128)(2,1)} %bitcast.205, f32[16,680,680]{1,2,0:T(8,128)} %fusion.70, f32[16,680]{1,0:T(8,128)} %reduce.31, pred[680,680]{0,1:T(8,128)(4,1)} %iota_compare_fusion), kind=kOutput, calls=%fused_computation.54 | convolution fusion | flops 977285120 | bytes 35670080 | tf_op jit(solution)/shard_map/vmap(fgs,gfu->sfu)/dot_general | solution.py:124
  332.8 31.7 %multiply_reduce_fusion = (f32[16,680]{1,0:T(8,128)}, f32[16,680,680]{1,2,0:T(8,128)}) fusion(f32[16,680,680]{1,2,0:T(8,128)} %fusion.70, f32[16,680]{1,0:T(8,128)} %reduce.31, pred[680,680]{0,1:T(8,128)(4,1)} %iota_compare_fusion, bf16[680,16,64]{0,2,1:T(8,128)(2,1)} %bitcast.206, bf16[680,16,64]{0,2,1:T(8,128)(2,1)} %bitcast.204), kind=kOutput, calls=%fused_computation.1 | convolution fusion | flops 983976320 | bytes 62521920 | tf_op jit(solution)/shard_map/vmap(nkz,vkz->knv)/dot_general | solution.py:121
  364.6 28.6 %multiply_convert_fusion = bf16[16,680,680]{1,2,0:T(8,128)(2,1)} fusion(f32[16,680,680]{1,2,0:T(8,128)} %get-tuple-element.69, f32[16,680,680]{1,2,0:T(8,128)} %fusion.70, f32[16,680]{1,0:T(8,128)} %get-tuple-element.68, f32[16,680]{1,0:T(8,128)} %reduce.31, pred[680,680]{0,1:T(8,128)(4,1)} %iota_compare_fusion), kind=kLoop, calls=%fused_computation | loop fusion | flops 44390400 | bytes 74533440 | tf_op jit(solution)/shard_map/vmap()/convert_element_type | solution.py:133
  393.2 11.7 %fusion.32 = (f32[680,16]{0,1:T(8,128)S(1)}, f32[16,64,680]{2,1,0:T(8,128)}) fusion(f32[1,680,16,64]{1,3,2,0:T(8,128)S(1)} %bitcast.195, f32[16,64]{1,0:T(8,128)} %broadcast_multiply_fusion.1, bf16[16,680,680]{1,2,0:T(8,128)(2,1)} %multiply_convert_fusion, f32[680,16,64]{0,2,1:T(8,128)} %bitcast.200, f32[16,64]{1,0:T(8,128)S(1)} %reshape.826, ...), kind=kOutput, calls=%fused_computation.62 | convolution fusion | flops 951162240 | bytes 23247872 | tf_op jit(solution)/shard_map/vmap(wcv,vwn->cwn)/dot_general | solution.py:134
  405.0 9.6 %fusion.29 = (f32[16,64]{1,0:T(8,128)}, f32[680,16]{0,1:T(8,128)S(1)}, f32[16,64,680]{2,1,0:T(8,128)S(1)}) fusion(f32[1,680,16,64]{1,3,2,0:T(8,128)S(1)} %bitcast.201, f32[680,16]{0,1:T(8,128)S(1)} %copy-done.13, f32[16,64]{1,0:T(8,128)S(1)} %copy-done.26, bf16[16,680,680]{1,2,0:T(8,128)(2,1)} %multiply_convert_fusion, f32[680,16,64]{0,2,1:T(8,128)S(1)} %bitcast.196, ...), kind=kOutput, calls=%fused_computation.50 | convolution fusion | flops 953946496 | bytes 23295488 | tf_op jit(solution)/shard_map/vmap(fgs,gfu->sfu)/dot_general | solution.py:137
  420.5 10.7 %convolution_convert_fusion.2 = bf16[1024,3072]{1,0:T(8,128)(2,1)} fusion(bf16[680,1024]{0,1:T(8,128)(2,1)S(1)} %bitcast.238, bf16[680,1024]{0,1:T(8,128)(2,1)S(1)} %bitcast.211, bf16[680,1024]{0,1:T(8,128)(2,1)S(1)} %bitcast.208, bf16[1,680,1024]{2,1,0:T(8,128)(2,1)S(1)} %copy-done.3, f32[1024]{0:T(1024)S(1)} %bitcast.232, f32[1024]{0:T(1024)S(1)} %bitcast.215, ...), kind=kOutput, calls=%fused_computation.25 | convolution fusion | flops 4298047488 | bytes 11875648 | tf_op jit(solution)/shard_map/crk,cre->ke/dot_general | solution.py:104
  432.6 14.0 %convolution_convert_fusion = bf16[4096,1024]{1,0:T(8,128)(2,1)} fusion(bf16[1,680,1024]{2,1,0:T(8,128)(2,1)S(1)} %copy-done.20, f32[1024]{0:T(1024)S(1)} %bitcast.230, f32[680,4096]{1,0:T(8,128)} %fusion.13, f32[4096]{0:T(1024)S(1)} %copy-done.54), kind=kOutput, calls=%fused_computation.18 | convolution fusion | flops 5738389504 | bytes 20942848 | tf_op jit(solution)/shard_map/crk,cre->ke/dot_general | solution.py:104
  450.7 10.2 %convolution_convert_fusion.1 = bf16[1024,4096]{1,0:T(8,128)(2,1)S(1)} fusion(bf16[680,4096]{1,0:T(8,128)(2,1)} %copy-done.74, f32[1,680,1024]{2,1,0:T(8,128)S(1)} %copy-done.11, f32[1024]{0:T(1024)S(1)} %bitcast.227, f32[1024]{0:T(1024)S(1)} %bitcast.224, f32[680]{0:T(1024)S(1)} %copy-done.51, f32[680]{0:T(1024)S(1)} %copy-done.34), kind=kOutput, calls=%fused_computation.19 | convolution fusion | flops 5711929344 | bytes 16758080 | tf_op jit(solution)/shard_map/crk,cre->ke/dot_general | solution.py:104
  460.9 7.8 %pad_maximum_fusion = bf16[1024,5120]{1,0:T(8,128)(2,1)} fusion(bf16[1024,1024]{1,0:T(8,128)(2,1)S(1)} %convolution_convert_fusion.3, bf16[1024,4096]{1,0:T(8,128)(2,1)S(1)} %convolution_convert_fusion.1), kind=kLoop, calls=%fused_computation.17 | loop fusion | flops 20971520 | bytes 20971520 | tf_op jit(solution)/shard_map/concatenate | solution.py:298
  470.7 9.9 %fusion.37 = (f32[680]{0:T(1024)S(1)}, f32[680,1024]{1,0:T(8,128)S(1)}) fusion(bf16[1,680,1024]{2,1,0:T(8,128)(2,1)} %param.17, f32[1024]{0:T(1024)S(1)} %bitcast.216, f32[680]{0:T(1024)S(1)} %copy-done.31, bf16[1024,8192]{1,0:T(8,128)(2,1)} %all-gather.8.cloned.1.call-done, bf16[680,1024]{0,1:T(8,128)(2,1)} %bitcast.237, bf16[680,1024]{0,1:T(8,128)(2,1)} %bitcast.210, ...), kind=kOutput, calls=%fused_computation.73 | convolution fusion | flops 4294204672 | bytes 15197504 | tf_op jit(solution)/shard_map/rfw,uw->rfu/dot_general | solution.py:98
  483.6 4.5 all-gather.3
  488.2 23.5 %all-gather.4 = bf16[16,2,6144]{2,1,0:T(2,128)(2,1)} all-gather(bf16[1,2,6144]{2,1,0:T(2,128)(2,1)S(1)} %bitcast.213), channel_id=1, replica_groups=mesh['wide'=16,'narrow'=2] {'wide'}, dimensions={0}, use_global_device_ids=true | all-gather | bytes 417792 | tf_op jit(solution)/shard_map/all_gather | solution.py:144
  520.2 4.4 add_add_fusion.4
  528.0 5.8 all-to-all-start.2
  535.7 5.6 all-to-all-done.2
  544.0 78.2 %reduce-scatter.8.cloned.1.call-done = bf16[256,1024]{1,0:T(8,128)(2,1)} async-done(((bf16[4096,1024]{1,0:T(8,128)(2,1)}), bf16[256,1024]{1,0:T(8,128)(2,1)}) %reduce-scatter.8.cloned.1.call-update) | async-done | bytes 524304 | tf_op jit(solution)/shard_map/reduce_scatter | solution.py:162
  624.7 120.6 %reduce-scatter.6.cloned.1.call-done = bf16[64,5120]{1,0:T(8,128)(2,1)} async-done(((bf16[1024,5120]{1,0:T(8,128)(2,1)}), bf16[64,5120]{1,0:T(8,128)(2,1)}) %reduce-scatter.6.cloned.1.call-update) | async-done | bytes 655376 | tf_op jit(solution)/shard_map/reduce_scatter | solution.py:162
  (272 shorter events, 106.5 us)
Async XLA Ops:
  7.2 37.7 %copy-start = (bf16[32,6144]{1,0:T(8,128)(2,1)S(1)}, bf16[32,6144]{1,0:T(8,128)(2,1)}, u32[]{:S(2)}) copy-start(bf16[32,6144]{1,0:T(8,128)(2,1)} %param.20) | copy-start | bytes 1179652
  7.2 136.8 %all-gather.8.cloned.1.call-start = ((), (), s32[]{:S(2)}) async-start(), calls=%async_computation.6 | async-start | bytes 17301504 | tf_op jit(solution)/shard_map/all_gather | solution.py:216
  9.1 42.0 %copy-start.71 = (s32[10]{0:T(128)S(1)}, s32[10]{0:T(128)}, u32[]{:S(2)}) copy-start(s32[10]{0:T(128)} %param.19) | copy-start | bytes 124
  9.2 44.7 %copy-start.2 = (bf16[1,680,1024]{2,1,0:T(8,128)(2,1)S(1)}, bf16[1,680,1024]{2,1,0:T(8,128)(2,1)}, u32[]{:S(2)}) copy-start(bf16[1,680,1024]{2,1,0:T(8,128)(2,1)} %param.17) | copy-start | bytes 4177924
  9.2 227.4 %all-gather.10.cloned.1.call-start = ((), (), s32[]{:S(2)}) async-start(), calls=%async_computation.7 | async-start | bytes 8650752 | tf_op jit(solution)/shard_map/all_gather | solution.py:223
  46.9 39.3 %all-to-all-start = ((f32[32,1,6144]{2,1,0:T(1,128)}), f32[32,1,6144]{2,1,0:T(1,128)S(1)}, u32[]{:S(2)}, u32[]{:S(2)}) async-start(f32[32,1,6144]{2,1,0:T(1,128)} %copy.93), calls=%async_computation | async-start | bytes 1572864 | tf_op jit(solution)/shard_map/all_to_all | solution.py:230
  49.5 493.0 %reduce-scatter.4.cloned.1.call-start = ((), (), s32[]{:S(2)}) async-start(), calls=%async_computation.8 | async-start | bytes 6684672 | tf_op jit(solution)/shard_map/reduce_scatter | solution.py:162
  54.1 89.9 %copy-start.30 = (f32[680]{0:T(1024)}, f32[680]{0:T(1024)S(1)}, u32[]{:S(2)}) copy-start(f32[680]{0:T(1024)S(1)} %broadcast_multiply_fusion.3) | copy-start | bytes 8164
  54.6 89.4 %copy-start.35 = (f32[680]{0:T(1024)}, f32[680]{0:T(1024)S(1)}, u32[]{:S(2)}) copy-start(f32[680]{0:T(1024)S(1)} %fusion.36) | copy-start | bytes 8164
  54.6 89.4 %copy-start.28 = (f32[680]{0:T(1024)}, f32[680]{0:T(1024)S(1)}, u32[]{:S(2)}) copy-start(f32[680]{0:T(1024)S(1)} %fusion.80) | copy-start | bytes 8164
  87.3 56.7 %copy-start.39 = (f32[1,1024]{1,0:T(1,128)}, f32[1,1024]{1,0:T(1,128)S(1)}, u32[]{:S(2)}) copy-start(f32[1,1024]{1,0:T(1,128)S(1)} %get-tuple-element.56) | copy-start | bytes 12292
  87.3 56.7 %copy-start.63 = (f32[1,1024]{1,0:T(1,128)}, f32[1,1024]{1,0:T(1,128)S(1)}, u32[]{:S(2)}) copy-start(f32[1,1024]{1,0:T(1,128)S(1)} %get-tuple-element.55) | copy-start | bytes 12292
  236.6 19.3 %copy-start.10 = (f32[1,680,1024]{2,1,0:T(8,128)S(1)}, f32[1,680,1024]{2,1,0:T(8,128)}, u32[]{:S(2)}) copy-start(f32[1,680,1024]{2,1,0:T(8,128)} %copy-done.9) | copy-start | bytes 8355844
  236.6 19.3 %copy-start.33 = (f32[680]{0:T(1024)S(1)}, f32[680]{0:T(1024)}, u32[]{:S(2)}) copy-start(f32[680]{0:T(1024)} %copy-done.32) | copy-start | bytes 8164
  236.6 19.3 %copy-start.45 = (f32[1,1024]{1,0:T(1,128)S(1)}, f32[1,1024]{1,0:T(1,128)}, u32[]{:S(2)}) copy-start(f32[1,1024]{1,0:T(1,128)} %get-tuple-element.54) | copy-start | bytes 12292
  236.6 19.3 %copy-start.50 = (f32[680]{0:T(1024)S(1)}, f32[680]{0:T(1024)}, u32[]{:S(2)}) copy-start(f32[680]{0:T(1024)} %copy-done.49) | copy-start | bytes 8164
  255.9 11.7 %copy-start.74 = (bf16[680,4096]{1,0:T(8,128)(2,1)}, bf16[680,4096]{1,0:T(8,128)(2,1)S(1)}, u32[]{:S(2)}) copy-start(bf16[680,4096]{1,0:T(8,128)(2,1)S(1)} %get-tuple-element.76) | copy-start | bytes 16711684
  255.9 11.7 %copy-start.38 = (f32[680]{0:T(1024)S(1)}, f32[680]{0:T(1024)}, u32[]{:S(2)}) copy-start(f32[680]{0:T(1024)} %copy-done.37) | copy-start | bytes 8164
  269.2 18.2 %copy-start.6 = (f32[1,680,1024]{2,1,0:T(8,128)}, f32[1,680,1024]{2,1,0:T(8,128)S(1)}, u32[]{:S(2)}) copy-start(f32[1,680,1024]{2,1,0:T(8,128)S(1)} %get-tuple-element.34) | copy-start | bytes 8355844
  269.2 18.2 %copy-start.47 = (f32[680]{0:T(1024)}, f32[680]{0:T(1024)S(1)}, u32[]{:S(2)}) copy-start(f32[680]{0:T(1024)S(1)} %negate_multiply_fusion.1) | copy-start | bytes 8164
  393.2 11.8 %copy-start.1 = (f32[1,680,1024]{1,2,0:T(8,128)S(1)}, f32[1,680,1024]{1,2,0:T(8,128)}, u32[]{:S(2)}) copy-start(f32[1,680,1024]{1,2,0:T(8,128)} %copy.96) | copy-start | bytes 8355844
  393.2 11.8 %copy-start.13 = (f32[680,16]{0,1:T(8,128)S(1)}, f32[680,16]{0,1:T(8,128)}, u32[]{:S(2)}) copy-start(f32[680,16]{0,1:T(8,128)} %copy-done.12) | copy-start | bytes 130564
  393.2 11.8 %copy-start.16 = (f32[680,16]{0,1:T(8,128)S(1)}, f32[680,16]{0,1:T(8,128)}, u32[]{:S(2)}) copy-start(f32[680,16]{0,1:T(8,128)} %copy-done.15) | copy-start | bytes 130564
  393.2 11.7 %copy-start.26 = (f32[16,64]{1,0:T(8,128)S(1)}, f32[16,64]{1,0:T(8,128)}, u32[]{:S(2)}) copy-start(f32[16,64]{1,0:T(8,128)} %broadcast_multiply_fusion) | copy-start | bytes 12292
  431.3 190.9 %reduce-scatter.8.cloned.1.call-start = ((), (), s32[]{:S(2)}) async-start(), calls=%async_computation.10 | async-start | bytes 8912896 | tf_op jit(solution)/shard_map/reduce_scatter | solution.py:162
  446.6 298.6 %reduce-scatter.6.cloned.1.call-start = ((), (), s32[]{:S(2)}) async-start(), calls=%async_computation.9 | async-start | bytes 11141120 | tf_op jit(solution)/shard_map/reduce_scatter | solution.py:162
  480.9 39.3 %copy-start.48 = (f32[680]{0:T(1024)S(1)}, f32[680]{0:T(1024)}, u32[]{:S(2)}) copy-start(f32[680]{0:T(1024)} %copy-done.47) | copy-start | bytes 8164
  515.4 12.5 %all-to-all-start.1 = ((f32[32,1,32]{2,1,0:T(1,128)}), f32[32,1,32]{2,1,0:T(1,128)S(1)}, u32[]{:S(2)}, u32[]{:S(2)}) async-start(f32[32,1,32]{2,1,0:T(1,128)} %bitcast.48), calls=%async_computation.1 | async-start | bytes 32768 | tf_op jit(solution)/shard_map/all_to_all | solution.py:385
  528.0 13.3 %all-to-all-start.2 = ((f32[32,1,320]{2,1,0:T(1,128)}), f32[32,1,320]{2,1,0:T(1,128)S(1)}, u32[]{:S(2)}, u32[]{:S(2)}) async-start(f32[32,1,320]{2,1,0:T(1,128)} %reshape.817), calls=%async_computation.3 | async-start | bytes 98304 | tf_op jit(solution)/shard_map/all_to_all | solution.py:168
  543.5 204.3 %collective-permute-start = (bf16[32,3072]{1,0:T(8,128)(2,1)S(1)}, bf16[32,3072]{1,0:T(8,128)(2,1)S(1)}, u32[]{:S(2)}, u32[]{:S(2)}) collective-permute-start(bf16[32,3072]{1,0:T(8,128)(2,1)S(1)} %constant_dynamic-slice_fusion.2), channel_id=1, source_target_pairs={{0,1},{1,0},{2,3},{3,2},{4,5},{5,4},{6,7},{7,6},{8,9},{9,8},{10,11... | collective-permute-start | bytes 589832 | tf_op jit(solution)/shard_map/ppermute | solution.py:157
  623.1 126.4 %collective-permute-start.2 = (bf16[128,1024]{1,0:T(8,128)(2,1)S(1)}, bf16[128,1024]{1,0:T(8,128)(2,1)S(1)}, u32[]{:S(2)}, u32[]{:S(2)}) collective-permute-start(bf16[128,1024]{1,0:T(8,128)(2,1)S(1)} %constant_dynamic-slice_fusion), channel_id=1, source_target_pairs={{0,1},{1,0},{2,3},{3,2},{4,5},{5,4},{6,7},{7,6},{8,9},{9,8},{10,11... | collective-permute-start | bytes 786440 | tf_op jit(solution)/shard_map/ppermute | solution.py:157
  746.2 9.1 %collective-permute-start.1 = (bf16[32,5120]{1,0:T(8,128)(2,1)S(1)}, bf16[32,5120]{1,0:T(8,128)(2,1)S(1)}, u32[]{:S(2)}, u32[]{:S(2)}) collective-permute-start(bf16[32,5120]{1,0:T(8,128)(2,1)S(1)} %constant_dynamic-slice_fusion.1), channel_id=1, source_target_pairs={{0,1},{1,0},{2,3},{3,2},{4,5},{5,4},{6,7},{7,6},{8,9},{9,8},{10,11... | collective-permute-start | bytes 983048 | tf_op jit(solution)/shard_map/ppermute | solution.py:157
  (55 other events, 194.7 us)
Sparse Core Ops, SparseCore 0:
  11.6 132.3 all-gather.7
  147.0 75.2 all-gather.9
  431.4 84.0 reduce-scatter.3
  519.4 102.7 reduce-scatter.7
  626.1 119.1 reduce-scatter.5

commit v11 on v7

--- a/solution.py
+++ b/solution.py
@@ -254,9 +254,7 @@
     attended_grad = (middle_grad * gamma_attn[:, None, :]).astype(jnp.bfloat16)
     proj_grad = weight_grad(context, attended_grad)
     proj_bias_grad = jnp.sum(attended_grad.astype(jnp.float32), axis=(0, 1))
-    both_sum = scatter_natural(jnp.concatenate([up_grad, proj_grad], axis=1))
-    up_sum = both_sum[:, : up_grad.shape[1]]
-    proj_sum = both_sum[:, up_grad.shape[1] :]
+    up_sum = scatter_natural(up_grad)
     context_gradient = (
         matmul_back(attended_grad, proj_full).astype(jnp.bfloat16).reshape(head_shape)
     )
@@ -274,7 +272,9 @@
         jnp.bfloat16
     )
     qkv_grad = weight_grad(normed_attn, projected_grad)
-    qkv_sum = scatter_natural(qkv_grad)
+    both_sum = scatter_natural(jnp.concatenate([qkv_grad, proj_grad], axis=1))
+    qkv_sum = both_sum[:, : qkv_grad.shape[1]]
+    proj_sum = both_sum[:, qkv_grad.shape[1] :]
     (
         query_bias_sum,
         value_bias_sum,

time: 730 us -> 600 us (0.82)
  waiting for transfers between devices: 297 us -> 162 us
    reduce_scatter x3, waiting for transfers between devices: 199 us -> 62.5 us  [scatter_natural(): lax.psum_scatter(member.astype(jnp.bfloat16), 'wide', scatter_dimension=0...]
  transfers between devices with their start and end apart: 11 -> 11, of which waited for: 6 -> 5; matrix products, arithmetic and copies ran while one was open for 24% -> 51% of each run, Pallas kernels for 0% -> 0%
where the time goes in v11:
time: 600 us; the launch traced here: 596 us
  matrix products  220 us (37%)
  waiting for transfers between devices  162 us (27%)
  other arithmetic  86.8 us (14%)
  blocking collectives  57.5 us (10%)
  local copies, waits for them, and re-layouts  39 us (6%)
  between operations  15.1 us (3%)
  starting transfers between devices  14.9 us (2%)
    reduce_scatter x3, waiting for transfers between devices, scatter_natural(): lax.psum_scatter(member.astype(jnp.bfloat16), 'wide', scatter_dimension=0...  62.5 us
    all_gather x1, waiting for transfers between devices, layer(): lax.all_gather(jnp.concatenate([w_qkv, w_proj, w_up], axis=1), AXES, axis...  56.7 us
    all_gather x2, blocking collectives, nested_gather(): lax.all_gather(lax.all_gather(member, 'narrow', axis=0, tiled=True), 'wid...  47.7 us
    dot_general x4, matrix products, matmul_back(): jnp.einsum('rfw,uw->rfu', first_operand, second_operand, preferred_elemen...  43.4 us
    dot_general x4, matrix products, matmul_rows(): jnp.einsum('fyg,gq->fyq', first_operand, second_operand, preferred_elemen...  42.2 us
    dot_general x4, matrix products, weight_grad(): jnp.einsum('crk,cre->ke', first_operand, second_operand, preferred_elemen...  37.1 us
    all_to_all x1, waiting for transfers between devices, layer(): lax.all_to_all(ada_partial.reshape(count, sequences, ada_cols), AXES, spl...  32 us
    convert_element_type x1, other arithmetic, attend_backward(): score_gradient = (attention_probabilities * (prob_grad - jnp.sum(prob_gra...  28.4 us
  transfers between devices with their start and end apart: 11, of which 5 were waited for; matrix products, arithmetic and copies ran while one was open for 51% of the time, Pallas kernels for 0%

profile of v11, /device:TPU:0, one launch (start us, length us, event | category | flops | bytes accessed | tf_op | source)
XLA Modules:
  0.0 595.5 jit_solution(15125779799570789294)
XLA Ops:
  11.2 5.4 concatenate.51
  16.7 5.3 all-gather.1
  22.0 22.8 %all-gather.2 = bf16[16,2,1536]{2,1,0:T(2,128)(2,1)S(1)} all-gather(bf16[1,2,1536]{2,1,0:T(2,128)(2,1)S(1)} %bitcast.211), channel_id=1, replica_groups=mesh['wide'=16,'narrow'=2] {'wide'}, dimensions={0}, use_global_device_ids=true | all-gather | bytes 104448 | tf_op jit(solution)/shard_map/all_gather | solution.py:109
  54.2 32.0 %all-to-all-done = f32[32,1,6144]{2,1,0:T(1,128)S(1)} async-done(((f32[32,1,6144]{2,1,0:T(1,128)}), f32[32,1,6144]{2,1,0:T(1,128)S(1)}, u32[]{:S(2)}, u32[]{:S(2)}) %all-to-all-start) | async-done | bytes 786464 | tf_op jit(solution)/shard_map/all_to_all | solution.py:195
  87.3 56.7 %all-gather.8.cloned.1.call-done = bf16[1024,8192]{1,0:T(8,128)(2,1)} async-done(((bf16[32,8192]{1,0:T(8,128)(2,1)}), bf16[1024,8192]{1,0:T(8,128)(2,1)}) %all-gather.8.cloned.1.call-update) | async-done | bytes 16777232 | tf_op jit(solution)/shard_map/all_gather | solution.py:181
  144.0 7.8 %fusion.21 = f32[1,680,3072]{2,1,0:T(8,128)S(1)} fusion(bf16[1024,8192]{1,0:T(8,128)(2,1)} %all-gather.8.cloned.1.call-done, bf16[1,680,1024]{2,1,0:T(8,128)(2,1)S(1)} %copy-done.5, f32[1024]{0:T(1024)S(1)} %bitcast.217, f32[1024]{0:T(1024)S(1)} %bitcast.205, f32[680]{0:T(1024)S(1)} %fusion.78, f32[680]{0:T(1024)S(1)} %broadcast_multiply_fusion.3), kind=kOutput, calls=%fused_computation.35 | convolution fusion | flops 4282368000 | bytes 16053568 | tf_op jit(solution)/shard_map/fyg,gq->fyq/dot_general | solution.py:45
  166.2 14.0 %fusion.94 = (f32[16,680]{1,0:T(8,128)S(1)}, f32[16,680,680]{1,2,0:T(8,128)}) fusion(f32[680,16,64]{0,2,1:T(8,128)S(1)} %bitcast.191, f32[16,64]{1,0:T(8,128)S(1)} %reshape.836, f32[680,16]{0,1:T(8,128)S(1)} %get-tuple-element.76, f32[680,16,64]{0,2,1:T(8,128)S(1)} %bitcast.185, f32[16,64]{1,0:T(8,128)S(1)} %reshape.835, ...), kind=kOutput, calls=%fused_computation.190 | convolution fusion | flops 973357440 | bytes 35765312 | tf_op jit(solution)/shard_map/vmap(nkz,vkz->knv)/dot_general | solution.py:63
  180.3 13.4 %fusion = f32[16,680]{1,0:T(8,128)S(1)} fusion(f32[16,680,680]{1,2,0:T(8,128)} %get-tuple-element.61, f32[16,680]{1,0:T(8,128)S(1)} %get-tuple-element.60), kind=kLoop, calls=%fused_computation.6 | loop fusion | flops 14785920 | bytes 29680640 | tf_op jit(solution)/shard_map/vmap()/reduce_sum | solution.py:73
  193.8 15.4 %fusion.51 = bf16[16,64,680]{2,1,0:T(8,128)(2,1)} fusion(bf16[680,16,64]{0,2,1:T(8,128)(2,1)S(1)} %bitcast.195, f32[16,680,680]{1,2,0:T(8,128)} %get-tuple-element.61, f32[16,680]{1,0:T(8,128)S(1)} %fusion, f32[16,680]{1,0:T(8,128)S(1)} %get-tuple-element.60), kind=kOutput, calls=%fused_computation.104 | convolution fusion | flops 969886720 | bytes 32465920 | tf_op jit(solution)/shard_map/vmap(wcv,vwn->cwn)/dot_general | solution.py:75
  209.2 5.5 fusion.91
  215.2 12.5 %fusion.15 = f32[680,4096]{1,0:T(8,128)} fusion(bf16[1024,8192]{1,0:T(8,128)(2,1)} %all-gather.8.cloned.1.call-done, f32[1,680,1024]{2,1,0:T(8,128)S(1)} %get-tuple-element.32, f32[1024]{0:T(1024)S(1)} %bitcast.224, f32[1024]{0:T(1024)S(1)} %bitcast.212, f32[680]{0:T(1024)S(1)} %fusion.79, f32[680]{0:T(1024)S(1)} %broadcast_multiply_fusion.2), kind=kOutput, calls=%fused_computation.27 | convolution fusion | flops 5707735040 | bytes 22328640 | tf_op jit(solution)/shard_map/fyg,gq->fyq/dot_general | solution.py:45
  227.7 17.6 %convert_reduce_fusion = (f32[4096]{0:T(1024)}, bf16[680,4096]{1,0:T(8,128)(2,1)S(1)}) fusion(f32[680,4096]{1,0:T(8,128)} %fusion.15, f32[4096]{0:T(1024)S(1)} %copy-done.47, bf16[4096,1024]{1,0:T(8,128)(2,1)} %all-gather.10.cloned.1.call-done, f32[1024]{0:T(1024)S(1)} %bitcast.219, bf16[1,680,1024]{2,1,0:T(8,128)(2,1)} %param.33), kind=kOutput, calls=%fused_computation.20 | convolution fusion | flops 5770399744 | bytes 26529792 | tf_op jit(solution)/shard_map/rfw,uw->rfu/dot_general | solution.py:51
  247.9 9.8 %convolution_convert_fusion.1 = bf16[1024,4096]{1,0:T(8,128)(2,1)} fusion(bf16[680,4096]{1,0:T(8,128)(2,1)S(1)} %get-tuple-element.74, f32[1,680,1024]{2,1,0:T(8,128)S(1)} %get-tuple-element.32, f32[1024]{0:T(1024)S(1)} %bitcast.225, f32[1024]{0:T(1024)S(1)} %bitcast.213, f32[680]{0:T(1024)S(1)} %fusion.79, f32[680]{0:T(1024)S(1)} %broadcast_multiply_fusion.2), kind=kOutput, calls=%fused_computation.24 | convolution fusion | flops 5711929344 | bytes 16758080 | tf_op jit(solution)/shard_map/crk,cre->ke/dot_general | solution.py:57
  259.7 11.5 %fusion.43 = (bf16[1024]{0:T(1024)(128)(2,1)}, f32[680]{0:T(1024)S(1)}, f32[680,1024]{1,0:T(8,128)S(1)}) fusion(f32[1,680,1024]{2,1,0:T(8,128)S(1)} %get-tuple-element.32, f32[680]{0:T(1024)S(1)} %fusion.79, f32[680]{0:T(1024)S(1)} %broadcast_multiply_fusion.2, f32[1024]{0:T(1024)S(1)} %bitcast.214, bf16[680,4096]{1,0:T(8,128)(2,1)} %copy-done.64, ...), kind=kOutput, calls=%fused_computation.85 | convolution fusion | flops 5709126144 | bytes 19544032 | tf_op jit(solution)/shard_map/rfw,uw->rfu/dot_general | solution.py:51
  275.8 16.3 %convert_reduce_fusion.2 = (f32[1024]{0:T(1024)}, bf16[1024]{0:T(1024)(128)(2,1)}, bf16[1024]{0:T(1024)(128)(2,1)}, f32[1024]{0:T(1024)}, bf16[1,680,1024]{2,1,0:T(8,128)(2,1)S(1)}, /*index=5*/bf16[1,680,1024]{2,1,0:T(8,128)(2,1)}) fusion(f32[1024]{0:T(1024)S(1)} %bitcast.220, bf16[1,680,1024]{2,1,0:T(8,128)(2,1)S(1)} %copy-done.21, ...), kind=kOutput, calls=%fused_computation.92 | convolution fusion | flops 5746028544 | bytes 32111264 | tf_op jit(solution)/shard_map/fyg,gq->fyq/dot_general | solution.py:45
  293.1 4.5 fusion.52
  300.0 13.9 %convolution_convert_fusion = bf16[4096,1024]{1,0:T(8,128)(2,1)} fusion(bf16[1,680,1024]{2,1,0:T(8,128)(2,1)S(1)} %copy-done.22, f32[1024]{0:T(1024)S(1)} %bitcast.221, f32[680,4096]{1,0:T(8,128)} %fusion.15, f32[4096]{0:T(1024)S(1)} %copy-done.47), kind=kOutput, calls=%fused_computation.23 | convolution fusion | flops 5738389504 | bytes 20942848 | tf_op jit(solution)/shard_map/crk,cre->ke/dot_general | solution.py:57
  315.4 26.3 %multiply_reduce_fusion = (f32[16,680]{1,0:T(8,128)}, f32[16,680,680]{1,2,0:T(8,128)}) fusion(f32[16,680,680]{1,2,0:T(8,128)} %get-tuple-element.61, f32[16,680]{1,0:T(8,128)} %log_add_fusion, bf16[680,16,64]{0,2,1:T(8,128)(2,1)S(1)} %bitcast.193, bf16[680,16,64]{0,2,1:T(8,128)(2,1)S(1)} %bitcast.196), kind=kOutput, calls=%fused_computation.1 | convolution fusion | flops 969179520 | bytes 62059520 | tf_op jit(solution)/shard_map/vmap(nkz,vkz->knv)/dot_general | solution.py:86
  341.6 28.4 %multiply_convert_fusion = bf16[16,680,680]{1,2,0:T(8,128)(2,1)} fusion(f32[16,680,680]{1,2,0:T(8,128)} %get-tuple-element.67, f32[16,680,680]{1,2,0:T(8,128)} %get-tuple-element.61, f32[16,680]{1,0:T(8,128)} %get-tuple-element.66, f32[16,680]{1,0:T(8,128)} %log_add_fusion), kind=kLoop, calls=%fused_computation | loop fusion | flops 29593600 | bytes 74071040 | tf_op jit(solution)/shard_map/vmap()/convert_element_type | solution.py:98
  370.1 12.2 %fusion.31 = (f32[16,64]{1,0:T(8,128)}, f32[680,16]{0,1:T(8,128)S(1)}, f32[16,64,680]{2,1,0:T(8,128)S(1)}) fusion(f32[1,680,16,64]{1,3,2,0:T(8,128)} %bitcast.190, f32[680,16]{0,1:T(8,128)} %copy-done.15, f32[16,64]{1,0:T(8,128)} %broadcast_multiply_fusion, bf16[16,680,680]{1,2,0:T(8,128)(2,1)} %multiply_convert_fusion, f32[680,16,64]{0,2,1:T(8,128)S(1)} %bitcast.186, ...), kind=kOutput, calls=%fused_computation.55 | convolution fusion | flops 953946496 | bytes 23295488 | tf_op jit(solution)/shard_map/vmap(fgs,gfu->sfu)/dot_general | solution.py:102
  382.4 8.5 %fusion.34 = (f32[680,16]{0,1:T(8,128)S(1)}, f32[16,64,680]{2,1,0:T(8,128)S(1)}) fusion(f32[1,680,16,64]{1,3,2,0:T(8,128)S(1)} %bitcast.187, f32[16,64]{1,0:T(8,128)S(1)} %copy-done.30, bf16[16,680,680]{1,2,0:T(8,128)(2,1)} %multiply_convert_fusion, f32[680,16,64]{0,2,1:T(8,128)S(1)} %bitcast.192, f32[16,64]{1,0:T(8,128)S(1)} %reshape.836, ...), kind=kOutput, calls=%fused_computation.67 | convolution fusion | flops 951162240 | bytes 23247872 | tf_op jit(solution)/shard_map/vmap(wcv,vwn->cwn)/dot_general | solution.py:99
  399.2 16.5 %bitcast_convert_fusion = (bf16[1,680,16,64]{1,3,2,0:T(8,128)(2,1)}, f32[16,64,680]{2,1,0:T(8,128)}) fusion(bf16[680,16,64]{0,2,1:T(8,128)(2,1)} %bitcast.194, f32[16,680,680]{1,2,0:T(8,128)} %get-tuple-element.61, f32[16,680]{1,0:T(8,128)} %log_add_fusion), kind=kOutput, calls=%fused_computation.59 | convolution fusion | flops 962488320 | bytes 35207680 | tf_op jit(solution)/shard_map/vmap(fgs,gfu->sfu)/dot_general | solution.py:89
  415.8 10.3 %convolution_convert_fusion.2 = bf16[1024,3072]{1,0:T(8,128)(2,1)} fusion(bf16[680,1024]{0,1:T(8,128)(2,1)} %bitcast.201, bf16[680,1024]{0,1:T(8,128)(2,1)} %bitcast.199, bf16[680,1024]{0,1:T(8,128)(2,1)S(1)} %bitcast.198, bf16[1,680,1024]{2,1,0:T(8,128)(2,1)S(1)} %copy-done.7, f32[1024]{0:T(1024)S(1)} %bitcast.218, f32[1024]{0:T(1024)S(1)} %bitcast.206, ...), kind=kOutput, calls=%fused_computation.30 | convolution fusion | flops 4298047488 | bytes 11875648 | tf_op jit(solution)/shard_map/crk,cre->ke/dot_general | solution.py:57
  426.1 7.7 %pad_maximum_fusion = bf16[1024,4096]{1,0:T(8,128)(2,1)} fusion(bf16[1024,1024]{1,0:T(8,128)(2,1)} %convolution_convert_fusion.3, bf16[1024,3072]{1,0:T(8,128)(2,1)} %convolution_convert_fusion.2), kind=kLoop, calls=%fused_computation.22 | loop fusion | flops 16777216 | bytes 16777216 | tf_op jit(solution)/shard_map/concatenate | solution.py:275
  435.8 9.9 %fusion.39 = (f32[680]{0:T(1024)S(1)}, f32[680,1024]{1,0:T(8,128)S(1)}) fusion(bf16[1,680,1024]{2,1,0:T(8,128)(2,1)} %param.17, f32[1024]{0:T(1024)S(1)} %bitcast.207, f32[680]{0:T(1024)S(1)} %copy-done.37, bf16[1024,8192]{1,0:T(8,128)(2,1)} %all-gather.8.cloned.1.call-done, bf16[680,1024]{0,1:T(8,128)(2,1)} %bitcast.202, bf16[680,1024]{0,1:T(8,128)(2,1)} %bitcast.200, ...), kind=kOutput, calls=%fused_computation.78 | convolution fusion | flops 4294204672 | bytes 15197504 | tf_op jit(solution)/shard_map/rfw,uw->rfu/dot_general | solution.py:51
  448.8 4.5 all-gather.3
  453.4 24.9 %all-gather.4 = bf16[16,2,6144]{2,1,0:T(2,128)(2,1)} all-gather(bf16[1,2,6144]{2,1,0:T(2,128)(2,1)S(1)} %bitcast.204), channel_id=1, replica_groups=mesh['wide'=16,'narrow'=2] {'wide'}, dimensions={0}, use_global_device_ids=true | all-gather | bytes 417792 | tf_op jit(solution)/shard_map/all_gather | solution.py:109
  486.9 5.0 add_add_fusion.4
  495.2 5.8 all-to-all-start.2
  502.9 5.7 all-to-all-done.2
  514.0 62.5 %reduce-scatter.4.cloned.1.call-done = bf16[64,4096]{1,0:T(8,128)(2,1)} async-done(((bf16[1024,4096]{1,0:T(8,128)(2,1)}), bf16[64,4096]{1,0:T(8,128)(2,1)}) %reduce-scatter.4.cloned.1.call-update) | async-done | bytes 524304 | tf_op jit(solution)/shard_map/reduce_scatter | solution.py:127
  580.8 4.4 collective-permute-done
  (246 shorter events, 83.5 us)
Async XLA Ops:
  7.2 37.7 %copy-start = (bf16[32,6144]{1,0:T(8,128)(2,1)S(1)}, bf16[32,6144]{1,0:T(8,128)(2,1)}, u32[]{:S(2)}) copy-start(bf16[32,6144]{1,0:T(8,128)(2,1)} %param.20) | copy-start | bytes 1179652
  7.2 136.8 %all-gather.8.cloned.1.call-start = ((), (), s32[]{:S(2)}) async-start(), calls=%async_computation.6 | async-start | bytes 17301504 | tf_op jit(solution)/shard_map/all_gather | solution.py:181
  9.1 41.1 %copy-start.61 = (s32[10]{0:T(128)S(1)}, s32[10]{0:T(128)}, u32[]{:S(2)}) copy-start(s32[10]{0:T(128)} %param.19) | copy-start | bytes 124
  9.2 42.4 %copy-start.5 = (bf16[1,680,1024]{2,1,0:T(8,128)(2,1)S(1)}, bf16[1,680,1024]{2,1,0:T(8,128)(2,1)}, u32[]{:S(2)}) copy-start(bf16[1,680,1024]{2,1,0:T(8,128)(2,1)} %param.17) | copy-start | bytes 4177924
  9.2 218.6 %all-gather.10.cloned.1.call-start = ((), (), s32[]{:S(2)}) async-start(), calls=%async_computation.7 | async-start | bytes 8650752 | tf_op jit(solution)/shard_map/all_gather | solution.py:188
  46.9 39.3 %all-to-all-start = ((f32[32,1,6144]{2,1,0:T(1,128)}), f32[32,1,6144]{2,1,0:T(1,128)S(1)}, u32[]{:S(2)}, u32[]{:S(2)}) async-start(f32[32,1,6144]{2,1,0:T(1,128)} %copy.87), calls=%async_computation | async-start | bytes 1572864 | tf_op jit(solution)/shard_map/all_to_all | solution.py:195
  49.5 460.3 %reduce-scatter.6.cloned.1.call-start = ((), (), s32[]{:S(2)}) async-start(), calls=%async_computation.9 | async-start | bytes 8912896 | tf_op jit(solution)/shard_map/reduce_scatter | solution.py:127
  51.8 92.1 %copy-start.36 = (f32[680]{0:T(1024)}, f32[680]{0:T(1024)S(1)}, u32[]{:S(2)}) copy-start(f32[680]{0:T(1024)S(1)} %broadcast_multiply_fusion.3) | copy-start | bytes 8164
  52.3 91.6 %copy-start.38 = (f32[680]{0:T(1024)}, f32[680]{0:T(1024)S(1)}, u32[]{:S(2)}) copy-start(f32[680]{0:T(1024)S(1)} %fusion.38) | copy-start | bytes 8164
  52.4 91.6 %copy-start.33 = (f32[680]{0:T(1024)}, f32[680]{0:T(1024)S(1)}, u32[]{:S(2)}) copy-start(f32[680]{0:T(1024)S(1)} %fusion.78) | copy-start | bytes 8164
  87.3 56.7 %copy-start.40 = (f32[1,1024]{1,0:T(1,128)}, f32[1,1024]{1,0:T(1,128)S(1)}, u32[]{:S(2)}) copy-start(f32[1,1024]{1,0:T(1,128)S(1)} %get-tuple-element.52) | copy-start | bytes 12292
  87.3 56.7 %copy-start.52 = (f32[1,1024]{1,0:T(1,128)}, f32[1,1024]{1,0:T(1,128)S(1)}, u32[]{:S(2)}) copy-start(f32[1,1024]{1,0:T(1,128)S(1)} %get-tuple-element.51) | copy-start | bytes 12292
  193.7 15.4 %copy-start.6 = (bf16[1,680,1024]{2,1,0:T(8,128)(2,1)S(1)}, bf16[1,680,1024]{2,1,0:T(8,128)(2,1)}, u32[]{:S(2)}) copy-start(bf16[1,680,1024]{2,1,0:T(8,128)(2,1)} %param.17) | copy-start | bytes 4177924
  193.7 15.4 %copy-start.54 = (f32[1024]{0:T(1024)S(1)}, f32[1024]{0:T(1024)}, u32[]{:S(2)}) copy-start(f32[1024]{0:T(1024)} %reshape.837) | copy-start | bytes 12292
  257.7 253.6 %reduce-scatter.8.cloned.1.call-start = ((), (), s32[]{:S(2)}) async-start(), calls=%async_computation.10 | async-start | bytes 8912896 | tf_op jit(solution)/shard_map/reduce_scatter | solution.py:127
  272.7 19.4 %copy-start.10 = (f32[1,680,1024]{2,1,0:T(8,128)}, f32[1,680,1024]{2,1,0:T(8,128)S(1)}, u32[]{:S(2)}) copy-start(f32[1,680,1024]{2,1,0:T(8,128)S(1)} %get-tuple-element.30) | copy-start | bytes 8355844
  272.7 19.4 %copy-start.44 = (f32[680]{0:T(1024)}, f32[680]{0:T(1024)S(1)}, u32[]{:S(2)}) copy-start(f32[680]{0:T(1024)S(1)} %negate_multiply_fusion.1) | copy-start | bytes 8164
  314.0 262.5 %reduce-scatter.4.cloned.1.call-start = ((), (), s32[]{:S(2)}) async-start(), calls=%async_computation.8 | async-start | bytes 8912896 | tf_op jit(solution)/shard_map/reduce_scatter | solution.py:127
  341.6 28.4 %copy-start.2 = (f32[1,680,1024]{1,2,0:T(8,128)S(1)}, f32[1,680,1024]{1,2,0:T(8,128)}, u32[]{:S(2)}) copy-start(f32[1,680,1024]{1,2,0:T(8,128)} %copy-done.1) | copy-start | bytes 8355844
  399.2 16.6 %copy-start.7 = (bf16[1,680,1024]{2,1,0:T(8,128)(2,1)S(1)}, bf16[1,680,1024]{2,1,0:T(8,128)(2,1)}, u32[]{:S(2)}) copy-start(bf16[1,680,1024]{2,1,0:T(8,128)(2,1)} %param.17) | copy-start | bytes 4177924
  399.2 16.6 %copy-start.20 = (bf16[1,680,16,64]{1,3,2,0:T(8,128)(2,1)S(1)}, bf16[1,680,16,64]{1,3,2,0:T(8,128)(2,1)}, u32[]{:S(2)}) copy-start(bf16[1,680,16,64]{1,3,2,0:T(8,128)(2,1)} %get-tuple-element.40) | copy-start | bytes 4177924
  399.2 16.6 %copy-start.34 = (f32[680]{0:T(1024)S(1)}, f32[680]{0:T(1024)}, u32[]{:S(2)}) copy-start(f32[680]{0:T(1024)} %copy-done.33) | copy-start | bytes 8164
  399.2 16.6 %copy-start.37 = (f32[680]{0:T(1024)S(1)}, f32[680]{0:T(1024)}, u32[]{:S(2)}) copy-start(f32[680]{0:T(1024)} %copy-done.36) | copy-start | bytes 8164
  399.2 16.6 %copy-start.41 = (f32[1,1024]{1,0:T(1,128)S(1)}, f32[1,1024]{1,0:T(1,128)}, u32[]{:S(2)}) copy-start(f32[1,1024]{1,0:T(1,128)} %copy-done.40) | copy-start | bytes 12292
  399.2 16.6 %copy-start.53 = (f32[1,1024]{1,0:T(1,128)S(1)}, f32[1,1024]{1,0:T(1,128)}, u32[]{:S(2)}) copy-start(f32[1,1024]{1,0:T(1,128)} %copy-done.52) | copy-start | bytes 12292
  445.9 41.0 %copy-start.45 = (f32[680]{0:T(1024)S(1)}, f32[680]{0:T(1024)}, u32[]{:S(2)}) copy-start(f32[680]{0:T(1024)} %copy-done.44) | copy-start | bytes 8164
  482.0 13.1 %all-to-all-start.1 = ((f32[32,1,32]{2,1,0:T(1,128)}), f32[32,1,32]{2,1,0:T(1,128)S(1)}, u32[]{:S(2)}, u32[]{:S(2)}) async-start(f32[32,1,32]{2,1,0:T(1,128)} %bitcast.46), calls=%async_computation.1 | async-start | bytes 32768 | tf_op jit(solution)/shard_map/all_to_all | solution.py:344
  495.2 13.4 %all-to-all-start.2 = ((f32[32,1,320]{2,1,0:T(1,128)}), f32[32,1,320]{2,1,0:T(1,128)S(1)}, u32[]{:S(2)}, u32[]{:S(2)}) async-start(f32[32,1,320]{2,1,0:T(1,128)} %reshape.831), calls=%async_computation.3 | async-start | bytes 98304 | tf_op jit(solution)/shard_map/all_to_all | solution.py:133
  510.8 68.2 %collective-permute-start.1 = (bf16[32,4096]{1,0:T(8,128)(2,1)S(1)}, bf16[32,4096]{1,0:T(8,128)(2,1)S(1)}, u32[]{:S(2)}, u32[]{:S(2)}) collective-permute-start(bf16[32,4096]{1,0:T(8,128)(2,1)S(1)} %constant_dynamic-slice_fusion.1), channel_id=1, source_target_pairs={{0,1},{1,0},{2,3},{3,2},{4,5},{5,4},{6,7},{7,6},{8,9},{9,8},{10,11... | collective-permute-start | bytes 786440 | tf_op jit(solution)/shard_map/ppermute | solution.py:122
  511.3 76.3 %copy-start.23 = (bf16[256,1024]{1,0:T(8,128)(2,1)S(1)}, bf16[256,1024]{1,0:T(8,128)(2,1)}, u32[]{:S(2)}) copy-start(bf16[256,1024]{1,0:T(8,128)(2,1)} %reduce-scatter.8.cloned.1.call-done) | copy-start | bytes 1572868
  512.4 75.3 %collective-permute-start.2 = (bf16[128,1024]{1,0:T(8,128)(2,1)S(1)}, bf16[128,1024]{1,0:T(8,128)(2,1)S(1)}, u32[]{:S(2)}, u32[]{:S(2)}) collective-permute-start(bf16[128,1024]{1,0:T(8,128)(2,1)S(1)} %constant_dynamic-slice_fusion), channel_id=1, source_target_pairs={{0,1},{1,0},{2,3},{3,2},{4,5},{5,4},{6,7},{7,6},{8,9},{9,8},{10,11... | collective-permute-start | bytes 786440 | tf_op jit(solution)/shard_map/ppermute | solution.py:122
  577.5 7.8 %collective-permute-start = (bf16[32,4096]{1,0:T(8,128)(2,1)S(1)}, bf16[32,4096]{1,0:T(8,128)(2,1)S(1)}, u32[]{:S(2)}, u32[]{:S(2)}) collective-permute-start(bf16[32,4096]{1,0:T(8,128)(2,1)S(1)} %constant_dynamic-slice_fusion.2), channel_id=1, source_target_pairs={{0,1},{1,0},{2,3},{3,2},{4,5},{5,4},{6,7},{7,6},{8,9},{9,8},{10,11... | collective-permute-start | bytes 786440 | tf_op jit(solution)/shard_map/ppermute | solution.py:122
  (46 other events, 331.1 us)
Sparse Core Ops, SparseCore 0:
  11.6 132.3 all-gather.7
  147.0 75.2 all-gather.9
  257.8 103.0 reduce-scatter.5
  364.8 104.3 reduce-scatter.7
  473.2 103.3 reduce-scatter.3

commit v12 on v10

--- a/solution.py
+++ b/solution.py
@@ -46,46 +46,70 @@
     return places[None, :] < block_limits(scale_tokens)[:, None]
 
 
-def attn_kernel(limit_ref, q_ref, k_ref, v_ref, ctx_ref, lse_ref):
+def attn_kernel(
+    limit_ref, q_ref, k_ref, v_ref, qb_ref, vb_ref, qg_ref, kg_ref,
+    ctx_ref, lse_ref, qo_ref, ko_ref, vo_ref,
+):
     length = q_ref.shape[0]
     dim = q_ref.shape[1] // 2
     cols = lax.broadcasted_iota(jnp.int32, (length, length), 1)
     allowed = cols < limit_ref[...]
-    outs = []
+    query_all = q_ref[...] + qb_ref[...]
+    key_all = k_ref[...]
+    value = (v_ref[...] + vb_ref[...]).astype(jnp.bfloat16)
+    vo_ref[...] = value
+    outs, queries, keys = [], [], []
     for i in range(2):
-        q = q_ref[:, i * dim : (i + 1) * dim]
-        k = k_ref[:, i * dim : (i + 1) * dim]
-        v = v_ref[:, i * dim : (i + 1) * dim]
+        part = slice(i * dim, (i + 1) * dim)
+        qp = query_all[:, part]
+        kp = key_all[:, part]
+        q = (qp * lax.rsqrt(jnp.mean(qp * qp, axis=1, keepdims=True) + EPSILON) * qg_ref[:, part]).astype(jnp.bfloat16)
+        k = (kp * lax.rsqrt(jnp.mean(kp * kp, axis=1, keepdims=True) + EPSILON) * kg_ref[:, part]).astype(jnp.bfloat16)
+        queries.append(q)
+        keys.append(k)
         s = lax.dot_general(q, k, (((1,), (1,)), ((), ())), preferred_element_type=jnp.float32)
         s = jnp.where(allowed, s * dim ** (-0.5), MASKED)
         m = jnp.max(s, axis=1, keepdims=True)
         e = jnp.exp(s - m)
         l = jnp.sum(e, axis=1, keepdims=True)
         p = (e / l).astype(jnp.bfloat16)
-        outs.append(jnp.dot(p, v, preferred_element_type=jnp.float32).astype(jnp.bfloat16))
+        outs.append(jnp.dot(p, value[:, part], preferred_element_type=jnp.float32).astype(jnp.bfloat16))
         lse_ref[i] = m + jnp.log(l)
     ctx_ref[...] = jnp.concatenate(outs, axis=1)
-
-
-def attention_forward(queries, keys, values, limits, heads):
-    length, width = queries.shape
+    qo_ref[...] = jnp.concatenate(queries, axis=1)
+    ko_ref[...] = jnp.concatenate(keys, axis=1)
+
+
+def attention_forward(projected, query_bias, value_bias, query_gain, key_gain, limits, heads):
+    length = projected.shape[0]
+    width = projected.shape[1] // 3
     pair = 2 * (width // heads)
+    pairs = heads // 2
     spec = pl.BlockSpec((length, pair), lambda h: (0, h))
+    vec = pl.BlockSpec((1, pair), lambda h: (0, h))
+    wide = jax.ShapeDtypeStruct((length, width), jnp.bfloat16)
     return pl.pallas_call(
         attn_kernel,
-        grid=(heads // 2,),
-        in_specs=[pl.BlockSpec((length, 1), lambda h: (0, 0)), spec, spec, spec],
-        out_specs=[spec, pl.BlockSpec((2, length, 1), lambda h: (h, 0, 0))],
-        out_shape=[
-            jax.ShapeDtypeStruct((length, width), jnp.bfloat16),
-            jax.ShapeDtypeStruct((heads, length, 1), jnp.float32),
+        grid=(pairs,),
+        in_specs=[
+            pl.BlockSpec((length, 1), lambda h: (0, 0)),
+            spec,
+            pl.BlockSpec((length, pair), lambda h: (0, h + pairs)),
+            pl.BlockSpec((length, pair), lambda h: (0, h + 2 * pairs)),
+            vec, vec, vec, vec,
         ],
+        out_specs=[spec, pl.BlockSpec((2, length, 1), lambda h: (h, 0, 0)), spec, spec, spec],
+        out_shape=[wide, jax.ShapeDtypeStruct((heads, length, 1), jnp.float32), wide, wide, wide],
         cost_estimate=pl.CostEstimate(
             flops=4 * length * length * width,
             transcendentals=heads * length * length,
-            bytes_accessed=4 * length * width * 2 + heads * length * 4,
+            bytes_accessed=length * width * (12 + 8) + heads * length * 4,
         ),
-    )(limits, queries, keys, values)
+    )(
+        limits, projected, projected, projected,
+        query_bias.reshape(1, width), value_bias.reshape(1, width),
+        query_gain.reshape(1, width), key_gain.reshape(1, width),
+    )
 
 
 def matmul_rows(first_operand, second_operand):
@@ -238,17 +262,19 @@
     projected = matmul_rows(normed_attn, qkv_full)
     query_pre = projected[..., :width] + query_bias
     key_pre = projected[..., width : 2 * width]
-    queries = head_norm(query_pre, query_gain).astype(jnp.bfloat16)
-    key_rows = head_norm(key_pre, key_gain).astype(jnp.bfloat16)
-    value_rows = (projected[..., 2 * width :] + value_bias).astype(jnp.bfloat16).reshape(head_shape)
     limits = block_limits(scale_tokens).astype(jnp.int32)[:, None]
-    context, logsum = attention_forward(
-        queries.reshape(length, width),
-        key_rows.reshape(length, width),
-        value_rows.reshape(length, width),
+    context, logsum, queries, key_rows, value_rows = attention_forward(
+        projected.reshape(length, 3 * width),
+        query_bias,
+        value_bias,
+        query_gain,
+        key_gain,
         limits,
         HEADS,
     )
+    queries = queries.reshape(head_shape)
+    key_rows = key_rows.reshape(head_shape)
+    value_rows = value_rows.reshape(head_shape)
     context = context.reshape(sequences, length, width)
     logsum = logsum.reshape(sequences, HEADS, length)
     attended = matmul_rows(context, proj_full) + proj_bias

time: 769 us -> 762 us (level)
  Pallas kernels: 31 us -> 50.1 us
  other arithmetic: 83.9 us -> 70.7 us
    pallas_call x1, Pallas kernels: 31 us -> 50.1 us  [attention_forward(): pl.pallas_call(attn_kernel, grid=(pairs,), in_specs=[pl.BlockSpec((length...]
    convert_element_type x2 -> x0, other arithmetic: 10.6 us -> none  [the longest x1 6.69 us: layer(): key_rows = head_norm(key_pre, key_gain).astype(jnp.bfloat16)]
    mul x4 -> x2, local copies, waits for them, and re-layouts: 10.9 us -> 1.33 us  [head_norm(): return scaled * channel_gain.reshape(HEADS, HEAD_DIM)]
    pallas_call x0 -> x3, local copies, waits for them, and re-layouts: none -> 7.78 us  [attention_forward(): pl.pallas_call(attn_kernel, grid=(pairs,), in_specs=[pl.BlockSpec((length...]
  transfers between devices with their start and end apart: 11 -> 11, of which waited for: 6 -> 6; matrix products, arithmetic and copies ran while one was open for 19% -> 18% of each run, Pallas kernels for 4% -> 7%
where the time goes in v12:
time: 762 us; the launch traced here: 757 us
  waiting for transfers between devices  293 us (38%)
  matrix products  210 us (28%)
  other arithmetic  70.7 us (9%)
  blocking collectives  56 us (7%)
  Pallas kernels  50.1 us (7%)
  local copies, waits for them, and re-layouts  47.2 us (6%)
  between operations  15.2 us (2%)
  starting transfers between devices  14.8 us (2%)
    reduce_scatter x3, waiting for transfers between devices, scatter_natural(): lax.psum_scatter(member.astype(jnp.bfloat16), 'wide', scatter_dimension=0...  198 us
    all_gather x1, waiting for transfers between devices, layer(): lax.all_gather(jnp.concatenate([w_qkv, w_proj, w_up], axis=1), AXES, axis...  56.7 us
    pallas_call x1, Pallas kernels, attention_forward(): pl.pallas_call(attn_kernel, grid=(pairs,), in_specs=[pl.BlockSpec((length...  50.1 us
    all_gather x2, blocking collectives, nested_gather(): lax.all_gather(lax.all_gather(member, 'narrow', axis=0, tiled=True), 'wid...  46.2 us
    dot_general x4, matrix products, matmul_back(): jnp.einsum('rfw,uw->rfu', first_operand, second_operand, preferred_elemen...  42.1 us
    dot_general x4, matrix products, matmul_rows(): jnp.einsum('fyg,gq->fyq', first_operand, second_operand, preferred_elemen...  41.8 us
    dot_general x4, matrix products, weight_grad(): jnp.einsum('crk,cre->ke', first_operand, second_operand, preferred_elemen...  39.3 us
    dot_general x1, matrix products, attend_backward(): jnp.einsum('nkz,vkz->knv', context_gradient, value_sequence, preferred_el...  28.1 us
  transfers between devices with their start and end apart: 11, of which 6 were waited for; matrix products, arithmetic and copies ran while one was open for 18% of the time, Pallas kernels for 7%

profile of v12, /device:TPU:0, one launch (start us, length us, event | category | flops | bytes accessed | tf_op | source)
XLA Modules:
  0.0 757.2 jit_solution(8212602937556805828)
XLA Ops:
  11.2 5.4 concatenate.51
  16.7 5.3 all-gather.1
  22.0 22.8 %all-gather.2 = bf16[16,2,1536]{2,1,0:T(2,128)(2,1)S(1)} all-gather(bf16[1,2,1536]{2,1,0:T(2,128)(2,1)S(1)} %bitcast.205), channel_id=1, replica_groups=mesh['wide'=16,'narrow'=2] {'wide'}, dimensions={0}, use_global_device_ids=true | all-gather | bytes 104448 | tf_op jit(solution)/shard_map/all_gather | solution.py:168
  58.4 27.8 %all-to-all-done = f32[32,1,6144]{2,1,0:T(1,128)S(1)} async-done(((f32[32,1,6144]{2,1,0:T(1,128)}), f32[32,1,6144]{2,1,0:T(1,128)S(1)}, u32[]{:S(2)}, u32[]{:S(2)}) %all-to-all-start) | async-done | bytes 786464 | tf_op jit(solution)/shard_map/all_to_all | solution.py:254
  87.3 56.7 %all-gather.8.cloned.1.call-done = bf16[1024,8192]{1,0:T(8,128)(2,1)} async-done(((bf16[32,8192]{1,0:T(8,128)(2,1)}), bf16[1024,8192]{1,0:T(8,128)(2,1)}) %all-gather.8.cloned.1.call-update) | async-done | bytes 16777232 | tf_op jit(solution)/shard_map/all_gather | solution.py:240
  144.0 7.8 %fusion.17.q_ref.k_ref.v_ref = f32[680,3072]{1,0:T(8,128)S(1)} fusion(bf16[1024,8192]{1,0:T(8,128)(2,1)} %all-gather.8.cloned.1.call-done, bf16[1,680,1024]{2,1,0:T(8,128)(2,1)S(1)} %copy-done.6, f32[1024]{0:T(1024)S(1)} %bitcast.216, f32[1024]{0:T(1024)S(1)} %bitcast.199, f32[680]{0:T(1024)S(1)} %fusion.69, f32[680]{0:T(1024)S(1)} %broadcast_multiply_fusion.3), kind=kOutput, calls=%fused_computation.28 | convolution fusion | flops 4282368000 | bytes 16053568 | tf_op jit(solution)/shard_map/fyg,gq->fyq/dot_general | solution.py:116
  160.6 50.1 %shard_map.288 = (bf16[680,1024]{1,0:T(8,128)(2,1)}, f32[16,680,1]{2,1,0:T(8,128)}, bf16[680,1024]{1,0:T(8,128)(2,1)}, bf16[680,1024]{1,0:T(8,128)(2,1)}, bf16[680,1024]{1,0:T(8,128)(2,1)}) custom-call(s32[680,1]{1,0:T(8,128)} %broadcast_in_dim.53.limit_ref, f32[680,3072]{1,0:T(8,128)} %copy-done.1, f32[680,3072]{1,0:T(8,128)} %copy-done.1, ...), custom_call_target="tpu_custom_call" | custom-call | flops 1893990400 | bytes 13969920 | tf_op jit(solution)/shard_map/pallas_call | solution.py:91
  218.5 5.9 fusion.84
  226.1 12.7 %fusion.13 = f32[680,4096]{1,0:T(8,128)} fusion(bf16[1024,8192]{1,0:T(8,128)(2,1)} %all-gather.8.cloned.1.call-done, f32[1,680,1024]{2,1,0:T(8,128)S(1)} %get-tuple-element.44, f32[1024]{0:T(1024)S(1)} %bitcast.211, f32[1024]{0:T(1024)S(1)} %bitcast.206, f32[680]{0:T(1024)S(1)} %fusion.70, f32[680]{0:T(1024)S(1)} %broadcast_multiply_fusion.2), kind=kOutput, calls=%fused_computation.22 | convolution fusion | flops 5707735040 | bytes 22328640 | tf_op jit(solution)/shard_map/fyg,gq->fyq/dot_general | solution.py:116
  238.8 17.3 %convert_reduce_fusion = (f32[4096]{0:T(1024)}, bf16[680,4096]{1,0:T(8,128)(2,1)S(1)}) fusion(f32[680,4096]{1,0:T(8,128)} %fusion.13, f32[4096]{0:T(1024)S(1)} %copy-done.43, bf16[4096,1024]{1,0:T(8,128)(2,1)} %all-gather.10.cloned.1.call-done, f32[1024]{0:T(1024)S(1)} %bitcast.213, bf16[1,680,1024]{2,1,0:T(8,128)(2,1)S(1)} %copy-done.19), kind=kOutput, calls=%fused_computation.15 | convolution fusion | flops 5770399744 | bytes 26529792 | tf_op jit(solution)/shard_map/rfw,uw->rfu/dot_general | solution.py:122
  256.2 11.7 %fusion.37 = (bf16[1024]{0:T(1024)(128)(2,1)}, f32[680]{0:T(1024)S(1)}, f32[680,1024]{1,0:T(8,128)S(1)}) fusion(f32[1,680,1024]{2,1,0:T(8,128)S(1)} %copy-done.13, f32[680]{0:T(1024)S(1)} %fusion.70, f32[680]{0:T(1024)S(1)} %broadcast_multiply_fusion.2, f32[1024]{0:T(1024)S(1)} %bitcast.207, bf16[680,4096]{1,0:T(8,128)(2,1)S(1)} %get-tuple-element.86, ...), kind=kOutput, calls=%fused_computation.75 | convolution fusion | flops 5709126144 | bytes 19544032 | tf_op jit(solution)/shard_map/rfw,uw->rfu/dot_general | solution.py:122
  271.3 15.4 %convert_reduce_fusion.2 = (f32[1024]{0:T(1024)}, bf16[1024]{0:T(1024)(128)(2,1)}, bf16[1024]{0:T(1024)(128)(2,1)}, f32[1024]{0:T(1024)}, bf16[1,680,1024]{2,1,0:T(8,128)(2,1)S(1)}, /*index=5*/bf16[1,680,1024]{2,1,0:T(8,128)(2,1)}) fusion(f32[1024]{0:T(1024)S(1)} %bitcast.214, bf16[1,680,1024]{2,1,0:T(8,128)(2,1)S(1)} %copy-done.19, ...), kind=kOutput, calls=%fused_computation.82 | convolution fusion | flops 5746028544 | bytes 32111264 | tf_op jit(solution)/shard_map/fyg,gq->fyq/dot_general | solution.py:116
  293.0 4.4 reduce.31
  297.4 17.0 %fusion.86 = f32[16,680,680]{1,2,0:T(8,128)} fusion(bf16[680,16,64]{0,2,1:T(8,128)(2,1)} %bitcast.188, bf16[680,16,64]{0,2,1:T(8,128)(2,1)S(1)} %bitcast.186), kind=kOutput, calls=%fused_computation.177 | convolution fusion | flops 946995200 | bytes 32378880 | tf_op jit(solution)/shard_map/vmap(nkz,vkz->knv)/dot_general | solution.py:134
  314.5 17.4 %bitcast_convert_fusion = (bf16[1,680,16,64]{1,3,2,0:T(8,128)(2,1)}, f32[16,64,680]{2,1,0:T(8,128)}) fusion(bf16[680,16,64]{0,2,1:T(8,128)(2,1)} %bitcast.191, f32[16,680,680]{1,2,0:T(8,128)} %fusion.86, f32[16,680]{1,0:T(8,128)S(1)} %reduce.31, pred[680,680]{0,1:T(8,128)(4,1)S(1)} %copy-done.15), kind=kOutput, calls=%fused_computation.53 | convolution fusion | flops 977285120 | bytes 35670080 | tf_op jit(solution)/shard_map/vmap(fgs,gfu->sfu)/dot_general | solution.py:148
  331.9 28.1 %multiply_reduce_fusion = (f32[16,680]{1,0:T(8,128)S(1)}, f32[16,680,680]{1,2,0:T(8,128)}) fusion(f32[16,680,680]{1,2,0:T(8,128)} %fusion.86, f32[16,680]{1,0:T(8,128)S(1)} %reduce.31, pred[680,680]{0,1:T(8,128)(4,1)S(1)} %copy-done.15, bf16[680,16,64]{0,2,1:T(8,128)(2,1)} %bitcast.192, bf16[680,16,64]{0,2,1:T(8,128)(2,1)} %bitcast.190), kind=kOutput, calls=%fused_computation.1 | convolution fusion | flops 983976320 | bytes 62521920 | tf_op jit(solution)/shard_map/vmap(nkz,vkz->knv)/dot_general | solution.py:145
  360.0 27.7 %multiply_convert_fusion = bf16[16,680,680]{1,2,0:T(8,128)(2,1)} fusion(f32[16,680,680]{1,2,0:T(8,128)} %get-tuple-element.80, f32[16,680,680]{1,2,0:T(8,128)} %fusion.86, f32[16,680]{1,0:T(8,128)S(1)} %get-tuple-element.79, f32[16,680]{1,0:T(8,128)S(1)} %reduce.31, pred[680,680]{0,1:T(8,128)(4,1)S(1)} %copy-done.15), kind=kLoop, calls=%fused_computation | loop fusion | flops 44390400 | bytes 74533440 | tf_op jit(solution)/shard_map/vmap()/convert_element_type | solution.py:157
  387.7 12.3 %fusion.26 = (f32[16,64]{1,0:T(8,128)S(1)}, f32[680,16]{0,1:T(8,128)}, f32[16,64,680]{2,1,0:T(8,128)}) fusion(f32[1,680,16,64]{1,3,2,0:T(8,128)} %bitcast.185, f32[680,16]{0,1:T(8,128)} %fusion.62, f32[16,64]{1,0:T(8,128)S(1)} %copy-done.25, bf16[680,16,64]{0,2,1:T(8,128)(2,1)} %bitcast.189, bf16[16,680,680]{1,2,0:T(8,128)(2,1)} %multiply_convert_fusion), kind=kOutput, calls=%fused_computation.49 | convolution fusion | flops 951857536 | bytes 21855232 | tf_op jit(solution)/shard_map/vmap(fgs,gfu->sfu)/dot_general | solution.py:161
  400.9 7.6 %multiply_reduce_fusion.2 = (f32[680,16]{0,1:T(8,128)S(1)}, f32[680,16]{0,1:T(8,128)S(1)}, f32[16,64,680]{2,1,0:T(8,128)S(1)}) fusion(f32[1,680,16,64]{1,3,2,0:T(8,128)S(1)} %bitcast.182, f32[16,64]{1,0:T(8,128)S(1)} %copy-done.23, bf16[680,16,64]{0,2,1:T(8,128)(2,1)S(1)} %bitcast.187, bf16[16,680,680]{1,2,0:T(8,128)(2,1)} %multiply_convert_fusion), kind=kOutput, calls=%fused_computation.65 | convolution fusion | flops 950455040 | bytes 21851136 | tf_op jit(solution)/shard_map/vmap(wcv,vwn->cwn)/dot_general | solution.py:158
  412.6 11.1 %convolution_convert_fusion.2 = bf16[1024,3072]{1,0:T(8,128)(2,1)} fusion(bf16[680,1024]{0,1:T(8,128)(2,1)S(1)} %bitcast.223, bf16[680,1024]{0,1:T(8,128)(2,1)S(1)} %bitcast.195, bf16[680,1024]{0,1:T(8,128)(2,1)S(1)} %bitcast.193, bf16[1,680,1024]{2,1,0:T(8,128)(2,1)S(1)} %copy-done.7, f32[1024]{0:T(1024)S(1)} %bitcast.217, f32[1024]{0:T(1024)S(1)} %bitcast.200, ...), kind=kOutput, calls=%fused_computation.25 | convolution fusion | flops 4298047488 | bytes 11875648 | tf_op jit(solution)/shard_map/crk,cre->ke/dot_general | solution.py:128
  425.0 14.0 %convolution_convert_fusion = bf16[4096,1024]{1,0:T(8,128)(2,1)} fusion(bf16[1,680,1024]{2,1,0:T(8,128)(2,1)S(1)} %copy-done.20, f32[1024]{0:T(1024)S(1)} %bitcast.215, f32[680,4096]{1,0:T(8,128)} %fusion.13, f32[4096]{0:T(1024)S(1)} %copy-done.44), kind=kOutput, calls=%fused_computation.18 | convolution fusion | flops 5738389504 | bytes 20942848 | tf_op jit(solution)/shard_map/crk,cre->ke/dot_general | solution.py:128
  443.2 10.2 %convolution_convert_fusion.1 = bf16[1024,4096]{1,0:T(8,128)(2,1)S(1)} fusion(bf16[680,4096]{1,0:T(8,128)(2,1)} %copy-done.66, f32[1,680,1024]{2,1,0:T(8,128)S(1)} %copy-done.14, f32[1024]{0:T(1024)S(1)} %bitcast.212, f32[1024]{0:T(1024)S(1)} %bitcast.209, f32[680]{0:T(1024)S(1)} %copy-done.41, f32[680]{0:T(1024)S(1)} %copy-done.31), kind=kOutput, calls=%fused_computation.19 | convolution fusion | flops 5711929344 | bytes 16758080 | tf_op jit(solution)/shard_map/crk,cre->ke/dot_general | solution.py:128
  453.4 7.9 %pad_maximum_fusion = bf16[1024,5120]{1,0:T(8,128)(2,1)} fusion(bf16[1024,1024]{1,0:T(8,128)(2,1)S(1)} %convolution_convert_fusion.3, bf16[1024,4096]{1,0:T(8,128)(2,1)S(1)} %convolution_convert_fusion.1), kind=kLoop, calls=%fused_computation.17 | loop fusion | flops 20971520 | bytes 20971520 | tf_op jit(solution)/shard_map/concatenate | solution.py:324
  463.3 9.9 %fusion.34 = (f32[680]{0:T(1024)S(1)}, f32[680,1024]{1,0:T(8,128)S(1)}) fusion(bf16[1,680,1024]{2,1,0:T(8,128)(2,1)} %param.17, f32[1024]{0:T(1024)S(1)} %bitcast.201, f32[680]{0:T(1024)S(1)} %copy-done.29, bf16[1024,8192]{1,0:T(8,128)(2,1)} %all-gather.8.cloned.1.call-done, bf16[680,1024]{0,1:T(8,128)(2,1)} %bitcast.222, bf16[680,1024]{0,1:T(8,128)(2,1)} %bitcast.196, ...), kind=kOutput, calls=%fused_computation.70 | convolution fusion | flops 4294204672 | bytes 15197504 | tf_op jit(solution)/shard_map/rfw,uw->rfu/dot_general | solution.py:122
  476.6 4.5 all-gather.3
  481.1 23.4 %all-gather.4 = bf16[16,2,6144]{2,1,0:T(2,128)(2,1)} all-gather(bf16[1,2,6144]{2,1,0:T(2,128)(2,1)S(1)} %bitcast.198), channel_id=1, replica_groups=mesh['wide'=16,'narrow'=2] {'wide'}, dimensions={0}, use_global_device_ids=true | all-gather | bytes 417792 | tf_op jit(solution)/shard_map/all_gather | solution.py:168
  513.1 4.4 add_add_fusion.4
  520.8 5.8 all-to-all-start.2
  528.5 5.6 all-to-all-done.2
  536.8 77.6 %reduce-scatter.8.cloned.1.call-done = bf16[256,1024]{1,0:T(8,128)(2,1)} async-done(((bf16[4096,1024]{1,0:T(8,128)(2,1)}), bf16[256,1024]{1,0:T(8,128)(2,1)}) %reduce-scatter.8.cloned.1.call-update) | async-done | bytes 524304 | tf_op jit(solution)/shard_map/reduce_scatter | solution.py:186
  617.0 120.5 %reduce-scatter.6.cloned.1.call-done = bf16[64,5120]{1,0:T(8,128)(2,1)} async-done(((bf16[1024,5120]{1,0:T(8,128)(2,1)}), bf16[64,5120]{1,0:T(8,128)(2,1)}) %reduce-scatter.6.cloned.1.call-update) | async-done | bytes 655376 | tf_op jit(solution)/shard_map/reduce_scatter | solution.py:186
  743.6 4.1 collective-permute-done.1
  (251 shorter events, 89.3 us)
Async XLA Ops:
  7.2 37.7 %copy-start = (bf16[32,6144]{1,0:T(8,128)(2,1)S(1)}, bf16[32,6144]{1,0:T(8,128)(2,1)}, u32[]{:S(2)}) copy-start(bf16[32,6144]{1,0:T(8,128)(2,1)} %param.20) | copy-start | bytes 1179652
  7.2 136.8 %all-gather.8.cloned.1.call-start = ((), (), s32[]{:S(2)}) async-start(), calls=%async_computation.6 | async-start | bytes 17301504 | tf_op jit(solution)/shard_map/all_gather | solution.py:240
  9.2 41.3 %copy-start.63 = (s32[10]{0:T(128)S(1)}, s32[10]{0:T(128)}, u32[]{:S(2)}) copy-start(s32[10]{0:T(128)} %param.19) | copy-start | bytes 124
  9.2 229.6 %all-gather.10.cloned.1.call-start = ((), (), s32[]{:S(2)}) async-start(), calls=%async_computation.7 | async-start | bytes 8650752 | tf_op jit(solution)/shard_map/all_gather | solution.py:247
  46.9 39.3 %all-to-all-start = ((f32[32,1,6144]{2,1,0:T(1,128)}), f32[32,1,6144]{2,1,0:T(1,128)S(1)}, u32[]{:S(2)}, u32[]{:S(2)}) async-start(f32[32,1,6144]{2,1,0:T(1,128)} %copy.87), calls=%async_computation | async-start | bytes 1572864 | tf_op jit(solution)/shard_map/all_to_all | solution.py:254
  49.5 485.8 %reduce-scatter.4.cloned.1.call-start = ((), (), s32[]{:S(2)}) async-start(), calls=%async_computation.8 | async-start | bytes 6684672 | tf_op jit(solution)/shard_map/reduce_scatter | solution.py:186
  52.8 165.7 %copy-start.56 = (f32[1024]{0:T(1024)}, f32[1024]{0:T(1024)S(1)}, u32[]{:S(2)}) copy-start(f32[1024]{0:T(1024)S(1)} %reshape.850) | copy-start | bytes 12292
  56.1 95.7 %copy-start.28 = (f32[680]{0:T(1024)}, f32[680]{0:T(1024)S(1)}, u32[]{:S(2)}) copy-start(f32[680]{0:T(1024)S(1)} %broadcast_multiply_fusion.3) | copy-start | bytes 8164
  56.6 95.2 %copy-start.32 = (f32[680]{0:T(1024)}, f32[680]{0:T(1024)S(1)}, u32[]{:S(2)}) copy-start(f32[680]{0:T(1024)S(1)} %fusion.33) | copy-start | bytes 8164
  56.6 95.2 %copy-start.26 = (f32[680]{0:T(1024)}, f32[680]{0:T(1024)S(1)}, u32[]{:S(2)}) copy-start(f32[680]{0:T(1024)S(1)} %fusion.69) | copy-start | bytes 8164
  87.3 64.5 %copy-start.34 = (f32[1,1024]{1,0:T(1,128)}, f32[1,1024]{1,0:T(1,128)S(1)}, u32[]{:S(2)}) copy-start(f32[1,1024]{1,0:T(1,128)S(1)} %get-tuple-element.67) | copy-start | bytes 12292
  87.3 64.5 %copy-start.53 = (f32[1,1024]{1,0:T(1,128)}, f32[1,1024]{1,0:T(1,128)S(1)}, u32[]{:S(2)}) copy-start(f32[1,1024]{1,0:T(1,128)S(1)} %get-tuple-element.66) | copy-start | bytes 12292
  87.3 131.2 %copy-start.58 = (f32[1,1024]{1,0:T(1,128)}, f32[1,1024]{1,0:T(1,128)S(1)}, u32[]{:S(2)}) copy-start(f32[1,1024]{1,0:T(1,128)S(1)} %get-tuple-element.68) | copy-start | bytes 12292
  87.3 180.5 %copy-start.36 = (f32[1,1024]{1,0:T(1,128)}, f32[1,1024]{1,0:T(1,128)S(1)}, u32[]{:S(2)}) copy-start(f32[1,1024]{1,0:T(1,128)S(1)} %get-tuple-element.65) | copy-start | bytes 12292
  160.6 64.3 %copy-start.3 = (f32[1,680,1024]{1,2,0:T(8,128)}, f32[1,680,1024]{1,2,0:T(8,128)S(1)}, u32[]{:S(2)}) copy-start(f32[1,680,1024]{1,2,0:T(8,128)S(1)} %copy.96) | copy-start | bytes 8355844
  224.5 43.4 %copy-start.30 = (f32[680]{0:T(1024)}, f32[680]{0:T(1024)S(1)}, u32[]{:S(2)}) copy-start(f32[680]{0:T(1024)S(1)} %broadcast_multiply_fusion.2) | copy-start | bytes 8164
  224.9 43.0 %copy-start.40 = (f32[680]{0:T(1024)}, f32[680]{0:T(1024)S(1)}, u32[]{:S(2)}) copy-start(f32[680]{0:T(1024)S(1)} %fusion.70) | copy-start | bytes 8164
  238.8 17.4 %copy-start.13 = (f32[1,680,1024]{2,1,0:T(8,128)S(1)}, f32[1,680,1024]{2,1,0:T(8,128)}, u32[]{:S(2)}) copy-start(f32[1,680,1024]{2,1,0:T(8,128)} %copy-done.12) | copy-start | bytes 8355844
  269.4 17.3 %copy-start.9 = (f32[1,680,1024]{2,1,0:T(8,128)}, f32[1,680,1024]{2,1,0:T(8,128)S(1)}, u32[]{:S(2)}) copy-start(f32[1,680,1024]{2,1,0:T(8,128)S(1)} %get-tuple-element.42) | copy-start | bytes 8355844
  269.4 17.3 %copy-start.38 = (f32[680]{0:T(1024)}, f32[680]{0:T(1024)S(1)}, u32[]{:S(2)}) copy-start(f32[680]{0:T(1024)S(1)} %negate_multiply_fusion.1) | copy-start | bytes 8164
  297.4 17.0 %copy-start.15 = (pred[680,680]{0,1:T(8,128)(4,1)S(1)}, pred[680,680]{0,1:T(8,128)(4,1)}, u32[]{:S(2)}) copy-start(pred[680,680]{0,1:T(8,128)(4,1)} %iota_compare_fusion) | copy-start | bytes 1387204
  360.0 27.7 %copy-start.25 = (f32[16,64]{1,0:T(8,128)S(1)}, f32[16,64]{1,0:T(8,128)}, u32[]{:S(2)}) copy-start(f32[16,64]{1,0:T(8,128)} %mul.554) | copy-start | bytes 12292
  387.7 13.2 %copy-start.2 = (f32[1,680,1024]{1,2,0:T(8,128)S(1)}, f32[1,680,1024]{1,2,0:T(8,128)}, u32[]{:S(2)}) copy-start(f32[1,680,1024]{1,2,0:T(8,128)} %copy.94) | copy-start | bytes 8355844
  387.7 13.2 %copy-start.23 = (f32[16,64]{1,0:T(8,128)S(1)}, f32[16,64]{1,0:T(8,128)}, u32[]{:S(2)}) copy-start(f32[16,64]{1,0:T(8,128)} %mul.542) | copy-start | bytes 12292
  423.7 190.8 %reduce-scatter.8.cloned.1.call-start = ((), (), s32[]{:S(2)}) async-start(), calls=%async_computation.10 | async-start | bytes 8912896 | tf_op jit(solution)/shard_map/reduce_scatter | solution.py:186
  439.1 298.4 %reduce-scatter.6.cloned.1.call-start = ((), (), s32[]{:S(2)}) async-start(), calls=%async_computation.9 | async-start | bytes 11141120 | tf_op jit(solution)/shard_map/reduce_scatter | solution.py:186
  473.9 39.2 %copy-start.39 = (f32[680]{0:T(1024)S(1)}, f32[680]{0:T(1024)}, u32[]{:S(2)}) copy-start(f32[680]{0:T(1024)} %copy-done.38) | copy-start | bytes 8164
  508.3 12.5 %all-to-all-start.1 = ((f32[32,1,32]{2,1,0:T(1,128)}), f32[32,1,32]{2,1,0:T(1,128)S(1)}, u32[]{:S(2)}, u32[]{:S(2)}) async-start(f32[32,1,32]{2,1,0:T(1,128)} %bitcast.43), calls=%async_computation.1 | async-start | bytes 32768 | tf_op jit(solution)/shard_map/all_to_all | solution.py:411
  520.8 13.3 %all-to-all-start.2 = ((f32[32,1,320]{2,1,0:T(1,128)}), f32[32,1,320]{2,1,0:T(1,128)S(1)}, u32[]{:S(2)}, u32[]{:S(2)}) async-start(f32[32,1,320]{2,1,0:T(1,128)} %reshape.844), calls=%async_computation.3 | async-start | bytes 98304 | tf_op jit(solution)/shard_map/all_to_all | solution.py:192
  536.3 203.7 %collective-permute-start = (bf16[32,3072]{1,0:T(8,128)(2,1)S(1)}, bf16[32,3072]{1,0:T(8,128)(2,1)S(1)}, u32[]{:S(2)}, u32[]{:S(2)}) collective-permute-start(bf16[32,3072]{1,0:T(8,128)(2,1)S(1)} %constant_dynamic-slice_fusion.2), channel_id=1, source_target_pairs={{0,1},{1,0},{2,3},{3,2},{4,5},{5,4},{6,7},{7,6},{8,9},{9,8},{10,11... | collective-permute-start | bytes 589832 | tf_op jit(solution)/shard_map/ppermute | solution.py:181
  615.4 126.3 %collective-permute-start.2 = (bf16[128,1024]{1,0:T(8,128)(2,1)S(1)}, bf16[128,1024]{1,0:T(8,128)(2,1)S(1)}, u32[]{:S(2)}, u32[]{:S(2)}) collective-permute-start(bf16[128,1024]{1,0:T(8,128)(2,1)S(1)} %constant_dynamic-slice_fusion), channel_id=1, source_target_pairs={{0,1},{1,0},{2,3},{3,2},{4,5},{5,4},{6,7},{7,6},{8,9},{9,8},{10,11... | collective-permute-start | bytes 786440 | tf_op jit(solution)/shard_map/ppermute | solution.py:181
  738.5 9.2 %collective-permute-start.1 = (bf16[32,5120]{1,0:T(8,128)(2,1)S(1)}, bf16[32,5120]{1,0:T(8,128)(2,1)S(1)}, u32[]{:S(2)}, u32[]{:S(2)}) collective-permute-start(bf16[32,5120]{1,0:T(8,128)(2,1)S(1)} %constant_dynamic-slice_fusion.1), channel_id=1, source_target_pairs={{0,1},{1,0},{2,3},{3,2},{4,5},{5,4},{6,7},{7,6},{8,9},{9,8},{10,11... | collective-permute-start | bytes 983048 | tf_op jit(solution)/shard_map/ppermute | solution.py:181
  (47 other events, 190.9 us)
Sparse Core Ops, SparseCore 0:
  11.6 132.3 all-gather.7
  147.0 75.3 all-gather.9
  423.8 83.9 reduce-scatter.3
  511.7 102.7 reduce-scatter.7
  618.3 119.1 reduce-scatter.5
